TPU v7x, 32 devices: a whole 2x2x4 slice. The times are simulated.
32 devices in a mesh: fsdp: 8 (over z, x), tensor: 4 (over y, core).
Axes of the slice: x: 2, y: 2, z: 4, core: 2. Of those that a mesh axis runs over, the one named last changes fastest.
Arguments:
- hidden: bfloat16 [16384, 1024], P(('fsdp', 'tensor')), may hold values from -6 to 6
- out_grad: bfloat16 [16384, 1024], P(('fsdp', 'tensor')), may hold values from -6 to 6
- lengths: int32 [4, 3], replicated, may hold values from 0 to 4096, as said below
- q_weight: float32 [1024, 2048], P('fsdp', 'tensor'), may hold values from -0.1875 to 0.1875
- key_matrix: float32 [1024, 1024], P('fsdp', 'tensor'), may hold values from -0.1875 to 0.1875
- value_matrix: float32 [1024, 1024], P('fsdp', 'tensor'), may hold values from -0.1875 to 0.1875
- o_weight: float32 [2048, 1024], P('tensor', 'fsdp'), may hold values from -0.375 to 0.375
- gate_weight: float32 [1024, 3072], P('fsdp', 'tensor'), may hold values from -0.1875 to 0.1875
- up_weight: float32 [1024, 3072], P('fsdp', 'tensor'), may hold values from -0.1875 to 0.1875
- down_weight: float32 [3072, 1024], P('tensor', 'fsdp'), may hold values from -0.109375 to 0.109375
- input_gain: float32 [1024], P('fsdp'), may hold values from 0.1 to 1.9
- q_gain: float32 [128], P('fsdp'), may hold values from 1.2 to 1.8
- k_gain: float32 [128], P('fsdp'), may hold values from 1.2 to 1.8
- post_gain: float32 [1024], P('fsdp'), may hold values from 0.1 to 1.9
Outputs:
- output: bfloat16 [16384, 1024], P(('fsdp', 'tensor'))
- input_grad: bfloat16 [16384, 1024], P(('fsdp', 'tensor'))
- q_weight_grad: float32 [1024, 2048], P('fsdp', 'tensor')
- k_weight_grad: float32 [1024, 1024], P('fsdp', 'tensor')
- v_weight_grad: float32 [1024, 1024], P('fsdp', 'tensor')
- o_weight_grad: float32 [2048, 1024], P('tensor', 'fsdp')
- gate_weight_grad: float32 [1024, 3072], P('fsdp', 'tensor')
- up_weight_grad: float32 [1024, 3072], P('fsdp', 'tensor')
- down_weight_grad: float32 [3072, 1024], P('tensor', 'fsdp')
- input_gain_grad: float32 [1024], P('fsdp')
- q_gain_grad: float32 [128], P('fsdp')
- k_gain_grad: float32 [128], P('fsdp')
- post_gain_grad: float32 [1024], P('fsdp')
Inputs may be any that keep to these rules, and one draw needn't show every extreme that they name: `lengths`: row s lists the sequences packed from the start of slot s: its first one to 3 entries are 1024 or more, the rest are zero; a row sums to more than half of 4096 and at most 4096; row 0 holds one sequence of 4096.
All inputs are finite; a program needn't handle non-finite values.
Results may differ from a plain program's by a relative error of at most 0.022.
The roundings to bfloat16 on the way count: a program that leaves them out, or rounds other values in their place, can miss the bound.
Values may be sent and summed in bfloat16 or wider, within the bound.
No kernel may reach another device: no remote copies, remote signals or barrier semaphores. Data moves between devices by JAX's collectives and lax.ppermute only.
A program may use at most 192 MiB of HBM per device.

v0:
```python
import jax
import jax.numpy as jnp
from jax import lax
from jax.sharding import PartitionSpec as P

HEAD_SIZE = 128
SLOT_TOKENS = 4096
PIECES = 2


EPSILON = 1e-06
THETA = 1000000.0


def swapped(shard, axis, distance):
    return lax.ppermute(shard, axis, [(i, i ^ 1 << distance) for i in range(lax.axis_size(axis))])


def rms_scale(values, gain):
    inverse = lax.rsqrt(jnp.mean(values * values, axis=-1, keepdims=True) + EPSILON)
    return values * inverse * gain


def rotary(values, start_offset):
    half = values.shape[-1] // 2
    frequency = THETA ** (-(jnp.arange(half, dtype=jnp.float32) * 2.0 / values.shape[-1]))
    angle = start_offset.astype(jnp.float32)[:, None] * frequency[None, :]
    cosine = jnp.cos(angle)[:, None, :]
    sine = jnp.sin(angle)[:, None, :]
    first = values[..., :half]
    second = values[..., half:]
    return jnp.concatenate(
        [first * cosine - second * sine, second * cosine + first * sine], axis=-1
    )


def prepare_inputs(projected, gain, start_offset, head_groups):
    shaped = projected.reshape(projected.shape[0], head_groups, -1)
    return rotary(rms_scale(shaped, gain), start_offset)


def slot_tables(lengths_row, slot_length):
    ends = jnp.cumsum(lengths_row)
    place = jnp.arange(slot_length, dtype=jnp.int32)
    passed = place[:, None] >= ends[None, :]
    segment_ids = jnp.sum(passed.astype(jnp.int32), axis=1)
    start = jnp.sum(jnp.where(passed, lengths_row[None, :], 0), axis=1)
    return (segment_ids, place - start, place < ends[-1])


def piece_places(which, group_rows):
    quarter = group_rows // 2
    local = jnp.arange(group_rows, dtype=jnp.int32)
    chosen = jnp.where(local < quarter, which, 3 - which)
    return chosen * quarter + local % quarter


def contract_rows(left, right):
    return lax.dot_general(
        left, right, (((0,), (0,)), ((), ())), preferred_element_type=jnp.float32
    )


def contract_last(left, right):
    return lax.dot_general(
        left, right, (((1,), (1,)), ((), ())), preferred_element_type=jnp.float32
    )


def token_gather(values):
    return lax.all_gather(values, "tensor", axis=0, tiled=True)


def token_sum(term, rows):
    return lax.psum_scatter(
        term(jnp.int32(0), rows * lax.axis_size("tensor")).astype(jnp.bfloat16),
        "tensor",
        scatter_dimension=0,
        tiled=True,
    ).astype(jnp.float32)


def block_weights(query_block, key_rows, query_segment, query_place, key_segment, key_place, scale):
    scores = (
        jnp.einsum("qkgd,nkd->kgqn", query_block, key_rows, preferred_element_type=jnp.float32)
        * scale
    )
    allowed = (query_segment[:, None] == key_segment[None, :]) & (
        key_place[None, :] <= query_place[:, None]
    )
    return jnp.where(allowed[None, None], jnp.exp(scores), 0.0)


def forward_block(query_block, query_segment, query_place, key_sets, scale, size):
    kv_heads = query_block.shape[1]
    share = query_block.shape[2]
    summed = jnp.zeros(query_block.shape, jnp.float32)
    total = jnp.zeros((kv_heads, share, size), jnp.float32)
    for key_rows, values, key_segment, key_place in key_sets:

        def forward_add_block(index, state):
            summed_now, total_now = state
            begin = index * size
            key_part = lax.dynamic_slice_in_dim(key_rows, begin, size, 0)
            value_part = lax.dynamic_slice_in_dim(values, begin, size, 0)
            segment_part = lax.dynamic_slice_in_dim(key_segment, begin, size, 0)
            place_part = lax.dynamic_slice_in_dim(key_place, begin, size, 0)
            weights = block_weights(
                query_block, key_part, query_segment, query_place, segment_part, place_part, scale
            )
            total_now = total_now + jnp.sum(weights, axis=-1)
            summed_now = summed_now + jnp.einsum(
                "kgqn,nkd->qkgd",
                weights.astype(jnp.bfloat16),
                value_part,
                preferred_element_type=jnp.float32,
            )
            return (summed_now, total_now)

        summed, total = lax.fori_loop(
            0, key_rows.shape[0] // size, forward_add_block, (summed, total)
        )
    return (summed / jnp.transpose(total, (2, 0, 1))[..., None], total)


def shards(
    hidden,
    out_grad,
    lengths,
    q_weight,
    key_matrix,
    value_matrix,
    o_weight,
    gate_weight,
    up_weight,
    down_weight,
    input_gain,
    q_gain,
    k_gain,
    post_gain,
):
    split = lax.axis_size("tensor")
    rows = hidden.shape[0]
    group_rows = rows * split
    q_heads = q_weight.shape[1] // HEAD_SIZE
    kv_heads = key_matrix.shape[1] // HEAD_SIZE
    share = q_heads // kv_heads
    scale = HEAD_SIZE ** (-0.5)
    size = min(512, group_rows)
    blocks = group_rows // size
    member = lax.axis_index("fsdp")
    slot = member // PIECES
    piece = member % PIECES
    segment_ids, start_offset, valid = slot_tables(
        lax.dynamic_index_in_dim(lengths, slot, 0, keepdims=False), SLOT_TOKENS
    )
    group_place = piece_places(piece, group_rows)
    group_segment = jnp.take(segment_ids, group_place)
    group_offset = jnp.take(start_offset, group_place)
    local_valid = lax.dynamic_slice_in_dim(
        jnp.take(valid, group_place), lax.axis_index("tensor") * rows, rows, 0
    )
    attn_gathered = (
        lax.all_gather(q_weight.astype(jnp.bfloat16), "fsdp", axis=0, tiled=True),
        lax.all_gather(key_matrix.astype(jnp.bfloat16), "fsdp", axis=0, tiled=True),
        lax.all_gather(value_matrix.astype(jnp.bfloat16), "fsdp", axis=0, tiled=True),
        lax.all_gather(jnp.transpose(o_weight).astype(jnp.bfloat16), "fsdp", axis=0, tiled=True),
        lax.all_gather(input_gain.astype(jnp.bfloat16), "fsdp", axis=0, tiled=True),
        lax.all_gather(q_gain.astype(jnp.bfloat16), "fsdp", axis=0, tiled=True),
        lax.all_gather(k_gain.astype(jnp.bfloat16), "fsdp", axis=0, tiled=True),
    )
    w_query, w_key, w_value, w_out, gain_in, gain_query, gain_keys = attn_gathered
    x_float = hidden.astype(jnp.float32)
    gain_first = gain_in.astype(jnp.float32)
    first_all = token_gather(rms_scale(x_float, gain_first).astype(jnp.bfloat16))
    query_projected = jnp.dot(first_all, w_query, preferred_element_type=jnp.float32)
    key_projected = jnp.dot(first_all, w_key, preferred_element_type=jnp.float32)
    value_rows = (
        jnp.dot(first_all, w_value, preferred_element_type=jnp.float32)
        .astype(jnp.bfloat16)
        .reshape(group_rows, kv_heads, HEAD_SIZE)
    )
    gain_q = gain_query.astype(jnp.float32)
    gain_k = gain_keys.astype(jnp.float32)
    query_rope = (
        prepare_inputs(query_projected, gain_q, group_offset, q_heads)
        .astype(jnp.bfloat16)
        .reshape(group_rows, kv_heads, share, HEAD_SIZE)
    )
    key_rope = prepare_inputs(key_projected, gain_k, group_offset, kv_heads).astype(jnp.bfloat16)
    moved = swapped(jnp.stack([key_rope, value_rows]), "fsdp", 0)
    far_place = piece_places(1 - piece, group_rows)
    far_segment = jnp.take(segment_ids, far_place)
    key_sets = [
        (key_rope, value_rows, group_segment, group_place),
        (moved[0], moved[1], far_segment, far_place),
    ]

    def forward_rows(index):
        begin = index * size
        query_block = lax.dynamic_slice_in_dim(query_rope, begin, size, 0)
        query_segment = lax.dynamic_slice_in_dim(group_segment, begin, size, 0)
        query_place = lax.dynamic_slice_in_dim(group_place, begin, size, 0)
        return forward_block(query_block, query_segment, query_place, key_sets, scale, size)

    heads_out, totals = lax.map(forward_rows, jnp.arange(blocks, dtype=jnp.int32))
    heads_out = heads_out.reshape(group_rows, kv_heads, share, HEAD_SIZE)
    row_totals = jnp.transpose(totals, (0, 3, 1, 2)).reshape(group_rows, kv_heads, share)
    out_rows = heads_out.reshape(group_rows, q_heads * HEAD_SIZE).astype(jnp.bfloat16)

    def out_term(start, count):
        return contract_last(out_rows, w_out)

    after_attn = x_float + token_sum(out_term, rows)
    mlp_gathered = (
        lax.all_gather(gate_weight.astype(jnp.bfloat16), "fsdp", axis=0, tiled=True),
        lax.all_gather(up_weight.astype(jnp.bfloat16), "fsdp", axis=0, tiled=True),
        lax.all_gather(jnp.transpose(down_weight).astype(jnp.bfloat16), "fsdp", axis=0, tiled=True),
        lax.all_gather(post_gain.astype(jnp.bfloat16), "fsdp", axis=0, tiled=True),
    )
    w_gate, w_up, w_down_t, gain_post = mlp_gathered
    gain_second = gain_post.astype(jnp.float32)
    second_all = token_gather(rms_scale(after_attn, gain_second).astype(jnp.bfloat16))
    gate_out = jnp.dot(second_all, w_gate, preferred_element_type=jnp.float32)
    up_out = jnp.dot(second_all, w_up, preferred_element_type=jnp.float32)
    activated = (jax.nn.silu(gate_out) * up_out).astype(jnp.bfloat16)

    def down_term(start, count):
        return contract_last(activated, w_down_t)

    output = (after_attn + token_sum(down_term, rows)).astype(jnp.bfloat16)
    cotangent = out_grad.astype(jnp.float32) * local_valid[:, None].astype(jnp.float32)
    mlp_grad_all = token_gather(cotangent.astype(jnp.bfloat16))
    w_gate, w_up, w_down_t = (
        lax.all_gather(gate_weight.astype(jnp.bfloat16), "fsdp", axis=0, tiled=True),
        lax.all_gather(up_weight.astype(jnp.bfloat16), "fsdp", axis=0, tiled=True),
        lax.all_gather(jnp.transpose(down_weight).astype(jnp.bfloat16), "fsdp", axis=0, tiled=True),
    )
    grad_act = jnp.dot(mlp_grad_all, w_down_t, preferred_element_type=jnp.float32)
    unused, pull_gate = jax.vjp(
        lambda gate_in, up_in: jax.nn.silu(gate_in) * up_in, gate_out, up_out
    )
    grad_gate, grad_up = pull_gate(grad_act)
    grad_gate = grad_gate.astype(jnp.bfloat16)
    grad_up = grad_up.astype(jnp.bfloat16)
    down_grad_t = contract_rows(mlp_grad_all, activated)
    gate_grad = contract_rows(second_all, grad_gate)
    up_grad = contract_rows(second_all, grad_up)

    def second_term(start, count):
        return contract_last(grad_gate, w_gate) + contract_last(grad_up, w_up)

    second_back = token_sum(second_term, rows)
    unused, pull_second = jax.vjp(rms_scale, after_attn, gain_second)
    norm_second_grad, post_gain_part = pull_second(second_back)
    residual_grad = cotangent + norm_second_grad
    mlp_shards = (
        lax.psum_scatter(gate_grad, "fsdp", scatter_dimension=0, tiled=True),
        lax.psum_scatter(up_grad, "fsdp", scatter_dimension=0, tiled=True),
        lax.psum_scatter(down_grad_t, "fsdp", scatter_dimension=0, tiled=True),
    )
    w_query, w_key, w_value, w_out = (
        lax.all_gather(q_weight.astype(jnp.bfloat16), "fsdp", axis=0, tiled=True),
        lax.all_gather(key_matrix.astype(jnp.bfloat16), "fsdp", axis=0, tiled=True),
        lax.all_gather(value_matrix.astype(jnp.bfloat16), "fsdp", axis=0, tiled=True),
        lax.all_gather(jnp.transpose(o_weight).astype(jnp.bfloat16), "fsdp", axis=0, tiled=True),
    )
    attn_grad_all = token_gather(residual_grad.astype(jnp.bfloat16))
    out_weight_grad_t = contract_rows(attn_grad_all, out_rows)
    head_grad = jnp.dot(attn_grad_all, w_out, preferred_element_type=jnp.float32).astype(
        jnp.bfloat16
    )
    head_float = head_grad.astype(jnp.float32).reshape(group_rows, kv_heads, share, HEAD_SIZE)
    scaled_grad = (head_float / row_totals[..., None]).astype(jnp.bfloat16)
    delta = jnp.sum(head_float * heads_out, axis=-1) / row_totals

    def backward_rows(carry, index):
        begin = index * size
        query_block = lax.dynamic_slice_in_dim(query_rope, begin, size, 0)
        grad_block = lax.dynamic_slice_in_dim(scaled_grad, begin, size, 0)
        delta_block = jnp.transpose(lax.dynamic_slice_in_dim(delta, begin, size, 0), (1, 2, 0))
        query_segment = lax.dynamic_slice_in_dim(group_segment, begin, size, 0)
        query_place = lax.dynamic_slice_in_dim(group_place, begin, size, 0)
        grad_query = jnp.zeros(query_block.shape, jnp.float32)
        updated = []
        for number, (key_rows, values, key_segment, key_place) in enumerate(key_sets):

            def backward_add_block(inner, state):
                grad_query_now, grad_keys, grad_values = state
                start = inner * size
                key_part = lax.dynamic_slice_in_dim(key_rows, start, size, 0)
                value_part = lax.dynamic_slice_in_dim(values, start, size, 0)
                segment_part = lax.dynamic_slice_in_dim(key_segment, start, size, 0)
                place_part = lax.dynamic_slice_in_dim(key_place, start, size, 0)
                weights = block_weights(
                    query_block,
                    key_part,
                    query_segment,
                    query_place,
                    segment_part,
                    place_part,
                    scale,
                )
                grad_prob = jnp.einsum(
                    "qkgd,nkd->kgqn", grad_block, value_part, preferred_element_type=jnp.float32
                )
                grad_score = (weights * (grad_prob - delta_block[..., None])).astype(jnp.bfloat16)
                grad_query_now = grad_query_now + scale * jnp.einsum(
                    "kgqn,nkd->qkgd", grad_score, key_part, preferred_element_type=jnp.float32
                )
                key_term = scale * jnp.einsum(
                    "kgqn,qkgd->nkd", grad_score, query_block, preferred_element_type=jnp.float32
                )
                value_term = jnp.einsum(
                    "kgqn,qkgd->nkd",
                    weights.astype(jnp.bfloat16),
                    grad_block,
                    preferred_element_type=jnp.float32,
                )
                grad_keys = lax.dynamic_update_slice_in_dim(
                    grad_keys,
                    lax.dynamic_slice_in_dim(grad_keys, start, size, 0) + key_term,
                    start,
                    0,
                )
                grad_values = lax.dynamic_update_slice_in_dim(
                    grad_values,
                    lax.dynamic_slice_in_dim(grad_values, start, size, 0) + value_term,
                    start,
                    0,
                )
                return (grad_query_now, grad_keys, grad_values)

            grad_query, grad_keys_set, grad_values_set = lax.fori_loop(
                0,
                key_rows.shape[0] // size,
                backward_add_block,
                (grad_query, carry[number][0], carry[number][1]),
            )
            updated.append((grad_keys_set, grad_values_set))
        return (updated, grad_query)

    empty_grads = [
        (
            jnp.zeros((group_rows, kv_heads, HEAD_SIZE), jnp.float32),
            jnp.zeros((group_rows, kv_heads, HEAD_SIZE), jnp.float32),
        )
        for entry in key_sets
    ]
    key_grads, query_grads = lax.scan(
        backward_rows, empty_grads, jnp.arange(blocks, dtype=jnp.int32)
    )
    returned = swapped(
        jnp.stack([key_grads[1][0], key_grads[1][1]]).astype(jnp.bfloat16), "fsdp", 0
    ).astype(jnp.float32)
    grad_keys_total = key_grads[0][0] + returned[0]
    grad_values_total = key_grads[0][1] + returned[1]
    query_grads = query_grads.reshape(group_rows, q_heads, HEAD_SIZE)
    unused, pull_query = jax.vjp(
        lambda projected, gain: prepare_inputs(projected, gain, group_offset, q_heads),
        query_projected,
        gain_q,
    )
    query_proj_grad, q_gain_part = pull_query(query_grads)
    unused, pull_key = jax.vjp(
        lambda projected, gain: prepare_inputs(projected, gain, group_offset, kv_heads),
        key_projected,
        gain_k,
    )
    key_proj_grad, k_gain_part = pull_key(grad_keys_total)
    query_low = query_proj_grad.astype(jnp.bfloat16)
    key_low = key_proj_grad.astype(jnp.bfloat16)
    value_low = grad_values_total.reshape(group_rows, kv_heads * HEAD_SIZE).astype(jnp.bfloat16)
    query_weight_grad = contract_rows(first_all, query_low)
    key_weight_grad = contract_rows(first_all, key_low)
    value_weight_grad = contract_rows(first_all, value_low)

    def first_term(start, count):
        return (
            contract_last(query_low, w_query)
            + contract_last(key_low, w_key)
            + contract_last(value_low, w_value)
        )

    first_back = token_sum(first_term, rows)
    unused, pull_first = jax.vjp(rms_scale, x_float, gain_first)
    norm_first_grad, input_gain_part = pull_first(first_back)
    input_grad = (residual_grad + norm_first_grad).astype(jnp.bfloat16)
    gain_totals = lax.psum((input_gain_part, q_gain_part, k_gain_part, post_gain_part), "tensor")
    attn_shards = (
        lax.psum_scatter(query_weight_grad, "fsdp", scatter_dimension=0, tiled=True),
        lax.psum_scatter(key_weight_grad, "fsdp", scatter_dimension=0, tiled=True),
        lax.psum_scatter(value_weight_grad, "fsdp", scatter_dimension=0, tiled=True),
        lax.psum_scatter(out_weight_grad_t, "fsdp", scatter_dimension=0, tiled=True),
        lax.psum_scatter(gain_totals[0], "fsdp", scatter_dimension=0, tiled=True),
        lax.psum_scatter(gain_totals[1], "fsdp", scatter_dimension=0, tiled=True),
        lax.psum_scatter(gain_totals[2], "fsdp", scatter_dimension=0, tiled=True),
        lax.psum_scatter(gain_totals[3], "fsdp", scatter_dimension=0, tiled=True),
    )
    gate_shard, up_shard, down_shard_t = mlp_shards
    (
        query_shard,
        key_shard,
        value_shard,
        out_shard_t,
        input_gain_shard,
        q_gain_shard,
        k_gain_shard,
        post_gain_shard,
    ) = attn_shards
    return (
        output,
        input_grad,
        query_shard,
        key_shard,
        value_shard,
        jnp.transpose(out_shard_t),
        gate_shard,
        up_shard,
        jnp.transpose(down_shard_t),
        input_gain_shard,
        q_gain_shard,
        k_gain_shard,
        post_gain_shard,
    )


def solution(mesh):
    placed = (
        P(("fsdp", "tensor"), None),
        P(("fsdp", "tensor"), None),
        P(),
        P("fsdp", "tensor"),
        P("fsdp", "tensor"),
        P("fsdp", "tensor"),
        P("tensor", "fsdp"),
        P("fsdp", "tensor"),
        P("fsdp", "tensor"),
        P("tensor", "fsdp"),
        P("fsdp"),
        P("fsdp"),
        P("fsdp"),
        P("fsdp"),
    )
    return jax.shard_map(
        shards,
        mesh=mesh,
        in_specs=placed,
        out_specs=(
            P(("fsdp", "tensor"), None),
            P(("fsdp", "tensor"), None),
            P("fsdp", "tensor"),
            P("fsdp", "tensor"),
            P("fsdp", "tensor"),
            P("tensor", "fsdp"),
            P("fsdp", "tensor"),
            P("fsdp", "tensor"),
            P("tensor", "fsdp"),
            P("fsdp"),
            P("fsdp"),
            P("fsdp"),
            P("fsdp"),
        ),
        check_vma=False,
    )
```

profile of v0, /device:TPU:0, one launch (start us, length us, event | category | flops | bytes accessed | tf_op | source)
XLA Modules:
  0.0 1801.8 jit_solution(5631656755196389620)
XLA Ops:
  49.8 33.7 %all_gather.57 = bf16[1024,256]{1,0:T(8,128)(2,1)} all-gather(bf16[128,256]{1,0:T(8,128)(2,1)S(1)} %convert_element_type.229), channel_id=1, replica_groups=mesh['fsdp'=8,'tensor'=4] {'fsdp'}, dimensions={0}, use_global_device_ids=true | all-gather | bytes 589824 | tf_op jit(solution)/shard_map/all_gather | solution.py:165
  102.7 34.0 %all_gather.56 = bf16[1024,256]{1,0:T(8,128)(2,1)} all-gather(bf16[128,256]{1,0:T(8,128)(2,1)S(1)} %convert_element_type.227), channel_id=1, replica_groups=mesh['fsdp'=8,'tensor'=4] {'fsdp'}, dimensions={0}, use_global_device_ids=true | all-gather | bytes 589824 | tf_op jit(solution)/shard_map/all_gather | solution.py:166
  206.9 210.4 %while.104 = (s32[]{:T(128)}, f32[4,512,2,2,128]{1,4,3,2,0:T(8,128)}, f32[4,2,2,512]{3,2,1,0:T(2,128)S(1)}, s32[4]{0:T(128)S(1)}, bf16[2048,2,2,128]{3,0,2,1:T(8...) while((s32[]{:T(128)}, ...), condition=%wide.region_13.15_spmd.clone, body=%wide.region_6.14_spmd.clone.sunk | while | flops 1088968704 | bytes 27927992 | solution.py:206
  368.0 32.5 %while.108 = (s32[]{:T(128)}, f32[512,2,2,128]{0,3,2,1:T(8,128)S(1)}, f32[2,2,512]{2,1,0:T(2,128)S(1)}, bf16[2048,2,128]{0,2,1:T(8,128)(2,1)}, s32[512]{0:T(512)...) while((s32[]{:T(128)}, ...), condition=%wide.region_9.10_spmd.clone, body=%wide.region_7.9_spmd.clone.sunk | while | flops 544475136 | bytes 12370126 | solution.py:120
  527.2 34.3 %all-gather.18.cloned.1.call-done = bf16[2048,1024]{1,0:T(8,128)(2,1)} async-done(((bf16[512,1024]{1,0:T(8,128)(2,1)}), bf16[2048,1024]{1,0:T(8,128)(2,1)}) %all-gather.18.cloned.1.call-update) | async-done | bytes 4194320 | tf_op jit(solution)/shard_map/all_gather | solution.py:71
  570.2 38.2 %all-gather.22.cloned.1.call-done = bf16[1024,768]{1,0:T(8,128)(2,1)} async-done(((bf16[128,768]{1,0:T(8,128)(2,1)}), bf16[1024,768]{1,0:T(8,128)(2,1)}) %all-gather.22.cloned.1.call-update) | async-done | bytes 1572880 | tf_op jit(solution)/shard_map/all_gather | solution.py:217
  617.3 36.6 %all-gather.24.cloned.1.call-done = bf16[1024,768]{0,1:T(8,128)(2,1)} async-done(((bf16[128,768]{0,1:T(8,128)(2,1)}), bf16[1024,768]{0,1:T(8,128)(2,1)}) %all-gather.24.cloned.1.call-update) | async-done | bytes 1572880 | tf_op jit(solution)/shard_map/all_gather | solution.py:218
  653.9 34.2 %all-gather.26.cloned.1.call-done = bf16[2048,1024]{1,0:T(8,128)(2,1)} async-done(((bf16[512,1024]{1,0:T(8,128)(2,1)}), bf16[2048,1024]{1,0:T(8,128)(2,1)}) %all-gather.26.cloned.1.call-update) | async-done | bytes 4194320 | tf_op jit(solution)/shard_map/all_gather | solution.py:71
  709.0 44.7 %reduce-scatter.16.cloned.1.call-done = bf16[512,1024]{1,0:T(8,128)(2,1)} async-done(((bf16[2048,1024]{1,0:T(8,128)(2,1)}), bf16[512,1024]{1,0:T(8,128)(2,1)}) %reduce-scatter.16.cloned.1.call-update) | async-done | bytes 1048592 | tf_op jit(solution)/shard_map/reduce_scatter | solution.py:75
  814.9 417.7 %while.107 = (s32[]{:T(128)}, f32[2048,2,128]{2,0,1:T(8,128)}, f32[2048,2,128]{2,0,1:T(8,128)}, f32[2048,2,128]{2,0,1:T(8,128)}, f32[2048,2,128]{2,0,1:T(8,128)}...) while((s32[]{:T(128)}, f32[2048,2,128]{2,0,1:T(8,128)}, ...), condition=%wide.region_25.27_spmd.clone, body=%wide.region_20.26_spmd.clone.sunk | while | flops 2704822272 | bytes 110184184 | solution.py:350
  817.7 51.6 %while.110 = (s32[]{:T(128)}, f32[512,2,2,128]{0,3,2,1:T(8,128)}, f32[2048,2,128]{2,0,1:T(8,128)}, f32[2048,2,128]{2,0,1:T(8,128)}, bf16[2048,2,128]{2,0,1:T(8,1...) while((s32[]{:T(128)}, f32[512,2,2,128]{0,3,2,1:T(8,128)}, ...), condition=%wide.region_22.23_spmd.clone, body=%wide.region_21.22_spmd.clone.sunk | while | flops 1352531968 | bytes 60317992 | solution.py:334
  869.3 47.5 %while.111 = (s32[]{:T(128)}, f32[512,2,2,128]{0,3,2,1:T(8,128)}, f32[2048,2,128]{2,0,1:T(8,128)}, f32[2048,2,128]{2,0,1:T(8,128)}, bf16[2048,2,128]{2,0,1:T(8,1...) while((s32[]{:T(128)}, f32[512,2,2,128]{0,3,2,1:T(8,128)}, ...), condition=%wide.region_24.25_spmd, body=%wide.region_23.24_spmd.sunk | while | flops 1352269824 | bytes 35152160 | solution.py:334
  922.3 51.4 %while.110 = (s32[]{:T(128)}, f32[512,2,2,128]{0,3,2,1:T(8,128)}, f32[2048,2,128]{2,0,1:T(8,128)}, f32[2048,2,128]{2,0,1:T(8,128)}, bf16[2048,2,128]{2,0,1:T(8,1...) while((s32[]{:T(128)}, f32[512,2,2,128]{0,3,2,1:T(8,128)}, ...), condition=%wide.region_22.23_spmd.clone, body=%wide.region_21.22_spmd.clone.sunk | while | flops 1352531968 | bytes 60317992 | solution.py:334
  973.7 47.5 %while.111 = (s32[]{:T(128)}, f32[512,2,2,128]{0,3,2,1:T(8,128)}, f32[2048,2,128]{2,0,1:T(8,128)}, f32[2048,2,128]{2,0,1:T(8,128)}, bf16[2048,2,128]{2,0,1:T(8,1...) while((s32[]{:T(128)}, f32[512,2,2,128]{0,3,2,1:T(8,128)}, ...), condition=%wide.region_24.25_spmd, body=%wide.region_23.24_spmd.sunk | while | flops 1352269824 | bytes 35152160 | solution.py:334
  1026.7 51.4 %while.110 = (s32[]{:T(128)}, f32[512,2,2,128]{0,3,2,1:T(8,128)}, f32[2048,2,128]{2,0,1:T(8,128)}, f32[2048,2,128]{2,0,1:T(8,128)}, bf16[2048,2,128]{2,0,1:T(8,1...) while((s32[]{:T(128)}, f32[512,2,2,128]{0,3,2,1:T(8,128)}, ...), condition=%wide.region_22.23_spmd.clone, body=%wide.region_21.22_spmd.clone.sunk | while | flops 1352531968 | bytes 60317992 | solution.py:334
  1078.1 47.5 %while.111 = (s32[]{:T(128)}, f32[512,2,2,128]{0,3,2,1:T(8,128)}, f32[2048,2,128]{2,0,1:T(8,128)}, f32[2048,2,128]{2,0,1:T(8,128)}, bf16[2048,2,128]{2,0,1:T(8,1...) while((s32[]{:T(128)}, f32[512,2,2,128]{0,3,2,1:T(8,128)}, ...), condition=%wide.region_24.25_spmd, body=%wide.region_23.24_spmd.sunk | while | flops 1352269824 | bytes 35152160 | solution.py:334
  1131.0 51.4 %while.110 = (s32[]{:T(128)}, f32[512,2,2,128]{0,3,2,1:T(8,128)}, f32[2048,2,128]{2,0,1:T(8,128)}, f32[2048,2,128]{2,0,1:T(8,128)}, bf16[2048,2,128]{2,0,1:T(8,1...) while((s32[]{:T(128)}, f32[512,2,2,128]{0,3,2,1:T(8,128)}, ...), condition=%wide.region_22.23_spmd.clone, body=%wide.region_21.22_spmd.clone.sunk | while | flops 1352531968 | bytes 60317992 | solution.py:334
  1182.5 47.5 %while.111 = (s32[]{:T(128)}, f32[512,2,2,128]{0,3,2,1:T(8,128)}, f32[2048,2,128]{2,0,1:T(8,128)}, f32[2048,2,128]{2,0,1:T(8,128)}, bf16[2048,2,128]{2,0,1:T(8,1...) while((s32[]{:T(128)}, f32[512,2,2,128]{0,3,2,1:T(8,128)}, ...), condition=%wide.region_24.25_spmd, body=%wide.region_23.24_spmd.sunk | while | flops 1352269824 | bytes 35152160 | solution.py:334
  1347.6 38.3 %reduce-scatter.18.cloned.1.call-done = bf16[512,1024]{1,0:T(8,128)(2,1)} async-done(((bf16[2048,1024]{1,0:T(8,128)(2,1)}), bf16[512,1024]{1,0:T(8,128)(2,1)}) %reduce-scatter.18.cloned.1.call-update) | async-done | bytes 1048592 | tf_op jit(solution)/shard_map/reduce_scatter | solution.py:75
  1437.0 74.5 %reduce-scatter.28.cloned.1.call-done = f32[128,768]{1,0:T(8,128)} async-done(((f32[1024,768]{1,0:T(8,128)}), f32[128,768]{1,0:T(8,128)}) %reduce-scatter.28.cloned.1.call-update) | async-done | bytes 393232 | tf_op jit(solution)/shard_map/reduce_scatter | solution.py:258
  1511.5 77.5 %reduce-scatter.30.cloned.1.call-done = f32[128,768]{1,0:T(8,128)} async-done(((f32[1024,768]{1,0:T(8,128)}), f32[128,768]{1,0:T(8,128)}) %reduce-scatter.30.cloned.1.call-update) | async-done | bytes 393232 | tf_op jit(solution)/shard_map/reduce_scatter | solution.py:259
  1589.0 71.5 %reduce-scatter.20.cloned.1.call-done = f32[128,512]{1,0:T(8,128)} async-done(((f32[1024,512]{1,0:T(8,128)}), f32[128,512]{1,0:T(8,128)}) %reduce-scatter.20.cloned.1.call-update) | async-done | bytes 262160 | tf_op jit(solution)/shard_map/reduce_scatter | solution.py:391
  1660.5 67.3 %reduce-scatter.22.cloned.1.call-done = f32[128,256]{1,0:T(8,128)} async-done(((f32[1024,256]{1,0:T(8,128)}), f32[128,256]{1,0:T(8,128)}) %reduce-scatter.22.cloned.1.call-update) | async-done | bytes 131088 | tf_op jit(solution)/shard_map/reduce_scatter | solution.py:392
  1727.8 67.0 %reduce-scatter.24.cloned.1.call-done = f32[128,256]{1,0:T(8,128)} async-done(((f32[1024,256]{1,0:T(8,128)}), f32[128,256]{1,0:T(8,128)}) %reduce-scatter.24.cloned.1.call-update) | async-done | bytes 131088 | tf_op jit(solution)/shard_map/reduce_scatter | solution.py:393
  (997 shorter events, 1283.7 us)
Async XLA Ops:
  7.2 156.3 %all-gather.12.cloned.1.call-start = ((), (), s32[]{:S(2)}) async-start(), calls=%async_computation.11 | async-start | bytes 5242880 | tf_op jit(solution)/shard_map/all_gather | solution.py:71
  34.9 140.4 %all-gather.14.cloned.1.call-start = ((), (), s32[]{:S(2)}) async-start(), calls=%async_computation.12 | async-start | bytes 1179648 | tf_op jit(solution)/shard_map/all_gather | solution.py:164
  35.6 395.8 %all-gather.16.cloned.1.call-start = ((), (), s32[]{:S(2)}) async-start(), calls=%async_computation.13 | async-start | bytes 1179648 | tf_op jit(solution)/shard_map/all_gather | solution.py:167
  36.4 444.1 %reduce-scatter.12.cloned.1.call-start = ((), (), s32[]{:S(2)}) async-start(), calls=%async_computation.14 | async-start | bytes 5242880 | tf_op jit(solution)/shard_map/reduce_scatter | solution.py:75
  175.3 29.3 %collective-permute-start = (bf16[2,2048,2,128]{1,3,2,0:T(8,128)(2,1)}, bf16[2,2048,2,128]{1,3,2,0:T(8,128)(2,1)}, u32[]{:S(2)}, u32[]{:S(2)}) collective-permute-start(bf16[2,2048,2,128]{1,3,2,0:T(8,128)(2,1)} %pad_maximum_fusion.1), channel_id=1, source_target_pairs={{0,4},{4,0},{8,12},{12,8},{16,20},{20,16},{24,28},{28,24},{1,5},{5... | collective-permute-start | bytes 6291464 | tf_op jit(solution)/shard_map/ppermute | solution.py:16
  437.6 89.6 %all-gather.20.cloned.1.call-start = ((), (), s32[]{:S(2)}) async-start(), calls=%async_computation.16 | async-start | bytes 1769472 | tf_op jit(solution)/shard_map/all_gather | solution.py:216
  439.5 122.0 %all-gather.18.cloned.1.call-start = ((), (), s32[]{:S(2)}) async-start(), calls=%async_computation.15 | async-start | bytes 5242880 | tf_op jit(solution)/shard_map/all_gather | solution.py:71
  457.2 299.8 %copy-start.41 = (f32[8,1,128]{2,1,0:T(1,128)}, f32[8,1,128]{2,1,0:T(1,128)S(1)}, u32[]{:S(2)}) copy-start(f32[8,1,128]{2,1,0:T(1,128)S(1)} %convert_element_type.270) | copy-start | bytes 12292
  482.1 274.8 %copy-start.47 = (f32[512]{0:T(512)}, f32[512]{0:T(512)S(1)}, u32[]{:S(2)}) copy-start(f32[512]{0:T(512)S(1)} %fusion.162) | copy-start | bytes 6148
  484.8 123.7 %all-gather.22.cloned.1.call-start = ((), (), s32[]{:S(2)}) async-start(), calls=%async_computation.17 | async-start | bytes 1769472 | tf_op jit(solution)/shard_map/all_gather | solution.py:217
  486.5 167.3 %all-gather.24.cloned.1.call-start = ((), (), s32[]{:S(2)}) async-start(), calls=%async_computation.18 | async-start | bytes 1769472 | tf_op jit(solution)/shard_map/all_gather | solution.py:218
  488.3 199.8 %all-gather.26.cloned.1.call-start = ((), (), s32[]{:S(2)}) async-start(), calls=%async_computation.20 | async-start | bytes 5242880 | tf_op jit(solution)/shard_map/all_gather | solution.py:71
  505.3 248.4 %reduce-scatter.16.cloned.1.call-start = ((), (), s32[]{:S(2)}) async-start(), calls=%async_computation.21 | async-start | bytes 5242880 | tf_op jit(solution)/shard_map/reduce_scatter | solution.py:75
  708.9 84.5 %all-gather.28.cloned.1.call-start = ((), (), s32[]{:S(2)}) async-start(), calls=%async_computation.22 | async-start | bytes 5242880 | tf_op jit(solution)/shard_map/all_gather | solution.py:71
  758.9 585.0 %reduce-scatter.32.cloned.1.call-start = ((), (), s32[]{:S(2)}) async-start(), calls=%async_computation.30 | async-start | bytes 3538944 | tf_op jit(solution)/shard_map/reduce_scatter | solution.py:260
  776.7 569.0 %reduce-scatter.26.cloned.1.call-start = ((), (), s32[]{:S(2)}) async-start(), calls=%async_computation.27 | async-start | bytes 2359296 | tf_op jit(solution)/shard_map/reduce_scatter | solution.py:394
  1239.0 50.9 %collective-permute-start.1 = (bf16[2,2048,2,128]{1,3,2,0:T(8,128)(2,1)}, bf16[2,2048,2,128]{1,3,2,0:T(8,128)(2,1)}, u32[]{:S(2)}, u32[]{:S(2)}) collective-permute-start(bf16[2,2048,2,128]{1,3,2,0:T(8,128)(2,1)} %pad_maximum_fusion.2), channel_id=1, source_target_pairs={{0,4},{4,0},{8,12},{12,8},{16,20},{20,16},{24,28},{28,24},{1,5},{5... | collective-permute-start | bytes 6291464 | tf_op jit(solution)/shard_map/ppermute | solution.py:16
  1270.5 115.4 %reduce-scatter.18.cloned.1.call-start = ((), (), s32[]{:S(2)}) async-start(), calls=%async_computation.23 | async-start | bytes 5242880 | tf_op jit(solution)/shard_map/reduce_scatter | solution.py:75
  1301.3 131.7 %reduce-scatter.14.cloned.1.call-start = ((), (), s32[]{:S(2)}) async-start(), calls=%async_computation.19 | async-start | bytes 5242880 | tf_op jit(solution)/shard_map/reduce_scatter | solution.py:75
  1309.2 202.3 %reduce-scatter.28.cloned.1.call-start = ((), (), s32[]{:S(2)}) async-start(), calls=%async_computation.28 | async-start | bytes 3538944 | tf_op jit(solution)/shard_map/reduce_scatter | solution.py:258
  1317.8 271.2 %reduce-scatter.30.cloned.1.call-start = ((), (), s32[]{:S(2)}) async-start(), calls=%async_computation.29 | async-start | bytes 3538944 | tf_op jit(solution)/shard_map/reduce_scatter | solution.py:259
  1326.2 334.3 %reduce-scatter.20.cloned.1.call-start = ((), (), s32[]{:S(2)}) async-start(), calls=%async_computation.24 | async-start | bytes 2359296 | tf_op jit(solution)/shard_map/reduce_scatter | solution.py:391
  1332.9 394.9 %reduce-scatter.22.cloned.1.call-start = ((), (), s32[]{:S(2)}) async-start(), calls=%async_computation.25 | async-start | bytes 1179648 | tf_op jit(solution)/shard_map/reduce_scatter | solution.py:392
  1337.5 457.2 %reduce-scatter.24.cloned.1.call-start = ((), (), s32[]{:S(2)}) async-start(), calls=%async_computation.26 | async-start | bytes 1179648 | tf_op jit(solution)/shard_map/reduce_scatter | solution.py:393
  (139 other events, 2042.4 us)
Sparse Core Ops, SparseCore 0:
  35.0 31.7 all-gather.11
  69.5 41.6 all-gather.13
  113.8 38.8 all-gather.15
  437.8 42.6 reduce-scatter.11
  483.0 44.1 all-gather.19
  528.6 32.8 all-gather.17
  564.3 44.1 all-gather.21
  611.1 42.7 all-gather.23
  655.5 32.6 all-gather.25
  709.1 44.5 reduce-scatter.15
  759.0 34.4 all-gather.27
  796.9 74.2 reduce-scatter.31
  1270.6 69.1 reduce-scatter.25
  1342.2 43.6 reduce-scatter.17
  1388.3 44.6 reduce-scatter.13
  1437.0 74.4 reduce-scatter.27
  1515.5 73.4 reduce-scatter.29
  1593.0 67.4 reduce-scatter.19
  1664.5 63.2 reduce-scatter.21
  1731.6 63.1 reduce-scatter.23
where the time goes:
time: 1810 us; the launch traced here: 1800 us
  waiting for transfers between devices  685 us (38%)
  matrix products  684 us (38%)
  local copies, waits for them, and re-layouts  154 us (9%)
  blocking collectives  154 us (9%)
  other arithmetic  96.1 us (5%)
    dot_general x64, matrix products, block_weights(): jnp.einsum('qkgd,nkd->kgqn', query_block, key_rows, preferred_element_typ...  156 us
    reduce_scatter x4, waiting for transfers between devices, token_sum(): lax.psum_scatter(term(jnp.int32(0), rows * lax.axis_size('tensor')).astyp...  122 us
    dot_general x32, matrix products, backward_add_block(): jnp.einsum('kgqn,qkgd->nkd', weights.astype(jnp.bfloat16), grad_block, pr...  94.3 us
    all_gather x4, waiting for transfers between devices, token_gather(): return lax.all_gather(values, 'tensor', axis=0, tiled=True)  85.2 us
    dot_general x32, matrix products, backward_add_block(): jnp.einsum('kgqn,qkgd->nkd', grad_score, query_block, preferred_element_t...  83.7 us
    dot_general x32, matrix products, backward_add_block(): jnp.einsum('qkgd,nkd->kgqn', grad_block, value_part, preferred_element_ty...  77.7 us
    reduce_scatter x1, waiting for transfers between devices, shards(): lax.psum_scatter(up_grad, 'fsdp', scatter_dimension=0, tiled=True)  77.5 us
    reduce_scatter x1, waiting for transfers between devices, shards(): lax.psum_scatter(gate_grad, 'fsdp', scatter_dimension=0, tiled=True)  74.5 us
  transfers between devices with their start and end apart: 22, of which 17 were waited for; matrix products, arithmetic and copies ran while one was open for 49% of the time, Pallas kernels for 0%

commit v1 on v0

--- a/solution.py
+++ b/solution.py
@@ -1,9 +1,222 @@
+import functools
+
+import numpy as np
 import jax
 import jax.numpy as jnp
 from jax import lax
+from jax.experimental import pallas as pl
+from jax.experimental.pallas import tpu as pltpu
 from jax.sharding import PartitionSpec as P
 
 HEAD_SIZE = 128
+TRANS_B = (((1,), (1,)), ((), ()))
+TRANS_A = (((0,), (0,)), ((), ()))
+
+
+def _own_place(p, quarter, r):
+    return (p * quarter + r) if r < quarter else ((3 - p) * quarter + r - quarter)
+
+
+def _far_place(p, quarter, r):
+    return ((1 - p) * quarter + r) if r < quarter else ((2 + p) * quarter + r - quarter)
+
+
+def _pair_tables(p, quarter, block, by_key):
+    rows = 2 * quarter
+    count = rows // block
+    kmap = {}
+    for src, fn in ((0, _own_place), (1, _far_place)):
+        for j in range(count):
+            kmap[fn(p, quarter, j * block) // block] = (src, j)
+    pairs = []
+    for j in range(count):
+        qpb = _own_place(p, quarter, j * block) // block
+        for kpb in range(qpb + 1):
+            pairs.append((j, qpb, kpb))
+    if by_key:
+        pairs.sort(key=lambda t: (t[2], t[0]))
+    group = [t[2] if by_key else t[0] for t in pairs]
+    first = [1 if n == 0 or group[n - 1] != group[n] else 0 for n in range(len(pairs))]
+    last = [1 if n == len(pairs) - 1 or group[n + 1] != group[n] else 0 for n in range(len(pairs))]
+    table = np.array(
+        [
+            [t[0] for t in pairs],
+            [t[1] for t in pairs],
+            [t[2] for t in pairs],
+            [kmap[t[2]][0] for t in pairs],
+            [kmap[t[2]][1] for t in pairs],
+            first,
+            last,
+        ],
+        np.int32,
+    )
+    return table
+
+
+def pair_tables(piece, quarter, block, by_key):
+    t0 = _pair_tables(0, quarter, block, by_key)
+    t1 = _pair_tables(1, quarter, block, by_key)
+    assert t0.shape == t1.shape
+    return jnp.where(piece == 0, jnp.asarray(t0), jnp.asarray(t1))
+
+
+def _mask(qpb, kpb, qs, block):
+    qp = qpb * block + lax.broadcasted_iota(jnp.int32, (block, block), 0)
+    kp = kpb * block + lax.broadcasted_iota(jnp.int32, (block, block), 1)
+    start = jnp.tile(qs, (1, block // 128))
+    return (kp >= start) & (kp <= qp)
+
+
+def _fwd_kernel(tab_ref, q_ref, qs_ref, k_ref, v_ref, o_ref, l_ref, acc_ref, sum_ref, *, scale, block):
+    n = pl.program_id(1)
+    share = q_ref.shape[1]
+
+    @pl.when(tab_ref[5, n] == 1)
+    def _():
+        acc_ref[...] = jnp.zeros(acc_ref.shape, acc_ref.dtype)
+        sum_ref[...] = jnp.zeros(sum_ref.shape, sum_ref.dtype)
+
+    q = q_ref[0].reshape(share * block, HEAD_SIZE)
+    k = k_ref[0, 0]
+    v = v_ref[0, 0]
+    s = lax.dot_general(q, k, TRANS_B, preferred_element_type=jnp.float32) * scale
+    allowed = _mask(tab_ref[1, n], tab_ref[2, n], qs_ref[...], block)
+    e = jnp.where(allowed[None], jnp.exp(s.reshape(share, block, block)), 0.0)
+    sum_ref[...] += jnp.sum(e, axis=-1, keepdims=True)
+    acc_ref[...] += jnp.dot(
+        e.reshape(share * block, block).astype(jnp.bfloat16), v, preferred_element_type=jnp.float32
+    )
+
+    @pl.when(tab_ref[6, n] == 1)
+    def _():
+        total = sum_ref[...]
+        o_ref[0] = acc_ref[...].reshape(share, block, HEAD_SIZE) / total
+        l_ref[0] = jnp.broadcast_to(total, (share, block, 128))
+
+
+def attention_forward(q, qs, k_all, v_all, piece, quarter, block=512):
+    kvh, share, rows, _ = q.shape
+    tab = pair_tables(piece, quarter, block, False)
+    npairs = tab.shape[1]
+    scale = HEAD_SIZE ** (-0.5)
+    grid_spec = pltpu.PrefetchScalarGridSpec(
+        num_scalar_prefetch=1,
+        grid=(kvh, npairs),
+        in_specs=[
+            pl.BlockSpec((1, share, block, HEAD_SIZE), lambda h, n, t: (h, 0, t[0, n], 0)),
+            pl.BlockSpec((block, 128), lambda h, n, t: (t[0, n], 0)),
+            pl.BlockSpec((1, 1, block, HEAD_SIZE), lambda h, n, t: (t[3, n], h, t[4, n], 0)),
+            pl.BlockSpec((1, 1, block, HEAD_SIZE), lambda h, n, t: (t[3, n], h, t[4, n], 0)),
+        ],
+        out_specs=[
+            pl.BlockSpec((1, share, block, HEAD_SIZE), lambda h, n, t: (h, 0, t[0, n], 0)),
+            pl.BlockSpec((1, share, block, 128), lambda h, n, t: (h, 0, t[0, n], 0)),
+        ],
+        scratch_shapes=[
+            pltpu.VMEM((share * block, HEAD_SIZE), jnp.float32),
+            pltpu.VMEM((share, block, 1), jnp.float32),
+        ],
+    )
+    flops = 4 * kvh * npairs * share * block * block * HEAD_SIZE
+    return pl.pallas_call(
+        functools.partial(_fwd_kernel, scale=scale, block=block),
+        grid_spec=grid_spec,
+        out_shape=[
+            jax.ShapeDtypeStruct((kvh, share, rows, HEAD_SIZE), jnp.float32),
+            jax.ShapeDtypeStruct((kvh, share, rows, 128), jnp.float32),
+        ],
+        compiler_params=pltpu.CompilerParams(
+            dimension_semantics=("arbitrary", "arbitrary"), vmem_limit_bytes=48 * 1024 * 1024
+        ),
+        cost_estimate=pl.CostEstimate(
+            flops=flops, transcendentals=kvh * npairs * share * block * block,
+            bytes_accessed=kvh * npairs * (4 * block * HEAD_SIZE * 2),
+        ),
+        name="attn_fwd",
+    )(tab, q, qs, k_all, v_all)
+
+
+def _bwd_kernel(tab_ref, q_ref, h_ref, dl_ref, qs_ref, k_ref, v_ref, dq_ref, dk_ref, dv_ref, dk_acc, dv_acc, *, scale, block):
+    n = pl.program_id(1)
+    share = q_ref.shape[1]
+
+    @pl.when(n == 0)
+    def _():
+        dq_ref[...] = jnp.zeros(dq_ref.shape, dq_ref.dtype)
+
+    @pl.when(tab_ref[5, n] == 1)
+    def _():
+        dk_acc[...] = jnp.zeros(dk_acc.shape, dk_acc.dtype)
+        dv_acc[...] = jnp.zeros(dv_acc.shape, dv_acc.dtype)
+
+    q = q_ref[0].reshape(share * block, HEAD_SIZE)
+    hh = h_ref[0].reshape(share * block, HEAD_SIZE)
+    k = k_ref[0, 0]
+    v = v_ref[0, 0]
+    s = lax.dot_general(q, k, TRANS_B, preferred_element_type=jnp.float32) * scale
+    allowed = _mask(tab_ref[1, n], tab_ref[2, n], qs_ref[...], block)
+    e = jnp.where(allowed[None], jnp.exp(s.reshape(share, block, block)), 0.0)
+    dp = lax.dot_general(hh, v, TRANS_B, preferred_element_type=jnp.float32).reshape(share, block, block)
+    delta = jnp.tile(dl_ref[0], (1, 1, block // 128))
+    ds = (e * (dp - delta)).reshape(share * block, block).astype(jnp.bfloat16)
+    rows = pl.ds(pl.multiple_of(tab_ref[0, n] * block, block), block)
+    dq_ref[0, :, rows, :] += jnp.dot(ds, k, preferred_element_type=jnp.float32).reshape(share, block, HEAD_SIZE)
+    dk_acc[...] += lax.dot_general(ds, q, TRANS_A, preferred_element_type=jnp.float32)
+    dv_acc[...] += lax.dot_general(
+        e.reshape(share * block, block).astype(jnp.bfloat16), hh, TRANS_A, preferred_element_type=jnp.float32
+    )
+
+    @pl.when(tab_ref[6, n] == 1)
+    def _():
+        dk_ref[0, 0] = dk_acc[...] * scale
+        dv_ref[0, 0] = dv_acc[...]
+
+
+def attention_backward(q, hgrad, delta, qs, k_all, v_all, piece, quarter, block=512):
+    kvh, share, rows, _ = q.shape
+    tab = pair_tables(piece, quarter, block, True)
+    npairs = tab.shape[1]
+    scale = HEAD_SIZE ** (-0.5)
+    grid_spec = pltpu.PrefetchScalarGridSpec(
+        num_scalar_prefetch=1,
+        grid=(kvh, npairs),
+        in_specs=[
+            pl.BlockSpec((1, share, block, HEAD_SIZE), lambda h, n, t: (h, 0, t[0, n], 0)),
+            pl.BlockSpec((1, share, block, HEAD_SIZE), lambda h, n, t: (h, 0, t[0, n], 0)),
+            pl.BlockSpec((1, share, block, 128), lambda h, n, t: (h, 0, t[0, n], 0)),
+            pl.BlockSpec((block, 128), lambda h, n, t: (t[0, n], 0)),
+            pl.BlockSpec((1, 1, block, HEAD_SIZE), lambda h, n, t: (t[3, n], h, t[4, n], 0)),
+            pl.BlockSpec((1, 1, block, HEAD_SIZE), lambda h, n, t: (t[3, n], h, t[4, n], 0)),
+        ],
+        out_specs=[
+            pl.BlockSpec((1, share, rows, HEAD_SIZE), lambda h, n, t: (h, 0, 0, 0)),
+            pl.BlockSpec((1, 1, block, HEAD_SIZE), lambda h, n, t: (t[3, n], h, t[4, n], 0)),
+            pl.BlockSpec((1, 1, block, HEAD_SIZE), lambda h, n, t: (t[3, n], h, t[4, n], 0)),
+        ],
+        scratch_shapes=[
+            pltpu.VMEM((block, HEAD_SIZE), jnp.float32),
+            pltpu.VMEM((block, HEAD_SIZE), jnp.float32),
+        ],
+    )
+    flops = 10 * kvh * npairs * share * block * block * HEAD_SIZE
+    return pl.pallas_call(
+        functools.partial(_bwd_kernel, scale=scale, block=block),
+        grid_spec=grid_spec,
+        out_shape=[
+            jax.ShapeDtypeStruct((kvh, share, rows, HEAD_SIZE), jnp.float32),
+            jax.ShapeDtypeStruct(k_all.shape, jnp.float32),
+            jax.ShapeDtypeStruct(v_all.shape, jnp.float32),
+        ],
+        compiler_params=pltpu.CompilerParams(
+            dimension_semantics=("arbitrary", "arbitrary"), vmem_limit_bytes=56 * 1024 * 1024
+        ),
+        cost_estimate=pl.CostEstimate(
+            flops=flops, transcendentals=kvh * npairs * share * block * block,
+            bytes_accessed=kvh * npairs * (8 * block * HEAD_SIZE * 2),
+        ),
+        name="attn_bwd",
+    )(tab, q, hgrad, delta, qs, k_all, v_all)
+
 SLOT_TOKENS = 4096
 PIECES = 2
 
@@ -78,49 +291,6 @@
         scatter_dimension=0,
         tiled=True,
     ).astype(jnp.float32)
-
-
-def block_weights(query_block, key_rows, query_segment, query_place, key_segment, key_place, scale):
-    scores = (
-        jnp.einsum("qkgd,nkd->kgqn", query_block, key_rows, preferred_element_type=jnp.float32)
-        * scale
-    )
-    allowed = (query_segment[:, None] == key_segment[None, :]) & (
-        key_place[None, :] <= query_place[:, None]
-    )
-    return jnp.where(allowed[None, None], jnp.exp(scores), 0.0)
-
-
-def forward_block(query_block, query_segment, query_place, key_sets, scale, size):
-    kv_heads = query_block.shape[1]
-    share = query_block.shape[2]
-    summed = jnp.zeros(query_block.shape, jnp.float32)
-    total = jnp.zeros((kv_heads, share, size), jnp.float32)
-    for key_rows, values, key_segment, key_place in key_sets:
-
-        def forward_add_block(index, state):
-            summed_now, total_now = state
-            begin = index * size
-            key_part = lax.dynamic_slice_in_dim(key_rows, begin, size, 0)
-            value_part = lax.dynamic_slice_in_dim(values, begin, size, 0)
-            segment_part = lax.dynamic_slice_in_dim(key_segment, begin, size, 0)
-            place_part = lax.dynamic_slice_in_dim(key_place, begin, size, 0)
-            weights = block_weights(
-                query_block, key_part, query_segment, query_place, segment_part, place_part, scale
-            )
-            total_now = total_now + jnp.sum(weights, axis=-1)
-            summed_now = summed_now + jnp.einsum(
-                "kgqn,nkd->qkgd",
-                weights.astype(jnp.bfloat16),
-                value_part,
-                preferred_element_type=jnp.float32,
-            )
-            return (summed_now, total_now)
-
-        summed, total = lax.fori_loop(
-            0, key_rows.shape[0] // size, forward_add_block, (summed, total)
-        )
-    return (summed / jnp.transpose(total, (2, 0, 1))[..., None], total)
 
 
 def shards(
@@ -189,23 +359,14 @@
     )
     key_rope = prepare_inputs(key_projected, gain_k, group_offset, kv_heads).astype(jnp.bfloat16)
     moved = swapped(jnp.stack([key_rope, value_rows]), "fsdp", 0)
-    far_place = piece_places(1 - piece, group_rows)
-    far_segment = jnp.take(segment_ids, far_place)
-    key_sets = [
-        (key_rope, value_rows, group_segment, group_place),
-        (moved[0], moved[1], far_segment, far_place),
-    ]
-
-    def forward_rows(index):
-        begin = index * size
-        query_block = lax.dynamic_slice_in_dim(query_rope, begin, size, 0)
-        query_segment = lax.dynamic_slice_in_dim(group_segment, begin, size, 0)
-        query_place = lax.dynamic_slice_in_dim(group_place, begin, size, 0)
-        return forward_block(query_block, query_segment, query_place, key_sets, scale, size)
-
-    heads_out, totals = lax.map(forward_rows, jnp.arange(blocks, dtype=jnp.int32))
-    heads_out = heads_out.reshape(group_rows, kv_heads, share, HEAD_SIZE)
-    row_totals = jnp.transpose(totals, (0, 3, 1, 2)).reshape(group_rows, kv_heads, share)
+    quarter = group_rows // 2
+    query_start = jnp.broadcast_to((group_place - group_offset)[:, None], (group_rows, 128))
+    query_t = jnp.transpose(query_rope, (1, 2, 0, 3))
+    keys_all = jnp.stack([jnp.transpose(key_rope, (1, 0, 2)), jnp.transpose(moved[0], (1, 0, 2))])
+    values_all = jnp.stack([jnp.transpose(value_rows, (1, 0, 2)), jnp.transpose(moved[1], (1, 0, 2))])
+    heads_t, totals_t = attention_forward(query_t, query_start, keys_all, values_all, piece, quarter)
+    heads_out = jnp.transpose(heads_t, (2, 0, 1, 3))
+    row_totals = jnp.transpose(totals_t[..., 0], (2, 0, 1))
     out_rows = heads_out.reshape(group_rows, q_heads * HEAD_SIZE).astype(jnp.bfloat16)
 
     def out_term(start, count):
@@ -274,87 +435,18 @@
     scaled_grad = (head_float / row_totals[..., None]).astype(jnp.bfloat16)
     delta = jnp.sum(head_float * heads_out, axis=-1) / row_totals
 
-    def backward_rows(carry, index):
-        begin = index * size
-        query_block = lax.dynamic_slice_in_dim(query_rope, begin, size, 0)
-        grad_block = lax.dynamic_slice_in_dim(scaled_grad, begin, size, 0)
-        delta_block = jnp.transpose(lax.dynamic_slice_in_dim(delta, begin, size, 0), (1, 2, 0))
-        query_segment = lax.dynamic_slice_in_dim(group_segment, begin, size, 0)
-        query_place = lax.dynamic_slice_in_dim(group_place, begin, size, 0)
-        grad_query = jnp.zeros(query_block.shape, jnp.float32)
-        updated = []
-        for number, (key_rows, values, key_segment, key_place) in enumerate(key_sets):
-
-            def backward_add_block(inner, state):
-                grad_query_now, grad_keys, grad_values = state
-                start = inner * size
-                key_part = lax.dynamic_slice_in_dim(key_rows, start, size, 0)
-                value_part = lax.dynamic_slice_in_dim(values, start, size, 0)
-                segment_part = lax.dynamic_slice_in_dim(key_segment, start, size, 0)
-                place_part = lax.dynamic_slice_in_dim(key_place, start, size, 0)
-                weights = block_weights(
-                    query_block,
-                    key_part,
-                    query_segment,
-                    query_place,
-                    segment_part,
-                    place_part,
-                    scale,
-                )
-                grad_prob = jnp.einsum(
-                    "qkgd,nkd->kgqn", grad_block, value_part, preferred_element_type=jnp.float32
-                )
-                grad_score = (weights * (grad_prob - delta_block[..., None])).astype(jnp.bfloat16)
-                grad_query_now = grad_query_now + scale * jnp.einsum(
-                    "kgqn,nkd->qkgd", grad_score, key_part, preferred_element_type=jnp.float32
-                )
-                key_term = scale * jnp.einsum(
-                    "kgqn,qkgd->nkd", grad_score, query_block, preferred_element_type=jnp.float32
-                )
-                value_term = jnp.einsum(
-                    "kgqn,qkgd->nkd",
-                    weights.astype(jnp.bfloat16),
-                    grad_block,
-                    preferred_element_type=jnp.float32,
-                )
-                grad_keys = lax.dynamic_update_slice_in_dim(
-                    grad_keys,
-                    lax.dynamic_slice_in_dim(grad_keys, start, size, 0) + key_term,
-                    start,
-                    0,
-                )
-                grad_values = lax.dynamic_update_slice_in_dim(
-                    grad_values,
-                    lax.dynamic_slice_in_dim(grad_values, start, size, 0) + value_term,
-                    start,
-                    0,
-                )
-                return (grad_query_now, grad_keys, grad_values)
-
-            grad_query, grad_keys_set, grad_values_set = lax.fori_loop(
-                0,
-                key_rows.shape[0] // size,
-                backward_add_block,
-                (grad_query, carry[number][0], carry[number][1]),
-            )
-            updated.append((grad_keys_set, grad_values_set))
-        return (updated, grad_query)
-
-    empty_grads = [
-        (
-            jnp.zeros((group_rows, kv_heads, HEAD_SIZE), jnp.float32),
-            jnp.zeros((group_rows, kv_heads, HEAD_SIZE), jnp.float32),
-        )
-        for entry in key_sets
-    ]
-    key_grads, query_grads = lax.scan(
-        backward_rows, empty_grads, jnp.arange(blocks, dtype=jnp.int32)
-    )
-    returned = swapped(
-        jnp.stack([key_grads[1][0], key_grads[1][1]]).astype(jnp.bfloat16), "fsdp", 0
-    ).astype(jnp.float32)
-    grad_keys_total = key_grads[0][0] + returned[0]
-    grad_values_total = key_grads[0][1] + returned[1]
+    dq_raw, dk_all, dv_all = attention_backward(
+        query_t,
+        jnp.transpose(scaled_grad, (1, 2, 0, 3)),
+        jnp.broadcast_to(jnp.transpose(delta, (1, 2, 0))[..., None], (kv_heads, share, group_rows, 128)),
+        query_start, keys_all, values_all, piece, quarter,
+    )
+    unseen = (piece == 1) & (jnp.arange(group_rows) >= quarter)
+    far_grads = jnp.where(unseen[None, None, :, None], 0.0, jnp.stack([dk_all[1], dv_all[1]]))
+    returned = swapped(far_grads.astype(jnp.bfloat16), "fsdp", 0).astype(jnp.float32)
+    grad_keys_total = jnp.transpose(dk_all[0] + returned[0], (1, 0, 2))
+    grad_values_total = jnp.transpose(dv_all[0] + returned[1], (1, 0, 2))
+    query_grads = jnp.transpose(dq_raw, (2, 0, 1, 3)) * scale
     query_grads = query_grads.reshape(group_rows, q_heads, HEAD_SIZE)
     unused, pull_query = jax.vjp(
         lambda projected, gain: prepare_inputs(projected, gain, group_offset, q_heads),

time: 1810 us -> 1270 us (0.70)
  matrix products: 684 us -> 135 us
  Pallas kernels: 0 us -> 125 us
  local copies, waits for them, and re-layouts: 154 us -> 85.4 us
  other arithmetic: 96.1 us -> 66.8 us
    dot_general x224 -> x0, matrix products: 557 us -> none  [the longest x64 156 us: block_weights(): jnp.einsum('qkgd,nkd->kgqn', query_block, key_rows, preferred_element_typ...]
    pallas_call x0 -> x2, Pallas kernels: none -> 125 us  [the longest x1 78 us: attention_backward(): pl.pallas_call(functools.partial(_bwd_kernel, scale=scale, block=block),...]
    dynamic_slice x160 -> x0, local copies, waits for them, and re-layouts: 28.5 us -> none  [the longest x4 7.53 us: forward_rows(): query_block = lax.dynamic_slice_in_dim(query_rope, begin, size, 0)]
    reduce_scatter x4, waiting for transfers between devices: 122 us -> 94.1 us  [token_sum(): lax.psum_scatter(term(jnp.int32(0), rows * lax.axis_size('tensor')).astyp...]
    gather x2 -> x0, local copies, waits for them, and re-layouts: 24.1 us -> none  [the longest x1 12.3 us: shards(): group_segment = jnp.take(segment_ids, group_place)]
  transfers between devices with their start and end apart: 22 -> 22, of which waited for: 17 -> 17; matrix products, arithmetic and copies ran while one was open for 49% -> 19% of each run, Pallas kernels for 0% -> 10%
where the time goes in v1:
time: 1270 us
  waiting for transfers between devices  680 us (54%)
  blocking collectives  154 us (12%)
  matrix products  135 us (11%)
  Pallas kernels  125 us (10%)
  local copies, waits for them, and re-layouts  85.4 us (7%)
  other arithmetic  66.8 us (5%)
  between operations  17.6 us (1%)
    reduce_scatter x4, waiting for transfers between devices, token_sum(): lax.psum_scatter(term(jnp.int32(0), rows * lax.axis_size('tensor')).astyp...  94.1 us
    all_gather x4, waiting for transfers between devices, token_gather(): return lax.all_gather(values, 'tensor', axis=0, tiled=True)  92 us
    pallas_call x1, Pallas kernels, attention_backward(): pl.pallas_call(functools.partial(_bwd_kernel, scale=scale, block=block),...  78 us
    reduce_scatter x1, waiting for transfers between devices, shards(): lax.psum_scatter(up_grad, 'fsdp', scatter_dimension=0, tiled=True)  77.5 us
    reduce_scatter x1, waiting for transfers between devices, shards(): lax.psum_scatter(gate_grad, 'fsdp', scatter_dimension=0, tiled=True)  74.5 us
    reduce_scatter x1, waiting for transfers between devices, shards(): lax.psum_scatter(query_weight_grad, 'fsdp', scatter_dimension=0, tiled=True)  71.4 us
    reduce_scatter x1, waiting for transfers between devices, shards(): lax.psum_scatter(value_weight_grad, 'fsdp', scatter_dimension=0, tiled=True)  67.3 us
    reduce_scatter x1, waiting for transfers between devices, shards(): lax.psum_scatter(key_weight_grad, 'fsdp', scatter_dimension=0, tiled=True)  67.2 us
  transfers between devices with their start and end apart: 22, of which 17 were waited for; matrix products, arithmetic and copies ran while one was open for 19% of the time, Pallas kernels for 10%

profile of v1, /device:TPU:0, one launch (start us, length us, event | category | flops | bytes accessed | tf_op | source)
XLA Modules:
  0.0 1266.9 jit_solution(512897253037564856)
XLA Ops:
  10.0 22.3 %all-gather = bf16[8,1,128]{2,1,0:T(2,128)(2,1)S(1)} all-gather(bf16[1,1,128]{2,1,0:T(2,128)(2,1)S(1)} %convert_bitcast_fusion.3), channel_id=1, replica_groups=mesh['fsdp'=8,'tensor'=4] {'fsdp'}, dimensions={0}, use_global_device_ids=true | all-gather | bytes 2304 | tf_op jit(solution)/shard_map/all_gather | solution.py:338
  38.3 17.1 %all-reduce.12 = (bf16[128]{0:T(256)(128)(2,1)S(1)}, bf16[128]{0:T(256)(128)(2,1)S(1)}) all-reduce(bf16[128]{0:T(256)(128)(2,1)S(1)} %dynamic-update-slice, bf16[128]{0:T(256)(128)(2,1)S(1)} %dynamic-update-slice.1), channel_id=1, replica_groups=mesh['fsdp'=8,'tensor'=4] {'fsdp'}, use_global_device_ids=true, to_apply=%add.4 | all-reduce | flops 256 | bytes 1024
  68.8 32.0 %all_gather.58 = bf16[1024,256]{1,0:T(8,128)(2,1)S(1)} all-gather(bf16[128,256]{1,0:T(8,128)(2,1)S(1)} %convert_element_type.196), channel_id=1, replica_groups=mesh['fsdp'=8,'tensor'=4] {'fsdp'}, dimensions={0}, use_global_device_ids=true | all-gather | bytes 589824 | tf_op jit(solution)/shard_map/all_gather | solution.py:336
  100.8 33.8 %all_gather.56 = bf16[1024,256]{1,0:T(8,128)(2,1)} all-gather(bf16[128,256]{1,0:T(8,128)(2,1)S(1)} %convert_element_type.193), channel_id=1, replica_groups=mesh['fsdp'=8,'tensor'=4] {'fsdp'}, dimensions={0}, use_global_device_ids=true | all-gather | bytes 589824 | tf_op jit(solution)/shard_map/all_gather | solution.py:335
  175.7 16.1 %collective-permute-done = bf16[2,2048,2,128]{3,1,2,0:T(8,128)(2,1)} collective-permute-done((bf16[2,2048,2,128]{3,1,2,0:T(8,128)(2,1)}, bf16[2,2048,2,128]{3,1,2,0:T(8,128)(2,1)}, u32[]{:S(2)}, u32[]{:S(2)}) %collective-permute-start) | collective-permute-done | bytes 2097184 | tf_op jit(solution)/shard_map/ppermute | solution.py:229
  195.5 47.4 %attn_fwd.1 = (f32[2,2,2048,128]{3,2,1,0:T(8,128)}, f32[2,2,2048,128]{3,2,1,0:T(8,128)}) custom-call(s32[7,18]{1,0:T(8,128)S(1)} %broadcast_select_fusion.1.tab_ref, bf16[2,2,2048,128]{3,2,1,0:T(8,128)(2,1)S(1)} %maximum_bitcast_fusion.q_ref, s32[2048,128]{1,0:T(8,128)S(1)} %broadcast_in_dim.70.qs_ref, ...), custom_call_target="tpu_custom_call" | custom-call | flops 9663676416 | bytes 18874368 | tf_op jit(solution)/shard_map/attn_fwd/pallas_call | solution.py:121
  256.1 19.7 %all-gather.1 = bf16[8,1,128]{2,1,0:T(2,128)(2,1)S(1)} all-gather(bf16[1,1,128]{2,1,0:T(2,128)(2,1)S(1)} %convert_bitcast_fusion.2), channel_id=1, replica_groups=mesh['fsdp'=8,'tensor'=4] {'fsdp'}, dimensions={0}, use_global_device_ids=true | all-gather | bytes 2304 | tf_op jit(solution)/shard_map/all_gather | solution.py:380
  275.7 23.4 %reduce-scatter.12.cloned.1.call-done = bf16[512,1024]{1,0:T(8,128)(2,1)} async-done(((bf16[2048,1024]{1,0:T(8,128)(2,1)}), bf16[512,1024]{1,0:T(8,128)(2,1)}) %reduce-scatter.12.cloned.1.call-update) | async-done | bytes 1048592 | tf_op jit(solution)/shard_map/reduce_scatter | solution.py:288
  320.6 25.3 %all-gather.22.cloned.1.call-done = bf16[1024,768]{1,0:T(8,128)(2,1)} async-done(((bf16[128,768]{1,0:T(8,128)(2,1)}), bf16[1024,768]{1,0:T(8,128)(2,1)}) %all-gather.22.cloned.1.call-update) | async-done | bytes 1572880 | tf_op jit(solution)/shard_map/all_gather | solution.py:378
  345.9 34.8 %all-gather.18.cloned.1.call-done = bf16[2048,1024]{1,0:T(8,128)(2,1)} async-done(((bf16[512,1024]{1,0:T(8,128)(2,1)}), bf16[2048,1024]{1,0:T(8,128)(2,1)}) %all-gather.18.cloned.1.call-update) | async-done | bytes 4194320 | tf_op jit(solution)/shard_map/all_gather | solution.py:284
  389.6 38.1 %all-gather.20.cloned.1.call-done = bf16[1024,768]{1,0:T(8,128)(2,1)} async-done(((bf16[128,768]{1,0:T(8,128)(2,1)}), bf16[1024,768]{1,0:T(8,128)(2,1)}) %all-gather.20.cloned.1.call-update) | async-done | bytes 1572880 | tf_op jit(solution)/shard_map/all_gather | solution.py:377
  436.5 36.7 %all-gather.24.cloned.1.call-done = bf16[1024,768]{0,1:T(8,128)(2,1)} async-done(((bf16[128,768]{0,1:T(8,128)(2,1)}), bf16[1024,768]{0,1:T(8,128)(2,1)}) %all-gather.24.cloned.1.call-update) | async-done | bytes 1572880 | tf_op jit(solution)/shard_map/all_gather | solution.py:379
  473.2 34.2 %all-gather.26.cloned.1.call-done = bf16[2048,1024]{1,0:T(8,128)(2,1)} async-done(((bf16[512,1024]{1,0:T(8,128)(2,1)}), bf16[2048,1024]{1,0:T(8,128)(2,1)}) %all-gather.26.cloned.1.call-update) | async-done | bytes 4194320 | tf_op jit(solution)/shard_map/all_gather | solution.py:284
  528.2 44.7 %reduce-scatter.16.cloned.1.call-done = bf16[512,1024]{1,0:T(8,128)(2,1)} async-done(((bf16[2048,1024]{1,0:T(8,128)(2,1)}), bf16[512,1024]{1,0:T(8,128)(2,1)}) %reduce-scatter.16.cloned.1.call-update) | async-done | bytes 1048592 | tf_op jit(solution)/shard_map/reduce_scatter | solution.py:288
  588.8 22.9 %all-gather.28.cloned.1.call-done = bf16[2048,1024]{1,0:T(8,128)(2,1)} async-done(((bf16[512,1024]{1,0:T(8,128)(2,1)}), bf16[2048,1024]{1,0:T(8,128)(2,1)}) %all-gather.28.cloned.1.call-update) | async-done | bytes 4194320 | tf_op jit(solution)/shard_map/all_gather | solution.py:284
  629.9 78.0 %attn_bwd.1 = (f32[2,2,2048,128]{3,2,1,0:T(8,128)}, f32[2,2,2048,128]{3,2,1,0:T(8,128)}, f32[2,2,2048,128]{3,2,1,0:T(8,128)}) custom-call(s32[7,18]{1,0:T(8,128)} %broadcast_select_fusion.tab_ref, bf16[2,2,2048,128]{3,2,1,0:T(8,128)(2,1)} %copy-done, bf16[2,2,2048,128]{3,2,1,0:T(8,128)(2,1)} %get-tuple-element.120.h_ref, ...), custom_call_target="tpu_custom_call" | custom-call | flops 24159191040 | bytes 37748736 | tf_op jit(solution)/shard_map/attn_bwd/pallas_call | solution.py:202
  746.9 19.8 %collective-permute-done.1 = bf16[2,2,2048,128]{3,2,1,0:T(8,128)(2,1)} collective-permute-done((bf16[2,2,2048,128]{3,2,1,0:T(8,128)(2,1)}, bf16[2,2,2048,128]{3,2,1,0:T(8,128)(2,1)}, u32[]{:S(2)}, u32[]{:S(2)}) %collective-permute-start.1) | collective-permute-done | bytes 2097184 | tf_op jit(solution)/shard_map/ppermute | solution.py:229
  853.1 21.9 %all-reduce.10 = (f32[1024]{0:T(1024)S(1)}, f32[128]{0:T(128)S(1)}, f32[128]{0:T(128)S(1)}, f32[1024]{0:T(1024)S(1)}) all-reduce(f32[1024]{0:T(1024)S(1)} %get-tuple-element.94, f32[128]{0:T(128)S(1)} %get-tuple-element.90, f32[128]{0:T(128)S(1)} %get-tuple-element.88, ...), channel_id=13, replica_groups=mesh['fsdp'=8,'tensor'=4] {'fsdp'}, use_global_device_ids=true, to_apply=%region_24.25.clone | all-reduce | flops 2304 | bytes 18432
  882.3 15.8 %reduce-scatter.14.cloned.1.call-done = bf16[512,1024]{1,0:T(8,128)(2,1)} async-done(((bf16[2048,1024]{1,0:T(8,128)(2,1)}), bf16[512,1024]{1,0:T(8,128)(2,1)}) %reduce-scatter.14.cloned.1.call-update) | async-done | bytes 1048592 | tf_op jit(solution)/shard_map/reduce_scatter | solution.py:288
  902.0 74.5 %reduce-scatter.28.cloned.1.call-done = f32[128,768]{1,0:T(8,128)} async-done(((f32[1024,768]{1,0:T(8,128)}), f32[128,768]{1,0:T(8,128)}) %reduce-scatter.28.cloned.1.call-update) | async-done | bytes 393232 | tf_op jit(solution)/shard_map/reduce_scatter | solution.py:419
  976.5 77.5 %reduce-scatter.30.cloned.1.call-done = f32[128,768]{1,0:T(8,128)} async-done(((f32[1024,768]{1,0:T(8,128)}), f32[128,768]{1,0:T(8,128)}) %reduce-scatter.30.cloned.1.call-update) | async-done | bytes 393232 | tf_op jit(solution)/shard_map/reduce_scatter | solution.py:420
  1054.0 71.4 %reduce-scatter.20.cloned.1.call-done = f32[128,512]{1,0:T(8,128)} async-done(((f32[1024,512]{1,0:T(8,128)}), f32[128,512]{1,0:T(8,128)}) %reduce-scatter.20.cloned.1.call-update) | async-done | bytes 262160 | tf_op jit(solution)/shard_map/reduce_scatter | solution.py:483
  1125.4 67.3 %reduce-scatter.24.cloned.1.call-done = f32[128,256]{1,0:T(8,128)} async-done(((f32[1024,256]{1,0:T(8,128)}), f32[128,256]{1,0:T(8,128)}) %reduce-scatter.24.cloned.1.call-update) | async-done | bytes 131088 | tf_op jit(solution)/shard_map/reduce_scatter | solution.py:485
  1192.7 67.2 %reduce-scatter.22.cloned.1.call-done = f32[128,256]{1,0:T(8,128)} async-done(((f32[1024,256]{1,0:T(8,128)}), f32[128,256]{1,0:T(8,128)}) %reduce-scatter.22.cloned.1.call-update) | async-done | bytes 131088 | tf_op jit(solution)/shard_map/reduce_scatter | solution.py:484
  (322 shorter events, 307.5 us)
Async XLA Ops:
  7.2 132.0 %all-gather.12.cloned.1.call-start = ((), (), s32[]{:S(2)}) async-start(), calls=%async_computation.11 | async-start | bytes 5242880 | tf_op jit(solution)/shard_map/all_gather | solution.py:284
  34.8 123.0 %all-gather.14.cloned.1.call-start = ((), (), s32[]{:S(2)}) async-start(), calls=%async_computation.12 | async-start | bytes 1179648 | tf_op jit(solution)/shard_map/all_gather | solution.py:334
  35.6 212.5 %all-gather.16.cloned.1.call-start = ((), (), s32[]{:S(2)}) async-start(), calls=%async_computation.13 | async-start | bytes 1179648 | tf_op jit(solution)/shard_map/all_gather | solution.py:337
  36.4 262.7 %reduce-scatter.12.cloned.1.call-start = ((), (), s32[]{:S(2)}) async-start(), calls=%async_computation.14 | async-start | bytes 5242880 | tf_op jit(solution)/shard_map/reduce_scatter | solution.py:288
  55.4 107.6 %copy-start.55 = (f32[128]{0:T(128)}, f32[128]{0:T(128)S(1)}, u32[]{:S(2)}) copy-start(f32[128]{0:T(128)S(1)} %convert_element_type.191) | copy-start | bytes 1540
  55.4 96.9 %copy-start.57 = (f32[128]{0:T(128)}, f32[128]{0:T(128)S(1)}, u32[]{:S(2)}) copy-start(f32[128]{0:T(128)S(1)} %convert_element_type.195) | copy-start | bytes 1540
  157.8 34.0 %collective-permute-start = (bf16[2,2048,2,128]{3,1,2,0:T(8,128)(2,1)}, bf16[2,2048,2,128]{3,1,2,0:T(8,128)(2,1)}, u32[]{:S(2)}, u32[]{:S(2)}) collective-permute-start(bf16[2,2048,2,128]{3,1,2,0:T(8,128)(2,1)} %pad_maximum_fusion), channel_id=1, source_target_pairs={{0,4},{4,0},{8,12},{12,8},{16,20},{20,16},{24,28},{28,24},{1,5},{5... | collective-permute-start | bytes 6291464 | tf_op jit(solution)/shard_map/ppermute | solution.py:229
  254.3 91.6 %all-gather.22.cloned.1.call-start = ((), (), s32[]{:S(2)}) async-start(), calls=%async_computation.17 | async-start | bytes 1769472 | tf_op jit(solution)/shard_map/all_gather | solution.py:378
  256.0 124.8 %all-gather.18.cloned.1.call-start = ((), (), s32[]{:S(2)}) async-start(), calls=%async_computation.15 | async-start | bytes 5242880 | tf_op jit(solution)/shard_map/all_gather | solution.py:284
  302.3 125.4 %all-gather.20.cloned.1.call-start = ((), (), s32[]{:S(2)}) async-start(), calls=%async_computation.16 | async-start | bytes 1769472 | tf_op jit(solution)/shard_map/all_gather | solution.py:377
  303.1 170.1 %all-gather.24.cloned.1.call-start = ((), (), s32[]{:S(2)}) async-start(), calls=%async_computation.18 | async-start | bytes 1769472 | tf_op jit(solution)/shard_map/all_gather | solution.py:379
  304.9 202.5 %all-gather.26.cloned.1.call-start = ((), (), s32[]{:S(2)}) async-start(), calls=%async_computation.20 | async-start | bytes 5242880 | tf_op jit(solution)/shard_map/all_gather | solution.py:284
  320.6 252.2 %reduce-scatter.16.cloned.1.call-start = ((), (), s32[]{:S(2)}) async-start(), calls=%async_computation.21 | async-start | bytes 5242880 | tf_op jit(solution)/shard_map/reduce_scatter | solution.py:288
  528.1 83.6 %all-gather.28.cloned.1.call-start = ((), (), s32[]{:S(2)}) async-start(), calls=%async_computation.22 | async-start | bytes 5242880 | tf_op jit(solution)/shard_map/all_gather | solution.py:284
  577.1 259.8 %reduce-scatter.32.cloned.1.call-start = ((), (), s32[]{:S(2)}) async-start(), calls=%async_computation.30 | async-start | bytes 3538944 | tf_op jit(solution)/shard_map/reduce_scatter | solution.py:421
  588.5 250.3 %reduce-scatter.26.cloned.1.call-start = ((), (), s32[]{:S(2)}) async-start(), calls=%async_computation.27 | async-start | bytes 2359296 | tf_op jit(solution)/shard_map/reduce_scatter | solution.py:486
  713.0 53.7 %collective-permute-start.1 = (bf16[2,2,2048,128]{3,2,1,0:T(8,128)(2,1)}, bf16[2,2,2048,128]{3,2,1,0:T(8,128)(2,1)}, u32[]{:S(2)}, u32[]{:S(2)}) collective-permute-start(bf16[2,2,2048,128]{3,2,1,0:T(8,128)(2,1)} %fusion.5), channel_id=1, source_target_pairs={{0,4},{4,0},{8,12},{12,8},{16,20},{20,16},{24,28},{28,24},{1,5},{5... | collective-permute-start | bytes 6291464 | tf_op jit(solution)/shard_map/ppermute | solution.py:229
  733.6 117.4 %reduce-scatter.18.cloned.1.call-start = ((), (), s32[]{:S(2)}) async-start(), calls=%async_computation.23 | async-start | bytes 5242880 | tf_op jit(solution)/shard_map/reduce_scatter | solution.py:288
  793.6 104.4 %reduce-scatter.14.cloned.1.call-start = ((), (), s32[]{:S(2)}) async-start(), calls=%async_computation.19 | async-start | bytes 5242880 | tf_op jit(solution)/shard_map/reduce_scatter | solution.py:288
  801.5 175.0 %reduce-scatter.28.cloned.1.call-start = ((), (), s32[]{:S(2)}) async-start(), calls=%async_computation.28 | async-start | bytes 3538944 | tf_op jit(solution)/shard_map/reduce_scatter | solution.py:419
  809.9 244.0 %reduce-scatter.30.cloned.1.call-start = ((), (), s32[]{:S(2)}) async-start(), calls=%async_computation.29 | async-start | bytes 3538944 | tf_op jit(solution)/shard_map/reduce_scatter | solution.py:420
  819.2 306.1 %reduce-scatter.20.cloned.1.call-start = ((), (), s32[]{:S(2)}) async-start(), calls=%async_computation.24 | async-start | bytes 2359296 | tf_op jit(solution)/shard_map/reduce_scatter | solution.py:483
  825.9 366.8 %reduce-scatter.24.cloned.1.call-start = ((), (), s32[]{:S(2)}) async-start(), calls=%async_computation.26 | async-start | bytes 1179648 | tf_op jit(solution)/shard_map/reduce_scatter | solution.py:485
  830.7 429.2 %reduce-scatter.22.cloned.1.call-start = ((), (), s32[]{:S(2)}) async-start(), calls=%async_computation.25 | async-start | bytes 1179648 | tf_op jit(solution)/shard_map/reduce_scatter | solution.py:484
  (73 other events, 734.2 us)
Sparse Core Ops, SparseCore 0:
  35.0 31.7 all-gather.11
  69.4 42.0 all-gather.13
  114.1 42.0 all-gather.15
  254.4 44.6 reduce-scatter.11
  301.7 44.1 all-gather.21
  347.9 32.8 all-gather.17
  383.5 44.1 all-gather.19
  430.4 42.7 all-gather.23
  474.7 32.6 all-gather.25
  528.2 44.5 reduce-scatter.15
  577.2 34.4 all-gather.27
  615.2 74.6 reduce-scatter.31
  733.7 71.1 reduce-scatter.25
  807.2 43.6 reduce-scatter.17
  853.3 44.6 reduce-scatter.13
  902.1 74.3 reduce-scatter.27
  980.5 73.4 reduce-scatter.29
  1057.9 67.4 reduce-scatter.19
  1129.4 63.3 reduce-scatter.23
  1196.5 63.3 reduce-scatter.21

commit v2 on v1

--- a/solution.py
+++ b/solution.py
@@ -278,6 +278,41 @@
     return lax.dot_general(
         left, right, (((1,), (1,)), ((), ())), preferred_element_type=jnp.float32
     )
+
+
+def gain_column(values, rows_f):
+    column = values.astype(jnp.bfloat16)
+    return jnp.pad(column, (0, rows_f - column.shape[0]))[:, None]
+
+
+def gain_rows(column, fs, rows_f, own):
+    return column.reshape(fs, rows_f)[:, :own].reshape(fs * own)
+
+
+def split_columns(full, widths):
+    parts = []
+    at = 0
+    for width in widths:
+        parts.append(full[:, at : at + width])
+        at += width
+    return parts
+
+
+def grad_scatter(grads):
+    packed = jnp.concatenate([g.astype(jnp.bfloat16) for g in grads], axis=1)
+    shard = lax.psum_scatter(packed, "fsdp", scatter_dimension=0, tiled=True)
+    return [part.astype(jnp.float32) for part in split_columns(shard, [g.shape[1] for g in grads])]
+
+
+def all_sum(values):
+    for axis in ("tensor", "fsdp"):
+        distance = 1
+        while distance < lax.axis_size(axis):
+            values = values + lax.ppermute(
+                values, axis, [(i, i ^ distance) for i in range(lax.axis_size(axis))]
+            )
+            distance *= 2
+    return values
 
 
 def token_gather(values):
@@ -330,16 +365,33 @@
     local_valid = lax.dynamic_slice_in_dim(
         jnp.take(valid, group_place), lax.axis_index("tensor") * rows, rows, 0
     )
-    attn_gathered = (
-        lax.all_gather(q_weight.astype(jnp.bfloat16), "fsdp", axis=0, tiled=True),
-        lax.all_gather(key_matrix.astype(jnp.bfloat16), "fsdp", axis=0, tiled=True),
-        lax.all_gather(value_matrix.astype(jnp.bfloat16), "fsdp", axis=0, tiled=True),
-        lax.all_gather(jnp.transpose(o_weight).astype(jnp.bfloat16), "fsdp", axis=0, tiled=True),
-        lax.all_gather(input_gain.astype(jnp.bfloat16), "fsdp", axis=0, tiled=True),
-        lax.all_gather(q_gain.astype(jnp.bfloat16), "fsdp", axis=0, tiled=True),
-        lax.all_gather(k_gain.astype(jnp.bfloat16), "fsdp", axis=0, tiled=True),
-    )
-    w_query, w_key, w_value, w_out, gain_in, gain_query, gain_keys = attn_gathered
+    fs = lax.axis_size("fsdp")
+    rows_f = q_weight.shape[0]
+    attn_full = lax.all_gather(
+        jnp.concatenate(
+            [
+                q_weight.astype(jnp.bfloat16),
+                key_matrix.astype(jnp.bfloat16),
+                value_matrix.astype(jnp.bfloat16),
+                jnp.transpose(o_weight).astype(jnp.bfloat16),
+                gain_column(input_gain, rows_f),
+                gain_column(q_gain, rows_f),
+                gain_column(k_gain, rows_f),
+                gain_column(post_gain, rows_f),
+            ],
+            axis=1,
+        ),
+        "fsdp",
+        axis=0,
+        tiled=True,
+    )
+    widths = (q_weight.shape[1], key_matrix.shape[1], value_matrix.shape[1], o_weight.shape[0])
+    w_query, w_key, w_value, w_out = split_columns(attn_full, widths)
+    gains_at = sum(widths)
+    gain_in = attn_full[:, gains_at]
+    gain_query = gain_rows(attn_full[:, gains_at + 1], fs, rows_f, q_gain.shape[0])
+    gain_keys = gain_rows(attn_full[:, gains_at + 2], fs, rows_f, k_gain.shape[0])
+    gain_post = attn_full[:, gains_at + 3]
     x_float = hidden.astype(jnp.float32)
     gain_first = gain_in.astype(jnp.float32)
     first_all = token_gather(rms_scale(x_float, gain_first).astype(jnp.bfloat16))
@@ -373,13 +425,22 @@
         return contract_last(out_rows, w_out)
 
     after_attn = x_float + token_sum(out_term, rows)
-    mlp_gathered = (
-        lax.all_gather(gate_weight.astype(jnp.bfloat16), "fsdp", axis=0, tiled=True),
-        lax.all_gather(up_weight.astype(jnp.bfloat16), "fsdp", axis=0, tiled=True),
-        lax.all_gather(jnp.transpose(down_weight).astype(jnp.bfloat16), "fsdp", axis=0, tiled=True),
-        lax.all_gather(post_gain.astype(jnp.bfloat16), "fsdp", axis=0, tiled=True),
-    )
-    w_gate, w_up, w_down_t, gain_post = mlp_gathered
+    mlp_full = lax.all_gather(
+        jnp.concatenate(
+            [
+                gate_weight.astype(jnp.bfloat16),
+                up_weight.astype(jnp.bfloat16),
+                jnp.transpose(down_weight).astype(jnp.bfloat16),
+            ],
+            axis=1,
+        ),
+        "fsdp",
+        axis=0,
+        tiled=True,
+    )
+    w_gate, w_up, w_down_t = split_columns(
+        mlp_full, (gate_weight.shape[1], up_weight.shape[1], down_weight.shape[0])
+    )
     gain_second = gain_post.astype(jnp.float32)
     second_all = token_gather(rms_scale(after_attn, gain_second).astype(jnp.bfloat16))
     gate_out = jnp.dot(second_all, w_gate, preferred_element_type=jnp.float32)
@@ -392,11 +453,6 @@
     output = (after_attn + token_sum(down_term, rows)).astype(jnp.bfloat16)
     cotangent = out_grad.astype(jnp.float32) * local_valid[:, None].astype(jnp.float32)
     mlp_grad_all = token_gather(cotangent.astype(jnp.bfloat16))
-    w_gate, w_up, w_down_t = (
-        lax.all_gather(gate_weight.astype(jnp.bfloat16), "fsdp", axis=0, tiled=True),
-        lax.all_gather(up_weight.astype(jnp.bfloat16), "fsdp", axis=0, tiled=True),
-        lax.all_gather(jnp.transpose(down_weight).astype(jnp.bfloat16), "fsdp", axis=0, tiled=True),
-    )
     grad_act = jnp.dot(mlp_grad_all, w_down_t, preferred_element_type=jnp.float32)
     unused, pull_gate = jax.vjp(
         lambda gate_in, up_in: jax.nn.silu(gate_in) * up_in, gate_out, up_out
@@ -415,19 +471,11 @@
     unused, pull_second = jax.vjp(rms_scale, after_attn, gain_second)
     norm_second_grad, post_gain_part = pull_second(second_back)
     residual_grad = cotangent + norm_second_grad
-    mlp_shards = (
-        lax.psum_scatter(gate_grad, "fsdp", scatter_dimension=0, tiled=True),
-        lax.psum_scatter(up_grad, "fsdp", scatter_dimension=0, tiled=True),
-        lax.psum_scatter(down_grad_t, "fsdp", scatter_dimension=0, tiled=True),
-    )
-    w_query, w_key, w_value, w_out = (
-        lax.all_gather(q_weight.astype(jnp.bfloat16), "fsdp", axis=0, tiled=True),
-        lax.all_gather(key_matrix.astype(jnp.bfloat16), "fsdp", axis=0, tiled=True),
-        lax.all_gather(value_matrix.astype(jnp.bfloat16), "fsdp", axis=0, tiled=True),
-        lax.all_gather(jnp.transpose(o_weight).astype(jnp.bfloat16), "fsdp", axis=0, tiled=True),
-    )
     attn_grad_all = token_gather(residual_grad.astype(jnp.bfloat16))
     out_weight_grad_t = contract_rows(attn_grad_all, out_rows)
+    mlp_shards = grad_scatter(
+        (gate_grad, up_grad, down_grad_t, out_weight_grad_t)
+    )
     head_grad = jnp.dot(attn_grad_all, w_out, preferred_element_type=jnp.float32).astype(
         jnp.bfloat16
     )
@@ -478,28 +526,22 @@
     unused, pull_first = jax.vjp(rms_scale, x_float, gain_first)
     norm_first_grad, input_gain_part = pull_first(first_back)
     input_grad = (residual_grad + norm_first_grad).astype(jnp.bfloat16)
-    gain_totals = lax.psum((input_gain_part, q_gain_part, k_gain_part, post_gain_part), "tensor")
-    attn_shards = (
-        lax.psum_scatter(query_weight_grad, "fsdp", scatter_dimension=0, tiled=True),
-        lax.psum_scatter(key_weight_grad, "fsdp", scatter_dimension=0, tiled=True),
-        lax.psum_scatter(value_weight_grad, "fsdp", scatter_dimension=0, tiled=True),
-        lax.psum_scatter(out_weight_grad_t, "fsdp", scatter_dimension=0, tiled=True),
-        lax.psum_scatter(gain_totals[0], "fsdp", scatter_dimension=0, tiled=True),
-        lax.psum_scatter(gain_totals[1], "fsdp", scatter_dimension=0, tiled=True),
-        lax.psum_scatter(gain_totals[2], "fsdp", scatter_dimension=0, tiled=True),
-        lax.psum_scatter(gain_totals[3], "fsdp", scatter_dimension=0, tiled=True),
-    )
-    gate_shard, up_shard, down_shard_t = mlp_shards
-    (
-        query_shard,
-        key_shard,
-        value_shard,
-        out_shard_t,
-        input_gain_shard,
-        q_gain_shard,
-        k_gain_shard,
-        post_gain_shard,
-    ) = attn_shards
+    query_shard, key_shard, value_shard = grad_scatter(
+        (query_weight_grad, key_weight_grad, value_weight_grad)
+    )
+    gain_totals = all_sum(
+        jnp.concatenate([input_gain_part, q_gain_part, k_gain_part, post_gain_part])
+    )
+    member_f = lax.axis_index("fsdp")
+    sizes = (input_gain.shape[0], q_gain.shape[0], k_gain.shape[0], post_gain.shape[0])
+    gain_shards = []
+    at = 0
+    for own in sizes:
+        whole = own * fs
+        gain_shards.append(lax.dynamic_slice_in_dim(gain_totals, at + member_f * own, own, 0))
+        at += whole
+    input_gain_shard, q_gain_shard, k_gain_shard, post_gain_shard = gain_shards
+    gate_shard, up_shard, down_shard_t, out_shard_t = mlp_shards
     return (
         output,
         input_grad,

time: 1270 us -> 1030 us (0.81)
  blocking collectives: 154 us -> 0 us
  waiting for transfers between devices: 680 us -> 559 us
  local copies, waits for them, and re-layouts: 85.4 us -> 112 us
  other arithmetic: 66.8 us -> 87.8 us
  matrix products: 135 us -> 116 us
    reduce_scatter x7 -> x0, waiting for transfers between devices: 358 us -> none  [the longest x1 77.5 us: shards(): lax.psum_scatter(up_grad, 'fsdp', scatter_dimension=0, tiled=True)]
    unnamed x20 -> x14, waiting for transfers between devices: 0.33 us -> 152 us
    all_gather x4 -> x0, blocking collectives: 108 us -> none  [the longest x1 33.8 us: shards(): lax.all_gather(key_matrix.astype(jnp.bfloat16), 'fsdp', axis=0, tiled=True)]
    unnamed x2 -> x0, blocking collectives: 39.1 us -> none
    reduce_scatter x4, waiting for transfers between devices: 94.1 us -> 123 us  [token_sum(): lax.psum_scatter(term(jnp.int32(0), rows * lax.axis_size('tensor')).astyp...]
    all_gather x5 -> x2, waiting for transfers between devices: 100 us -> 128 us  [the longest x1 64.8 us: shards(): lax.all_gather(jnp.concatenate([q_weight.astype(jnp.bfloat16), key_matrix...]
    dot_general x7, matrix products: 47.2 us -> 24.2 us  [contract_rows(): lax.dot_general(left, right, (((0,), (0,)), ((), ())), preferred_element_...]
    concatenate x0 -> x4, other arithmetic: none -> 18.5 us  [the longest x2 17.6 us: grad_scatter(): packed = jnp.concatenate([g.astype(jnp.bfloat16) for g in grads], axis=1)]
  transfers between devices with their start and end apart: 22 -> 19, of which waited for: 17 -> 16; matrix products, arithmetic and copies ran while one was open for 19% -> 17% of each run, Pallas kernels for 10% -> 0%
where the time goes in v2:
time: 1030 us; the launch traced here: 1020 us
  waiting for transfers between devices  559 us (54%)
  Pallas kernels  125 us (12%)
  matrix products  116 us (11%)
  local copies, waits for them, and re-layouts  112 us (11%)
  other arithmetic  87.8 us (9%)
  between operations  15.7 us (2%)
    unnamed x14, waiting for transfers between devices  152 us
    reduce_scatter x4, waiting for transfers between devices, token_sum(): lax.psum_scatter(term(jnp.int32(0), rows * lax.axis_size('tensor')).astyp...  123 us
    all_gather x4, waiting for transfers between devices, token_gather(): return lax.all_gather(values, 'tensor', axis=0, tiled=True)  99.9 us
    pallas_call x1, Pallas kernels, attention_backward(): pl.pallas_call(functools.partial(_bwd_kernel, scale=scale, block=block),...  78 us
    all_gather x1, waiting for transfers between devices, shards(): lax.all_gather(jnp.concatenate([q_weight.astype(jnp.bfloat16), key_matrix...  64.8 us
    all_gather x1, waiting for transfers between devices, shards(): lax.all_gather(jnp.concatenate([gate_weight.astype(jnp.bfloat16), up_weig...  63.6 us
    ppermute x2, waiting for transfers between devices, swapped(): lax.ppermute(shard, axis, [(i, i ^ 1 << distance) for i in range(lax.axis...  48.3 us
    pallas_call x1, Pallas kernels, attention_forward(): pl.pallas_call(functools.partial(_fwd_kernel, scale=scale, block=block),...  47.1 us
  transfers between devices with their start and end apart: 19, of which 16 were waited for; matrix products, arithmetic and copies ran while one was open for 17% of the time, Pallas kernels for 0%

profile of v2, /device:TPU:0, one launch (start us, length us, event | category | flops | bytes accessed | tf_op | source)
XLA Modules:
  0.0 1023.1 jit_solution(17345833878579853564)
XLA Ops:
  17.6 64.8 %all-gather.7.cloned.1.call-done = bf16[1024,1540]{0,1:T(8,128)(2,1)} async-done(((bf16[128,1540]{0,1:T(8,128)(2,1)}), bf16[1024,1540]{0,1:T(8,128)(2,1)}) %all-gather.7.cloned.1.call-update) | async-done | bytes 3153936 | tf_op jit(solution)/shard_map/all_gather | solution.py:370
  86.3 11.8 %gather_fusion = s32[2048]{0:T(1024)S(1)} fusion(s32[4096]{0:T(1024)S(1)} %iota_subtract_fusion, s32[2048]{0:T(1024)S(1)} %broadcast_clamp_fusion), kind=kCustom, calls=%fused_computation | custom fusion | bytes 24576 | tf_op jit(solution)/shard_map/jit(_take)/gather | solution.py:364
  102.9 15.1 %all-gather.9.cloned.1.call-done = bf16[2048,1024]{1,0:T(8,128)(2,1)} async-done(((bf16[512,1024]{1,0:T(8,128)(2,1)}), bf16[2048,1024]{1,0:T(8,128)(2,1)}) %all-gather.9.cloned.1.call-update) | async-done | bytes 4194320 | tf_op jit(solution)/shard_map/all_gather | solution.py:319
  155.8 28.9 %collective-permute-done = bf16[2,2048,2,128]{3,1,2,0:T(8,128)(2,1)} collective-permute-done((bf16[2,2048,2,128]{3,1,2,0:T(8,128)(2,1)}, bf16[2,2048,2,128]{3,1,2,0:T(8,128)(2,1)}, u32[]{:S(2)}, u32[]{:S(2)}) %collective-permute-start) | collective-permute-done | bytes 2097184 | tf_op jit(solution)/shard_map/ppermute | solution.py:229
  188.5 47.1 %attn_fwd.1 = (f32[2,2,2048,128]{3,2,1,0:T(8,128)}, f32[2,2,2048,128]{3,2,1,0:T(8,128)}) custom-call(s32[7,18]{1,0:T(8,128)S(1)} %broadcast_select_fusion.1.tab_ref, bf16[2,2,2048,128]{3,2,1,0:T(8,128)(2,1)S(1)} %maximum_bitcast_fusion.q_ref, s32[2048,128]{1,0:T(8,128)S(1)} %broadcast_in_dim.136.qs_ref, ...), custom_call_target="tpu_custom_call" | custom-call | flops 9663676416 | bytes 18874368 | tf_op jit(solution)/shard_map/attn_fwd/pallas_call | solution.py:121
  249.4 42.5 %reduce-scatter.11.cloned.1.call-done = bf16[512,1024]{1,0:T(8,128)(2,1)} async-done(((bf16[2048,1024]{1,0:T(8,128)(2,1)}), bf16[512,1024]{1,0:T(8,128)(2,1)}) %reduce-scatter.11.cloned.1.call-update) | async-done | bytes 1048592 | tf_op jit(solution)/shard_map/reduce_scatter | solution.py:323
  296.3 13.1 %gather_fusion.1 = pred[2048]{0:T(1024)(128)(4,1)S(1)} fusion(pred[4096]{0:T(1024)(128)(4,1)S(1)} %iota_compare_fusion.1, s32[2048]{0:T(1024)S(1)} %broadcast_clamp_fusion), kind=kCustom, calls=%fused_computation.1 | custom fusion | bytes 12288 | tf_op jit(solution)/shard_map/jit(_take)/gather | solution.py:366
  310.8 63.6 %all-gather.13.cloned.1.call-done = bf16[1024,2304]{0,1:T(8,128)(2,1)} async-done(((bf16[128,2304]{0,1:T(8,128)(2,1)}), bf16[1024,2304]{0,1:T(8,128)(2,1)}) %all-gather.13.cloned.1.call-update) | async-done | bytes 4718608 | tf_op jit(solution)/shard_map/all_gather | solution.py:428
  374.4 34.7 %all-gather.11.cloned.1.call-done = bf16[2048,1024]{1,0:T(8,128)(2,1)} async-done(((bf16[512,1024]{1,0:T(8,128)(2,1)}), bf16[2048,1024]{1,0:T(8,128)(2,1)}) %all-gather.11.cloned.1.call-update) | async-done | bytes 4194320 | tf_op jit(solution)/shard_map/all_gather | solution.py:319
  409.1 9.1 fusion.29
  418.2 7.1 fusion.33
  425.3 19.7 %all-gather.15.cloned.1.call-done = bf16[2048,1024]{1,0:T(8,128)(2,1)} async-done(((bf16[512,1024]{1,0:T(8,128)(2,1)}), bf16[2048,1024]{1,0:T(8,128)(2,1)}) %all-gather.15.cloned.1.call-update) | async-done | bytes 4194320 | tf_op jit(solution)/shard_map/all_gather | solution.py:319
  445.0 13.7 %multiply_convert_fusion = (bf16[2048,768]{1,0:T(8,128)(2,1)S(1)}, bf16[2048,768]{1,0:T(8,128)(2,1)S(1)}, bf16[2048,768]{1,0:T(8,128)(2,1)}) fusion(f32[2048,768]{1,0:T(8,128)} %fusion.33, f32[2048,768]{1,0:T(8,128)} %fusion.29, bf16[2048,1024]{1,0:T(8,128)(2,1)} %all-gather.15.cloned.1.call-done, bf16[1024,2304]{0,1:T(8,128)(2,1)} %all-gather.13.cloned.1.call-done), kind=kOutput, calls=%fused_computation.9 | convolution fusion | flops 3246391296 | bytes 27787264 | tf_op jit(solution)/shard_map/dot_general | solution.py:456
  471.2 44.7 %reduce-scatter.15.cloned.1.call-done = bf16[512,1024]{1,0:T(8,128)(2,1)} async-done(((bf16[2048,1024]{1,0:T(8,128)(2,1)}), bf16[512,1024]{1,0:T(8,128)(2,1)}) %reduce-scatter.15.cloned.1.call-update) | async-done | bytes 1048592 | tf_op jit(solution)/shard_map/reduce_scatter | solution.py:323
  524.5 30.3 %all-gather.17.cloned.1.call-done = bf16[2048,1024]{1,0:T(8,128)(2,1)} async-done(((bf16[512,1024]{1,0:T(8,128)(2,1)}), bf16[2048,1024]{1,0:T(8,128)(2,1)}) %all-gather.17.cloned.1.call-update) | async-done | bytes 4194320 | tf_op jit(solution)/shard_map/all_gather | solution.py:319
  573.0 78.0 %attn_bwd.1 = (f32[2,2,2048,128]{3,2,1,0:T(8,128)}, f32[2,2,2048,128]{3,2,1,0:T(8,128)}, f32[2,2,2048,128]{3,2,1,0:T(8,128)}) custom-call(s32[7,18]{1,0:T(8,128)} %broadcast_select_fusion.tab_ref, bf16[2,2,2048,128]{3,2,1,0:T(8,128)(2,1)} %copy-done, bf16[2,2,2048,128]{3,2,1,0:T(8,128)(2,1)} %get-tuple-element.112.h_ref, ...), custom_call_target="tpu_custom_call" | custom-call | flops 24159191040 | bytes 37748736 | tf_op jit(solution)/shard_map/attn_bwd/pallas_call | solution.py:202
  679.4 7.7 fusion.38
  687.2 19.4 %collective-permute-done.1 = bf16[2,2,2048,128]{3,2,1,0:T(8,128)(2,1)} collective-permute-done((bf16[2,2,2048,128]{3,2,1,0:T(8,128)(2,1)}, bf16[2,2,2048,128]{3,2,1,0:T(8,128)(2,1)}, u32[]{:S(2)}, u32[]{:S(2)}) %collective-permute-start.1) | collective-permute-done | bytes 2097184 | tf_op jit(solution)/shard_map/ppermute | solution.py:229
  746.7 7.8 convolution_convert_fusion.1
  771.3 16.1 %pad_maximum_fusion = bf16[1024,2816]{0,1:T(8,128)(2,1)} fusion(bf16[1024,512]{0,1:T(8,128)(2,1)S(1)} %convolution_convert_fusion.7, bf16[1024,768]{0,1:T(8,128)(2,1)S(1)} %convolution_convert_fusion.4, bf16[1024,768]{0,1:T(8,128)(2,1)S(1)} %convolution_convert_fusion.5, bf16[1024,768]{0,1:T(8,128)(2,1)S(1)} %convolution_convert_fusion.6), kind=kLoop, calls=%fused_computation.13 | loop fusion | flops 23068672 | bytes 11534336 | tf_op jit(solution)/shard_map/concatenate | solution.py:302
  787.4 8.4 copy.150
  806.2 43.2 %reduce-scatter.19.cloned.1.call-done = bf16[128,1024]{1,0:T(8,128)(2,1)} async-done(((bf16[1024,1024]{1,0:T(8,128)(2,1)}), bf16[128,1024]{1,0:T(8,128)(2,1)}) %reduce-scatter.19.cloned.1.call-update) | async-done | bytes 262160
  859.6 36.0 %reduce-scatter.13.cloned.1.call-done = bf16[512,1024]{1,0:T(8,128)(2,1)} async-done(((bf16[2048,1024]{1,0:T(8,128)(2,1)}), bf16[512,1024]{1,0:T(8,128)(2,1)}) %reduce-scatter.13.cloned.1.call-update) | async-done | bytes 1048592 | tf_op jit(solution)/shard_map/reduce_scatter | solution.py:323
  900.9 108.9 %reduce-scatter.21.cloned.1.call-done = bf16[128,2816]{1,0:T(8,128)(2,1)} async-done(((bf16[1024,2816]{1,0:T(8,128)(2,1)}), bf16[128,2816]{1,0:T(8,128)(2,1)}) %reduce-scatter.21.cloned.1.call-update) | async-done | bytes 720912
  (296 shorter events, 235.6 us)
Async XLA Ops:
  7.2 75.2 %all-gather.7.cloned.1.call-start = ((), (), s32[]{:S(2)}) async-start(), calls=%async_computation.6 | async-start | bytes 3557376 | tf_op jit(solution)/shard_map/all_gather | solution.py:370
  16.7 101.3 %all-gather.9.cloned.1.call-start = ((), (), s32[]{:S(2)}) async-start(), calls=%async_computation.7 | async-start | bytes 5242880 | tf_op jit(solution)/shard_map/all_gather | solution.py:319
  17.6 80.5 %copy-start.42 = (f32[512]{0:T(512)}, f32[512]{0:T(512)S(1)}, u32[]{:S(2)}) copy-start(f32[512]{0:T(512)S(1)} %fusion.58) | copy-start | bytes 6148
  85.2 206.7 %reduce-scatter.11.cloned.1.call-start = ((), (), s32[]{:S(2)}) async-start(), calls=%async_computation.8 | async-start | bytes 5242880 | tf_op jit(solution)/shard_map/reduce_scatter | solution.py:323
  100.1 44.5 %copy-start.18 = (f32[2048,64]{0,1:T(8,128)}, f32[2048,64]{0,1:T(8,128)S(1)}, u32[]{:S(2)}) copy-start(f32[2048,64]{0,1:T(8,128)S(1)} %get-tuple-element.130) | copy-start | bytes 1572868
  136.6 48.1 %collective-permute-start = (bf16[2,2048,2,128]{3,1,2,0:T(8,128)(2,1)}, bf16[2,2048,2,128]{3,1,2,0:T(8,128)(2,1)}, u32[]{:S(2)}, u32[]{:S(2)}) collective-permute-start(bf16[2,2048,2,128]{3,1,2,0:T(8,128)(2,1)} %pad_maximum_fusion.1), channel_id=1, source_target_pairs={{0,4},{4,0},{8,12},{12,8},{16,20},{20,16},{24,28},{28,24},{1,5},{5... | collective-permute-start | bytes 6291464 | tf_op jit(solution)/shard_map/ppermute | solution.py:229
  188.1 47.4 %copy-start.1 = (bf16[2,2,2048,128]{3,2,1,0:T(8,128)(2,1)}, bf16[2,2,2048,128]{3,2,1,0:T(8,128)(2,1)S(1)}, u32[]{:S(2)}) copy-start(bf16[2,2,2048,128]{3,2,1,0:T(8,128)(2,1)S(1)} %pad_maximum_fusion.2.k_ref) | copy-start | bytes 6291460
  188.5 47.1 %copy-start.2 = (s32[2048,128]{1,0:T(8,128)}, s32[2048,128]{1,0:T(8,128)S(1)}, u32[]{:S(2)}) copy-start(s32[2048,128]{1,0:T(8,128)S(1)} %broadcast_in_dim.136.qs_ref) | copy-start | bytes 3145732
  247.1 44.8 %copy-start.6 = (bf16[512,1024]{1,0:T(8,128)(2,1)S(1)}, bf16[512,1024]{1,0:T(8,128)(2,1)}, u32[]{:S(2)}) copy-start(bf16[512,1024]{1,0:T(8,128)(2,1)} %param.18) | copy-start | bytes 3145732
  247.1 127.3 %all-gather.13.cloned.1.call-start = ((), (), s32[]{:S(2)}) async-start(), calls=%async_computation.10 | async-start | bytes 5308416 | tf_op jit(solution)/shard_map/all_gather | solution.py:428
  249.4 159.7 %all-gather.11.cloned.1.call-start = ((), (), s32[]{:S(2)}) async-start(), calls=%async_computation.9 | async-start | bytes 5242880 | tf_op jit(solution)/shard_map/all_gather | solution.py:319
  295.1 149.9 %all-gather.15.cloned.1.call-start = ((), (), s32[]{:S(2)}) async-start(), calls=%async_computation.12 | async-start | bytes 5242880 | tf_op jit(solution)/shard_map/all_gather | solution.py:319
  310.8 205.2 %reduce-scatter.15.cloned.1.call-start = ((), (), s32[]{:S(2)}) async-start(), calls=%async_computation.13 | async-start | bytes 5242880 | tf_op jit(solution)/shard_map/reduce_scatter | solution.py:323
  471.2 83.6 %all-gather.17.cloned.1.call-start = ((), (), s32[]{:S(2)}) async-start(), calls=%async_computation.14 | async-start | bytes 5242880 | tf_op jit(solution)/shard_map/all_gather | solution.py:319
  520.2 275.7 %reduce-scatter.17.cloned.1.call-start = ((), (), s32[]{:S(2)}) async-start(), calls=%async_computation.15 | async-start | bytes 5242880 | tf_op jit(solution)/shard_map/reduce_scatter | solution.py:323
  658.5 48.1 %collective-permute-start.1 = (bf16[2,2,2048,128]{3,2,1,0:T(8,128)(2,1)}, bf16[2,2,2048,128]{3,2,1,0:T(8,128)(2,1)}, u32[]{:S(2)}, u32[]{:S(2)}) collective-permute-start(bf16[2,2,2048,128]{3,2,1,0:T(8,128)(2,1)} %fusion.5), channel_id=1, source_target_pairs={{0,4},{4,0},{8,12},{12,8},{16,20},{20,16},{24,28},{28,24},{1,5},{5... | collective-permute-start | bytes 6291464 | tf_op jit(solution)/shard_map/ppermute | solution.py:229
  733.0 116.4 %reduce-scatter.19.cloned.1.call-start = ((), (), s32[]{:S(2)}) async-start(), calls=%async_computation.16 | async-start | bytes 2359296
  746.6 149.0 %reduce-scatter.13.cloned.1.call-start = ((), (), s32[]{:S(2)}) async-start(), calls=%async_computation.11 | async-start | bytes 5242880 | tf_op jit(solution)/shard_map/reduce_scatter | solution.py:323
  754.5 255.3 %reduce-scatter.21.cloned.1.call-start = ((), (), s32[]{:S(2)}) async-start(), calls=%async_computation.17 | async-start | bytes 6488064
  799.3 1.2 collective-permute-start.2
  800.5 3.8 collective-permute-start.3
  804.8 49.1 %collective-permute-start.4 = (f32[2304]{0:T(1024)}, f32[2304]{0:T(1024)}, u32[]{:S(2)}, u32[]{:S(2)}) collective-permute-start(f32[2304]{0:T(1024)} %add.264), channel_id=1, source_target_pairs={{0,4},{4,0},{8,12},{12,8},{16,20},{20,16},{24,28},{28,24},{1,5},{5... | collective-permute-start | bytes 27656 | tf_op jit(solution)/shard_map/ppermute | solution.py:311
  854.7 3.7 collective-permute-start.5
  858.4 41.3 %collective-permute-start.6 = (f32[2304]{0:T(1024)S(1)}, f32[2304]{0:T(1024)S(1)}, u32[]{:S(2)}, u32[]{:S(2)}) collective-permute-start(f32[2304]{0:T(1024)S(1)} %add.266), channel_id=1, source_target_pairs={{0,16},{4,20},{8,24},{12,28},{16,0},{20,4},{24,8},{28,12},{1,17},{... | collective-permute-start | bytes 27656 | tf_op jit(solution)/shard_map/ppermute | solution.py:311
  (56 other events, 331.6 us)
Sparse Core Ops, SparseCore 0:
  16.8 65.5 all-gather.6
  85.3 32.6 all-gather.8
  247.3 44.5 reduce-scatter.10
  293.8 80.6 all-gather.12
  376.4 32.6 all-gather.10
  410.5 34.4 all-gather.14
  471.3 44.5 reduce-scatter.14
  520.3 34.4 all-gather.16
  733.1 44.3 reduce-scatter.16
  780.9 68.4 reduce-scatter.18
  851.9 43.6 reduce-scatter.12
  899.2 110.5 reduce-scatter.20

commit v3 on v2

--- a/solution.py
+++ b/solution.py
@@ -7,6 +7,7 @@
 from jax.experimental import pallas as pl
 from jax.experimental.pallas import tpu as pltpu
 from jax.sharding import PartitionSpec as P
+
 
 HEAD_SIZE = 128
 TRANS_B = (((1,), (1,)), ((), ()))
@@ -217,6 +218,7 @@
         name="attn_bwd",
     )(tab, q, hgrad, delta, qs, k_all, v_all)
 
+
 SLOT_TOKENS = 4096
 PIECES = 2
 
@@ -298,10 +300,24 @@
     return parts
 
 
-def grad_scatter(grads):
-    packed = jnp.concatenate([g.astype(jnp.bfloat16) for g in grads], axis=1)
-    shard = lax.psum_scatter(packed, "fsdp", scatter_dimension=0, tiled=True)
-    return [part.astype(jnp.float32) for part in split_columns(shard, [g.shape[1] for g in grads])]
+def halving_scatter(grads):
+    widths = [g.shape[1] for g in grads]
+    packed = jnp.concatenate(grads, axis=1)
+    count = lax.axis_size("fsdp")
+    me = lax.axis_index("fsdp")
+    rows_f = packed.shape[0] // count
+    bits = count.bit_length() - 1
+    buf = packed.reshape((2,) * bits + (rows_f, packed.shape[1]))
+    for bit in range(bits):
+        axis = bits - 1 - bit
+        mine = (me >> bit) & 1
+        keep = lax.dynamic_index_in_dim(buf, mine, axis, keepdims=False)
+        send = lax.dynamic_index_in_dim(buf, 1 - mine, axis, keepdims=False)
+        got = lax.ppermute(
+            send.astype(jnp.bfloat16), "fsdp", [(i, i ^ (1 << bit)) for i in range(count)]
+        )
+        buf = keep + got.astype(jnp.float32)
+    return split_columns(buf, widths)
 
 
 def all_sum(values):
@@ -315,17 +331,35 @@
     return values
 
 
+def exchange(values, distance):
+    count = lax.axis_size("tensor")
+    return lax.ppermute(values, "tensor", [(i, i ^ distance) for i in range(count)])
+
+
 def token_gather(values):
-    return lax.all_gather(values, "tensor", axis=0, tiled=True)
+    rows = values.shape[0]
+    me = lax.axis_index("tensor")
+    across = exchange(values, 2)
+    pair = jnp.stack([values, across])
+    beside = exchange(pair, 1)
+    full = jnp.zeros((4 * rows,) + values.shape[1:], values.dtype)
+    for part, place in ((values, me), (across, me ^ 2), (beside[0], me ^ 1), (beside[1], me ^ 3)):
+        full = lax.dynamic_update_slice_in_dim(full, part, place * rows, 0)
+    return full
 
 
 def token_sum(term, rows):
-    return lax.psum_scatter(
-        term(jnp.int32(0), rows * lax.axis_size("tensor")).astype(jnp.bfloat16),
-        "tensor",
-        scatter_dimension=0,
-        tiled=True,
-    ).astype(jnp.float32)
+    partial = term(jnp.int32(0), rows * lax.axis_size("tensor"))
+    me = lax.axis_index("tensor")
+
+    def block(place):
+        return lax.dynamic_slice_in_dim(partial, place * rows, rows, 0)
+
+    sent = jnp.stack([block(me ^ 1), block(me ^ 3)]).astype(jnp.bfloat16)
+    got = exchange(sent, 1).astype(jnp.float32)
+    mine = block(me) + got[0]
+    other = (block(me ^ 2) + got[1]).astype(jnp.bfloat16)
+    return mine + exchange(other, 2).astype(jnp.float32)
 
 
 def shards(
@@ -351,8 +385,6 @@
     kv_heads = key_matrix.shape[1] // HEAD_SIZE
     share = q_heads // kv_heads
     scale = HEAD_SIZE ** (-0.5)
-    size = min(512, group_rows)
-    blocks = group_rows // size
     member = lax.axis_index("fsdp")
     slot = member // PIECES
     piece = member % PIECES
@@ -473,8 +505,9 @@
     residual_grad = cotangent + norm_second_grad
     attn_grad_all = token_gather(residual_grad.astype(jnp.bfloat16))
     out_weight_grad_t = contract_rows(attn_grad_all, out_rows)
-    mlp_shards = grad_scatter(
-        (gate_grad, up_grad, down_grad_t, out_weight_grad_t)
+    mlp_packed = jnp.concatenate(
+        [g.astype(jnp.bfloat16) for g in (gate_grad, up_grad, down_grad_t, out_weight_grad_t)],
+        axis=1,
     )
     head_grad = jnp.dot(attn_grad_all, w_out, preferred_element_type=jnp.float32).astype(
         jnp.bfloat16
@@ -483,12 +516,20 @@
     scaled_grad = (head_float / row_totals[..., None]).astype(jnp.bfloat16)
     delta = jnp.sum(head_float * heads_out, axis=-1) / row_totals
 
+    grad_t = jnp.transpose(scaled_grad, (1, 2, 0, 3))
+    delta_t = jnp.broadcast_to(
+        jnp.transpose(delta, (1, 2, 0))[..., None], (kv_heads, share, group_rows, 128)
+    )
+    mlp_packed, grad_t, delta_t = lax.optimization_barrier((mlp_packed, grad_t, delta_t))
+    mlp_shards = split_columns(
+        lax.psum_scatter(mlp_packed, "fsdp", scatter_dimension=0, tiled=True),
+        [g.shape[1] for g in (gate_grad, up_grad, down_grad_t, out_weight_grad_t)],
+    )
+    mlp_shards = [part.astype(jnp.float32) for part in mlp_shards]
     dq_raw, dk_all, dv_all = attention_backward(
-        query_t,
-        jnp.transpose(scaled_grad, (1, 2, 0, 3)),
-        jnp.broadcast_to(jnp.transpose(delta, (1, 2, 0))[..., None], (kv_heads, share, group_rows, 128)),
-        query_start, keys_all, values_all, piece, quarter,
-    )
+        query_t, grad_t, delta_t, query_start, keys_all, values_all, piece, quarter
+    )
+    mlp_shards, dq_raw = lax.optimization_barrier((mlp_shards, dq_raw))
     unseen = (piece == 1) & (jnp.arange(group_rows) >= quarter)
     far_grads = jnp.where(unseen[None, None, :, None], 0.0, jnp.stack([dk_all[1], dv_all[1]]))
     returned = swapped(far_grads.astype(jnp.bfloat16), "fsdp", 0).astype(jnp.float32)
@@ -526,7 +567,7 @@
     unused, pull_first = jax.vjp(rms_scale, x_float, gain_first)
     norm_first_grad, input_gain_part = pull_first(first_back)
     input_grad = (residual_grad + norm_first_grad).astype(jnp.bfloat16)
-    query_shard, key_shard, value_shard = grad_scatter(
+    query_shard, key_shard, value_shard = halving_scatter(
         (query_weight_grad, key_weight_grad, value_weight_grad)
     )
     gain_totals = all_sum(
@@ -560,6 +601,10 @@
 
 
 def solution(mesh):
+    return layer_program(mesh)
+
+
+def layer_program(mesh):
     placed = (
         P(("fsdp", "tensor"), None),
         P(("fsdp", "tensor"), None),

time: 1030 us -> 832 us (0.81)
  waiting for transfers between devices: 559 us -> 270 us
  local copies, waits for them, and re-layouts: 112 us -> 164 us
  other arithmetic: 87.8 us -> 109 us
  starting transfers between devices: 7.92 us -> 27.4 us
    unnamed x14 -> x4, waiting for transfers between devices: 152 us -> 0.05 us
    ppermute x0 -> x19, waiting for transfers between devices: none -> 128 us  [the longest x16 118 us: exchange(): lax.ppermute(values, 'tensor', [(i, i ^ distance) for i in range(count)])]
    reduce_scatter x4 -> x0, waiting for transfers between devices: 123 us -> none  [token_sum(): lax.psum_scatter(term(jnp.int32(0), rows * lax.axis_size('tensor')).astyp...]
    all_gather x4 -> x0, waiting for transfers between devices: 99.9 us -> none  [token_gather(): return lax.all_gather(values, 'tensor', axis=0, tiled=True)]
    all_gather x1, waiting for transfers between devices: 63.6 us -> 0.01 us  [shards(): lax.all_gather(jnp.concatenate([gate_weight.astype(jnp.bfloat16), up_weig...]
    unnamed x143 -> x221, local copies, waits for them, and re-layouts: 37.3 us -> 58.2 us
    ppermute x2, waiting for transfers between devices: 48.3 us -> 68.7 us  [swapped(): lax.ppermute(shard, axis, [(i, i ^ 1 << distance) for i in range(lax.axis...]
    ppermute x0 -> x19, starting transfers between devices: none -> 16.3 us  [the longest x16 12 us: exchange(): lax.ppermute(values, 'tensor', [(i, i ^ distance) for i in range(count)])]
  transfers between devices with their start and end apart: 19 -> 29, of which waited for: 16 -> 18; matrix products, arithmetic and copies ran while one was open for 17% -> 31% of each run, Pallas kernels for 0% -> 15%
where the time goes in v3:
time: 832 us; the launch traced here: 820 us
  waiting for transfers between devices  270 us (32%)
  local copies, waits for them, and re-layouts  164 us (20%)
  Pallas kernels  125 us (15%)
  other arithmetic  109 us (13%)
  matrix products  108 us (13%)
  starting transfers between devices  27.4 us (3%)
  between operations  15.8 us (2%)
    ppermute x16, waiting for transfers between devices, exchange(): lax.ppermute(values, 'tensor', [(i, i ^ distance) for i in range(count)])  118 us
    pallas_call x1, Pallas kernels, attention_backward(): pl.pallas_call(functools.partial(_bwd_kernel, scale=scale, block=block),...  77.9 us
    ppermute x2, waiting for transfers between devices, swapped(): lax.ppermute(shard, axis, [(i, i ^ 1 << distance) for i in range(lax.axis...  68.7 us
    all_gather x1, waiting for transfers between devices, shards(): lax.all_gather(jnp.concatenate([q_weight.astype(jnp.bfloat16), key_matrix...  64.2 us
    unnamed x221, local copies, waits for them, and re-layouts  58.2 us
    pallas_call x1, Pallas kernels, attention_forward(): pl.pallas_call(functools.partial(_fwd_kernel, scale=scale, block=block),...  47 us
    dot_general x7, matrix products, contract_last(): lax.dot_general(left, right, (((1,), (1,)), ((), ())), preferred_element_...  34 us
    dot_general x7, matrix products, contract_rows(): lax.dot_general(left, right, (((0,), (0,)), ((), ())), preferred_element_...  29.4 us
  transfers between devices with their start and end apart: 29, of which 18 were waited for; matrix products, arithmetic and copies ran while one was open for 31% of the time, Pallas kernels for 15%

profile of v3, /device:TPU:0, one launch (start us, length us, event | category | flops | bytes accessed | tf_op | source)
XLA Modules:
  0.0 820.3 jit_solution(8722236221738841779)
XLA Ops:
  18.2 64.2 %all-gather.3.cloned.1.call-done = bf16[1024,1540]{0,1:T(8,128)(2,1)} async-done(((bf16[128,1540]{0,1:T(8,128)(2,1)}), bf16[1024,1540]{0,1:T(8,128)(2,1)}) %all-gather.3.cloned.1.call-update) | async-done | bytes 3153936 | tf_op jit(solution)/shard_map/all_gather | solution.py:402
  91.9 18.5 %collective-permute-done = bf16[512,1024]{0,1:T(8,128)(2,1)S(1)} collective-permute-done((bf16[512,1024]{0,1:T(8,128)(2,1)S(1)}, bf16[512,1024]{0,1:T(8,128)(2,1)S(1)}, u32[]{:S(2)}, u32[]{:S(2)}) %collective-permute-start) | collective-permute-done | bytes 1048608 | tf_op jit(solution)/shard_map/ppermute | solution.py:336
  112.1 11.8 %gather_fusion = s32[2048]{0:T(1024)S(1)} fusion(s32[4096]{0:T(1024)S(1)} %iota_subtract_fusion, s32[2048]{0:T(1024)S(1)} %broadcast_clamp_fusion), kind=kCustom, calls=%fused_computation | custom fusion | bytes 24576 | tf_op jit(solution)/shard_map/jit(_take)/gather | solution.py:396
  173.7 29.0 %collective-permute-done.2 = bf16[2,2048,2,128]{3,1,2,0:T(8,128)(2,1)} collective-permute-done((bf16[2,2048,2,128]{3,1,2,0:T(8,128)(2,1)}, bf16[2,2048,2,128]{3,1,2,0:T(8,128)(2,1)}, u32[]{:S(2)}, u32[]{:S(2)}) %collective-permute-start.2) | collective-permute-done | bytes 2097184 | tf_op jit(solution)/shard_map/ppermute | solution.py:231
  206.5 47.0 %attn_fwd.1 = (f32[2,2,2048,128]{3,2,1,0:T(8,128)}, f32[2,2,2048,128]{3,2,1,0:T(8,128)}) custom-call(s32[7,18]{1,0:T(8,128)S(1)} %broadcast_select_fusion.1.tab_ref, bf16[2,2,2048,128]{3,2,1,0:T(8,128)(2,1)S(1)} %maximum_bitcast_fusion.q_ref, s32[2048,128]{1,0:T(8,128)S(1)} %broadcast_in_dim.136.qs_ref, ...), custom_call_target="tpu_custom_call" | custom-call | flops 9663676416 | bytes 18874368 | tf_op jit(solution)/shard_map/attn_fwd/pallas_call | solution.py:122
  273.1 13.1 %gather_fusion.1 = pred[2048]{0:T(1024)(128)(4,1)S(1)} fusion(pred[4096]{0:T(1024)(128)(4,1)S(1)} %iota_compare_fusion.1, s32[2048]{0:T(1024)S(1)} %broadcast_clamp_fusion), kind=kCustom, calls=%fused_computation.1 | custom fusion | bytes 12288 | tf_op jit(solution)/shard_map/jit(_take)/gather | solution.py:398
  288.7 7.8 collective-permute-done.4
  304.3 14.6 %collective-permute-done.9 = bf16[512,1024]{0,1:T(8,128)(2,1)S(1)} collective-permute-done((bf16[512,1024]{0,1:T(8,128)(2,1)S(1)}, bf16[512,1024]{0,1:T(8,128)(2,1)S(1)}, u32[]{:S(2)}, u32[]{:S(2)}) %collective-permute-start.9) | collective-permute-done | bytes 1048608 | tf_op jit(solution)/shard_map/ppermute | solution.py:336
  319.1 21.4 %collective-permute-done.5 = bf16[512,1024]{0,1:T(8,128)(2,1)S(1)} collective-permute-done((bf16[512,1024]{0,1:T(8,128)(2,1)S(1)}, bf16[512,1024]{0,1:T(8,128)(2,1)S(1)}, u32[]{:S(2)}, u32[]{:S(2)}) %collective-permute-start.5) | collective-permute-done | bytes 1048608 | tf_op jit(solution)/shard_map/ppermute | solution.py:336
  347.3 9.0 %fusion.44 = f32[2048,768]{1,0:T(8,128)} fusion(bf16[2048,1024]{0,1:T(8,128)(2,1)} %fusion.63, bf16[1024,2304]{0,1:T(8,128)(2,1)} %all-gather.5.cloned.1.call-done), kind=kOutput, calls=%fused_computation.129 | convolution fusion | flops 3221225472 | bytes 12058624 | tf_op jit(solution)/shard_map/dot_general | solution.py:479
  356.2 8.5 %fusion.48 = f32[2048,768]{1,0:T(8,128)} fusion(bf16[2048,1024]{0,1:T(8,128)(2,1)} %fusion.63, bf16[1024,2304]{0,1:T(8,128)(2,1)S(1)} %copy-done.95), kind=kOutput, calls=%fused_computation.133 | convolution fusion | flops 3221225472 | bytes 12058624 | tf_op jit(solution)/shard_map/dot_general | solution.py:478
  364.7 11.5 %multiply_convert_fusion = (bf16[2048,768]{1,0:T(8,128)(2,1)S(1)}, bf16[2048,768]{1,0:T(8,128)(2,1)S(1)}, bf16[2048,768]{1,0:T(8,128)(2,1)}) fusion(f32[2048,768]{1,0:T(8,128)} %fusion.48, f32[2048,768]{1,0:T(8,128)} %fusion.44, bf16[2048,1024]{0,1:T(8,128)(2,1)S(1)} %copy-done.48, bf16[1024,2304]{0,1:T(8,128)(2,1)S(1)} %copy-done.95), kind=kOutput, calls=%fused_computation.8 | convolution fusion | flops 3246391296 | bytes 27787264 | tf_op jit(solution)/shard_map/dot_general | solution.py:488
  395.3 23.7 %collective-permute-done.12 = bf16[512,1024]{0,1:T(8,128)(2,1)S(1)} collective-permute-done((bf16[512,1024]{0,1:T(8,128)(2,1)S(1)}, bf16[512,1024]{0,1:T(8,128)(2,1)S(1)}, u32[]{:S(2)}, u32[]{:S(2)}) %collective-permute-start.12) | collective-permute-done | bytes 1048608 | tf_op jit(solution)/shard_map/ppermute | solution.py:336
  425.2 21.7 %collective-permute-done.13 = bf16[512,1024]{0,1:T(8,128)(2,1)S(1)} collective-permute-done((bf16[512,1024]{0,1:T(8,128)(2,1)S(1)}, bf16[512,1024]{0,1:T(8,128)(2,1)S(1)}, u32[]{:S(2)}, u32[]{:S(2)}) %collective-permute-start.13) | collective-permute-done | bytes 1048608 | tf_op jit(solution)/shard_map/ppermute | solution.py:336
  447.2 7.2 convolution_convert_fusion.3
  454.3 7.0 convolution_convert_fusion.4
  482.0 16.1 %pad_maximum_fusion = bf16[1024,2816]{0,1:T(8,128)(2,1)} fusion(bf16[1024,512]{0,1:T(8,128)(2,1)S(1)} %convolution_convert_fusion.5, bf16[1024,768]{0,1:T(8,128)(2,1)S(1)} %copy-done.58, bf16[1024,768]{0,1:T(8,128)(2,1)S(1)} %copy-done.56, bf16[1024,768]{0,1:T(8,128)(2,1)S(1)} %copy-done.57), kind=kLoop, calls=%fused_computation.12 | loop fusion | flops 23068672 | bytes 11534336 | tf_op jit(solution)/shard_map/concatenate | solution.py:508
  500.6 8.4 %copy.214 = bf16[1024,2816]{1,0:T(8,128)(2,1)} copy(bf16[1024,2816]{0,1:T(8,128)(2,1)} %pad_maximum_fusion) | data formatting | bytes 11534336
  510.3 77.9 %attn_bwd.1 = (f32[2,2,2048,128]{3,2,1,0:T(8,128)}, f32[2,2,2048,128]{3,2,1,0:T(8,128)}, f32[2,2,2048,128]{3,2,1,0:T(8,128)}) custom-call(s32[7,18]{1,0:T(8,128)} %broadcast_select_fusion.tab_ref, bf16[2,2,2048,128]{3,2,1,0:T(8,128)(2,1)} %copy-done, bf16[2,2,2048,128]{3,2,1,0:T(8,128)(2,1)} %get-tuple-element.29.h_ref, ...), custom_call_target="tpu_custom_call" | custom-call | flops 24159191040 | bytes 37748736 | tf_op jit(solution)/shard_map/attn_bwd/pallas_call | solution.py:203
  595.2 6.0 fusion.41
  606.2 39.7 %collective-permute-done.15 = bf16[2,2,2048,128]{3,2,1,0:T(8,128)(2,1)S(1)} collective-permute-done((bf16[2,2,2048,128]{3,2,1,0:T(8,128)(2,1)}, bf16[2,2,2048,128]{3,2,1,0:T(8,128)(2,1)S(1)}, u32[]{:S(2)}, u32[]{:S(2)}) %collective-permute-start.15) | collective-permute-done | bytes 2097184 | tf_op jit(solution)/shard_map/ppermute | solution.py:231
  713.3 6.8 reshape.348
  747.0 6.8 collective-permute-done.18
  786.1 7.0 collective-permute-done.22
  (433 shorter events, 320.0 us)
Async XLA Ops:
  7.2 75.2 %all-gather.3.cloned.1.call-start = ((), (), s32[]{:S(2)}) async-start(), calls=%async_computation.1 | async-start | bytes 3557376 | tf_op jit(solution)/shard_map/all_gather | solution.py:402
  16.7 330.6 %all-gather.5.cloned.1.call-start = ((), (), s32[]{:S(2)}) async-start(), calls=%async_computation.2 | async-start | bytes 5308416 | tf_op jit(solution)/shard_map/all_gather | solution.py:460
  86.2 24.2 %collective-permute-start = (bf16[512,1024]{0,1:T(8,128)(2,1)S(1)}, bf16[512,1024]{0,1:T(8,128)(2,1)S(1)}, u32[]{:S(2)}, u32[]{:S(2)}) collective-permute-start(bf16[512,1024]{0,1:T(8,128)(2,1)S(1)} %get-tuple-element.125), channel_id=1, source_target_pairs={{0,2},{1,3},{2,0},{3,1},{4,6},{5,7},{6,4},{7,5},{8,10},{9,11},{10,... | collective-permute-start | bytes 3145736 | tf_op jit(solution)/shard_map/ppermute | solution.py:336
  91.0 576.7 %reduce-scatter.4.cloned.1.call-start = ((), (), s32[]{:S(2)}) async-start(), calls=%async_computation.3 | async-start | bytes 6488064
  111.9 18.0 %collective-permute-start.1 = (bf16[2,512,1024]{1,2,0:T(8,128)(2,1)}, bf16[2,512,1024]{1,2,0:T(8,128)(2,1)}, u32[]{:S(2)}, u32[]{:S(2)}) collective-permute-start(bf16[2,512,1024]{1,2,0:T(8,128)(2,1)} %pad_maximum_fusion.2), channel_id=1, source_target_pairs={{0,1},{1,0},{2,3},{3,2},{4,5},{5,4},{6,7},{7,6},{8,9},{9,8},{10,11... | collective-permute-start | bytes 6291464 | tf_op jit(solution)/shard_map/ppermute | solution.py:336
  153.8 49.0 %collective-permute-start.2 = (bf16[2,2048,2,128]{3,1,2,0:T(8,128)(2,1)}, bf16[2,2048,2,128]{3,1,2,0:T(8,128)(2,1)}, u32[]{:S(2)}, u32[]{:S(2)}) collective-permute-start(bf16[2,2048,2,128]{3,1,2,0:T(8,128)(2,1)} %pad_maximum_fusion.3), channel_id=1, source_target_pairs={{0,4},{4,0},{8,12},{12,8},{16,20},{20,16},{24,28},{28,24},{1,5},{5... | collective-permute-start | bytes 6291464 | tf_op jit(solution)/shard_map/ppermute | solution.py:231
  263.5 4.2 collective-permute-start.3
  270.4 26.1 %collective-permute-start.4 = (bf16[512,1024]{0,1:T(8,128)(2,1)S(1)}, bf16[512,1024]{0,1:T(8,128)(2,1)}, u32[]{:S(2)}, u32[]{:S(2)}) collective-permute-start(bf16[512,1024]{0,1:T(8,128)(2,1)S(1)} %fusion.34), channel_id=1, source_target_pairs={{0,2},{1,3},{2,0},{3,1},{4,6},{5,7},{6,4},{7,5},{8,10},{9,11},{10,... | collective-permute-start | bytes 3145736 | tf_op jit(solution)/shard_map/ppermute | solution.py:336
  288.1 30.7 %collective-permute-start.9 = (bf16[512,1024]{0,1:T(8,128)(2,1)S(1)}, bf16[512,1024]{0,1:T(8,128)(2,1)S(1)}, u32[]{:S(2)}, u32[]{:S(2)}) collective-permute-start(bf16[512,1024]{0,1:T(8,128)(2,1)S(1)} %get-tuple-element.119), channel_id=1, source_target_pairs={{0,2},{1,3},{2,0},{3,1},{4,6},{5,7},{6,4},{7,5},{8,10},{9,11},{10,... | collective-permute-start | bytes 3145736 | tf_op jit(solution)/shard_map/ppermute | solution.py:336
  302.8 37.7 %collective-permute-start.5 = (bf16[512,1024]{0,1:T(8,128)(2,1)S(1)}, bf16[512,1024]{0,1:T(8,128)(2,1)S(1)}, u32[]{:S(2)}, u32[]{:S(2)}) collective-permute-start(bf16[512,1024]{0,1:T(8,128)(2,1)S(1)} %get-tuple-element.121), channel_id=1, source_target_pairs={{0,2},{1,3},{2,0},{3,1},{4,6},{5,7},{6,4},{7,5},{8,10},{9,11},{10,... | collective-permute-start | bytes 3145736 | tf_op jit(solution)/shard_map/ppermute | solution.py:336
  319.1 21.9 %collective-permute-start.10 = (bf16[2,512,1024]{1,2,0:T(8,128)(2,1)S(1)}, bf16[2,512,1024]{1,2,0:T(8,128)(2,1)S(1)}, u32[]{:S(2)}, u32[]{:S(2)}) collective-permute-start(bf16[2,512,1024]{1,2,0:T(8,128)(2,1)S(1)} %pad_maximum_fusion.9), channel_id=1, source_target_pairs={{0,1},{1,0},{2,3},{3,2},{4,5},{5,4},{6,7},{7,6},{8,9},{9,8},{10,11... | collective-permute-start | bytes 6291464 | tf_op jit(solution)/shard_map/ppermute | solution.py:336
  393.7 25.3 %collective-permute-start.12 = (bf16[512,1024]{0,1:T(8,128)(2,1)S(1)}, bf16[512,1024]{0,1:T(8,128)(2,1)S(1)}, u32[]{:S(2)}, u32[]{:S(2)}) collective-permute-start(bf16[512,1024]{0,1:T(8,128)(2,1)S(1)} %fusion.24), channel_id=1, source_target_pairs={{0,2},{1,3},{2,0},{3,1},{4,6},{5,7},{6,4},{7,5},{8,10},{9,11},{10,... | collective-permute-start | bytes 3145736 | tf_op jit(solution)/shard_map/ppermute | solution.py:336
  422.5 24.4 %collective-permute-start.13 = (bf16[512,1024]{0,1:T(8,128)(2,1)S(1)}, bf16[512,1024]{0,1:T(8,128)(2,1)S(1)}, u32[]{:S(2)}, u32[]{:S(2)}) collective-permute-start(bf16[512,1024]{0,1:T(8,128)(2,1)S(1)} %get-tuple-element.116), channel_id=1, source_target_pairs={{0,2},{1,3},{2,0},{3,1},{4,6},{5,7},{6,4},{7,5},{8,10},{9,11},{10,... | collective-permute-start | bytes 3145736 | tf_op jit(solution)/shard_map/ppermute | solution.py:336
  447.1 19.0 %collective-permute-start.14 = (bf16[2,512,1024]{1,2,0:T(8,128)(2,1)S(1)}, bf16[2,512,1024]{1,2,0:T(8,128)(2,1)S(1)}, u32[]{:S(2)}, u32[]{:S(2)}) collective-permute-start(bf16[2,512,1024]{1,2,0:T(8,128)(2,1)S(1)} %pad_maximum_fusion.11), channel_id=1, source_target_pairs={{0,1},{1,0},{2,3},{3,2},{4,5},{5,4},{6,7},{7,6},{8,9},{9,8},{10,11... | collective-permute-start | bytes 6291464 | tf_op jit(solution)/shard_map/ppermute | solution.py:336
  593.8 52.2 %collective-permute-start.15 = (bf16[2,2,2048,128]{3,2,1,0:T(8,128)(2,1)}, bf16[2,2,2048,128]{3,2,1,0:T(8,128)(2,1)S(1)}, u32[]{:S(2)}, u32[]{:S(2)}) collective-permute-start(bf16[2,2,2048,128]{3,2,1,0:T(8,128)(2,1)} %fusion.5), channel_id=1, source_target_pairs={{0,4},{4,0},{8,12},{12,8},{16,20},{20,16},{24,28},{28,24},{1,5},{5... | collective-permute-start | bytes 6291464 | tf_op jit(solution)/shard_map/ppermute | solution.py:231
  603.1 155.2 %collective-permute-start.7 = (bf16[2,512,1024]{1,2,0:T(8,128)(2,1)}, bf16[2,512,1024]{1,2,0:T(8,128)(2,1)}, u32[]{:S(2)}, u32[]{:S(2)}) collective-permute-start(bf16[2,512,1024]{1,2,0:T(8,128)(2,1)} %pad_maximum_fusion.8), channel_id=1, source_target_pairs={{0,1},{1,0},{2,3},{3,2},{4,5},{5,4},{6,7},{7,6},{8,9},{9,8},{10,11... | collective-permute-start | bytes 6291464 | tf_op jit(solution)/shard_map/ppermute | solution.py:336
  702.8 35.9 %collective-permute-start.16 = (bf16[2,512,1024]{1,2,0:T(8,128)(2,1)}, bf16[2,512,1024]{1,2,0:T(8,128)(2,1)}, u32[]{:S(2)}, u32[]{:S(2)}) collective-permute-start(bf16[2,512,1024]{1,2,0:T(8,128)(2,1)} %pad_maximum_fusion.12), channel_id=1, source_target_pairs={{0,1},{1,0},{2,3},{3,2},{4,5},{5,4},{6,7},{7,6},{8,9},{9,8},{10,11... | collective-permute-start | bytes 6291464 | tf_op jit(solution)/shard_map/ppermute | solution.py:336
  728.5 25.3 %collective-permute-start.18 = (bf16[2,2,128,1024]{3,2,0,1:T(8,128)(2,1)}, bf16[2,2,128,1024]{3,2,0,1:T(8,128)(2,1)}, u32[]{:S(2)}, u32[]{:S(2)}) collective-permute-start(bf16[2,2,128,1024]{3,2,0,1:T(8,128)(2,1)} %bitcast.211), channel_id=1, source_target_pairs={{0,4},{4,0},{8,12},{12,8},{16,20},{20,16},{24,28},{28,24},{1,5},{5... | collective-permute-start | bytes 3145736 | tf_op jit(solution)/shard_map/ppermute | solution.py:316
  745.4 28.7 %collective-permute-start.17 = (bf16[512,1024]{0,1:T(8,128)(2,1)}, bf16[512,1024]{0,1:T(8,128)(2,1)S(1)}, u32[]{:S(2)}, u32[]{:S(2)}) collective-permute-start(bf16[512,1024]{0,1:T(8,128)(2,1)} %fusion.18), channel_id=1, source_target_pairs={{0,2},{1,3},{2,0},{3,1},{4,6},{5,7},{6,4},{7,5},{8,10},{9,11},{10,... | collective-permute-start | bytes 3145736 | tf_op jit(solution)/shard_map/ppermute | solution.py:336
  756.8 13.0 %collective-permute-start.19 = (bf16[2,128,1024]{2,1,0:T(8,128)(2,1)S(1)}, bf16[2,128,1024]{2,1,0:T(8,128)(2,1)S(1)}, u32[]{:S(2)}, u32[]{:S(2)}) collective-permute-start(bf16[2,128,1024]{2,1,0:T(8,128)(2,1)S(1)} %fusion.74), channel_id=1, source_target_pairs={{0,8},{4,12},{8,0},{12,4},{16,24},{20,28},{24,16},{28,20},{1,9},{5... | collective-permute-start | bytes 1572872 | tf_op jit(solution)/shard_map/ppermute | solution.py:316
  765.1 37.9 %collective-permute-start.8 = (bf16[512,1024]{0,1:T(8,128)(2,1)}, bf16[512,1024]{0,1:T(8,128)(2,1)}, u32[]{:S(2)}, u32[]{:S(2)}) collective-permute-start(bf16[512,1024]{0,1:T(8,128)(2,1)} %fusion.28), channel_id=1, source_target_pairs={{0,2},{1,3},{2,0},{3,1},{4,6},{5,7},{6,4},{7,5},{8,10},{9,11},{10,... | collective-permute-start | bytes 3145736 | tf_op jit(solution)/shard_map/ppermute | solution.py:336
  771.6 13.3 %collective-permute-start.20 = (bf16[128,1024]{1,0:T(8,128)(2,1)}, bf16[128,1024]{1,0:T(8,128)(2,1)}, u32[]{:S(2)}, u32[]{:S(2)}) collective-permute-start(bf16[128,1024]{1,0:T(8,128)(2,1)} %fusion.81), channel_id=1, source_target_pairs={{0,16},{4,20},{8,24},{12,28},{16,0},{20,4},{24,8},{28,12},{1,17},{... | collective-permute-start | bytes 786440 | tf_op jit(solution)/shard_map/ppermute | solution.py:316
  783.2 9.9 %collective-permute-start.22 = (f32[2304]{0:T(1024)S(1)}, f32[2304]{0:T(1024)S(1)}, u32[]{:S(2)}, u32[]{:S(2)}) collective-permute-start(f32[2304]{0:T(1024)S(1)} %fusion.96), channel_id=1, source_target_pairs={{0,2},{1,3},{2,0},{3,1},{4,6},{5,7},{6,4},{7,5},{8,10},{9,11},{10,... | collective-permute-start | bytes 27656 | tf_op jit(solution)/shard_map/ppermute | solution.py:327
  800.5 11.7 %collective-permute-start.25 = (f32[2304]{0:T(1024)S(1)}, f32[2304]{0:T(1024)S(1)}, u32[]{:S(2)}, u32[]{:S(2)}) collective-permute-start(f32[2304]{0:T(1024)S(1)} %add.387), channel_id=1, source_target_pairs={{0,16},{4,20},{8,24},{12,28},{16,0},{20,4},{24,8},{28,12},{1,17},{... | collective-permute-start | bytes 27656 | tf_op jit(solution)/shard_map/ppermute | solution.py:327
  (106 other events, 1746.5 us)
Sparse Core Ops, SparseCore 0:
  16.8 65.5 all-gather.2
  91.1 77.8 all-gather.4
  509.2 111.3 reduce-scatter.3

commit v4 on v3

--- a/solution.py
+++ b/solution.py
@@ -22,7 +22,7 @@
     return ((1 - p) * quarter + r) if r < quarter else ((2 + p) * quarter + r - quarter)
 
 
-def _pair_tables(p, quarter, block, by_key):
+def _pair_tables(p, quarter, block, by_key, source):
     rows = 2 * quarter
     count = rows // block
     kmap = {}
@@ -33,13 +33,15 @@
     for j in range(count):
         qpb = _own_place(p, quarter, j * block) // block
         for kpb in range(qpb + 1):
-            pairs.append((j, qpb, kpb))
+            if kmap[kpb][0] == source:
+                pairs.append((j, qpb, kpb))
     if by_key:
         pairs.sort(key=lambda t: (t[2], t[0]))
     group = [t[2] if by_key else t[0] for t in pairs]
-    first = [1 if n == 0 or group[n - 1] != group[n] else 0 for n in range(len(pairs))]
-    last = [1 if n == len(pairs) - 1 or group[n + 1] != group[n] else 0 for n in range(len(pairs))]
-    table = np.array(
+    size = len(pairs)
+    first = [1 if n == 0 or group[n - 1] != group[n] else 0 for n in range(size)]
+    last = [1 if n == size - 1 or group[n + 1] != group[n] else 0 for n in range(size)]
+    return np.array(
         [
             [t[0] for t in pairs],
             [t[1] for t in pairs],
@@ -51,12 +53,11 @@
         ],
         np.int32,
     )
-    return table
-
-
-def pair_tables(piece, quarter, block, by_key):
-    t0 = _pair_tables(0, quarter, block, by_key)
-    t1 = _pair_tables(1, quarter, block, by_key)
+
+
+def pair_tables(piece, quarter, block, by_key, source):
+    t0 = _pair_tables(0, quarter, block, by_key, source)
+    t1 = _pair_tables(1, quarter, block, by_key, source)
     assert t0.shape == t1.shape
     return jnp.where(piece == 0, jnp.asarray(t0), jnp.asarray(t1))
 
@@ -68,18 +69,18 @@
     return (kp >= start) & (kp <= qp)
 
 
-def _fwd_kernel(tab_ref, q_ref, qs_ref, k_ref, v_ref, o_ref, l_ref, acc_ref, sum_ref, *, scale, block):
+def _fwd_kernel(tab_ref, q_ref, qs_ref, k_ref, v_ref, a_in_ref, l_in_ref, a_ref, l_ref, acc_ref, sum_ref, *, scale, block):
     n = pl.program_id(1)
     share = q_ref.shape[1]
 
     @pl.when(tab_ref[5, n] == 1)
     def _():
-        acc_ref[...] = jnp.zeros(acc_ref.shape, acc_ref.dtype)
-        sum_ref[...] = jnp.zeros(sum_ref.shape, sum_ref.dtype)
+        acc_ref[...] = a_in_ref[0].reshape(share * block, HEAD_SIZE)
+        sum_ref[...] = l_in_ref[0][:, :, :1]
 
     q = q_ref[0].reshape(share * block, HEAD_SIZE)
-    k = k_ref[0, 0]
-    v = v_ref[0, 0]
+    k = k_ref[0]
+    v = v_ref[0]
     s = lax.dot_general(q, k, TRANS_B, preferred_element_type=jnp.float32) * scale
     allowed = _mask(tab_ref[1, n], tab_ref[2, n], qs_ref[...], block)
     e = jnp.where(allowed[None], jnp.exp(s.reshape(share, block, block)), 0.0)
@@ -90,29 +91,30 @@
 
     @pl.when(tab_ref[6, n] == 1)
     def _():
-        total = sum_ref[...]
-        o_ref[0] = acc_ref[...].reshape(share, block, HEAD_SIZE) / total
-        l_ref[0] = jnp.broadcast_to(total, (share, block, 128))
-
-
-def attention_forward(q, qs, k_all, v_all, piece, quarter, block=512):
-    kvh, share, rows, _ = q.shape
-    tab = pair_tables(piece, quarter, block, False)
+        a_ref[0] = acc_ref[...].reshape(share, block, HEAD_SIZE)
+        l_ref[0] = jnp.broadcast_to(sum_ref[...], (share, block, 128))
+
+
+def attention_forward(q, qs, keys, values, a_in, l_in, piece, quarter, source, block=512):
+    kvh, share, _, _ = q.shape
+    tab = pair_tables(piece, quarter, block, False, source)
     npairs = tab.shape[1]
     scale = HEAD_SIZE ** (-0.5)
+    row_spec = pl.BlockSpec((1, share, block, HEAD_SIZE), lambda h, n, t: (h, 0, t[0, n], 0))
+    lane_spec = pl.BlockSpec((1, share, block, 128), lambda h, n, t: (h, 0, t[0, n], 0))
+    key_spec = pl.BlockSpec((1, block, HEAD_SIZE), lambda h, n, t: (h, t[4, n], 0))
     grid_spec = pltpu.PrefetchScalarGridSpec(
         num_scalar_prefetch=1,
         grid=(kvh, npairs),
         in_specs=[
-            pl.BlockSpec((1, share, block, HEAD_SIZE), lambda h, n, t: (h, 0, t[0, n], 0)),
+            row_spec,
             pl.BlockSpec((block, 128), lambda h, n, t: (t[0, n], 0)),
-            pl.BlockSpec((1, 1, block, HEAD_SIZE), lambda h, n, t: (t[3, n], h, t[4, n], 0)),
-            pl.BlockSpec((1, 1, block, HEAD_SIZE), lambda h, n, t: (t[3, n], h, t[4, n], 0)),
+            key_spec,
+            key_spec,
+            row_spec,
+            lane_spec,
         ],
-        out_specs=[
-            pl.BlockSpec((1, share, block, HEAD_SIZE), lambda h, n, t: (h, 0, t[0, n], 0)),
-            pl.BlockSpec((1, share, block, 128), lambda h, n, t: (h, 0, t[0, n], 0)),
-        ],
+        out_specs=[row_spec, lane_spec],
         scratch_shapes=[
             pltpu.VMEM((share * block, HEAD_SIZE), jnp.float32),
             pltpu.VMEM((share, block, 1), jnp.float32),
@@ -123,27 +125,29 @@
         functools.partial(_fwd_kernel, scale=scale, block=block),
         grid_spec=grid_spec,
         out_shape=[
-            jax.ShapeDtypeStruct((kvh, share, rows, HEAD_SIZE), jnp.float32),
-            jax.ShapeDtypeStruct((kvh, share, rows, 128), jnp.float32),
+            jax.ShapeDtypeStruct(a_in.shape, jnp.float32),
+            jax.ShapeDtypeStruct(l_in.shape, jnp.float32),
         ],
+        input_output_aliases={5: 0, 6: 1},
         compiler_params=pltpu.CompilerParams(
             dimension_semantics=("arbitrary", "arbitrary"), vmem_limit_bytes=48 * 1024 * 1024
         ),
         cost_estimate=pl.CostEstimate(
-            flops=flops, transcendentals=kvh * npairs * share * block * block,
-            bytes_accessed=kvh * npairs * (4 * block * HEAD_SIZE * 2),
+            flops=flops,
+            transcendentals=kvh * npairs * share * block * block,
+            bytes_accessed=kvh * npairs * (8 * block * HEAD_SIZE * 2),
         ),
         name="attn_fwd",
-    )(tab, q, qs, k_all, v_all)
-
-
-def _bwd_kernel(tab_ref, q_ref, h_ref, dl_ref, qs_ref, k_ref, v_ref, dq_ref, dk_ref, dv_ref, dk_acc, dv_acc, *, scale, block):
+    )(tab, q, qs, keys, values, a_in, l_in)
+
+
+def _bwd_kernel(tab_ref, q_ref, h_ref, dl_ref, qs_ref, k_ref, v_ref, dq_in_ref, dq_ref, dk_ref, dv_ref, dk_acc, dv_acc, *, scale, block):
     n = pl.program_id(1)
     share = q_ref.shape[1]
 
     @pl.when(n == 0)
     def _():
-        dq_ref[...] = jnp.zeros(dq_ref.shape, dq_ref.dtype)
+        dq_ref[...] = dq_in_ref[...]
 
     @pl.when(tab_ref[5, n] == 1)
     def _():
@@ -152,8 +156,8 @@
 
     q = q_ref[0].reshape(share * block, HEAD_SIZE)
     hh = h_ref[0].reshape(share * block, HEAD_SIZE)
-    k = k_ref[0, 0]
-    v = v_ref[0, 0]
+    k = k_ref[0]
+    v = v_ref[0]
     s = lax.dot_general(q, k, TRANS_B, preferred_element_type=jnp.float32) * scale
     allowed = _mask(tab_ref[1, n], tab_ref[2, n], qs_ref[...], block)
     e = jnp.where(allowed[None], jnp.exp(s.reshape(share, block, block)), 0.0)
@@ -169,31 +173,31 @@
 
     @pl.when(tab_ref[6, n] == 1)
     def _():
-        dk_ref[0, 0] = dk_acc[...] * scale
-        dv_ref[0, 0] = dv_acc[...]
-
-
-def attention_backward(q, hgrad, delta, qs, k_all, v_all, piece, quarter, block=512):
+        dk_ref[0] = dk_acc[...] * scale
+        dv_ref[0] = dv_acc[...]
+
+
+def attention_backward(q, hgrad, delta, qs, keys, values, dq_in, piece, quarter, source, block=512):
     kvh, share, rows, _ = q.shape
-    tab = pair_tables(piece, quarter, block, True)
+    tab = pair_tables(piece, quarter, block, True, source)
     npairs = tab.shape[1]
     scale = HEAD_SIZE ** (-0.5)
+    row_spec = pl.BlockSpec((1, share, block, HEAD_SIZE), lambda h, n, t: (h, 0, t[0, n], 0))
+    key_spec = pl.BlockSpec((1, block, HEAD_SIZE), lambda h, n, t: (h, t[4, n], 0))
+    full_spec = pl.BlockSpec((1, share, rows, HEAD_SIZE), lambda h, n, t: (h, 0, 0, 0))
     grid_spec = pltpu.PrefetchScalarGridSpec(
         num_scalar_prefetch=1,
         grid=(kvh, npairs),
         in_specs=[
-            pl.BlockSpec((1, share, block, HEAD_SIZE), lambda h, n, t: (h, 0, t[0, n], 0)),
-            pl.BlockSpec((1, share, block, HEAD_SIZE), lambda h, n, t: (h, 0, t[0, n], 0)),
+            row_spec,
+            row_spec,
             pl.BlockSpec((1, share, block, 128), lambda h, n, t: (h, 0, t[0, n], 0)),
             pl.BlockSpec((block, 128), lambda h, n, t: (t[0, n], 0)),
-            pl.BlockSpec((1, 1, block, HEAD_SIZE), lambda h, n, t: (t[3, n], h, t[4, n], 0)),
-            pl.BlockSpec((1, 1, block, HEAD_SIZE), lambda h, n, t: (t[3, n], h, t[4, n], 0)),
+            key_spec,
+            key_spec,
+            full_spec,
         ],
-        out_specs=[
-            pl.BlockSpec((1, share, rows, HEAD_SIZE), lambda h, n, t: (h, 0, 0, 0)),
-            pl.BlockSpec((1, 1, block, HEAD_SIZE), lambda h, n, t: (t[3, n], h, t[4, n], 0)),
-            pl.BlockSpec((1, 1, block, HEAD_SIZE), lambda h, n, t: (t[3, n], h, t[4, n], 0)),
-        ],
+        out_specs=[full_spec, key_spec, key_spec],
         scratch_shapes=[
             pltpu.VMEM((block, HEAD_SIZE), jnp.float32),
             pltpu.VMEM((block, HEAD_SIZE), jnp.float32),
@@ -204,22 +208,23 @@
         functools.partial(_bwd_kernel, scale=scale, block=block),
         grid_spec=grid_spec,
         out_shape=[
-            jax.ShapeDtypeStruct((kvh, share, rows, HEAD_SIZE), jnp.float32),
-            jax.ShapeDtypeStruct(k_all.shape, jnp.float32),
-            jax.ShapeDtypeStruct(v_all.shape, jnp.float32),
+            jax.ShapeDtypeStruct(dq_in.shape, jnp.float32),
+            jax.ShapeDtypeStruct(keys.shape, jnp.float32),
+            jax.ShapeDtypeStruct(values.shape, jnp.float32),
         ],
+        input_output_aliases={7: 0},
         compiler_params=pltpu.CompilerParams(
             dimension_semantics=("arbitrary", "arbitrary"), vmem_limit_bytes=56 * 1024 * 1024
         ),
         cost_estimate=pl.CostEstimate(
-            flops=flops, transcendentals=kvh * npairs * share * block * block,
-            bytes_accessed=kvh * npairs * (8 * block * HEAD_SIZE * 2),
+            flops=flops,
+            transcendentals=kvh * npairs * share * block * block,
+            bytes_accessed=kvh * npairs * (10 * block * HEAD_SIZE * 2),
         ),
         name="attn_bwd",
-    )(tab, q, hgrad, delta, qs, k_all, v_all)
-
-
-SLOT_TOKENS = 4096
+    )(tab, q, hgrad, delta, qs, keys, values, dq_in)
+
+
 PIECES = 2
 
 
@@ -254,15 +259,6 @@
     return rotary(rms_scale(shaped, gain), start_offset)
 
 
-def slot_tables(lengths_row, slot_length):
-    ends = jnp.cumsum(lengths_row)
-    place = jnp.arange(slot_length, dtype=jnp.int32)
-    passed = place[:, None] >= ends[None, :]
-    segment_ids = jnp.sum(passed.astype(jnp.int32), axis=1)
-    start = jnp.sum(jnp.where(passed, lengths_row[None, :], 0), axis=1)
-    return (segment_ids, place - start, place < ends[-1])
-
-
 def piece_places(which, group_rows):
     quarter = group_rows // 2
     local = jnp.arange(group_rows, dtype=jnp.int32)
@@ -280,15 +276,6 @@
     return lax.dot_general(
         left, right, (((1,), (1,)), ((), ())), preferred_element_type=jnp.float32
     )
-
-
-def gain_column(values, rows_f):
-    column = values.astype(jnp.bfloat16)
-    return jnp.pad(column, (0, rows_f - column.shape[0]))[:, None]
-
-
-def gain_rows(column, fs, rows_f, own):
-    return column.reshape(fs, rows_f)[:, :own].reshape(fs * own)
 
 
 def split_columns(full, widths):
@@ -318,6 +305,20 @@
         )
         buf = keep + got.astype(jnp.float32)
     return split_columns(buf, widths)
+
+
+def fsdp_gather(values):
+    count = lax.axis_size("fsdp")
+    me = lax.axis_index("fsdp")
+    distance = 1
+    while distance < count:
+        got = lax.ppermute(values, "fsdp", [(i, i ^ distance) for i in range(count)])
+        low = (me & distance) == 0
+        values = jnp.concatenate(
+            [jnp.where(low, values, got), jnp.where(low, got, values)]
+        )
+        distance *= 2
+    return values
 
 
 def all_sum(values):
@@ -388,28 +389,29 @@
     member = lax.axis_index("fsdp")
     slot = member // PIECES
     piece = member % PIECES
-    segment_ids, start_offset, valid = slot_tables(
-        lax.dynamic_index_in_dim(lengths, slot, 0, keepdims=False), SLOT_TOKENS
-    )
+    lengths_row = lax.dynamic_index_in_dim(lengths, slot, 0, keepdims=False)
+    ends = jnp.cumsum(lengths_row)
     group_place = piece_places(piece, group_rows)
-    group_segment = jnp.take(segment_ids, group_place)
-    group_offset = jnp.take(start_offset, group_place)
+    passed = group_place[:, None] >= ends[None, :]
+    group_start = jnp.sum(jnp.where(passed, lengths_row[None, :], 0), axis=1)
+    group_offset = group_place - group_start
     local_valid = lax.dynamic_slice_in_dim(
-        jnp.take(valid, group_place), lax.axis_index("tensor") * rows, rows, 0
+        group_place < ends[-1], lax.axis_index("tensor") * rows, rows, 0
     )
     fs = lax.axis_size("fsdp")
-    rows_f = q_weight.shape[0]
+    gain_sizes = (input_gain.shape[0], q_gain.shape[0], k_gain.shape[0], post_gain.shape[0])
+    gains_all = fsdp_gather(
+        jnp.concatenate([input_gain, q_gain, k_gain, post_gain]).astype(jnp.bfloat16)
+    ).reshape(fs, sum(gain_sizes))
+    gain_in, gain_query, gain_keys, gain_post = [
+        part.reshape(-1) for part in split_columns(gains_all, gain_sizes)
+    ]
     attn_full = lax.all_gather(
         jnp.concatenate(
             [
                 q_weight.astype(jnp.bfloat16),
                 key_matrix.astype(jnp.bfloat16),
                 value_matrix.astype(jnp.bfloat16),
-                jnp.transpose(o_weight).astype(jnp.bfloat16),
-                gain_column(input_gain, rows_f),
-                gain_column(q_gain, rows_f),
-                gain_column(k_gain, rows_f),
-                gain_column(post_gain, rows_f),
             ],
             axis=1,
         ),
@@ -417,13 +419,8 @@
         axis=0,
         tiled=True,
     )
-    widths = (q_weight.shape[1], key_matrix.shape[1], value_matrix.shape[1], o_weight.shape[0])
-    w_query, w_key, w_value, w_out = split_columns(attn_full, widths)
-    gains_at = sum(widths)
-    gain_in = attn_full[:, gains_at]
-    gain_query = gain_rows(attn_full[:, gains_at + 1], fs, rows_f, q_gain.shape[0])
-    gain_keys = gain_rows(attn_full[:, gains_at + 2], fs, rows_f, k_gain.shape[0])
-    gain_post = attn_full[:, gains_at + 3]
+    widths = (q_weight.shape[1], key_matrix.shape[1], value_matrix.shape[1])
+    w_query, w_key, w_value = split_columns(attn_full, widths)
     x_float = hidden.astype(jnp.float32)
     gain_first = gain_in.astype(jnp.float32)
     first_all = token_gather(rms_scale(x_float, gain_first).astype(jnp.bfloat16))
@@ -442,27 +439,32 @@
         .reshape(group_rows, kv_heads, share, HEAD_SIZE)
     )
     key_rope = prepare_inputs(key_projected, gain_k, group_offset, kv_heads).astype(jnp.bfloat16)
-    moved = swapped(jnp.stack([key_rope, value_rows]), "fsdp", 0)
     quarter = group_rows // 2
-    query_start = jnp.broadcast_to((group_place - group_offset)[:, None], (group_rows, 128))
+    query_start = jnp.broadcast_to(group_start[:, None], (group_rows, 128))
     query_t = jnp.transpose(query_rope, (1, 2, 0, 3))
-    keys_all = jnp.stack([jnp.transpose(key_rope, (1, 0, 2)), jnp.transpose(moved[0], (1, 0, 2))])
-    values_all = jnp.stack([jnp.transpose(value_rows, (1, 0, 2)), jnp.transpose(moved[1], (1, 0, 2))])
-    heads_t, totals_t = attention_forward(query_t, query_start, keys_all, values_all, piece, quarter)
+    own_keys = jnp.transpose(key_rope, (1, 0, 2))
+    own_values = jnp.transpose(value_rows, (1, 0, 2))
+    moved = swapped(jnp.stack([own_keys, own_values]), "fsdp", 0)
+    sums = jnp.zeros(query_t.shape, jnp.float32)
+    totals = jnp.zeros(query_t.shape[:3] + (128,), jnp.float32)
+    sums, totals = attention_forward(
+        query_t, query_start, own_keys, own_values, sums, totals, piece, quarter, 0
+    )
+    sums, totals_t = attention_forward(
+        query_t, query_start, moved[0], moved[1], sums, totals, piece, quarter, 1
+    )
+    heads_t = sums / totals_t[..., :1]
     heads_out = jnp.transpose(heads_t, (2, 0, 1, 3))
     row_totals = jnp.transpose(totals_t[..., 0], (2, 0, 1))
     out_rows = heads_out.reshape(group_rows, q_heads * HEAD_SIZE).astype(jnp.bfloat16)
 
-    def out_term(start, count):
-        return contract_last(out_rows, w_out)
-
-    after_attn = x_float + token_sum(out_term, rows)
     mlp_full = lax.all_gather(
         jnp.concatenate(
             [
                 gate_weight.astype(jnp.bfloat16),
                 up_weight.astype(jnp.bfloat16),
                 jnp.transpose(down_weight).astype(jnp.bfloat16),
+                jnp.transpose(o_weight).astype(jnp.bfloat16),
             ],
             axis=1,
         ),
@@ -470,9 +472,14 @@
         axis=0,
         tiled=True,
     )
-    w_gate, w_up, w_down_t = split_columns(
-        mlp_full, (gate_weight.shape[1], up_weight.shape[1], down_weight.shape[0])
-    )
+    w_gate, w_up, w_down_t, w_out = split_columns(
+        mlp_full, (gate_weight.shape[1], up_weight.shape[1], down_weight.shape[0], o_weight.shape[0])
+    )
+
+    def out_term(start, count):
+        return contract_last(out_rows, w_out)
+
+    after_attn = x_float + token_sum(out_term, rows)
     gain_second = gain_post.astype(jnp.float32)
     second_all = token_gather(rms_scale(after_attn, gain_second).astype(jnp.bfloat16))
     gate_out = jnp.dot(second_all, w_gate, preferred_element_type=jnp.float32)
@@ -526,15 +533,20 @@
         [g.shape[1] for g in (gate_grad, up_grad, down_grad_t, out_weight_grad_t)],
     )
     mlp_shards = [part.astype(jnp.float32) for part in mlp_shards]
-    dq_raw, dk_all, dv_all = attention_backward(
-        query_t, grad_t, delta_t, query_start, keys_all, values_all, piece, quarter
+    dq_raw, dk_far, dv_far = attention_backward(
+        query_t, grad_t, delta_t, query_start, moved[0], moved[1],
+        jnp.zeros(query_t.shape, jnp.float32), piece, quarter, 1,
+    )
+    unseen = (piece == 1) & (jnp.arange(group_rows) >= quarter)
+    far_grads = jnp.where(unseen[None, None, :, None], 0.0, jnp.stack([dk_far, dv_far]))
+    returned = swapped(far_grads.astype(jnp.bfloat16), "fsdp", 0)
+    dq_raw, dk_own, dv_own = attention_backward(
+        query_t, grad_t, delta_t, query_start, own_keys, own_values,
+        dq_raw, piece, quarter, 0,
     )
     mlp_shards, dq_raw = lax.optimization_barrier((mlp_shards, dq_raw))
-    unseen = (piece == 1) & (jnp.arange(group_rows) >= quarter)
-    far_grads = jnp.where(unseen[None, None, :, None], 0.0, jnp.stack([dk_all[1], dv_all[1]]))
-    returned = swapped(far_grads.astype(jnp.bfloat16), "fsdp", 0).astype(jnp.float32)
-    grad_keys_total = jnp.transpose(dk_all[0] + returned[0], (1, 0, 2))
-    grad_values_total = jnp.transpose(dv_all[0] + returned[1], (1, 0, 2))
+    grad_keys_total = jnp.transpose(dk_own + returned[0].astype(jnp.float32), (1, 0, 2))
+    grad_values_total = jnp.transpose(dv_own + returned[1].astype(jnp.float32), (1, 0, 2))
     query_grads = jnp.transpose(dq_raw, (2, 0, 1, 3)) * scale
     query_grads = query_grads.reshape(group_rows, q_heads, HEAD_SIZE)
     unused, pull_query = jax.vjp(

time: 832 us -> 731 us (0.88)
  waiting for transfers between devices: 270 us -> 194 us
  local copies, waits for them, and re-layouts: 164 us -> 129 us
  Pallas kernels: 125 us -> 135 us
  starting transfers between devices: 27.4 us -> 36.3 us
  matrix products: 108 us -> 99.3 us
    all_gather x1, waiting for transfers between devices: 64.2 us -> 0.01 us  [shards(): lax.all_gather(jnp.concatenate([q_weight.astype(jnp.bfloat16), key_matrix...]
    ppermute x2, waiting for transfers between devices: 68.7 us -> 36.2 us  [swapped(): lax.ppermute(shard, axis, [(i, i ^ 1 << distance) for i in range(lax.axis...]
    gather x2 -> x0, local copies, waits for them, and re-layouts: 24.9 us -> none  [the longest x1 13.1 us: shards(): jnp.take(valid, group_place)]
    ppermute x16, waiting for transfers between devices: 118 us -> 140 us  [exchange(): lax.ppermute(values, 'tensor', [(i, i ^ distance) for i in range(count)])]
    pallas_call x1 -> x2, Pallas kernels: 77.9 us -> 83.5 us  [attention_backward(): pl.pallas_call(functools.partial(_bwd_kernel, scale=scale, block=block),...]
    unnamed x221 -> x224, local copies, waits for them, and re-layouts: 58.2 us -> 52.9 us
    pallas_call x1 -> x2, Pallas kernels: 47 us -> 51.9 us  [attention_forward(): pl.pallas_call(functools.partial(_fwd_kernel, scale=scale, block=block),...]
  transfers between devices with their start and end apart: 29 -> 32, of which waited for: 18 -> 20; matrix products, arithmetic and copies ran while one was open for 31% -> 30% of each run, Pallas kernels for 15% -> 19%
where the time goes in v4:
time: 731 us; the launch traced here: 724 us
  waiting for transfers between devices  194 us (27%)
  Pallas kernels  135 us (18%)
  local copies, waits for them, and re-layouts  129 us (18%)
  other arithmetic  114 us (16%)
  matrix products  99.3 us (14%)
  starting transfers between devices  36.3 us (5%)
  between operations  15.5 us (2%)
    ppermute x16, waiting for transfers between devices, exchange(): lax.ppermute(values, 'tensor', [(i, i ^ distance) for i in range(count)])  140 us
    pallas_call x2, Pallas kernels, attention_backward(): pl.pallas_call(functools.partial(_bwd_kernel, scale=scale, block=block),...  83.5 us
    unnamed x224, local copies, waits for them, and re-layouts  52.9 us
    pallas_call x2, Pallas kernels, attention_forward(): pl.pallas_call(functools.partial(_fwd_kernel, scale=scale, block=block),...  51.9 us
    ppermute x2, waiting for transfers between devices, swapped(): lax.ppermute(shard, axis, [(i, i ^ 1 << distance) for i in range(lax.axis...  36.2 us
    dot_general x7, matrix products, contract_last(): lax.dot_general(left, right, (((1,), (1,)), ((), ())), preferred_element_...  34.5 us
    dot_general x7, matrix products, contract_rows(): lax.dot_general(left, right, (((0,), (0,)), ((), ())), preferred_element_...  24.6 us
    concatenate x1, other arithmetic, shards(): jnp.concatenate([g.astype(jnp.bfloat16) for g in (gate_grad, up_grad, dow...  15.8 us
  transfers between devices with their start and end apart: 32, of which 20 were waited for; matrix products, arithmetic and copies ran while one was open for 30% of the time, Pallas kernels for 19%

profile of v4, /device:TPU:0, one launch (start us, length us, event | category | flops | bytes accessed | tf_op | source)
XLA Modules:
  0.0 724.4 jit_solution(12937212715898872723)
XLA Ops:
  35.3 16.4 %collective-permute-done.3 = bf16[512,1024]{0,1:T(8,128)(2,1)S(1)} collective-permute-done((bf16[512,1024]{0,1:T(8,128)(2,1)S(1)}, bf16[512,1024]{0,1:T(8,128)(2,1)S(1)}, u32[]{:S(2)}, u32[]{:S(2)}) %collective-permute-start.3) | collective-permute-done | bytes 1048608 | tf_op jit(solution)/shard_map/ppermute | solution.py:337
  108.7 28.8 %attn_fwd.2 = (f32[2,2,2048,128]{3,2,1,0:T(8,128)}, f32[2,2,2048,128]{3,2,1,0:T(8,128)}) custom-call(s32[7,10]{1,0:T(8,128)S(1)} %broadcast_select_fusion.3.tab_ref, bf16[2,2,2048,128]{3,2,1,0:T(8,128)(2,1)S(1)} %maximum_bitcast_fusion.q_ref, s32[2048,128]{1,0:T(8,128)S(1)} %broadcast_in_dim.45.qs_ref, ...), custom_call_target="tpu_custom_call", output_to_operand_aliasing={{0}: (5, {}), {1}: (6, {})} | custom-call | flops 5368709120 | bytes 20971520 | tf_op jit(solution)/shard_map/attn_fwd/pallas_call | solution.py:124
  137.6 26.5 %collective-permute-done.5 = bf16[2,2,2048,128]{3,2,1,0:T(8,128)(2,1)} collective-permute-done((bf16[2,2,2048,128]{3,2,1,0:T(8,128)(2,1)}, bf16[2,2,2048,128]{3,2,1,0:T(8,128)(2,1)}, u32[]{:S(2)}, u32[]{:S(2)}) %collective-permute-start.5) | collective-permute-done | bytes 2097184 | tf_op jit(solution)/shard_map/ppermute | solution.py:236
  165.8 23.1 %attn_fwd.3 = (f32[2,2,2048,128]{3,2,1,0:T(8,128)}, f32[2,2,2048,128]{3,2,1,0:T(8,128)}) custom-call(s32[7,8]{1,0:T(8,128)S(1)} %broadcast_select_fusion.7.tab_ref, bf16[2,2,2048,128]{3,2,1,0:T(8,128)(2,1)S(1)} %maximum_bitcast_fusion.q_ref, s32[2048,128]{1,0:T(8,128)S(1)} %broadcast_in_dim.45.qs_ref, ...), custom_call_target="tpu_custom_call", output_to_operand_aliasing={{0}: (5, {}), {1}: (6, {})} | custom-call | flops 4294967296 | bytes 16777216 | tf_op jit(solution)/shard_map/attn_fwd/pallas_call | solution.py:124
  213.4 21.4 %collective-permute-done.7 = bf16[512,1024]{0,1:T(8,128)(2,1)S(1)} collective-permute-done((bf16[512,1024]{0,1:T(8,128)(2,1)}, bf16[512,1024]{0,1:T(8,128)(2,1)S(1)}, u32[]{:S(2)}, u32[]{:S(2)}) %collective-permute-start.7) | collective-permute-done | bytes 1048608 | tf_op jit(solution)/shard_map/ppermute | solution.py:337
  239.3 18.0 %collective-permute-done.12 = bf16[512,1024]{0,1:T(8,128)(2,1)S(1)} collective-permute-done((bf16[512,1024]{0,1:T(8,128)(2,1)S(1)}, bf16[512,1024]{0,1:T(8,128)(2,1)S(1)}, u32[]{:S(2)}, u32[]{:S(2)}) %collective-permute-start.12) | collective-permute-done | bytes 1048608 | tf_op jit(solution)/shard_map/ppermute | solution.py:337
  257.5 21.4 %collective-permute-done.8 = bf16[512,1024]{0,1:T(8,128)(2,1)S(1)} collective-permute-done((bf16[512,1024]{0,1:T(8,128)(2,1)S(1)}, bf16[512,1024]{0,1:T(8,128)(2,1)S(1)}, u32[]{:S(2)}, u32[]{:S(2)}) %collective-permute-start.8) | collective-permute-done | bytes 1048608 | tf_op jit(solution)/shard_map/ppermute | solution.py:337
  283.7 5.6 fusion.44
  289.4 5.4 fusion.48
  294.8 12.7 %multiply_convert_fusion = (bf16[2048,768]{1,0:T(8,128)(2,1)}, bf16[2048,768]{1,0:T(8,128)(2,1)}, bf16[2048,768]{1,0:T(8,128)(2,1)}) fusion(f32[2048,768]{1,0:T(8,128)} %fusion.48, f32[2048,768]{1,0:T(8,128)} %fusion.44, bf16[2048,1024]{0,1:T(8,128)(2,1)S(1)} %fusion.61, bf16[1024,2816]{0,1:T(8,128)(2,1)S(1)} %bitcast.275), kind=kOutput, calls=%fused_computation.6 | convolution fusion | flops 3246391296 | bytes 27787264 | tf_op jit(solution)/shard_map/dot_general | solution.py:495
  307.5 7.7 %fusion.46 = f32[2048,1024]{0,1:T(8,128)} fusion(bf16[2048,768]{1,0:T(8,128)(2,1)} %get-tuple-element.135, bf16[1024,2816]{0,1:T(8,128)(2,1)S(1)} %bitcast.275), kind=kOutput, calls=%fused_computation.128 | convolution fusion | flops 3221225472 | bytes 13107200 | tf_op jit(solution)/shard_map/dot_general | solution.py:276
  315.2 7.1 convolution_add_fusion
  329.4 23.9 %collective-permute-done.15 = bf16[512,1024]{0,1:T(8,128)(2,1)S(1)} collective-permute-done((bf16[512,1024]{0,1:T(8,128)(2,1)S(1)}, bf16[512,1024]{0,1:T(8,128)(2,1)S(1)}, u32[]{:S(2)}, u32[]{:S(2)}) %collective-permute-start.15) | collective-permute-done | bytes 1048608 | tf_op jit(solution)/shard_map/ppermute | solution.py:337
  358.1 23.0 %collective-permute-done.16 = bf16[512,1024]{0,1:T(8,128)(2,1)S(1)} collective-permute-done((bf16[512,1024]{0,1:T(8,128)(2,1)S(1)}, bf16[512,1024]{0,1:T(8,128)(2,1)S(1)}, u32[]{:S(2)}, u32[]{:S(2)}) %collective-permute-start.16) | collective-permute-done | bytes 1048608 | tf_op jit(solution)/shard_map/ppermute | solution.py:337
  407.9 7.2 fusion.6
  415.2 15.8 %pad_maximum_fusion = bf16[1024,2816]{0,1:T(8,128)(2,1)} fusion(bf16[1024,512]{0,1:T(8,128)(2,1)S(1)} %convolution_convert_fusion.5, bf16[1024,768]{0,1:T(8,128)(2,1)S(1)} %copy-done.50, bf16[1024,768]{0,1:T(8,128)(2,1)S(1)} %copy-done.49, bf16[1024,768]{0,1:T(8,128)(2,1)S(1)} %copy-done.48), kind=kLoop, calls=%fused_computation.10 | loop fusion | flops 23068672 | bytes 11534336 | tf_op jit(solution)/shard_map/concatenate | solution.py:515
  433.5 8.3 %copy.205 = bf16[1024,2816]{1,0:T(8,128)(2,1)} copy(bf16[1024,2816]{0,1:T(8,128)(2,1)} %pad_maximum_fusion) | data formatting | bytes 11534336
  446.0 37.9 %attn_bwd.2 = (f32[2,2,2048,128]{3,2,1,0:T(8,128)}, f32[2,2048,128]{2,1,0:T(8,128)}, f32[2,2048,128]{2,1,0:T(8,128)}) custom-call(s32[7,8]{1,0:T(8,128)} %broadcast_select_fusion.6.tab_ref, bf16[2,2,2048,128]{3,2,1,0:T(8,128)(2,1)} %copy-done.1, bf16[2,2,2048,128]{3,2,1,0:T(8,128)(2,1)} %get-tuple-element.36.h_ref, ...), custom_call_target="tpu_custom_call", output_to_operand_aliasing={{0}: (7, {})} | custom-call | flops 10737418240 | bytes 20971520 | tf_op jit(solution)/shard_map/attn_bwd/pallas_call | solution.py:207
  500.2 45.7 %attn_bwd.3 = (f32[2,2,2048,128]{3,2,1,0:T(8,128)}, f32[2,2048,128]{2,1,0:T(8,128)}, f32[2,2048,128]{2,1,0:T(8,128)}) custom-call(s32[7,10]{1,0:T(8,128)} %broadcast_select_fusion.2.tab_ref, bf16[2,2,2048,128]{3,2,1,0:T(8,128)(2,1)} %copy-done.1, bf16[2,2,2048,128]{3,2,1,0:T(8,128)(2,1)} %get-tuple-element.36.h_ref, ...), custom_call_target="tpu_custom_call", output_to_operand_aliasing={{0}: (7, {})} | custom-call | flops 13421772800 | bytes 26214400 | tf_op jit(solution)/shard_map/attn_bwd/pallas_call | solution.py:207
  545.9 9.7 %collective-permute-done.18 = bf16[2,2,2048,128]{3,2,1,0:T(8,128)(2,1)S(1)} collective-permute-done((bf16[2,2,2048,128]{3,2,1,0:T(8,128)(2,1)S(1)}, bf16[2,2,2048,128]{3,2,1,0:T(8,128)(2,1)S(1)}, u32[]{:S(2)}, u32[]{:S(2)}) %collective-permute-start.18) | collective-permute-done | bytes 2097184 | tf_op jit(solution)/shard_map/ppermute | solution.py:236
  570.9 5.5 fusion.77
  618.7 6.8 reshape.279
  690.4 6.9 collective-permute-done.25
  707.3 5.4 fusion.14
  (450 shorter events, 318.8 us)
Async XLA Ops:
  7.2 58.8 %all-gather.3.cloned.1.call-start = ((), (), s32[]{:S(2)}) async-start(), calls=%async_computation.1 | async-start | bytes 2359296 | tf_op jit(solution)/shard_map/all_gather | solution.py:409
  10.9 185.6 %all-gather.5.cloned.1.call-start = ((), (), s32[]{:S(2)}) async-start(), calls=%async_computation.2 | async-start | bytes 6488064 | tf_op jit(solution)/shard_map/all_gather | solution.py:461
  22.1 4.7 collective-permute-start.2
  30.0 21.7 %collective-permute-start.3 = (bf16[512,1024]{0,1:T(8,128)(2,1)S(1)}, bf16[512,1024]{0,1:T(8,128)(2,1)S(1)}, u32[]{:S(2)}, u32[]{:S(2)}) collective-permute-start(bf16[512,1024]{0,1:T(8,128)(2,1)S(1)} %get-tuple-element.133), channel_id=1, source_target_pairs={{0,2},{1,3},{2,0},{3,1},{4,6},{5,7},{6,4},{7,5},{8,10},{9,11},{10,... | collective-permute-start | bytes 3145736 | tf_op jit(solution)/shard_map/ppermute | solution.py:337
  53.2 8.2 %collective-permute-start.4 = (bf16[2,512,1024]{1,2,0:T(8,128)(2,1)}, bf16[2,512,1024]{1,2,0:T(8,128)(2,1)}, u32[]{:S(2)}, u32[]{:S(2)}) collective-permute-start(bf16[2,512,1024]{1,2,0:T(8,128)(2,1)} %pad_maximum_fusion.2), channel_id=1, source_target_pairs={{0,1},{1,0},{2,3},{3,2},{4,5},{5,4},{6,7},{7,6},{8,9},{9,8},{10,11... | collective-permute-start | bytes 6291464 | tf_op jit(solution)/shard_map/ppermute | solution.py:337
  54.2 522.2 %reduce-scatter.4.cloned.1.call-start = ((), (), s32[]{:S(2)}) async-start(), calls=%async_computation.3 | async-start | bytes 6488064
  86.6 77.4 %collective-permute-start.5 = (bf16[2,2,2048,128]{3,2,1,0:T(8,128)(2,1)}, bf16[2,2,2048,128]{3,2,1,0:T(8,128)(2,1)}, u32[]{:S(2)}, u32[]{:S(2)}) collective-permute-start(bf16[2,2,2048,128]{3,2,1,0:T(8,128)(2,1)} %pad_maximum_fusion.3), channel_id=1, source_target_pairs={{0,4},{4,0},{8,12},{12,8},{16,20},{20,16},{24,28},{28,24},{1,5},{5... | collective-permute-start | bytes 6291464 | tf_op jit(solution)/shard_map/ppermute | solution.py:236
  208.6 26.2 %collective-permute-start.7 = (bf16[512,1024]{0,1:T(8,128)(2,1)}, bf16[512,1024]{0,1:T(8,128)(2,1)S(1)}, u32[]{:S(2)}, u32[]{:S(2)}) collective-permute-start(bf16[512,1024]{0,1:T(8,128)(2,1)} %fusion.32), channel_id=1, source_target_pairs={{0,2},{1,3},{2,0},{3,1},{4,6},{5,7},{6,4},{7,5},{8,10},{9,11},{10,... | collective-permute-start | bytes 3145736 | tf_op jit(solution)/shard_map/ppermute | solution.py:337
  212.6 44.6 %collective-permute-start.12 = (bf16[512,1024]{0,1:T(8,128)(2,1)S(1)}, bf16[512,1024]{0,1:T(8,128)(2,1)S(1)}, u32[]{:S(2)}, u32[]{:S(2)}) collective-permute-start(bf16[512,1024]{0,1:T(8,128)(2,1)S(1)} %get-tuple-element.127), channel_id=1, source_target_pairs={{0,2},{1,3},{2,0},{3,1},{4,6},{5,7},{6,4},{7,5},{8,10},{9,11},{10,... | collective-permute-start | bytes 3145736 | tf_op jit(solution)/shard_map/ppermute | solution.py:337
  237.9 41.0 %collective-permute-start.8 = (bf16[512,1024]{0,1:T(8,128)(2,1)S(1)}, bf16[512,1024]{0,1:T(8,128)(2,1)S(1)}, u32[]{:S(2)}, u32[]{:S(2)}) collective-permute-start(bf16[512,1024]{0,1:T(8,128)(2,1)S(1)} %get-tuple-element.129), channel_id=1, source_target_pairs={{0,2},{1,3},{2,0},{3,1},{4,6},{5,7},{6,4},{7,5},{8,10},{9,11},{10,... | collective-permute-start | bytes 3145736 | tf_op jit(solution)/shard_map/ppermute | solution.py:337
  257.5 21.9 %collective-permute-start.13 = (bf16[2,512,1024]{1,2,0:T(8,128)(2,1)S(1)}, bf16[2,512,1024]{1,2,0:T(8,128)(2,1)S(1)}, u32[]{:S(2)}, u32[]{:S(2)}) collective-permute-start(bf16[2,512,1024]{1,2,0:T(8,128)(2,1)S(1)} %pad_maximum_fusion.7), channel_id=1, source_target_pairs={{0,1},{1,0},{2,3},{3,2},{4,5},{5,4},{6,7},{7,6},{8,9},{9,8},{10,11... | collective-permute-start | bytes 6291464 | tf_op jit(solution)/shard_map/ppermute | solution.py:337
  328.0 25.3 %collective-permute-start.15 = (bf16[512,1024]{0,1:T(8,128)(2,1)S(1)}, bf16[512,1024]{0,1:T(8,128)(2,1)S(1)}, u32[]{:S(2)}, u32[]{:S(2)}) collective-permute-start(bf16[512,1024]{0,1:T(8,128)(2,1)S(1)} %fusion.22), channel_id=1, source_target_pairs={{0,2},{1,3},{2,0},{3,1},{4,6},{5,7},{6,4},{7,5},{8,10},{9,11},{10,... | collective-permute-start | bytes 3145736 | tf_op jit(solution)/shard_map/ppermute | solution.py:337
  356.7 24.4 %collective-permute-start.16 = (bf16[512,1024]{0,1:T(8,128)(2,1)S(1)}, bf16[512,1024]{0,1:T(8,128)(2,1)S(1)}, u32[]{:S(2)}, u32[]{:S(2)}) collective-permute-start(bf16[512,1024]{0,1:T(8,128)(2,1)S(1)} %get-tuple-element.124), channel_id=1, source_target_pairs={{0,2},{1,3},{2,0},{3,1},{4,6},{5,7},{6,4},{7,5},{8,10},{9,11},{10,... | collective-permute-start | bytes 3145736 | tf_op jit(solution)/shard_map/ppermute | solution.py:337
  381.3 16.0 %collective-permute-start.17 = (bf16[2,512,1024]{1,2,0:T(8,128)(2,1)S(1)}, bf16[2,512,1024]{1,2,0:T(8,128)(2,1)S(1)}, u32[]{:S(2)}, u32[]{:S(2)}) collective-permute-start(bf16[2,512,1024]{1,2,0:T(8,128)(2,1)S(1)} %pad_maximum_fusion.9), channel_id=1, source_target_pairs={{0,1},{1,0},{2,3},{3,2},{4,5},{5,4},{6,7},{7,6},{8,9},{9,8},{10,11... | collective-permute-start | bytes 6291464 | tf_op jit(solution)/shard_map/ppermute | solution.py:337
  486.5 69.0 %collective-permute-start.18 = (bf16[2,2,2048,128]{3,2,1,0:T(8,128)(2,1)S(1)}, bf16[2,2,2048,128]{3,2,1,0:T(8,128)(2,1)S(1)}, u32[]{:S(2)}, u32[]{:S(2)}) collective-permute-start(bf16[2,2,2048,128]{3,2,1,0:T(8,128)(2,1)S(1)} %fusion.5), channel_id=1, source_target_pairs={{0,4},{4,0},{8,12},{12,8},{16,20},{20,16},{24,28},{28,24},{1,5},{5... | collective-permute-start | bytes 6291464 | tf_op jit(solution)/shard_map/ppermute | solution.py:236
  500.2 160.6 %collective-permute-start.10 = (bf16[2,512,1024]{1,2,0:T(8,128)(2,1)}, bf16[2,512,1024]{1,2,0:T(8,128)(2,1)}, u32[]{:S(2)}, u32[]{:S(2)}) collective-permute-start(bf16[2,512,1024]{1,2,0:T(8,128)(2,1)} %pad_maximum_fusion.6), channel_id=1, source_target_pairs={{0,1},{1,0},{2,3},{3,2},{4,5},{5,4},{6,7},{7,6},{8,9},{9,8},{10,11... | collective-permute-start | bytes 6291464 | tf_op jit(solution)/shard_map/ppermute | solution.py:337
  608.9 37.2 %collective-permute-start.19 = (bf16[2,512,1024]{1,2,0:T(8,128)(2,1)}, bf16[2,512,1024]{1,2,0:T(8,128)(2,1)}, u32[]{:S(2)}, u32[]{:S(2)}) collective-permute-start(bf16[2,512,1024]{1,2,0:T(8,128)(2,1)} %pad_maximum_fusion.10), channel_id=1, source_target_pairs={{0,1},{1,0},{2,3},{3,2},{4,5},{5,4},{6,7},{7,6},{8,9},{9,8},{10,11... | collective-permute-start | bytes 6291464 | tf_op jit(solution)/shard_map/ppermute | solution.py:337
  633.8 22.9 %collective-permute-start.21 = (bf16[2,2,128,1024]{3,2,0,1:T(8,128)(2,1)}, bf16[2,2,128,1024]{3,2,0,1:T(8,128)(2,1)}, u32[]{:S(2)}, u32[]{:S(2)}) collective-permute-start(bf16[2,2,128,1024]{3,2,0,1:T(8,128)(2,1)} %bitcast.206), channel_id=1, source_target_pairs={{0,4},{4,0},{8,12},{12,8},{16,20},{20,16},{24,28},{28,24},{1,5},{5... | collective-permute-start | bytes 3145736 | tf_op jit(solution)/shard_map/ppermute | solution.py:303
  652.8 26.2 %collective-permute-start.20 = (bf16[512,1024]{0,1:T(8,128)(2,1)}, bf16[512,1024]{0,1:T(8,128)(2,1)S(1)}, u32[]{:S(2)}, u32[]{:S(2)}) collective-permute-start(bf16[512,1024]{0,1:T(8,128)(2,1)} %fusion.18), channel_id=1, source_target_pairs={{0,2},{1,3},{2,0},{3,1},{4,6},{5,7},{6,4},{7,5},{8,10},{9,11},{10,... | collective-permute-start | bytes 3145736 | tf_op jit(solution)/shard_map/ppermute | solution.py:337
  659.6 10.1 %collective-permute-start.22 = (bf16[2,128,1024]{2,1,0:T(8,128)(2,1)S(1)}, bf16[2,128,1024]{2,1,0:T(8,128)(2,1)S(1)}, u32[]{:S(2)}, u32[]{:S(2)}) collective-permute-start(bf16[2,128,1024]{2,1,0:T(8,128)(2,1)S(1)} %fusion.74), channel_id=1, source_target_pairs={{0,8},{4,12},{8,0},{12,4},{16,24},{20,28},{24,16},{28,20},{1,9},{5... | collective-permute-start | bytes 1572872 | tf_op jit(solution)/shard_map/ppermute | solution.py:303
  667.7 39.6 %collective-permute-start.11 = (bf16[512,1024]{0,1:T(8,128)(2,1)}, bf16[512,1024]{0,1:T(8,128)(2,1)}, u32[]{:S(2)}, u32[]{:S(2)}) collective-permute-start(bf16[512,1024]{0,1:T(8,128)(2,1)} %fusion.26), channel_id=1, source_target_pairs={{0,2},{1,3},{2,0},{3,1},{4,6},{5,7},{6,4},{7,5},{8,10},{9,11},{10,... | collective-permute-start | bytes 3145736 | tf_op jit(solution)/shard_map/ppermute | solution.py:337
  671.6 17.6 %collective-permute-start.23 = (bf16[128,1024]{1,0:T(8,128)(2,1)}, bf16[128,1024]{1,0:T(8,128)(2,1)}, u32[]{:S(2)}, u32[]{:S(2)}) collective-permute-start(bf16[128,1024]{1,0:T(8,128)(2,1)} %fusion.81), channel_id=1, source_target_pairs={{0,16},{4,20},{8,24},{12,28},{16,0},{20,4},{24,8},{28,12},{1,17},{... | collective-permute-start | bytes 786440 | tf_op jit(solution)/shard_map/ppermute | solution.py:303
  688.2 9.1 %collective-permute-start.25 = (f32[2304]{0:T(1024)S(1)}, f32[2304]{0:T(1024)S(1)}, u32[]{:S(2)}, u32[]{:S(2)}) collective-permute-start(f32[2304]{0:T(1024)S(1)} %fusion.105), channel_id=1, source_target_pairs={{0,2},{1,3},{2,0},{3,1},{4,6},{5,7},{6,4},{7,5},{8,10},{9,11},{10,... | collective-permute-start | bytes 27656 | tf_op jit(solution)/shard_map/ppermute | solution.py:328
  704.7 11.7 %collective-permute-start.28 = (f32[2304]{0:T(1024)S(1)}, f32[2304]{0:T(1024)S(1)}, u32[]{:S(2)}, u32[]{:S(2)}) collective-permute-start(f32[2304]{0:T(1024)S(1)} %add.319), channel_id=1, source_target_pairs={{0,16},{4,20},{8,24},{12,28},{16,0},{20,4},{24,8},{28,12},{1,17},{... | collective-permute-start | bytes 27656 | tf_op jit(solution)/shard_map/ppermute | solution.py:328
  (113 other events, 1666.3 us)
Sparse Core Ops, SparseCore 0:
  11.0 51.7 all-gather.2
  64.9 120.8 all-gather.4
  442.0 130.3 reduce-scatter.3

commit v5 on v4

--- a/solution.py
+++ b/solution.py
@@ -245,13 +245,11 @@
     half = values.shape[-1] // 2
     frequency = THETA ** (-(jnp.arange(half, dtype=jnp.float32) * 2.0 / values.shape[-1]))
     angle = start_offset.astype(jnp.float32)[:, None] * frequency[None, :]
-    cosine = jnp.cos(angle)[:, None, :]
-    sine = jnp.sin(angle)[:, None, :]
-    first = values[..., :half]
-    second = values[..., half:]
-    return jnp.concatenate(
-        [first * cosine - second * sine, second * cosine + first * sine], axis=-1
-    )
+    cosine = jnp.cos(angle)
+    sine = jnp.sin(angle)
+    cos_full = jnp.concatenate([cosine, cosine], axis=-1)[:, None, :]
+    sin_signed = jnp.concatenate([-sine, sine], axis=-1)[:, None, :]
+    return values * cos_full + jnp.roll(values, half, axis=-1) * sin_signed
 
 
 def prepare_inputs(projected, gain, start_offset, head_groups):
@@ -289,21 +287,20 @@
 
 def halving_scatter(grads):
     widths = [g.shape[1] for g in grads]
-    packed = jnp.concatenate(grads, axis=1)
+    buf = jnp.concatenate(grads, axis=1)
     count = lax.axis_size("fsdp")
     me = lax.axis_index("fsdp")
-    rows_f = packed.shape[0] // count
-    bits = count.bit_length() - 1
-    buf = packed.reshape((2,) * bits + (rows_f, packed.shape[1]))
-    for bit in range(bits):
-        axis = bits - 1 - bit
-        mine = (me >> bit) & 1
-        keep = lax.dynamic_index_in_dim(buf, mine, axis, keepdims=False)
-        send = lax.dynamic_index_in_dim(buf, 1 - mine, axis, keepdims=False)
+    bit = count // 2
+    while bit >= 1:
+        half = buf.shape[0] // 2
+        mine = (me & bit) // bit
+        keep = lax.dynamic_slice_in_dim(buf, mine * half, half, 0)
+        send = lax.dynamic_slice_in_dim(buf, (1 - mine) * half, half, 0)
         got = lax.ppermute(
-            send.astype(jnp.bfloat16), "fsdp", [(i, i ^ (1 << bit)) for i in range(count)]
+            send.astype(jnp.bfloat16), "fsdp", [(i, i ^ bit) for i in range(count)]
         )
         buf = keep + got.astype(jnp.float32)
+        bit //= 2
     return split_columns(buf, widths)
 
 
@@ -424,6 +421,9 @@
     x_float = hidden.astype(jnp.float32)
     gain_first = gain_in.astype(jnp.float32)
     first_all = token_gather(rms_scale(x_float, gain_first).astype(jnp.bfloat16))
+    cotangent = out_grad.astype(jnp.float32) * local_valid[:, None].astype(jnp.float32)
+    mlp_grad_all = token_gather(cotangent.astype(jnp.bfloat16))
+    first_all, mlp_grad_all = lax.optimization_barrier((first_all, mlp_grad_all))
     query_projected = jnp.dot(first_all, w_query, preferred_element_type=jnp.float32)
     key_projected = jnp.dot(first_all, w_key, preferred_element_type=jnp.float32)
     value_rows = (
@@ -490,8 +490,6 @@
         return contract_last(activated, w_down_t)
 
     output = (after_attn + token_sum(down_term, rows)).astype(jnp.bfloat16)
-    cotangent = out_grad.astype(jnp.float32) * local_valid[:, None].astype(jnp.float32)
-    mlp_grad_all = token_gather(cotangent.astype(jnp.bfloat16))
     grad_act = jnp.dot(mlp_grad_all, w_down_t, preferred_element_type=jnp.float32)
     unused, pull_gate = jax.vjp(
         lambda gate_in, up_in: jax.nn.silu(gate_in) * up_in, gate_out, up_out

time: 731 us -> 748 us (1.023)
  other arithmetic: 114 us -> 122 us
  matrix products: 99.3 us -> 107 us
    ppermute x3, waiting for transfers between devices: 3.3 us -> 41.9 us  [halving_scatter(): lax.ppermute(send.astype(jnp.bfloat16), 'fsdp', [(i, i ^ bit) for i in ra...]
    ppermute x2, waiting for transfers between devices: 36.2 us -> 18.8 us  [swapped(): lax.ppermute(shard, axis, [(i, i ^ 1 << distance) for i in range(lax.axis...]
    dynamic_slice x3 -> x0, local copies, waits for them, and re-layouts: 13.9 us -> none  [the longest x2 9.86 us: halving_scatter(): keep = lax.dynamic_index_in_dim(buf, mine, axis, keepdims=False)]
    slice x0 -> x4, local copies, waits for them, and re-layouts: none -> 13.2 us  [rotary(): return values * cos_full + jnp.roll(values, half, axis=-1) * sin_signed]
    ppermute x16, waiting for transfers between devices: 140 us -> 129 us  [exchange(): lax.ppermute(values, 'tensor', [(i, i ^ distance) for i in range(count)])]
    unnamed x224 -> x218, local copies, waits for them, and re-layouts: 52.9 us -> 46.7 us
  transfers between devices with their start and end apart: 32 -> 32, of which waited for: 20 -> 18; matrix products, arithmetic and copies ran while one was open for 30% -> 32% of each run, Pallas kernels for 19% -> 18%
where the time goes in v5:
time: 748 us; the launch traced here: 738 us
  waiting for transfers between devices  200 us (27%)
  Pallas kernels  136 us (18%)
  local copies, waits for them, and re-layouts  126 us (17%)
  other arithmetic  122 us (16%)
  matrix products  107 us (14%)
  starting transfers between devices  32.5 us (4%)
  between operations  15.8 us (2%)
    ppermute x16, waiting for transfers between devices, exchange(): lax.ppermute(values, 'tensor', [(i, i ^ distance) for i in range(count)])  129 us
    pallas_call x2, Pallas kernels, attention_backward(): pl.pallas_call(functools.partial(_bwd_kernel, scale=scale, block=block),...  83.4 us
    pallas_call x2, Pallas kernels, attention_forward(): pl.pallas_call(functools.partial(_fwd_kernel, scale=scale, block=block),...  52.1 us
    unnamed x218, local copies, waits for them, and re-layouts  46.7 us
    ppermute x3, waiting for transfers between devices, halving_scatter(): lax.ppermute(send.astype(jnp.bfloat16), 'fsdp', [(i, i ^ bit) for i in ra...  41.9 us
    dot_general x7, matrix products, contract_last(): lax.dot_general(left, right, (((1,), (1,)), ((), ())), preferred_element_...  34.2 us
    dot_general x7, matrix products, contract_rows(): lax.dot_general(left, right, (((0,), (0,)), ((), ())), preferred_element_...  31.1 us
    ppermute x2, waiting for transfers between devices, swapped(): lax.ppermute(shard, axis, [(i, i ^ 1 << distance) for i in range(lax.axis...  18.8 us
  transfers between devices with their start and end apart: 32, of which 18 were waited for; matrix products, arithmetic and copies ran while one was open for 32% of the time, Pallas kernels for 18%

profile of v5, /device:TPU:0, one launch (start us, length us, event | category | flops | bytes accessed | tf_op | source)
XLA Modules:
  0.0 738.3 jit_solution(15209623413660580596)
XLA Ops:
  45.2 20.1 %collective-permute-done.3 = bf16[512,1024]{0,1:T(8,128)(2,1)} collective-permute-done((bf16[512,1024]{0,1:T(8,128)(2,1)}, bf16[512,1024]{0,1:T(8,128)(2,1)}, u32[]{:S(2)}, u32[]{:S(2)}) %collective-permute-start.3) | collective-permute-done | bytes 1048608 | tf_op jit(solution)/shard_map/ppermute | solution.py:334
  136.2 6.0 fusion.19.q_ref
  147.5 28.8 %attn_fwd.2 = (f32[2,2,2048,128]{3,2,1,0:T(8,128)}, f32[2,2,2048,128]{3,2,1,0:T(8,128)}) custom-call(s32[7,10]{1,0:T(8,128)S(1)} %broadcast_select_fusion.3.tab_ref, bf16[2,2,2048,128]{3,2,1,0:T(8,128)(2,1)S(1)} %fusion.19.q_ref, s32[2048,128]{1,0:T(8,128)S(1)} %broadcast_in_dim.45.qs_ref, ...), custom_call_target="tpu_custom_call", output_to_operand_aliasing={{0}: (5, {}), {1}: (6, {})} | custom-call | flops 5368709120 | bytes 20971520 | tf_op jit(solution)/shard_map/attn_fwd/pallas_call | solution.py:124
  176.3 6.3 collective-permute-done.7
  184.4 23.3 %attn_fwd.3 = (f32[2,2,2048,128]{3,2,1,0:T(8,128)}, f32[2,2,2048,128]{3,2,1,0:T(8,128)}) custom-call(s32[7,8]{1,0:T(8,128)S(1)} %broadcast_select_fusion.7.tab_ref, bf16[2,2,2048,128]{3,2,1,0:T(8,128)(2,1)S(1)} %fusion.19.q_ref, s32[2048,128]{1,0:T(8,128)S(1)} %broadcast_in_dim.45.qs_ref, ...), custom_call_target="tpu_custom_call", output_to_operand_aliasing={{0}: (5, {}), {1}: (6, {})} | custom-call | flops 4294967296 | bytes 16777216 | tf_op jit(solution)/shard_map/attn_fwd/pallas_call | solution.py:124
  226.8 23.7 %collective-permute-done.9 = bf16[512,1024]{0,1:T(8,128)(2,1)S(1)} collective-permute-done((bf16[512,1024]{0,1:T(8,128)(2,1)S(1)}, bf16[512,1024]{0,1:T(8,128)(2,1)S(1)}, u32[]{:S(2)}, u32[]{:S(2)}) %collective-permute-start.9) | collective-permute-done | bytes 1048608 | tf_op jit(solution)/shard_map/ppermute | solution.py:334
  253.6 22.9 %collective-permute-done.10 = bf16[512,1024]{0,1:T(8,128)(2,1)S(1)} collective-permute-done((bf16[512,1024]{0,1:T(8,128)(2,1)S(1)}, bf16[512,1024]{0,1:T(8,128)(2,1)S(1)}, u32[]{:S(2)}, u32[]{:S(2)}) %collective-permute-start.10) | collective-permute-done | bytes 1048608 | tf_op jit(solution)/shard_map/ppermute | solution.py:334
  281.3 5.4 fusion.48
  286.7 5.5 fusion.52
  292.3 12.1 %multiply_convert_fusion = (bf16[2048,768]{1,0:T(8,128)(2,1)S(1)}, bf16[2048,768]{1,0:T(8,128)(2,1)}, bf16[2048,768]{1,0:T(8,128)(2,1)}) fusion(f32[2048,768]{1,0:T(8,128)} %fusion.52, f32[2048,768]{1,0:T(8,128)} %fusion.48, bf16[2048,1024]{0,1:T(8,128)(2,1)S(1)} %copy-done.38, bf16[1024,2816]{0,1:T(8,128)(2,1)S(1)} %bitcast.269), kind=kOutput, calls=%fused_computation.6 | convolution fusion | flops 3246391296 | bytes 27787264 | tf_op jit(solution)/shard_map/dot_general | solution.py:493
  304.3 7.6 %fusion.50 = f32[2048,1024]{0,1:T(8,128)} fusion(bf16[2048,768]{1,0:T(8,128)(2,1)} %get-tuple-element.128, bf16[1024,2816]{0,1:T(8,128)(2,1)S(1)} %bitcast.269), kind=kOutput, calls=%fused_computation.130 | convolution fusion | flops 3221225472 | bytes 13107200 | tf_op jit(solution)/shard_map/dot_general | solution.py:274
  311.9 6.9 convolution_add_fusion
  326.1 23.7 %collective-permute-done.15 = bf16[512,1024]{0,1:T(8,128)(2,1)S(1)} collective-permute-done((bf16[512,1024]{0,1:T(8,128)(2,1)S(1)}, bf16[512,1024]{0,1:T(8,128)(2,1)S(1)}, u32[]{:S(2)}, u32[]{:S(2)}) %collective-permute-start.15) | collective-permute-done | bytes 1048608 | tf_op jit(solution)/shard_map/ppermute | solution.py:334
  355.4 22.9 %collective-permute-done.16 = bf16[512,1024]{0,1:T(8,128)(2,1)S(1)} collective-permute-done((bf16[512,1024]{0,1:T(8,128)(2,1)S(1)}, bf16[512,1024]{0,1:T(8,128)(2,1)S(1)}, u32[]{:S(2)}, u32[]{:S(2)}) %collective-permute-start.16) | collective-permute-done | bytes 1048608 | tf_op jit(solution)/shard_map/ppermute | solution.py:334
  405.3 7.2 fusion.8
  412.5 15.8 %pad_maximum_fusion = bf16[1024,2816]{0,1:T(8,128)(2,1)} fusion(bf16[1024,512]{0,1:T(8,128)(2,1)S(1)} %convolution_convert_fusion.5, bf16[1024,768]{0,1:T(8,128)(2,1)S(1)} %copy-done.45, bf16[1024,768]{0,1:T(8,128)(2,1)S(1)} %copy-done.44, bf16[1024,768]{0,1:T(8,128)(2,1)S(1)} %copy-done.43), kind=kLoop, calls=%fused_computation.10 | loop fusion | flops 23068672 | bytes 11534336 | tf_op jit(solution)/shard_map/concatenate | solution.py:513
  430.9 8.5 %copy.178 = bf16[1024,2816]{1,0:T(8,128)(2,1)} copy(bf16[1024,2816]{0,1:T(8,128)(2,1)} %pad_maximum_fusion) | data formatting | bytes 11534336
  445.8 37.9 %attn_bwd.2 = (f32[2,2,2048,128]{3,2,1,0:T(8,128)}, f32[2,2048,128]{2,1,0:T(8,128)}, f32[2,2048,128]{2,1,0:T(8,128)}) custom-call(s32[7,8]{1,0:T(8,128)} %broadcast_select_fusion.6.tab_ref, bf16[2,2,2048,128]{3,2,1,0:T(8,128)(2,1)} %copy-done.2, bf16[2,2,2048,128]{3,2,1,0:T(8,128)(2,1)} %get-tuple-element.40.h_ref, ...), custom_call_target="tpu_custom_call", output_to_operand_aliasing={{0}: (7, {})} | custom-call | flops 10737418240 | bytes 20971520 | tf_op jit(solution)/shard_map/attn_bwd/pallas_call | solution.py:207
  498.6 45.6 %attn_bwd.3 = (f32[2,2,2048,128]{3,2,1,0:T(8,128)}, f32[2,2048,128]{2,1,0:T(8,128)}, f32[2,2048,128]{2,1,0:T(8,128)}) custom-call(s32[7,10]{1,0:T(8,128)} %broadcast_select_fusion.2.tab_ref, bf16[2,2,2048,128]{3,2,1,0:T(8,128)(2,1)} %copy-done.2, bf16[2,2,2048,128]{3,2,1,0:T(8,128)(2,1)} %get-tuple-element.40.h_ref, ...), custom_call_target="tpu_custom_call", output_to_operand_aliasing={{0}: (7, {})} | custom-call | flops 13421772800 | bytes 26214400 | tf_op jit(solution)/shard_map/attn_bwd/pallas_call | solution.py:207
  544.2 12.5 %collective-permute-done.18 = bf16[2,2,2048,128]{3,2,1,0:T(8,128)(2,1)S(1)} collective-permute-done((bf16[2,2,2048,128]{3,2,1,0:T(8,128)(2,1)}, bf16[2,2,2048,128]{3,2,1,0:T(8,128)(2,1)S(1)}, u32[]{:S(2)}, u32[]{:S(2)}) %collective-permute-start.18) | collective-permute-done | bytes 2097184 | tf_op jit(solution)/shard_map/ppermute | solution.py:236
  573.5 5.6 fusion.80
  587.7 5.5 copy.155
  634.7 37.2 %collective-permute-done.21 = bf16[512,1024]{0,1:T(8,128)(2,1)} collective-permute-done((bf16[512,1024]{0,1:T(8,128)(2,1)S(1)}, bf16[512,1024]{0,1:T(8,128)(2,1)}, u32[]{:S(2)}, u32[]{:S(2)}) %collective-permute-start.21) | collective-permute-done | bytes 1048608 | tf_op jit(solution)/shard_map/ppermute | solution.py:299
  720.7 5.7 fusion.16
  (445 shorter events, 325.8 us)
Async XLA Ops:
  7.2 80.0 %all-gather.3.cloned.1.call-start = ((), (), s32[]{:S(2)}) async-start(), calls=%async_computation.1 | async-start | bytes 2359296 | tf_op jit(solution)/shard_map/all_gather | solution.py:406
  10.9 204.4 %all-gather.5.cloned.1.call-start = ((), (), s32[]{:S(2)}) async-start(), calls=%async_computation.2 | async-start | bytes 6488064 | tf_op jit(solution)/shard_map/all_gather | solution.py:461
  16.6 27.0 %collective-permute-start.5 = (bf16[512,1024]{0,1:T(8,128)(2,1)S(1)}, bf16[512,1024]{0,1:T(8,128)(2,1)S(1)}, u32[]{:S(2)}, u32[]{:S(2)}) collective-permute-start(bf16[512,1024]{0,1:T(8,128)(2,1)S(1)} %get-tuple-element.124), channel_id=1, source_target_pairs={{0,2},{1,3},{2,0},{3,1},{4,6},{5,7},{6,4},{7,5},{8,10},{9,11},{10,... | collective-permute-start | bytes 3145736 | tf_op jit(solution)/shard_map/ppermute | solution.py:334
  36.4 29.0 %collective-permute-start.3 = (bf16[512,1024]{0,1:T(8,128)(2,1)}, bf16[512,1024]{0,1:T(8,128)(2,1)}, u32[]{:S(2)}, u32[]{:S(2)}) collective-permute-start(bf16[512,1024]{0,1:T(8,128)(2,1)} %get-tuple-element.126), channel_id=1, source_target_pairs={{0,2},{1,3},{2,0},{3,1},{4,6},{5,7},{6,4},{7,5},{8,10},{9,11},{10,... | collective-permute-start | bytes 3145736 | tf_op jit(solution)/shard_map/ppermute | solution.py:334
  39.9 539.2 %reduce-scatter.4.cloned.1.call-start = ((), (), s32[]{:S(2)}) async-start(), calls=%async_computation.3 | async-start | bytes 6488064
  45.2 32.7 %collective-permute-start.6 = (bf16[2,512,1024]{1,2,0:T(8,128)(2,1)}, bf16[2,512,1024]{1,2,0:T(8,128)(2,1)}, u32[]{:S(2)}, u32[]{:S(2)}) collective-permute-start(bf16[2,512,1024]{1,2,0:T(8,128)(2,1)} %pad_maximum_fusion.3), channel_id=1, source_target_pairs={{0,1},{1,0},{2,3},{3,2},{4,5},{5,4},{6,7},{7,6},{8,9},{9,8},{10,11... | collective-permute-start | bytes 6291464 | tf_op jit(solution)/shard_map/ppermute | solution.py:334
  68.4 14.1 %collective-permute-start.4 = (bf16[2,512,1024]{1,2,0:T(8,128)(2,1)}, bf16[2,512,1024]{1,2,0:T(8,128)(2,1)}, u32[]{:S(2)}, u32[]{:S(2)}) collective-permute-start(bf16[2,512,1024]{1,2,0:T(8,128)(2,1)} %pad_maximum_fusion.2), channel_id=1, source_target_pairs={{0,1},{1,0},{2,3},{3,2},{4,5},{5,4},{6,7},{7,6},{8,9},{9,8},{10,11... | collective-permute-start | bytes 6291464 | tf_op jit(solution)/shard_map/ppermute | solution.py:334
  107.0 75.7 %collective-permute-start.7 = (bf16[2,2,2048,128]{3,2,1,0:T(8,128)(2,1)}, bf16[2,2,2048,128]{3,2,1,0:T(8,128)(2,1)}, u32[]{:S(2)}, u32[]{:S(2)}) collective-permute-start(bf16[2,2,2048,128]{3,2,1,0:T(8,128)(2,1)} %pad_maximum_fusion.4), channel_id=1, source_target_pairs={{0,4},{4,0},{8,12},{12,8},{16,20},{20,16},{24,28},{28,24},{1,5},{5... | collective-permute-start | bytes 6291464 | tf_op jit(solution)/shard_map/ppermute | solution.py:236
  225.3 25.3 %collective-permute-start.9 = (bf16[512,1024]{0,1:T(8,128)(2,1)S(1)}, bf16[512,1024]{0,1:T(8,128)(2,1)S(1)}, u32[]{:S(2)}, u32[]{:S(2)}) collective-permute-start(bf16[512,1024]{0,1:T(8,128)(2,1)S(1)} %fusion.35), channel_id=1, source_target_pairs={{0,2},{1,3},{2,0},{3,1},{4,6},{5,7},{6,4},{7,5},{8,10},{9,11},{10,... | collective-permute-start | bytes 3145736 | tf_op jit(solution)/shard_map/ppermute | solution.py:334
  252.1 24.4 %collective-permute-start.10 = (bf16[512,1024]{0,1:T(8,128)(2,1)S(1)}, bf16[512,1024]{0,1:T(8,128)(2,1)S(1)}, u32[]{:S(2)}, u32[]{:S(2)}) collective-permute-start(bf16[512,1024]{0,1:T(8,128)(2,1)S(1)} %get-tuple-element.120), channel_id=1, source_target_pairs={{0,2},{1,3},{2,0},{3,1},{4,6},{5,7},{6,4},{7,5},{8,10},{9,11},{10,... | collective-permute-start | bytes 3145736 | tf_op jit(solution)/shard_map/ppermute | solution.py:334
  324.5 25.3 %collective-permute-start.15 = (bf16[512,1024]{0,1:T(8,128)(2,1)S(1)}, bf16[512,1024]{0,1:T(8,128)(2,1)S(1)}, u32[]{:S(2)}, u32[]{:S(2)}) collective-permute-start(bf16[512,1024]{0,1:T(8,128)(2,1)S(1)} %fusion.25), channel_id=1, source_target_pairs={{0,2},{1,3},{2,0},{3,1},{4,6},{5,7},{6,4},{7,5},{8,10},{9,11},{10,... | collective-permute-start | bytes 3145736 | tf_op jit(solution)/shard_map/ppermute | solution.py:334
  353.9 24.4 %collective-permute-start.16 = (bf16[512,1024]{0,1:T(8,128)(2,1)S(1)}, bf16[512,1024]{0,1:T(8,128)(2,1)S(1)}, u32[]{:S(2)}, u32[]{:S(2)}) collective-permute-start(bf16[512,1024]{0,1:T(8,128)(2,1)S(1)} %get-tuple-element.117), channel_id=1, source_target_pairs={{0,2},{1,3},{2,0},{3,1},{4,6},{5,7},{6,4},{7,5},{8,10},{9,11},{10,... | collective-permute-start | bytes 3145736 | tf_op jit(solution)/shard_map/ppermute | solution.py:334
  378.5 16.2 %collective-permute-start.17 = (bf16[2,512,1024]{1,2,0:T(8,128)(2,1)S(1)}, bf16[2,512,1024]{1,2,0:T(8,128)(2,1)S(1)}, u32[]{:S(2)}, u32[]{:S(2)}) collective-permute-start(bf16[2,512,1024]{1,2,0:T(8,128)(2,1)S(1)} %pad_maximum_fusion.9), channel_id=1, source_target_pairs={{0,1},{1,0},{2,3},{3,2},{4,5},{5,4},{6,7},{7,6},{8,9},{9,8},{10,11... | collective-permute-start | bytes 6291464 | tf_op jit(solution)/shard_map/ppermute | solution.py:334
  487.4 69.3 %collective-permute-start.18 = (bf16[2,2,2048,128]{3,2,1,0:T(8,128)(2,1)}, bf16[2,2,2048,128]{3,2,1,0:T(8,128)(2,1)S(1)}, u32[]{:S(2)}, u32[]{:S(2)}) collective-permute-start(bf16[2,2,2048,128]{3,2,1,0:T(8,128)(2,1)} %fusion.7), channel_id=1, source_target_pairs={{0,4},{4,0},{8,12},{12,8},{16,20},{20,16},{24,28},{28,24},{1,5},{5... | collective-permute-start | bytes 6291464 | tf_op jit(solution)/shard_map/ppermute | solution.py:236
  498.6 176.1 %collective-permute-start.12 = (bf16[2,512,1024]{1,2,0:T(8,128)(2,1)}, bf16[2,512,1024]{1,2,0:T(8,128)(2,1)}, u32[]{:S(2)}, u32[]{:S(2)}) collective-permute-start(bf16[2,512,1024]{1,2,0:T(8,128)(2,1)} %pad_maximum_fusion.7), channel_id=1, source_target_pairs={{0,1},{1,0},{2,3},{3,2},{4,5},{5,4},{6,7},{7,6},{8,9},{9,8},{10,11... | collective-permute-start | bytes 6291464 | tf_op jit(solution)/shard_map/ppermute | solution.py:334
  611.9 14.7 %collective-permute-start.19 = (bf16[2,512,1024]{1,2,0:T(8,128)(2,1)}, bf16[2,512,1024]{1,2,0:T(8,128)(2,1)}, u32[]{:S(2)}, u32[]{:S(2)}) collective-permute-start(bf16[2,512,1024]{1,2,0:T(8,128)(2,1)} %pad_maximum_fusion.10), channel_id=1, source_target_pairs={{0,1},{1,0},{2,3},{3,2},{4,5},{5,4},{6,7},{7,6},{8,9},{9,8},{10,11... | collective-permute-start | bytes 6291464 | tf_op jit(solution)/shard_map/ppermute | solution.py:334
  624.1 47.9 %collective-permute-start.21 = (bf16[512,1024]{0,1:T(8,128)(2,1)S(1)}, bf16[512,1024]{0,1:T(8,128)(2,1)}, u32[]{:S(2)}, u32[]{:S(2)}) collective-permute-start(bf16[512,1024]{0,1:T(8,128)(2,1)S(1)} %dynamic-slice_convert_fusion), channel_id=1, source_target_pairs={{0,16},{4,20},{8,24},{12,28},{16,0},{20,4},{24,8},{28,12},{1,17},{... | collective-permute-start | bytes 3145736 | tf_op jit(solution)/shard_map/ppermute | solution.py:299
  633.3 58.3 %collective-permute-start.20 = (bf16[512,1024]{0,1:T(8,128)(2,1)}, bf16[512,1024]{0,1:T(8,128)(2,1)}, u32[]{:S(2)}, u32[]{:S(2)}) collective-permute-start(bf16[512,1024]{0,1:T(8,128)(2,1)} %fusion.21), channel_id=1, source_target_pairs={{0,2},{1,3},{2,0},{3,1},{4,6},{5,7},{6,4},{7,5},{8,10},{9,11},{10,... | collective-permute-start | bytes 3145736 | tf_op jit(solution)/shard_map/ppermute | solution.py:334
  674.4 13.2 %collective-permute-start.22 = (bf16[256,1024]{0,1:T(8,128)(2,1)}, bf16[256,1024]{0,1:T(8,128)(2,1)}, u32[]{:S(2)}, u32[]{:S(2)}) collective-permute-start(bf16[256,1024]{0,1:T(8,128)(2,1)} %dynamic-slice_convert_fusion.9), channel_id=1, source_target_pairs={{0,8},{4,12},{8,0},{12,4},{16,24},{20,28},{24,16},{28,20},{1,9},{5... | collective-permute-start | bytes 1572872 | tf_op jit(solution)/shard_map/ppermute | solution.py:299
  681.4 39.2 %collective-permute-start.13 = (bf16[512,1024]{0,1:T(8,128)(2,1)}, bf16[512,1024]{0,1:T(8,128)(2,1)}, u32[]{:S(2)}, u32[]{:S(2)}) collective-permute-start(bf16[512,1024]{0,1:T(8,128)(2,1)} %fusion.29), channel_id=1, source_target_pairs={{0,2},{1,3},{2,0},{3,1},{4,6},{5,7},{6,4},{7,5},{8,10},{9,11},{10,... | collective-permute-start | bytes 3145736 | tf_op jit(solution)/shard_map/ppermute | solution.py:334
  690.6 11.8 %collective-permute-start.23 = (bf16[128,1024]{0,1:T(8,128)(2,1)}, bf16[128,1024]{0,1:T(8,128)(2,1)}, u32[]{:S(2)}, u32[]{:S(2)}) collective-permute-start(bf16[128,1024]{0,1:T(8,128)(2,1)} %dynamic-slice_convert_fusion.10), channel_id=1, source_target_pairs={{0,4},{4,0},{8,12},{12,8},{16,20},{20,16},{24,28},{28,24},{1,5},{5... | collective-permute-start | bytes 786440 | tf_op jit(solution)/shard_map/ppermute | solution.py:299
  700.5 6.3 collective-permute-start.25
  707.4 5.4 collective-permute-start.26
  717.2 12.9 %collective-permute-start.28 = (f32[2304]{0:T(1024)S(1)}, f32[2304]{0:T(1024)S(1)}, u32[]{:S(2)}, u32[]{:S(2)}) collective-permute-start(f32[2304]{0:T(1024)S(1)} %add.319), channel_id=1, source_target_pairs={{0,16},{4,20},{8,24},{12,28},{16,0},{20,4},{24,8},{28,12},{1,17},{... | collective-permute-start | bytes 27656 | tf_op jit(solution)/shard_map/ppermute | solution.py:325
  (110 other events, 1365.1 us)
Sparse Core Ops, SparseCore 0:
  11.0 51.9 all-gather.2
  65.0 118.0 all-gather.4
  439.6 130.5 reduce-scatter.3

commit v6 on v5

--- a/solution.py
+++ b/solution.py
@@ -287,20 +287,22 @@
 
 def halving_scatter(grads):
     widths = [g.shape[1] for g in grads]
-    buf = jnp.concatenate(grads, axis=1)
+    packed = jnp.concatenate(grads, axis=1)
     count = lax.axis_size("fsdp")
     me = lax.axis_index("fsdp")
-    bit = count // 2
-    while bit >= 1:
+    bits = count.bit_length() - 1
+    rows_f = packed.shape[0] // count
+    order = [int(format(b, f"0{bits}b")[::-1], 2) for b in range(count)]
+    buf = jnp.concatenate([packed[b * rows_f : (b + 1) * rows_f] for b in order], axis=0)
+    for bit in range(bits):
         half = buf.shape[0] // 2
-        mine = (me & bit) // bit
+        mine = (me >> bit) & 1
         keep = lax.dynamic_slice_in_dim(buf, mine * half, half, 0)
         send = lax.dynamic_slice_in_dim(buf, (1 - mine) * half, half, 0)
         got = lax.ppermute(
-            send.astype(jnp.bfloat16), "fsdp", [(i, i ^ bit) for i in range(count)]
+            send.astype(jnp.bfloat16), "fsdp", [(i, i ^ (1 << bit)) for i in range(count)]
         )
         buf = keep + got.astype(jnp.float32)
-        bit //= 2
     return split_columns(buf, widths)
 
 
@@ -486,10 +488,7 @@
     up_out = jnp.dot(second_all, w_up, preferred_element_type=jnp.float32)
     activated = (jax.nn.silu(gate_out) * up_out).astype(jnp.bfloat16)
 
-    def down_term(start, count):
-        return contract_last(activated, w_down_t)
-
-    output = (after_attn + token_sum(down_term, rows)).astype(jnp.bfloat16)
+    down_partial = contract_last(activated, w_down_t)
     grad_act = jnp.dot(mlp_grad_all, w_down_t, preferred_element_type=jnp.float32)
     unused, pull_gate = jax.vjp(
         lambda gate_in, up_in: jax.nn.silu(gate_in) * up_in, gate_out, up_out
@@ -509,6 +508,8 @@
     norm_second_grad, post_gain_part = pull_second(second_back)
     residual_grad = cotangent + norm_second_grad
     attn_grad_all = token_gather(residual_grad.astype(jnp.bfloat16))
+    down_partial, attn_grad_all = lax.optimization_barrier((down_partial, attn_grad_all))
+    down_rows = token_sum(lambda start, count: down_partial, rows)
     out_weight_grad_t = contract_rows(attn_grad_all, out_rows)
     mlp_packed = jnp.concatenate(
         [g.astype(jnp.bfloat16) for g in (gate_grad, up_grad, down_grad_t, out_weight_grad_t)],
@@ -538,6 +539,8 @@
     unseen = (piece == 1) & (jnp.arange(group_rows) >= quarter)
     far_grads = jnp.where(unseen[None, None, :, None], 0.0, jnp.stack([dk_far, dv_far]))
     returned = swapped(far_grads.astype(jnp.bfloat16), "fsdp", 0)
+    down_rows, dq_raw = lax.optimization_barrier((down_rows, dq_raw))
+    output = (after_attn + down_rows).astype(jnp.bfloat16)
     dq_raw, dk_own, dv_own = attention_backward(
         query_t, grad_t, delta_t, query_start, own_keys, own_values,
         dq_raw, piece, quarter, 0,

time: 748 us -> 737 us (0.985)
  waiting for transfers between devices: 200 us -> 174 us
  local copies, waits for them, and re-layouts: 126 us -> 138 us
    ppermute x3, waiting for transfers between devices: 41.9 us -> 29.6 us  [halving_scatter(): lax.ppermute(send.astype(jnp.bfloat16), 'fsdp', [(i, i ^ 1 << bit) for i...]
    optimization_barrier x0 -> x1, local copies, waits for them, and re-layouts: none -> 9.3 us  [shards(): lax.optimization_barrier((down_partial, attn_grad_all))]
    ppermute x2, waiting for transfers between devices: 18.8 us -> 9.89 us  [swapped(): lax.ppermute(shard, axis, [(i, i ^ 1 << distance) for i in range(lax.axis...]
    unnamed x218 -> x217, local copies, waits for them, and re-layouts: 46.7 us -> 47.5 us
  transfers between devices with their start and end apart: 32 -> 32, of which waited for: 18 -> 19; matrix products, arithmetic and copies ran while one was open for 32% -> 30% of each run, Pallas kernels for 18% -> 19%
where the time goes in v6:
time: 737 us; the launch traced here: 728 us
  waiting for transfers between devices  174 us (24%)
  local copies, waits for them, and re-layouts  138 us (19%)
  Pallas kernels  135 us (18%)
  other arithmetic  123 us (17%)
  matrix products  110 us (15%)
  starting transfers between devices  32.2 us (4%)
  between operations  15.7 us (2%)
    ppermute x16, waiting for transfers between devices, exchange(): lax.ppermute(values, 'tensor', [(i, i ^ distance) for i in range(count)])  128 us
    pallas_call x2, Pallas kernels, attention_backward(): pl.pallas_call(functools.partial(_bwd_kernel, scale=scale, block=block),...  83 us
    pallas_call x2, Pallas kernels, attention_forward(): pl.pallas_call(functools.partial(_fwd_kernel, scale=scale, block=block),...  52.1 us
    unnamed x217, local copies, waits for them, and re-layouts  47.5 us
    dot_general x7, matrix products, contract_last(): lax.dot_general(left, right, (((1,), (1,)), ((), ())), preferred_element_...  36.3 us
    dot_general x7, matrix products, contract_rows(): lax.dot_general(left, right, (((0,), (0,)), ((), ())), preferred_element_...  32.2 us
    ppermute x3, waiting for transfers between devices, halving_scatter(): lax.ppermute(send.astype(jnp.bfloat16), 'fsdp', [(i, i ^ 1 << bit) for i...  29.6 us
    concatenate x1, other arithmetic, shards(): jnp.concatenate([g.astype(jnp.bfloat16) for g in (gate_grad, up_grad, dow...  15.8 us
  transfers between devices with their start and end apart: 32, of which 19 were waited for; matrix products, arithmetic and copies ran while one was open for 30% of the time, Pallas kernels for 19%

profile of v6, /device:TPU:0, one launch (start us, length us, event | category | flops | bytes accessed | tf_op | source)
XLA Modules:
  0.0 727.6 jit_solution(1135593102842841764)
XLA Ops:
  46.1 20.1 %collective-permute-done.3 = bf16[512,1024]{0,1:T(8,128)(2,1)} collective-permute-done((bf16[512,1024]{0,1:T(8,128)(2,1)}, bf16[512,1024]{0,1:T(8,128)(2,1)}, u32[]{:S(2)}, u32[]{:S(2)}) %collective-permute-start.3) | collective-permute-done | bytes 1048608 | tf_op jit(solution)/shard_map/ppermute | solution.py:336
  137.2 6.0 fusion.19.q_ref
  148.5 28.8 %attn_fwd.2 = (f32[2,2,2048,128]{3,2,1,0:T(8,128)}, f32[2,2,2048,128]{3,2,1,0:T(8,128)}) custom-call(s32[7,10]{1,0:T(8,128)S(1)} %broadcast_select_fusion.3.tab_ref, bf16[2,2,2048,128]{3,2,1,0:T(8,128)(2,1)S(1)} %fusion.19.q_ref, s32[2048,128]{1,0:T(8,128)S(1)} %broadcast_in_dim.45.qs_ref, ...), custom_call_target="tpu_custom_call", output_to_operand_aliasing={{0}: (5, {}), {1}: (6, {})} | custom-call | flops 5368709120 | bytes 20971520 | tf_op jit(solution)/shard_map/attn_fwd/pallas_call | solution.py:124
  184.2 23.3 %attn_fwd.3 = (f32[2,2,2048,128]{3,2,1,0:T(8,128)}, f32[2,2,2048,128]{3,2,1,0:T(8,128)}) custom-call(s32[7,8]{1,0:T(8,128)S(1)} %broadcast_select_fusion.7.tab_ref, bf16[2,2,2048,128]{3,2,1,0:T(8,128)(2,1)S(1)} %fusion.19.q_ref, s32[2048,128]{1,0:T(8,128)S(1)} %broadcast_in_dim.45.qs_ref, ...), custom_call_target="tpu_custom_call", output_to_operand_aliasing={{0}: (5, {}), {1}: (6, {})} | custom-call | flops 4294967296 | bytes 16777216 | tf_op jit(solution)/shard_map/attn_fwd/pallas_call | solution.py:124
  226.7 23.7 %collective-permute-done.9 = bf16[512,1024]{0,1:T(8,128)(2,1)S(1)} collective-permute-done((bf16[512,1024]{0,1:T(8,128)(2,1)S(1)}, bf16[512,1024]{0,1:T(8,128)(2,1)S(1)}, u32[]{:S(2)}, u32[]{:S(2)}) %collective-permute-start.9) | collective-permute-done | bytes 1048608 | tf_op jit(solution)/shard_map/ppermute | solution.py:336
  253.5 22.9 %collective-permute-done.10 = bf16[512,1024]{0,1:T(8,128)(2,1)S(1)} collective-permute-done((bf16[512,1024]{0,1:T(8,128)(2,1)S(1)}, bf16[512,1024]{0,1:T(8,128)(2,1)S(1)}, u32[]{:S(2)}, u32[]{:S(2)}) %collective-permute-start.10) | collective-permute-done | bytes 1048608 | tf_op jit(solution)/shard_map/ppermute | solution.py:336
  281.1 5.5 fusion.46
  286.7 5.6 fusion.50
  292.3 12.1 %multiply_convert_fusion = (bf16[2048,768]{1,0:T(8,128)(2,1)S(1)}, bf16[2048,768]{1,0:T(8,128)(2,1)}, bf16[2048,768]{1,0:T(8,128)(2,1)}) fusion(f32[2048,768]{1,0:T(8,128)} %fusion.50, f32[2048,768]{1,0:T(8,128)} %fusion.46, bf16[2048,1024]{0,1:T(8,128)(2,1)S(1)} %copy-done.33, bf16[1024,2816]{0,1:T(8,128)(2,1)S(1)} %bitcast.265), kind=kOutput, calls=%fused_computation.6 | convolution fusion | flops 3246391296 | bytes 27787264 | tf_op jit(solution)/shard_map/dot_general | solution.py:492
  304.3 7.6 %fusion.48 = f32[2048,1024]{0,1:T(8,128)} fusion(bf16[2048,768]{1,0:T(8,128)(2,1)} %get-tuple-element.136, bf16[1024,2816]{0,1:T(8,128)(2,1)S(1)} %bitcast.265), kind=kOutput, calls=%fused_computation.129 | convolution fusion | flops 3221225472 | bytes 13107200 | tf_op jit(solution)/shard_map/dot_general | solution.py:274
  312.0 6.9 convolution_add_fusion
  326.2 23.7 %collective-permute-done.13 = bf16[512,1024]{0,1:T(8,128)(2,1)S(1)} collective-permute-done((bf16[512,1024]{0,1:T(8,128)(2,1)S(1)}, bf16[512,1024]{0,1:T(8,128)(2,1)S(1)}, u32[]{:S(2)}, u32[]{:S(2)}) %collective-permute-start.13) | collective-permute-done | bytes 1048608 | tf_op jit(solution)/shard_map/ppermute | solution.py:336
  360.1 18.3 %collective-permute-done.14 = bf16[512,1024]{0,1:T(8,128)(2,1)S(1)} collective-permute-done((bf16[512,1024]{0,1:T(8,128)(2,1)S(1)}, bf16[512,1024]{0,1:T(8,128)(2,1)S(1)}, u32[]{:S(2)}, u32[]{:S(2)}) %collective-permute-start.14) | collective-permute-done | bytes 1048608 | tf_op jit(solution)/shard_map/ppermute | solution.py:336
  378.6 7.0 fusion.43
  405.9 7.2 fusion.8
  413.2 15.8 %pad_maximum_fusion = bf16[1024,2816]{0,1:T(8,128)(2,1)} fusion(bf16[1024,512]{0,1:T(8,128)(2,1)S(1)} %convolution_convert_fusion.5, bf16[1024,768]{0,1:T(8,128)(2,1)S(1)} %copy-done.41, bf16[1024,768]{0,1:T(8,128)(2,1)S(1)} %copy-done.40, bf16[1024,768]{0,1:T(8,128)(2,1)S(1)} %copy-done.39), kind=kLoop, calls=%fused_computation.10 | loop fusion | flops 23068672 | bytes 11534336 | tf_op jit(solution)/shard_map/concatenate | solution.py:514
  431.5 8.3 %copy.177 = bf16[1024,2816]{1,0:T(8,128)(2,1)} copy(bf16[1024,2816]{0,1:T(8,128)(2,1)} %pad_maximum_fusion) | data formatting | bytes 11534336
  439.8 9.3 %copy.148 = f32[2048,1024]{0,1:T(8,128)} copy(f32[2048,1024]{1,0:T(8,128)} %fusion.43) | data formatting | bytes 16777216 | tf_op jit(solution)/shard_map/optimization_barrier | solution.py:511
  467.0 37.4 %attn_bwd.2 = (f32[2,2,2048,128]{3,2,1,0:T(8,128)}, f32[2,2048,128]{2,1,0:T(8,128)}, f32[2,2048,128]{2,1,0:T(8,128)}) custom-call(s32[7,8]{1,0:T(8,128)} %broadcast_select_fusion.6.tab_ref, bf16[2,2,2048,128]{3,2,1,0:T(8,128)(2,1)} %copy-done.2, bf16[2,2,2048,128]{3,2,1,0:T(8,128)(2,1)} %get-tuple-element.45.h_ref, ...), custom_call_target="tpu_custom_call", output_to_operand_aliasing={{0}: (7, {})} | custom-call | flops 10737418240 | bytes 20971520 | tf_op jit(solution)/shard_map/attn_bwd/pallas_call | solution.py:207
  516.2 45.6 %attn_bwd.3 = (f32[2,2,2048,128]{3,2,1,0:T(8,128)}, f32[2,2048,128]{2,1,0:T(8,128)}, f32[2,2048,128]{2,1,0:T(8,128)}) custom-call(s32[7,10]{1,0:T(8,128)} %broadcast_select_fusion.2.tab_ref, bf16[2,2,2048,128]{3,2,1,0:T(8,128)(2,1)} %copy-done.2, bf16[2,2,2048,128]{3,2,1,0:T(8,128)(2,1)} %get-tuple-element.45.h_ref, ...), custom_call_target="tpu_custom_call", output_to_operand_aliasing={{0}: (7, {})} | custom-call | flops 13421772800 | bytes 26214400 | tf_op jit(solution)/shard_map/attn_bwd/pallas_call | solution.py:207
  589.1 5.6 fusion.78
  619.2 6.1 fusion.119
  647.4 16.9 %collective-permute-done.21 = bf16[512,1024]{0,1:T(8,128)(2,1)} collective-permute-done((bf16[512,1024]{0,1:T(8,128)(2,1)S(1)}, bf16[512,1024]{0,1:T(8,128)(2,1)}, u32[]{:S(2)}, u32[]{:S(2)}) %collective-permute-start.21) | collective-permute-done | bytes 1048608 | tf_op jit(solution)/shard_map/ppermute | solution.py:302
  667.3 12.7 %collective-permute-done.22 = bf16[256,1024]{0,1:T(8,128)(2,1)} collective-permute-done((bf16[256,1024]{0,1:T(8,128)(2,1)}, bf16[256,1024]{0,1:T(8,128)(2,1)}, u32[]{:S(2)}, u32[]{:S(2)}) %collective-permute-start.22) | collective-permute-done | bytes 524320 | tf_op jit(solution)/shard_map/ppermute | solution.py:302
  (447 shorter events, 335.5 us)
Async XLA Ops:
  7.2 81.1 %all-gather.3.cloned.1.call-start = ((), (), s32[]{:S(2)}) async-start(), calls=%async_computation.1 | async-start | bytes 2359296 | tf_op jit(solution)/shard_map/all_gather | solution.py:408
  10.8 204.4 %all-gather.5.cloned.1.call-start = ((), (), s32[]{:S(2)}) async-start(), calls=%async_computation.2 | async-start | bytes 6488064 | tf_op jit(solution)/shard_map/all_gather | solution.py:463
  17.5 27.0 %collective-permute-start.5 = (bf16[512,1024]{0,1:T(8,128)(2,1)S(1)}, bf16[512,1024]{0,1:T(8,128)(2,1)S(1)}, u32[]{:S(2)}, u32[]{:S(2)}) collective-permute-start(bf16[512,1024]{0,1:T(8,128)(2,1)S(1)} %get-tuple-element.132), channel_id=1, source_target_pairs={{0,2},{1,3},{2,0},{3,1},{4,6},{5,7},{6,4},{7,5},{8,10},{9,11},{10,... | collective-permute-start | bytes 3145736 | tf_op jit(solution)/shard_map/ppermute | solution.py:336
  28.0 4.5 collective-permute-start.2
  37.1 29.1 %collective-permute-start.3 = (bf16[512,1024]{0,1:T(8,128)(2,1)}, bf16[512,1024]{0,1:T(8,128)(2,1)}, u32[]{:S(2)}, u32[]{:S(2)}) collective-permute-start(bf16[512,1024]{0,1:T(8,128)(2,1)} %get-tuple-element.134), channel_id=1, source_target_pairs={{0,2},{1,3},{2,0},{3,1},{4,6},{5,7},{6,4},{7,5},{8,10},{9,11},{10,... | collective-permute-start | bytes 3145736 | tf_op jit(solution)/shard_map/ppermute | solution.py:336
  41.1 553.6 %reduce-scatter.4.cloned.1.call-start = ((), (), s32[]{:S(2)}) async-start(), calls=%async_computation.3 | async-start | bytes 6488064
  46.0 32.9 %collective-permute-start.6 = (bf16[2,512,1024]{1,2,0:T(8,128)(2,1)}, bf16[2,512,1024]{1,2,0:T(8,128)(2,1)}, u32[]{:S(2)}, u32[]{:S(2)}) collective-permute-start(bf16[2,512,1024]{1,2,0:T(8,128)(2,1)} %pad_maximum_fusion.3), channel_id=1, source_target_pairs={{0,1},{1,0},{2,3},{3,2},{4,5},{5,4},{6,7},{7,6},{8,9},{9,8},{10,11... | collective-permute-start | bytes 6291464 | tf_op jit(solution)/shard_map/ppermute | solution.py:336
  69.3 14.3 %collective-permute-start.4 = (bf16[2,512,1024]{1,2,0:T(8,128)(2,1)}, bf16[2,512,1024]{1,2,0:T(8,128)(2,1)}, u32[]{:S(2)}, u32[]{:S(2)}) collective-permute-start(bf16[2,512,1024]{1,2,0:T(8,128)(2,1)} %pad_maximum_fusion.2), channel_id=1, source_target_pairs={{0,1},{1,0},{2,3},{3,2},{4,5},{5,4},{6,7},{7,6},{8,9},{9,8},{10,11... | collective-permute-start | bytes 6291464 | tf_op jit(solution)/shard_map/ppermute | solution.py:336
  108.1 74.4 %collective-permute-start.7 = (bf16[2,2,2048,128]{3,2,1,0:T(8,128)(2,1)}, bf16[2,2,2048,128]{3,2,1,0:T(8,128)(2,1)}, u32[]{:S(2)}, u32[]{:S(2)}) collective-permute-start(bf16[2,2,2048,128]{3,2,1,0:T(8,128)(2,1)} %pad_maximum_fusion.4), channel_id=1, source_target_pairs={{0,4},{4,0},{8,12},{12,8},{16,20},{20,16},{24,28},{28,24},{1,5},{5... | collective-permute-start | bytes 6291464 | tf_op jit(solution)/shard_map/ppermute | solution.py:236
  225.1 25.3 %collective-permute-start.9 = (bf16[512,1024]{0,1:T(8,128)(2,1)S(1)}, bf16[512,1024]{0,1:T(8,128)(2,1)S(1)}, u32[]{:S(2)}, u32[]{:S(2)}) collective-permute-start(bf16[512,1024]{0,1:T(8,128)(2,1)S(1)} %fusion.33), channel_id=1, source_target_pairs={{0,2},{1,3},{2,0},{3,1},{4,6},{5,7},{6,4},{7,5},{8,10},{9,11},{10,... | collective-permute-start | bytes 3145736 | tf_op jit(solution)/shard_map/ppermute | solution.py:336
  251.9 24.4 %collective-permute-start.10 = (bf16[512,1024]{0,1:T(8,128)(2,1)S(1)}, bf16[512,1024]{0,1:T(8,128)(2,1)S(1)}, u32[]{:S(2)}, u32[]{:S(2)}) collective-permute-start(bf16[512,1024]{0,1:T(8,128)(2,1)S(1)} %get-tuple-element.128), channel_id=1, source_target_pairs={{0,2},{1,3},{2,0},{3,1},{4,6},{5,7},{6,4},{7,5},{8,10},{9,11},{10,... | collective-permute-start | bytes 3145736 | tf_op jit(solution)/shard_map/ppermute | solution.py:336
  324.6 25.3 %collective-permute-start.13 = (bf16[512,1024]{0,1:T(8,128)(2,1)S(1)}, bf16[512,1024]{0,1:T(8,128)(2,1)S(1)}, u32[]{:S(2)}, u32[]{:S(2)}) collective-permute-start(bf16[512,1024]{0,1:T(8,128)(2,1)S(1)} %fusion.29), channel_id=1, source_target_pairs={{0,2},{1,3},{2,0},{3,1},{4,6},{5,7},{6,4},{7,5},{8,10},{9,11},{10,... | collective-permute-start | bytes 3145736 | tf_op jit(solution)/shard_map/ppermute | solution.py:336
  353.9 24.4 %collective-permute-start.14 = (bf16[512,1024]{0,1:T(8,128)(2,1)S(1)}, bf16[512,1024]{0,1:T(8,128)(2,1)S(1)}, u32[]{:S(2)}, u32[]{:S(2)}) collective-permute-start(bf16[512,1024]{0,1:T(8,128)(2,1)S(1)} %get-tuple-element.125), channel_id=1, source_target_pairs={{0,2},{1,3},{2,0},{3,1},{4,6},{5,7},{6,4},{7,5},{8,10},{9,11},{10,... | collective-permute-start | bytes 3145736 | tf_op jit(solution)/shard_map/ppermute | solution.py:336
  378.6 17.0 %collective-permute-start.15 = (bf16[2,512,1024]{1,2,0:T(8,128)(2,1)S(1)}, bf16[2,512,1024]{1,2,0:T(8,128)(2,1)S(1)}, u32[]{:S(2)}, u32[]{:S(2)}) collective-permute-start(bf16[2,512,1024]{1,2,0:T(8,128)(2,1)S(1)} %pad_maximum_fusion.8), channel_id=1, source_target_pairs={{0,1},{1,0},{2,3},{3,2},{4,5},{5,4},{6,7},{7,6},{8,9},{9,8},{10,11... | collective-permute-start | bytes 6291464 | tf_op jit(solution)/shard_map/ppermute | solution.py:336
  453.1 4.5 collective-permute-start.16
  463.3 48.5 %collective-permute-start.17 = (bf16[512,1024]{0,1:T(8,128)(2,1)}, bf16[512,1024]{0,1:T(8,128)(2,1)}, u32[]{:S(2)}, u32[]{:S(2)}) collective-permute-start(bf16[512,1024]{0,1:T(8,128)(2,1)} %fusion.25), channel_id=1, source_target_pairs={{0,2},{1,3},{2,0},{3,1},{4,6},{5,7},{6,4},{7,5},{8,10},{9,11},{10,... | collective-permute-start | bytes 3145736 | tf_op jit(solution)/shard_map/ppermute | solution.py:336
  508.1 58.4 %collective-permute-start.18 = (bf16[2,2,2048,128]{3,2,1,0:T(8,128)(2,1)}, bf16[2,2,2048,128]{3,2,1,0:T(8,128)(2,1)}, u32[]{:S(2)}, u32[]{:S(2)}) collective-permute-start(bf16[2,2,2048,128]{3,2,1,0:T(8,128)(2,1)} %fusion.7), channel_id=1, source_target_pairs={{0,4},{4,0},{8,12},{12,8},{16,20},{20,16},{24,28},{28,24},{1,5},{5... | collective-permute-start | bytes 6291464 | tf_op jit(solution)/shard_map/ppermute | solution.py:236
  635.2 5.7 collective-permute-start.19
  639.2 25.2 %collective-permute-start.21 = (bf16[512,1024]{0,1:T(8,128)(2,1)S(1)}, bf16[512,1024]{0,1:T(8,128)(2,1)}, u32[]{:S(2)}, u32[]{:S(2)}) collective-permute-start(bf16[512,1024]{0,1:T(8,128)(2,1)S(1)} %dynamic-slice_convert_fusion), channel_id=1, source_target_pairs={{0,4},{4,0},{8,12},{12,8},{16,20},{20,16},{24,28},{28,24},{1,5},{5... | collective-permute-start | bytes 3145736 | tf_op jit(solution)/shard_map/ppermute | solution.py:302
  646.0 39.2 %collective-permute-start.20 = (bf16[512,1024]{0,1:T(8,128)(2,1)}, bf16[512,1024]{0,1:T(8,128)(2,1)}, u32[]{:S(2)}, u32[]{:S(2)}) collective-permute-start(bf16[512,1024]{0,1:T(8,128)(2,1)} %fusion.21), channel_id=1, source_target_pairs={{0,2},{1,3},{2,0},{3,1},{4,6},{5,7},{6,4},{7,5},{8,10},{9,11},{10,... | collective-permute-start | bytes 3145736 | tf_op jit(solution)/shard_map/ppermute | solution.py:336
  666.8 13.2 %collective-permute-start.22 = (bf16[256,1024]{0,1:T(8,128)(2,1)}, bf16[256,1024]{0,1:T(8,128)(2,1)}, u32[]{:S(2)}, u32[]{:S(2)}) collective-permute-start(bf16[256,1024]{0,1:T(8,128)(2,1)} %dynamic-slice_convert_fusion.9), channel_id=1, source_target_pairs={{0,8},{4,12},{8,0},{12,4},{16,24},{20,28},{24,16},{28,20},{1,9},{5... | collective-permute-start | bytes 1572872 | tf_op jit(solution)/shard_map/ppermute | solution.py:302
  683.0 13.6 %collective-permute-start.23 = (bf16[128,1024]{0,1:T(8,128)(2,1)}, bf16[128,1024]{0,1:T(8,128)(2,1)}, u32[]{:S(2)}, u32[]{:S(2)}) collective-permute-start(bf16[128,1024]{0,1:T(8,128)(2,1)} %dynamic-slice_convert_fusion.10), channel_id=1, source_target_pairs={{0,16},{4,20},{8,24},{12,28},{16,0},{20,4},{24,8},{28,12},{1,17},{... | collective-permute-start | bytes 786440 | tf_op jit(solution)/shard_map/ppermute | solution.py:302
  699.5 5.3 collective-permute-start.26
  709.2 10.3 %collective-permute-start.28 = (f32[2304]{0:T(1024)S(1)}, f32[2304]{0:T(1024)S(1)}, u32[]{:S(2)}, u32[]{:S(2)}) collective-permute-start(f32[2304]{0:T(1024)S(1)} %add.316), channel_id=1, source_target_pairs={{0,16},{4,20},{8,24},{12,28},{16,0},{20,4},{24,8},{28,12},{1,17},{... | collective-permute-start | bytes 27656 | tf_op jit(solution)/shard_map/ppermute | solution.py:327
  (106 other events, 1438.4 us)
Sparse Core Ops, SparseCore 0:
  10.9 51.8 all-gather.2
  64.9 116.6 all-gather.4
  439.9 119.9 reduce-scatter.3

commit v7 on v6

--- a/solution.py
+++ b/solution.py
@@ -245,11 +245,13 @@
     half = values.shape[-1] // 2
     frequency = THETA ** (-(jnp.arange(half, dtype=jnp.float32) * 2.0 / values.shape[-1]))
     angle = start_offset.astype(jnp.float32)[:, None] * frequency[None, :]
-    cosine = jnp.cos(angle)
-    sine = jnp.sin(angle)
-    cos_full = jnp.concatenate([cosine, cosine], axis=-1)[:, None, :]
-    sin_signed = jnp.concatenate([-sine, sine], axis=-1)[:, None, :]
-    return values * cos_full + jnp.roll(values, half, axis=-1) * sin_signed
+    cosine = jnp.cos(angle)[:, None, :]
+    sine = jnp.sin(angle)[:, None, :]
+    first = values[..., :half]
+    second = values[..., half:]
+    return jnp.concatenate(
+        [first * cosine - second * sine, second * cosine + first * sine], axis=-1
+    )
 
 
 def prepare_inputs(projected, gain, start_offset, head_groups):
@@ -488,7 +490,6 @@
     up_out = jnp.dot(second_all, w_up, preferred_element_type=jnp.float32)
     activated = (jax.nn.silu(gate_out) * up_out).astype(jnp.bfloat16)
 
-    down_partial = contract_last(activated, w_down_t)
     grad_act = jnp.dot(mlp_grad_all, w_down_t, preferred_element_type=jnp.float32)
     unused, pull_gate = jax.vjp(
         lambda gate_in, up_in: jax.nn.silu(gate_in) * up_in, gate_out, up_out
@@ -508,8 +509,8 @@
     norm_second_grad, post_gain_part = pull_second(second_back)
     residual_grad = cotangent + norm_second_grad
     attn_grad_all = token_gather(residual_grad.astype(jnp.bfloat16))
-    down_partial, attn_grad_all = lax.optimization_barrier((down_partial, attn_grad_all))
-    down_rows = token_sum(lambda start, count: down_partial, rows)
+    activated_late, attn_grad_all = lax.optimization_barrier((activated, attn_grad_all))
+    down_rows = token_sum(lambda start, count: contract_last(activated_late, w_down_t), rows)
     out_weight_grad_t = contract_rows(attn_grad_all, out_rows)
     mlp_packed = jnp.concatenate(
         [g.astype(jnp.bfloat16) for g in (gate_grad, up_grad, down_grad_t, out_weight_grad_t)],
@@ -580,9 +581,8 @@
     unused, pull_first = jax.vjp(rms_scale, x_float, gain_first)
     norm_first_grad, input_gain_part = pull_first(first_back)
     input_grad = (residual_grad + norm_first_grad).astype(jnp.bfloat16)
-    query_shard, key_shard, value_shard = halving_scatter(
-        (query_weight_grad, key_weight_grad, value_weight_grad)
-    )
+    (query_shard,) = halving_scatter((query_weight_grad,))
+    key_shard, value_shard = halving_scatter((key_weight_grad, value_weight_grad))
     gain_totals = all_sum(
         jnp.concatenate([input_gain_part, q_gain_part, k_gain_part, post_gain_part])
     )

time: 737 us -> 725 us (0.984)
  local copies, waits for them, and re-layouts: 138 us -> 119 us
  waiting for transfers between devices: 174 us -> 192 us
  other arithmetic: 123 us -> 115 us
    ppermute x2, waiting for transfers between devices: 9.89 us -> 33.8 us  [swapped(): lax.ppermute(shard, axis, [(i, i ^ 1 << distance) for i in range(lax.axis...]
    ppermute x3 -> x6, waiting for transfers between devices: 29.6 us -> 15 us  [halving_scatter(): lax.ppermute(send.astype(jnp.bfloat16), 'fsdp', [(i, i ^ 1 << bit) for i...]
    slice x4 -> x0, local copies, waits for them, and re-layouts: 13.1 us -> none  [rotary(): return values * cos_full + jnp.roll(values, half, axis=-1) * sin_signed]
    ppermute x16, waiting for transfers between devices: 128 us -> 139 us  [exchange(): lax.ppermute(values, 'tensor', [(i, i ^ distance) for i in range(count)])]
    optimization_barrier x1 -> x0, local copies, waits for them, and re-layouts: 9.3 us -> none  [shards(): lax.optimization_barrier((down_partial, attn_grad_all))]
    another operation x7 -> x9, local copies, waits for them, and re-layouts: 11.2 us -> 16.7 us
    unnamed x217 -> x232, local copies, waits for them, and re-layouts: 47.5 us -> 49.5 us
  transfers between devices with their start and end apart: 32 -> 35, of which waited for: 19 -> 20; matrix products, arithmetic and copies ran while one was open for 30% -> 30% of each run, Pallas kernels for 19% -> 19%
where the time goes in v7:
time: 725 us; the launch traced here: 717 us
  waiting for transfers between devices  192 us (26%)
  Pallas kernels  136 us (19%)
  local copies, waits for them, and re-layouts  119 us (16%)
  other arithmetic  115 us (16%)
  matrix products  107 us (15%)
  starting transfers between devices  32.6 us (4%)
  between operations  15.7 us (2%)
    ppermute x16, waiting for transfers between devices, exchange(): lax.ppermute(values, 'tensor', [(i, i ^ distance) for i in range(count)])  139 us
    pallas_call x2, Pallas kernels, attention_backward(): pl.pallas_call(functools.partial(_bwd_kernel, scale=scale, block=block),...  83.3 us
    pallas_call x2, Pallas kernels, attention_forward(): pl.pallas_call(functools.partial(_fwd_kernel, scale=scale, block=block),...  52.2 us
    unnamed x232, local copies, waits for them, and re-layouts  49.5 us
    dot_general x7, matrix products, contract_last(): lax.dot_general(left, right, (((1,), (1,)), ((), ())), preferred_element_...  34.6 us
    ppermute x2, waiting for transfers between devices, swapped(): lax.ppermute(shard, axis, [(i, i ^ 1 << distance) for i in range(lax.axis...  33.8 us
    dot_general x7, matrix products, contract_rows(): lax.dot_general(left, right, (((0,), (0,)), ((), ())), preferred_element_...  31 us
    another operation x9, local copies, waits for them, and re-layouts  16.7 us
  transfers between devices with their start and end apart: 35, of which 20 were waited for; matrix products, arithmetic and copies ran while one was open for 30% of the time, Pallas kernels for 19%

profile of v7, /device:TPU:0, one launch (start us, length us, event | category | flops | bytes accessed | tf_op | source)
XLA Modules:
  0.0 716.8 jit_solution(8957620236828217018)
XLA Ops:
  51.5 18.4 %collective-permute-done.3 = bf16[512,1024]{0,1:T(8,128)(2,1)} collective-permute-done((bf16[512,1024]{0,1:T(8,128)(2,1)}, bf16[512,1024]{0,1:T(8,128)(2,1)}, u32[]{:S(2)}, u32[]{:S(2)}) %collective-permute-start.3) | collective-permute-done | bytes 1048608 | tf_op jit(solution)/shard_map/ppermute | solution.py:338
  136.9 28.8 %attn_fwd.2 = (f32[2,2,2048,128]{3,2,1,0:T(8,128)}, f32[2,2,2048,128]{3,2,1,0:T(8,128)}) custom-call(s32[7,10]{1,0:T(8,128)S(1)} %broadcast_select_fusion.3.tab_ref, bf16[2,2,2048,128]{3,2,1,0:T(8,128)(2,1)S(1)} %maximum_bitcast_fusion.q_ref, s32[2048,128]{1,0:T(8,128)S(1)} %broadcast_in_dim.45.qs_ref, ...), custom_call_target="tpu_custom_call", output_to_operand_aliasing={{0}: (5, {}), {1}: (6, {})} | custom-call | flops 5368709120 | bytes 20971520 | tf_op jit(solution)/shard_map/attn_fwd/pallas_call | solution.py:124
  165.7 17.1 %collective-permute-done.7 = bf16[2,2,2048,128]{3,2,1,0:T(8,128)(2,1)} collective-permute-done((bf16[2,2,2048,128]{3,2,1,0:T(8,128)(2,1)}, bf16[2,2,2048,128]{3,2,1,0:T(8,128)(2,1)}, u32[]{:S(2)}, u32[]{:S(2)}) %collective-permute-start.7) | collective-permute-done | bytes 2097184 | tf_op jit(solution)/shard_map/ppermute | solution.py:236
  184.5 23.4 %attn_fwd.3 = (f32[2,2,2048,128]{3,2,1,0:T(8,128)}, f32[2,2,2048,128]{3,2,1,0:T(8,128)}) custom-call(s32[7,8]{1,0:T(8,128)S(1)} %broadcast_select_fusion.7.tab_ref, bf16[2,2,2048,128]{3,2,1,0:T(8,128)(2,1)S(1)} %maximum_bitcast_fusion.q_ref, s32[2048,128]{1,0:T(8,128)S(1)} %broadcast_in_dim.45.qs_ref, ...), custom_call_target="tpu_custom_call", output_to_operand_aliasing={{0}: (5, {}), {1}: (6, {})} | custom-call | flops 4294967296 | bytes 16777216 | tf_op jit(solution)/shard_map/attn_fwd/pallas_call | solution.py:124
  227.0 23.7 %collective-permute-done.9 = bf16[512,1024]{0,1:T(8,128)(2,1)S(1)} collective-permute-done((bf16[512,1024]{0,1:T(8,128)(2,1)S(1)}, bf16[512,1024]{0,1:T(8,128)(2,1)S(1)}, u32[]{:S(2)}, u32[]{:S(2)}) %collective-permute-start.9) | collective-permute-done | bytes 1048608 | tf_op jit(solution)/shard_map/ppermute | solution.py:338
  253.9 22.9 %collective-permute-done.10 = bf16[512,1024]{0,1:T(8,128)(2,1)S(1)} collective-permute-done((bf16[512,1024]{0,1:T(8,128)(2,1)S(1)}, bf16[512,1024]{0,1:T(8,128)(2,1)S(1)}, u32[]{:S(2)}, u32[]{:S(2)}) %collective-permute-start.10) | collective-permute-done | bytes 1048608 | tf_op jit(solution)/shard_map/ppermute | solution.py:338
  281.5 5.5 fusion.42
  287.0 5.6 fusion.46
  292.6 12.7 %multiply_convert_fusion = (bf16[2048,768]{1,0:T(8,128)(2,1)}, bf16[2048,768]{1,0:T(8,128)(2,1)}, bf16[2048,768]{1,0:T(8,128)(2,1)}) fusion(f32[2048,768]{1,0:T(8,128)} %fusion.46, f32[2048,768]{1,0:T(8,128)} %fusion.42, bf16[2048,1024]{0,1:T(8,128)(2,1)S(1)} %copy-done.35, bf16[1024,2816]{0,1:T(8,128)(2,1)S(1)} %bitcast.254), kind=kOutput, calls=%fused_computation.6 | convolution fusion | flops 3246391296 | bytes 27787264 | tf_op jit(solution)/shard_map/dot_general | solution.py:493
  305.3 7.8 %fusion.44 = f32[2048,1024]{0,1:T(8,128)} fusion(bf16[2048,768]{1,0:T(8,128)(2,1)} %get-tuple-element.147, bf16[1024,2816]{0,1:T(8,128)(2,1)S(1)} %bitcast.254), kind=kOutput, calls=%fused_computation.139 | convolution fusion | flops 3221225472 | bytes 13107200 | tf_op jit(solution)/shard_map/dot_general | solution.py:276
  313.1 6.9 convolution_add_fusion
  327.3 23.7 %collective-permute-done.13 = bf16[512,1024]{0,1:T(8,128)(2,1)S(1)} collective-permute-done((bf16[512,1024]{0,1:T(8,128)(2,1)S(1)}, bf16[512,1024]{0,1:T(8,128)(2,1)S(1)}, u32[]{:S(2)}, u32[]{:S(2)}) %collective-permute-start.13) | collective-permute-done | bytes 1048608 | tf_op jit(solution)/shard_map/ppermute | solution.py:338
  356.7 22.9 %collective-permute-done.14 = bf16[512,1024]{0,1:T(8,128)(2,1)S(1)} collective-permute-done((bf16[512,1024]{0,1:T(8,128)(2,1)S(1)}, bf16[512,1024]{0,1:T(8,128)(2,1)S(1)}, u32[]{:S(2)}, u32[]{:S(2)}) %collective-permute-start.14) | collective-permute-done | bytes 1048608 | tf_op jit(solution)/shard_map/ppermute | solution.py:338
  406.5 7.2 fusion.6
  413.8 15.9 %pad_maximum_fusion = bf16[1024,2816]{0,1:T(8,128)(2,1)} fusion(bf16[1024,512]{0,1:T(8,128)(2,1)S(1)} %convolution_convert_fusion.5, bf16[1024,768]{0,1:T(8,128)(2,1)S(1)} %copy-done.46, bf16[1024,768]{0,1:T(8,128)(2,1)S(1)} %copy-done.45, bf16[1024,768]{0,1:T(8,128)(2,1)S(1)} %copy-done.44), kind=kLoop, calls=%fused_computation.10 | loop fusion | flops 23068672 | bytes 11534336 | tf_op jit(solution)/shard_map/concatenate | solution.py:515
  441.0 8.3 %copy.205 = bf16[1024,2816]{1,0:T(8,128)(2,1)} copy(bf16[1024,2816]{0,1:T(8,128)(2,1)} %pad_maximum_fusion) | data formatting | bytes 11534336
  463.2 37.6 %attn_bwd.2 = (f32[2,2,2048,128]{3,2,1,0:T(8,128)}, f32[2,2048,128]{2,1,0:T(8,128)}, f32[2,2048,128]{2,1,0:T(8,128)}) custom-call(s32[7,8]{1,0:T(8,128)} %broadcast_select_fusion.6.tab_ref, bf16[2,2,2048,128]{3,2,1,0:T(8,128)(2,1)} %copy-done.1, bf16[2,2,2048,128]{3,2,1,0:T(8,128)(2,1)} %get-tuple-element.45.h_ref, ...), custom_call_target="tpu_custom_call", output_to_operand_aliasing={{0}: (7, {})} | custom-call | flops 10737418240 | bytes 20971520 | tf_op jit(solution)/shard_map/attn_bwd/pallas_call | solution.py:207
  509.8 45.8 %attn_bwd.3 = (f32[2,2,2048,128]{3,2,1,0:T(8,128)}, f32[2,2048,128]{2,1,0:T(8,128)}, f32[2,2048,128]{2,1,0:T(8,128)}) custom-call(s32[7,10]{1,0:T(8,128)} %broadcast_select_fusion.2.tab_ref, bf16[2,2,2048,128]{3,2,1,0:T(8,128)(2,1)} %copy-done.1, bf16[2,2,2048,128]{3,2,1,0:T(8,128)(2,1)} %get-tuple-element.45.h_ref, ...), custom_call_target="tpu_custom_call", output_to_operand_aliasing={{0}: (7, {})} | custom-call | flops 13421772800 | bytes 26214400 | tf_op jit(solution)/shard_map/attn_bwd/pallas_call | solution.py:207
  555.6 16.7 %collective-permute-done.18 = bf16[2,2,2048,128]{3,2,1,0:T(8,128)(2,1)} collective-permute-done((bf16[2,2,2048,128]{3,2,1,0:T(8,128)(2,1)S(1)}, bf16[2,2,2048,128]{3,2,1,0:T(8,128)(2,1)}, u32[]{:S(2)}, u32[]{:S(2)}) %collective-permute-start.18) | collective-permute-done | bytes 2097184 | tf_op jit(solution)/shard_map/ppermute | solution.py:236
  594.1 5.8 fusion.74
  599.9 7.1 collective-permute-done.24
  640.2 6.9 fusion.128
  666.5 8.1 %collective-permute-done.20 = bf16[512,1024]{0,1:T(8,128)(2,1)} collective-permute-done((bf16[512,1024]{0,1:T(8,128)(2,1)}, bf16[512,1024]{0,1:T(8,128)(2,1)}, u32[]{:S(2)}, u32[]{:S(2)}) %collective-permute-start.20) | collective-permute-done | bytes 1048608 | tf_op jit(solution)/shard_map/ppermute | solution.py:338
  674.6 5.2 fusion.10
  (475 shorter events, 317.1 us)
Async XLA Ops:
  7.2 84.0 %all-gather.3.cloned.1.call-start = ((), (), s32[]{:S(2)}) async-start(), calls=%async_computation.1 | async-start | bytes 2359296 | tf_op jit(solution)/shard_map/all_gather | solution.py:410
  10.9 204.7 %all-gather.5.cloned.1.call-start = ((), (), s32[]{:S(2)}) async-start(), calls=%async_computation.2 | async-start | bytes 6488064 | tf_op jit(solution)/shard_map/all_gather | solution.py:465
  13.6 12.1 %collective-permute-start = (bf16[288]{0:T(512)(128)(2,1)S(1)}, bf16[288]{0:T(512)(128)(2,1)S(1)}, u32[]{:S(2)}, u32[]{:S(2)}) collective-permute-start(bf16[288]{0:T(512)(128)(2,1)S(1)} %pad_maximum_fusion.18), channel_id=1, source_target_pairs={{0,4},{4,0},{8,12},{12,8},{16,20},{20,16},{24,28},{28,24},{1,5},{5... | collective-permute-start | bytes 1736 | tf_op jit(solution)/shard_map/ppermute | solution.py:316
  22.7 26.0 %collective-permute-start.5 = (bf16[512,1024]{0,1:T(8,128)(2,1)S(1)}, bf16[512,1024]{0,1:T(8,128)(2,1)S(1)}, u32[]{:S(2)}, u32[]{:S(2)}) collective-permute-start(bf16[512,1024]{0,1:T(8,128)(2,1)S(1)} %get-tuple-element.143), channel_id=1, source_target_pairs={{0,2},{1,3},{2,0},{3,1},{4,6},{5,7},{6,4},{7,5},{8,10},{9,11},{10,... | collective-permute-start | bytes 3145736 | tf_op jit(solution)/shard_map/ppermute | solution.py:338
  44.8 25.0 %collective-permute-start.3 = (bf16[512,1024]{0,1:T(8,128)(2,1)}, bf16[512,1024]{0,1:T(8,128)(2,1)}, u32[]{:S(2)}, u32[]{:S(2)}) collective-permute-start(bf16[512,1024]{0,1:T(8,128)(2,1)} %get-tuple-element.145), channel_id=1, source_target_pairs={{0,2},{1,3},{2,0},{3,1},{4,6},{5,7},{6,4},{7,5},{8,10},{9,11},{10,... | collective-permute-start | bytes 3145736 | tf_op jit(solution)/shard_map/ppermute | solution.py:338
  50.4 31.4 %collective-permute-start.6 = (bf16[2,512,1024]{1,2,0:T(8,128)(2,1)}, bf16[2,512,1024]{1,2,0:T(8,128)(2,1)}, u32[]{:S(2)}, u32[]{:S(2)}) collective-permute-start(bf16[2,512,1024]{1,2,0:T(8,128)(2,1)} %pad_maximum_fusion.2), channel_id=1, source_target_pairs={{0,1},{1,0},{2,3},{3,2},{4,5},{5,4},{6,7},{7,6},{8,9},{9,8},{10,11... | collective-permute-start | bytes 6291464 | tf_op jit(solution)/shard_map/ppermute | solution.py:338
  51.4 557.5 %reduce-scatter.4.cloned.1.call-start = ((), (), s32[]{:S(2)}) async-start(), calls=%async_computation.3 | async-start | bytes 6488064
  73.1 13.4 %collective-permute-start.4 = (bf16[2,512,1024]{1,2,0:T(8,128)(2,1)}, bf16[2,512,1024]{1,2,0:T(8,128)(2,1)}, u32[]{:S(2)}, u32[]{:S(2)}) collective-permute-start(bf16[2,512,1024]{1,2,0:T(8,128)(2,1)} %pad_maximum_fusion.1), channel_id=1, source_target_pairs={{0,1},{1,0},{2,3},{3,2},{4,5},{5,4},{6,7},{7,6},{8,9},{9,8},{10,11... | collective-permute-start | bytes 6291464 | tf_op jit(solution)/shard_map/ppermute | solution.py:338
  111.4 71.4 %collective-permute-start.7 = (bf16[2,2,2048,128]{3,2,1,0:T(8,128)(2,1)}, bf16[2,2,2048,128]{3,2,1,0:T(8,128)(2,1)}, u32[]{:S(2)}, u32[]{:S(2)}) collective-permute-start(bf16[2,2,2048,128]{3,2,1,0:T(8,128)(2,1)} %pad_maximum_fusion.3), channel_id=1, source_target_pairs={{0,4},{4,0},{8,12},{12,8},{16,20},{20,16},{24,28},{28,24},{1,5},{5... | collective-permute-start | bytes 6291464 | tf_op jit(solution)/shard_map/ppermute | solution.py:236
  225.5 25.3 %collective-permute-start.9 = (bf16[512,1024]{0,1:T(8,128)(2,1)S(1)}, bf16[512,1024]{0,1:T(8,128)(2,1)S(1)}, u32[]{:S(2)}, u32[]{:S(2)}) collective-permute-start(bf16[512,1024]{0,1:T(8,128)(2,1)S(1)} %fusion.30), channel_id=1, source_target_pairs={{0,2},{1,3},{2,0},{3,1},{4,6},{5,7},{6,4},{7,5},{8,10},{9,11},{10,... | collective-permute-start | bytes 3145736 | tf_op jit(solution)/shard_map/ppermute | solution.py:338
  252.3 24.4 %collective-permute-start.10 = (bf16[512,1024]{0,1:T(8,128)(2,1)S(1)}, bf16[512,1024]{0,1:T(8,128)(2,1)S(1)}, u32[]{:S(2)}, u32[]{:S(2)}) collective-permute-start(bf16[512,1024]{0,1:T(8,128)(2,1)S(1)} %get-tuple-element.139), channel_id=1, source_target_pairs={{0,2},{1,3},{2,0},{3,1},{4,6},{5,7},{6,4},{7,5},{8,10},{9,11},{10,... | collective-permute-start | bytes 3145736 | tf_op jit(solution)/shard_map/ppermute | solution.py:338
  325.7 25.3 %collective-permute-start.13 = (bf16[512,1024]{0,1:T(8,128)(2,1)S(1)}, bf16[512,1024]{0,1:T(8,128)(2,1)S(1)}, u32[]{:S(2)}, u32[]{:S(2)}) collective-permute-start(bf16[512,1024]{0,1:T(8,128)(2,1)S(1)} %fusion.26), channel_id=1, source_target_pairs={{0,2},{1,3},{2,0},{3,1},{4,6},{5,7},{6,4},{7,5},{8,10},{9,11},{10,... | collective-permute-start | bytes 3145736 | tf_op jit(solution)/shard_map/ppermute | solution.py:338
  355.1 24.4 %collective-permute-start.14 = (bf16[512,1024]{0,1:T(8,128)(2,1)S(1)}, bf16[512,1024]{0,1:T(8,128)(2,1)S(1)}, u32[]{:S(2)}, u32[]{:S(2)}) collective-permute-start(bf16[512,1024]{0,1:T(8,128)(2,1)S(1)} %get-tuple-element.136), channel_id=1, source_target_pairs={{0,2},{1,3},{2,0},{3,1},{4,6},{5,7},{6,4},{7,5},{8,10},{9,11},{10,... | collective-permute-start | bytes 3145736 | tf_op jit(solution)/shard_map/ppermute | solution.py:338
  379.8 16.2 %collective-permute-start.15 = (bf16[2,512,1024]{1,2,0:T(8,128)(2,1)S(1)}, bf16[2,512,1024]{1,2,0:T(8,128)(2,1)S(1)}, u32[]{:S(2)}, u32[]{:S(2)}) collective-permute-start(bf16[2,512,1024]{1,2,0:T(8,128)(2,1)S(1)} %pad_maximum_fusion.7), channel_id=1, source_target_pairs={{0,1},{1,0},{2,3},{3,2},{4,5},{5,4},{6,7},{7,6},{8,9},{9,8},{10,11... | collective-permute-start | bytes 6291464 | tf_op jit(solution)/shard_map/ppermute | solution.py:338
  459.4 45.9 %collective-permute-start.17 = (bf16[512,1024]{0,1:T(8,128)(2,1)S(1)}, bf16[512,1024]{0,1:T(8,128)(2,1)}, u32[]{:S(2)}, u32[]{:S(2)}) collective-permute-start(bf16[512,1024]{0,1:T(8,128)(2,1)S(1)} %fusion.22), channel_id=1, source_target_pairs={{0,2},{1,3},{2,0},{3,1},{4,6},{5,7},{6,4},{7,5},{8,10},{9,11},{10,... | collective-permute-start | bytes 3145736 | tf_op jit(solution)/shard_map/ppermute | solution.py:338
  503.2 69.1 %collective-permute-start.18 = (bf16[2,2,2048,128]{3,2,1,0:T(8,128)(2,1)S(1)}, bf16[2,2,2048,128]{3,2,1,0:T(8,128)(2,1)}, u32[]{:S(2)}, u32[]{:S(2)}) collective-permute-start(bf16[2,2,2048,128]{3,2,1,0:T(8,128)(2,1)S(1)} %fusion.5), channel_id=1, source_target_pairs={{0,4},{4,0},{8,12},{12,8},{16,20},{20,16},{24,28},{28,24},{1,5},{5... | collective-permute-start | bytes 6291464 | tf_op jit(solution)/shard_map/ppermute | solution.py:236
  593.5 13.6 %collective-permute-start.24 = (bf16[512,512]{0,1:T(8,128)(2,1)S(1)}, bf16[512,512]{0,1:T(8,128)(2,1)S(1)}, u32[]{:S(2)}, u32[]{:S(2)}) collective-permute-start(bf16[512,512]{0,1:T(8,128)(2,1)S(1)} %dynamic-slice_convert_fusion.8), channel_id=1, source_target_pairs={{0,4},{4,0},{8,12},{12,8},{16,20},{20,16},{24,28},{28,24},{1,5},{5... | collective-permute-start | bytes 1572872 | tf_op jit(solution)/shard_map/ppermute | solution.py:304
  608.1 44.4 %collective-permute-start.25 = (bf16[256,512]{0,1:T(8,128)(2,1)}, bf16[256,512]{0,1:T(8,128)(2,1)}, u32[]{:S(2)}, u32[]{:S(2)}) collective-permute-start(bf16[256,512]{0,1:T(8,128)(2,1)} %dynamic-slice_convert_fusion.10), channel_id=1, source_target_pairs={{0,8},{4,12},{8,0},{12,4},{16,24},{20,28},{24,16},{28,20},{1,9},{5... | collective-permute-start | bytes 786440 | tf_op jit(solution)/shard_map/ppermute | solution.py:304
  640.1 8.0 %collective-permute-start.19 = (bf16[2,512,1024]{1,2,0:T(8,128)(2,1)S(1)}, bf16[2,512,1024]{1,2,0:T(8,128)(2,1)S(1)}, u32[]{:S(2)}, u32[]{:S(2)}) collective-permute-start(bf16[2,512,1024]{1,2,0:T(8,128)(2,1)S(1)} %pad_maximum_fusion.9), channel_id=1, source_target_pairs={{0,1},{1,0},{2,3},{3,2},{4,5},{5,4},{6,7},{7,6},{8,9},{9,8},{10,11... | collective-permute-start | bytes 6291464 | tf_op jit(solution)/shard_map/ppermute | solution.py:338
  647.4 12.3 %collective-permute-start.21 = (bf16[512,512]{1,0:T(8,128)(2,1)S(1)}, bf16[512,512]{1,0:T(8,128)(2,1)S(1)}, u32[]{:S(2)}, u32[]{:S(2)}) collective-permute-start(bf16[512,512]{1,0:T(8,128)(2,1)S(1)} %dynamic-slice_convert_fusion.9), channel_id=1, source_target_pairs={{0,4},{4,0},{8,12},{12,8},{16,20},{20,16},{24,28},{28,24},{1,5},{5... | collective-permute-start | bytes 1572872 | tf_op jit(solution)/shard_map/ppermute | solution.py:304
  651.0 23.5 %collective-permute-start.20 = (bf16[512,1024]{0,1:T(8,128)(2,1)}, bf16[512,1024]{0,1:T(8,128)(2,1)}, u32[]{:S(2)}, u32[]{:S(2)}) collective-permute-start(bf16[512,1024]{0,1:T(8,128)(2,1)} %fusion.18), channel_id=1, source_target_pairs={{0,2},{1,3},{2,0},{3,1},{4,6},{5,7},{6,4},{7,5},{8,10},{9,11},{10,... | collective-permute-start | bytes 3145736 | tf_op jit(solution)/shard_map/ppermute | solution.py:338
  680.6 13.0 %collective-permute-start.23 = (bf16[128,512]{1,0:T(8,128)(2,1)}, bf16[128,512]{1,0:T(8,128)(2,1)}, u32[]{:S(2)}, u32[]{:S(2)}) collective-permute-start(bf16[128,512]{1,0:T(8,128)(2,1)} %dynamic-slice_convert_fusion.13), channel_id=1, source_target_pairs={{0,16},{4,20},{8,24},{12,28},{16,0},{20,4},{24,8},{28,12},{1,17},{... | collective-permute-start | bytes 393224 | tf_op jit(solution)/shard_map/ppermute | solution.py:304
  683.0 8.4 %collective-permute-start.28 = (f32[2304]{0:T(1024)}, f32[2304]{0:T(1024)}, u32[]{:S(2)}, u32[]{:S(2)}) collective-permute-start(f32[2304]{0:T(1024)} %fusion.116), channel_id=1, source_target_pairs={{0,2},{1,3},{2,0},{3,1},{4,6},{5,7},{6,4},{7,5},{8,10},{9,11},{10,... | collective-permute-start | bytes 27656 | tf_op jit(solution)/shard_map/ppermute | solution.py:329
  699.5 9.4 %collective-permute-start.31 = (f32[2304]{0:T(1024)S(1)}, f32[2304]{0:T(1024)S(1)}, u32[]{:S(2)}, u32[]{:S(2)}) collective-permute-start(f32[2304]{0:T(1024)S(1)} %add.331), channel_id=1, source_target_pairs={{0,16},{4,20},{8,24},{12,28},{16,0},{20,4},{24,8},{28,12},{1,17},{... | collective-permute-start | bytes 27656 | tf_op jit(solution)/shard_map/ppermute | solution.py:329
  (116 other events, 1944.4 us)
Sparse Core Ops, SparseCore 0:
  11.0 52.0 all-gather.2
  65.1 113.9 all-gather.4
  449.5 130.2 reduce-scatter.3

commit v8 on v7

--- a/solution.py
+++ b/solution.py
@@ -306,6 +306,23 @@
         )
         buf = keep + got.astype(jnp.float32)
     return split_columns(buf, widths)
+
+
+def doubling_gather(values):
+    count = lax.axis_size("fsdp")
+    me = lax.axis_index("fsdp")
+    rows_f = values.shape[0]
+    full = jnp.zeros((count,) + values.shape, values.dtype)
+    full = lax.dynamic_update_slice_in_dim(full, values[None], me, 0)
+    bit = count // 2
+    while bit >= 1:
+        view = full.reshape((count // (2 * bit), 2 * bit) + values.shape)
+        held = lax.dynamic_index_in_dim(view, me % (2 * bit), 1, keepdims=True)
+        got = lax.ppermute(held, "fsdp", [(i, i ^ bit) for i in range(count)])
+        view = lax.dynamic_update_slice_in_dim(view, got, (me ^ bit) % (2 * bit), 1)
+        full = view.reshape(full.shape)
+        bit //= 2
+    return full.reshape((count * rows_f,) + values.shape[1:])
 
 
 def fsdp_gather(values):
@@ -407,7 +424,7 @@
     gain_in, gain_query, gain_keys, gain_post = [
         part.reshape(-1) for part in split_columns(gains_all, gain_sizes)
     ]
-    attn_full = lax.all_gather(
+    attn_full = doubling_gather(
         jnp.concatenate(
             [
                 q_weight.astype(jnp.bfloat16),
@@ -415,10 +432,7 @@
                 value_matrix.astype(jnp.bfloat16),
             ],
             axis=1,
-        ),
-        "fsdp",
-        axis=0,
-        tiled=True,
+        )
     )
     widths = (q_weight.shape[1], key_matrix.shape[1], value_matrix.shape[1])
     w_query, w_key, w_value = split_columns(attn_full, widths)

time: 725 us -> 744 us (1.026)
  starting transfers between devices: 32.6 us -> 54 us
  local copies, waits for them, and re-layouts: 119 us -> 136 us
  waiting for transfers between devices: 192 us -> 178 us
    ppermute x0 -> x3, waiting for transfers between devices: none -> 33.8 us  [doubling_gather(): got = lax.ppermute(held, 'fsdp', [(i, i ^ bit) for i in range(count)])]
    ppermute x16, waiting for transfers between devices: 139 us -> 109 us  [exchange(): lax.ppermute(values, 'tensor', [(i, i ^ distance) for i in range(count)])]
    ppermute x6, starting transfers between devices: 7 us -> 25.7 us  [halving_scatter(): lax.ppermute(send.astype(jnp.bfloat16), 'fsdp', [(i, i ^ 1 << bit) for i...]
    ppermute x2, waiting for transfers between devices: 33.8 us -> 17.8 us  [swapped(): lax.ppermute(shard, axis, [(i, i ^ 1 << distance) for i in range(lax.axis...]
    unnamed x232 -> x238, local copies, waits for them, and re-layouts: 49.5 us -> 53.7 us
  transfers between devices with their start and end apart: 35 -> 37, of which waited for: 20 -> 19; matrix products, arithmetic and copies ran while one was open for 30% -> 30% of each run, Pallas kernels for 19% -> 18%
where the time goes in v8:
time: 744 us; the launch traced here: 737 us
  waiting for transfers between devices  178 us (24%)
  local copies, waits for them, and re-layouts  136 us (18%)
  Pallas kernels  135 us (18%)
  other arithmetic  115 us (15%)
  matrix products  102 us (14%)
  starting transfers between devices  54 us (7%)
  between operations  16.4 us (2%)
    ppermute x16, waiting for transfers between devices, exchange(): lax.ppermute(values, 'tensor', [(i, i ^ distance) for i in range(count)])  109 us
    pallas_call x2, Pallas kernels, attention_backward(): pl.pallas_call(functools.partial(_bwd_kernel, scale=scale, block=block),...  83.8 us
    unnamed x238, local copies, waits for them, and re-layouts  53.7 us
    pallas_call x2, Pallas kernels, attention_forward(): pl.pallas_call(functools.partial(_fwd_kernel, scale=scale, block=block),...  51.7 us
    ppermute x3, waiting for transfers between devices, doubling_gather(): got = lax.ppermute(held, 'fsdp', [(i, i ^ bit) for i in range(count)])  33.8 us
    dot_general x7, matrix products, contract_last(): lax.dot_general(left, right, (((1,), (1,)), ((), ())), preferred_element_...  31.8 us
    dot_general x7, matrix products, contract_rows(): lax.dot_general(left, right, (((0,), (0,)), ((), ())), preferred_element_...  30.5 us
    ppermute x6, starting transfers between devices, halving_scatter(): lax.ppermute(send.astype(jnp.bfloat16), 'fsdp', [(i, i ^ 1 << bit) for i...  25.7 us
  transfers between devices with their start and end apart: 37, of which 19 were waited for; matrix products, arithmetic and copies ran while one was open for 30% of the time, Pallas kernels for 18%

profile of v8, /device:TPU:0, one launch (start us, length us, event | category | flops | bytes accessed | tf_op | source)
XLA Modules:
  0.0 737.3 jit_solution(8744467730153450739)
XLA Ops:
  53.7 15.3 %collective-permute-done.8 = bf16[2,1,128,1024]{3,2,1,0:T(8,128)(2,1)} collective-permute-done((bf16[2,1,128,1024]{3,2,1,0:T(8,128)(2,1)}, bf16[2,1,128,1024]{3,2,1,0:T(8,128)(2,1)}, u32[]{:S(2)}, u32[]{:S(2)}) %collective-permute-start.8) | collective-permute-done | bytes 524320 | tf_op jit(solution)/shard_map/ppermute | solution.py:321
  87.5 18.5 %collective-permute-done.9 = bf16[4,1,128,1024]{3,2,1,0:T(8,128)(2,1)} collective-permute-done((bf16[4,1,128,1024]{3,2,1,0:T(8,128)(2,1)}, bf16[4,1,128,1024]{3,2,1,0:T(8,128)(2,1)}, u32[]{:S(2)}, u32[]{:S(2)}) %collective-permute-start.9) | collective-permute-done | bytes 1048608 | tf_op jit(solution)/shard_map/ppermute | solution.py:321
  163.1 28.8 %attn_fwd.2 = (f32[2,2,2048,128]{3,2,1,0:T(8,128)}, f32[2,2,2048,128]{3,2,1,0:T(8,128)}) custom-call(s32[7,10]{1,0:T(8,128)S(1)} %broadcast_select_fusion.3.tab_ref, bf16[2,2,2048,128]{3,2,1,0:T(8,128)(2,1)S(1)} %maximum_bitcast_fusion.q_ref, s32[2048,128]{1,0:T(8,128)S(1)} %broadcast_in_dim.45.qs_ref, ...), custom_call_target="tpu_custom_call", output_to_operand_aliasing={{0}: (5, {}), {1}: (6, {})} | custom-call | flops 5368709120 | bytes 20971520 | tf_op jit(solution)/shard_map/attn_fwd/pallas_call | solution.py:124
  193.6 22.9 %attn_fwd.3 = (f32[2,2,2048,128]{3,2,1,0:T(8,128)}, f32[2,2,2048,128]{3,2,1,0:T(8,128)}) custom-call(s32[7,8]{1,0:T(8,128)S(1)} %broadcast_select_fusion.7.tab_ref, bf16[2,2,2048,128]{3,2,1,0:T(8,128)(2,1)S(1)} %maximum_bitcast_fusion.q_ref, s32[2048,128]{1,0:T(8,128)S(1)} %broadcast_in_dim.45.qs_ref, ...), custom_call_target="tpu_custom_call", output_to_operand_aliasing={{0}: (5, {}), {1}: (6, {})} | custom-call | flops 4294967296 | bytes 16777216 | tf_op jit(solution)/shard_map/attn_fwd/pallas_call | solution.py:124
  236.4 23.5 %collective-permute-done.12 = bf16[512,1024]{0,1:T(8,128)(2,1)S(1)} collective-permute-done((bf16[512,1024]{0,1:T(8,128)(2,1)S(1)}, bf16[512,1024]{0,1:T(8,128)(2,1)S(1)}, u32[]{:S(2)}, u32[]{:S(2)}) %collective-permute-start.12) | collective-permute-done | bytes 1048608 | tf_op jit(solution)/shard_map/ppermute | solution.py:355
  263.3 22.7 %collective-permute-done.13 = bf16[512,1024]{0,1:T(8,128)(2,1)S(1)} collective-permute-done((bf16[512,1024]{0,1:T(8,128)(2,1)S(1)}, bf16[512,1024]{0,1:T(8,128)(2,1)S(1)}, u32[]{:S(2)}, u32[]{:S(2)}) %collective-permute-start.13) | collective-permute-done | bytes 1048608 | tf_op jit(solution)/shard_map/ppermute | solution.py:355
  294.5 5.4 fusion.46
  299.9 13.1 %multiply_convert_fusion = (bf16[2048,768]{1,0:T(8,128)(2,1)}, bf16[2048,768]{1,0:T(8,128)(2,1)}, bf16[2048,768]{1,0:T(8,128)(2,1)}) fusion(f32[2048,768]{1,0:T(8,128)} %fusion.46, f32[2048,768]{1,0:T(8,128)S(1)} %fusion.42, bf16[2048,1024]{0,1:T(8,128)(2,1)} %fusion.61, bf16[1024,2816]{0,1:T(8,128)(2,1)S(1)} %bitcast.267), kind=kOutput, calls=%fused_computation.6 | convolution fusion | flops 3246391296 | bytes 27787264 | tf_op jit(solution)/shard_map/dot_general | solution.py:507
  313.0 7.9 %fusion.44 = f32[2048,1024]{0,1:T(8,128)} fusion(bf16[2048,768]{1,0:T(8,128)(2,1)} %get-tuple-element.147, bf16[1024,2816]{0,1:T(8,128)(2,1)S(1)} %bitcast.267), kind=kOutput, calls=%fused_computation.139 | convolution fusion | flops 3221225472 | bytes 13107200 | tf_op jit(solution)/shard_map/dot_general | solution.py:276
  320.8 6.2 convolution_add_fusion
  334.5 23.5 %collective-permute-done.16 = bf16[512,1024]{0,1:T(8,128)(2,1)S(1)} collective-permute-done((bf16[512,1024]{0,1:T(8,128)(2,1)S(1)}, bf16[512,1024]{0,1:T(8,128)(2,1)S(1)}, u32[]{:S(2)}, u32[]{:S(2)}) %collective-permute-start.16) | collective-permute-done | bytes 1048608 | tf_op jit(solution)/shard_map/ppermute | solution.py:355
  363.9 22.7 %collective-permute-done.17 = bf16[512,1024]{0,1:T(8,128)(2,1)S(1)} collective-permute-done((bf16[512,1024]{0,1:T(8,128)(2,1)S(1)}, bf16[512,1024]{0,1:T(8,128)(2,1)S(1)}, u32[]{:S(2)}, u32[]{:S(2)}) %collective-permute-start.17) | collective-permute-done | bytes 1048608 | tf_op jit(solution)/shard_map/ppermute | solution.py:355
  397.8 6.8 convolution_convert_fusion.2
  415.4 7.2 fusion.6
  422.7 16.2 %pad_maximum_fusion = bf16[1024,2816]{0,1:T(8,128)(2,1)} fusion(bf16[1024,512]{0,1:T(8,128)(2,1)S(1)} %convolution_convert_fusion.5, bf16[1024,768]{0,1:T(8,128)(2,1)S(1)} %copy-done.45, bf16[1024,768]{0,1:T(8,128)(2,1)S(1)} %copy-done.44, bf16[1024,768]{0,1:T(8,128)(2,1)S(1)} %copy-done.43), kind=kLoop, calls=%fused_computation.10 | loop fusion | flops 23068672 | bytes 11534336 | tf_op jit(solution)/shard_map/concatenate | solution.py:529
  441.6 5.0 fusion.37
  450.1 8.3 %copy.205 = bf16[1024,2816]{1,0:T(8,128)(2,1)} copy(bf16[1024,2816]{0,1:T(8,128)(2,1)} %pad_maximum_fusion) | data formatting | bytes 11534336
  472.4 38.1 %attn_bwd.2 = (f32[2,2,2048,128]{3,2,1,0:T(8,128)}, f32[2,2048,128]{2,1,0:T(8,128)}, f32[2,2048,128]{2,1,0:T(8,128)}) custom-call(s32[7,8]{1,0:T(8,128)} %broadcast_select_fusion.6.tab_ref, bf16[2,2,2048,128]{3,2,1,0:T(8,128)(2,1)} %copy-done.1, bf16[2,2,2048,128]{3,2,1,0:T(8,128)(2,1)} %get-tuple-element.45.h_ref, ...), custom_call_target="tpu_custom_call", output_to_operand_aliasing={{0}: (7, {})} | custom-call | flops 10737418240 | bytes 20971520 | tf_op jit(solution)/shard_map/attn_bwd/pallas_call | solution.py:207
  519.9 45.8 %attn_bwd.3 = (f32[2,2,2048,128]{3,2,1,0:T(8,128)}, f32[2,2048,128]{2,1,0:T(8,128)}, f32[2,2048,128]{2,1,0:T(8,128)}) custom-call(s32[7,10]{1,0:T(8,128)} %broadcast_select_fusion.2.tab_ref, bf16[2,2,2048,128]{3,2,1,0:T(8,128)(2,1)} %copy-done.1, bf16[2,2,2048,128]{3,2,1,0:T(8,128)(2,1)} %get-tuple-element.45.h_ref, ...), custom_call_target="tpu_custom_call", output_to_operand_aliasing={{0}: (7, {})} | custom-call | flops 13421772800 | bytes 26214400 | tf_op jit(solution)/shard_map/attn_bwd/pallas_call | solution.py:207
  565.7 17.8 %collective-permute-done.21 = bf16[2,2,2048,128]{3,2,1,0:T(8,128)(2,1)} collective-permute-done((bf16[2,2,2048,128]{3,2,1,0:T(8,128)(2,1)S(1)}, bf16[2,2,2048,128]{3,2,1,0:T(8,128)(2,1)}, u32[]{:S(2)}, u32[]{:S(2)}) %collective-permute-start.21) | collective-permute-done | bytes 2097184 | tf_op jit(solution)/shard_map/ppermute | solution.py:236
  610.6 5.3 collective-permute-done.27
  665.3 11.0 %collective-permute-start.29 = (bf16[128,512]{0,1:T(8,128)(2,1)}, bf16[128,512]{0,1:T(8,128)(2,1)}, u32[]{:S(2)}, u32[]{:S(2)}) collective-permute-start(bf16[128,512]{0,1:T(8,128)(2,1)} %dynamic-slice_convert_fusion.12), channel_id=1, source_target_pairs={{0,16},{4,20},{8,24},{12,28},{16,0},{20,4},{24,8},{28,12},{1,17},{... | collective-permute-start | bytes 393224 | tf_op jit(solution)/shard_map/ppermute | solution.py:304
  686.3 5.2 fusion.10
  692.3 10.4 %collective-permute-start.26 = (bf16[128,512]{1,0:T(8,128)(2,1)}, bf16[128,512]{1,0:T(8,128)(2,1)}, u32[]{:S(2)}, u32[]{:S(2)}) collective-permute-start(bf16[128,512]{1,0:T(8,128)(2,1)} %dynamic-slice_convert_fusion.13), channel_id=1, source_target_pairs={{0,16},{4,20},{8,24},{12,28},{16,0},{20,4},{24,8},{28,12},{1,17},{... | collective-permute-start | bytes 393224 | tf_op jit(solution)/shard_map/ppermute | solution.py:304
  (490 shorter events, 333.6 us)
Async XLA Ops:
  7.2 217.4 %all-gather.2.cloned.1.call-start = ((), (), s32[]{:S(2)}) async-start(), calls=%async_computation.1 | async-start | bytes 6488064 | tf_op jit(solution)/shard_map/all_gather | solution.py:479
  15.7 35.0 %collective-permute-start.5 = (bf16[512,1024]{0,1:T(8,128)(2,1)}, bf16[512,1024]{0,1:T(8,128)(2,1)}, u32[]{:S(2)}, u32[]{:S(2)}) collective-permute-start(bf16[512,1024]{0,1:T(8,128)(2,1)} %get-tuple-element.143), channel_id=1, source_target_pairs={{0,2},{1,3},{2,0},{3,1},{4,6},{5,7},{6,4},{7,5},{8,10},{9,11},{10,... | collective-permute-start | bytes 3145736 | tf_op jit(solution)/shard_map/ppermute | solution.py:355
  21.5 25.1 %collective-permute-start.7 = (bf16[1,1,128,1024]{3,2,1,0:T(8,128)(2,1)}, bf16[1,1,128,1024]{3,2,1,0:T(8,128)(2,1)}, u32[]{:S(2)}, u32[]{:S(2)}) collective-permute-start(bf16[1,1,128,1024]{3,2,1,0:T(8,128)(2,1)} %constant_dynamic-slice_fusion.2), channel_id=1, source_target_pairs={{0,16},{4,20},{8,24},{12,28},{16,0},{20,4},{24,8},{28,12},{1,17},{... | collective-permute-start | bytes 786440 | tf_op jit(solution)/shard_map/ppermute | solution.py:321
  45.1 25.0 %collective-permute-start.3 = (bf16[512,1024]{0,1:T(8,128)(2,1)}, bf16[512,1024]{0,1:T(8,128)(2,1)}, u32[]{:S(2)}, u32[]{:S(2)}) collective-permute-start(bf16[512,1024]{0,1:T(8,128)(2,1)} %get-tuple-element.145), channel_id=1, source_target_pairs={{0,2},{1,3},{2,0},{3,1},{4,6},{5,7},{6,4},{7,5},{8,10},{9,11},{10,... | collective-permute-start | bytes 3145736 | tf_op jit(solution)/shard_map/ppermute | solution.py:355
  46.5 572.4 %reduce-scatter.4.cloned.1.call-start = ((), (), s32[]{:S(2)}) async-start(), calls=%async_computation.2 | async-start | bytes 6488064
  48.4 20.6 %collective-permute-start.8 = (bf16[2,1,128,1024]{3,2,1,0:T(8,128)(2,1)}, bf16[2,1,128,1024]{3,2,1,0:T(8,128)(2,1)}, u32[]{:S(2)}, u32[]{:S(2)}) collective-permute-start(bf16[2,1,128,1024]{3,2,1,0:T(8,128)(2,1)} %constant_dynamic-slice_fusion.1), channel_id=1, source_target_pairs={{0,8},{4,12},{8,0},{12,4},{16,24},{20,28},{24,16},{28,20},{1,9},{5... | collective-permute-start | bytes 1572872 | tf_op jit(solution)/shard_map/ppermute | solution.py:321
  53.7 53.7 %collective-permute-start.6 = (bf16[2,512,1024]{1,2,0:T(8,128)(2,1)}, bf16[2,512,1024]{1,2,0:T(8,128)(2,1)}, u32[]{:S(2)}, u32[]{:S(2)}) collective-permute-start(bf16[2,512,1024]{1,2,0:T(8,128)(2,1)} %pad_maximum_fusion.2), channel_id=1, source_target_pairs={{0,1},{1,0},{2,3},{3,2},{4,5},{5,4},{6,7},{7,6},{8,9},{9,8},{10,11... | collective-permute-start | bytes 6291464 | tf_op jit(solution)/shard_map/ppermute | solution.py:355
  73.2 39.7 %collective-permute-start.4 = (bf16[2,512,1024]{1,2,0:T(8,128)(2,1)}, bf16[2,512,1024]{1,2,0:T(8,128)(2,1)}, u32[]{:S(2)}, u32[]{:S(2)}) collective-permute-start(bf16[2,512,1024]{1,2,0:T(8,128)(2,1)} %pad_maximum_fusion.1), channel_id=1, source_target_pairs={{0,1},{1,0},{2,3},{3,2},{4,5},{5,4},{6,7},{7,6},{8,9},{9,8},{10,11... | collective-permute-start | bytes 6291464 | tf_op jit(solution)/shard_map/ppermute | solution.py:355
  74.2 31.8 %collective-permute-start.9 = (bf16[4,1,128,1024]{3,2,1,0:T(8,128)(2,1)}, bf16[4,1,128,1024]{3,2,1,0:T(8,128)(2,1)}, u32[]{:S(2)}, u32[]{:S(2)}) collective-permute-start(bf16[4,1,128,1024]{3,2,1,0:T(8,128)(2,1)} %constant_dynamic-slice_fusion), channel_id=1, source_target_pairs={{0,4},{4,0},{8,12},{12,8},{16,20},{20,16},{24,28},{28,24},{1,5},{5... | collective-permute-start | bytes 3145736 | tf_op jit(solution)/shard_map/ppermute | solution.py:321
  137.4 54.4 %collective-permute-start.10 = (bf16[2,2,2048,128]{3,2,1,0:T(8,128)(2,1)}, bf16[2,2,2048,128]{3,2,1,0:T(8,128)(2,1)}, u32[]{:S(2)}, u32[]{:S(2)}) collective-permute-start(bf16[2,2,2048,128]{3,2,1,0:T(8,128)(2,1)} %pad_maximum_fusion.3), channel_id=1, source_target_pairs={{0,4},{4,0},{8,12},{12,8},{16,20},{20,16},{24,28},{28,24},{1,5},{5... | collective-permute-start | bytes 6291464 | tf_op jit(solution)/shard_map/ppermute | solution.py:236
  234.7 25.3 %collective-permute-start.12 = (bf16[512,1024]{0,1:T(8,128)(2,1)S(1)}, bf16[512,1024]{0,1:T(8,128)(2,1)S(1)}, u32[]{:S(2)}, u32[]{:S(2)}) collective-permute-start(bf16[512,1024]{0,1:T(8,128)(2,1)S(1)} %fusion.30), channel_id=1, source_target_pairs={{0,2},{1,3},{2,0},{3,1},{4,6},{5,7},{6,4},{7,5},{8,10},{9,11},{10,... | collective-permute-start | bytes 3145736 | tf_op jit(solution)/shard_map/ppermute | solution.py:355
  261.6 24.4 %collective-permute-start.13 = (bf16[512,1024]{0,1:T(8,128)(2,1)S(1)}, bf16[512,1024]{0,1:T(8,128)(2,1)S(1)}, u32[]{:S(2)}, u32[]{:S(2)}) collective-permute-start(bf16[512,1024]{0,1:T(8,128)(2,1)S(1)} %get-tuple-element.139), channel_id=1, source_target_pairs={{0,2},{1,3},{2,0},{3,1},{4,6},{5,7},{6,4},{7,5},{8,10},{9,11},{10,... | collective-permute-start | bytes 3145736 | tf_op jit(solution)/shard_map/ppermute | solution.py:355
  332.8 25.3 %collective-permute-start.16 = (bf16[512,1024]{0,1:T(8,128)(2,1)S(1)}, bf16[512,1024]{0,1:T(8,128)(2,1)S(1)}, u32[]{:S(2)}, u32[]{:S(2)}) collective-permute-start(bf16[512,1024]{0,1:T(8,128)(2,1)S(1)} %fusion.26), channel_id=1, source_target_pairs={{0,2},{1,3},{2,0},{3,1},{4,6},{5,7},{6,4},{7,5},{8,10},{9,11},{10,... | collective-permute-start | bytes 3145736 | tf_op jit(solution)/shard_map/ppermute | solution.py:355
  362.1 24.4 %collective-permute-start.17 = (bf16[512,1024]{0,1:T(8,128)(2,1)S(1)}, bf16[512,1024]{0,1:T(8,128)(2,1)S(1)}, u32[]{:S(2)}, u32[]{:S(2)}) collective-permute-start(bf16[512,1024]{0,1:T(8,128)(2,1)S(1)} %get-tuple-element.136), channel_id=1, source_target_pairs={{0,2},{1,3},{2,0},{3,1},{4,6},{5,7},{6,4},{7,5},{8,10},{9,11},{10,... | collective-permute-start | bytes 3145736 | tf_op jit(solution)/shard_map/ppermute | solution.py:355
  386.7 18.0 %collective-permute-start.18 = (bf16[2,512,1024]{1,2,0:T(8,128)(2,1)S(1)}, bf16[2,512,1024]{1,2,0:T(8,128)(2,1)S(1)}, u32[]{:S(2)}, u32[]{:S(2)}) collective-permute-start(bf16[2,512,1024]{1,2,0:T(8,128)(2,1)S(1)} %pad_maximum_fusion.7), channel_id=1, source_target_pairs={{0,1},{1,0},{2,3},{3,2},{4,5},{5,4},{6,7},{7,6},{8,9},{9,8},{10,11... | collective-permute-start | bytes 6291464 | tf_op jit(solution)/shard_map/ppermute | solution.py:355
  468.5 46.9 %collective-permute-start.20 = (bf16[512,1024]{0,1:T(8,128)(2,1)S(1)}, bf16[512,1024]{0,1:T(8,128)(2,1)}, u32[]{:S(2)}, u32[]{:S(2)}) collective-permute-start(bf16[512,1024]{0,1:T(8,128)(2,1)S(1)} %fusion.22), channel_id=1, source_target_pairs={{0,2},{1,3},{2,0},{3,1},{4,6},{5,7},{6,4},{7,5},{8,10},{9,11},{10,... | collective-permute-start | bytes 3145736 | tf_op jit(solution)/shard_map/ppermute | solution.py:355
  513.1 70.4 %collective-permute-start.21 = (bf16[2,2,2048,128]{3,2,1,0:T(8,128)(2,1)S(1)}, bf16[2,2,2048,128]{3,2,1,0:T(8,128)(2,1)}, u32[]{:S(2)}, u32[]{:S(2)}) collective-permute-start(bf16[2,2,2048,128]{3,2,1,0:T(8,128)(2,1)S(1)} %fusion.5), channel_id=1, source_target_pairs={{0,4},{4,0},{8,12},{12,8},{16,20},{20,16},{24,28},{28,24},{1,5},{5... | collective-permute-start | bytes 6291464 | tf_op jit(solution)/shard_map/ppermute | solution.py:236
  604.3 11.6 %collective-permute-start.27 = (bf16[512,512]{0,1:T(8,128)(2,1)}, bf16[512,512]{0,1:T(8,128)(2,1)}, u32[]{:S(2)}, u32[]{:S(2)}) collective-permute-start(bf16[512,512]{0,1:T(8,128)(2,1)} %dynamic-slice_convert_fusion.8), channel_id=1, source_target_pairs={{0,4},{4,0},{8,12},{12,8},{16,20},{20,16},{24,28},{28,24},{1,5},{5... | collective-permute-start | bytes 1572872 | tf_op jit(solution)/shard_map/ppermute | solution.py:304
  618.8 44.8 %collective-permute-start.28 = (bf16[256,512]{0,1:T(8,128)(2,1)}, bf16[256,512]{0,1:T(8,128)(2,1)}, u32[]{:S(2)}, u32[]{:S(2)}) collective-permute-start(bf16[256,512]{0,1:T(8,128)(2,1)} %dynamic-slice_convert_fusion.10), channel_id=1, source_target_pairs={{0,8},{4,12},{8,0},{12,4},{16,24},{20,28},{24,16},{28,20},{1,9},{5... | collective-permute-start | bytes 786440 | tf_op jit(solution)/shard_map/ppermute | solution.py:304
  658.8 17.6 %collective-permute-start.24 = (bf16[512,512]{1,0:T(8,128)(2,1)S(1)}, bf16[512,512]{1,0:T(8,128)(2,1)S(1)}, u32[]{:S(2)}, u32[]{:S(2)}) collective-permute-start(bf16[512,512]{1,0:T(8,128)(2,1)S(1)} %dynamic-slice_convert_fusion.9), channel_id=1, source_target_pairs={{0,4},{4,0},{8,12},{12,8},{16,20},{20,16},{24,28},{28,24},{1,5},{5... | collective-permute-start | bytes 1572872 | tf_op jit(solution)/shard_map/ppermute | solution.py:304
  663.6 22.7 %collective-permute-start.23 = (bf16[512,1024]{0,1:T(8,128)(2,1)}, bf16[512,1024]{0,1:T(8,128)(2,1)}, u32[]{:S(2)}, u32[]{:S(2)}) collective-permute-start(bf16[512,1024]{0,1:T(8,128)(2,1)} %fusion.18), channel_id=1, source_target_pairs={{0,2},{1,3},{2,0},{3,1},{4,6},{5,7},{6,4},{7,5},{8,10},{9,11},{10,... | collective-permute-start | bytes 3145736 | tf_op jit(solution)/shard_map/ppermute | solution.py:355
  665.3 15.8 %collective-permute-start.29 = (bf16[128,512]{0,1:T(8,128)(2,1)}, bf16[128,512]{0,1:T(8,128)(2,1)}, u32[]{:S(2)}, u32[]{:S(2)}) collective-permute-start(bf16[128,512]{0,1:T(8,128)(2,1)} %dynamic-slice_convert_fusion.12), channel_id=1, source_target_pairs={{0,16},{4,20},{8,24},{12,28},{16,0},{20,4},{24,8},{28,12},{1,17},{... | collective-permute-start | bytes 393224 | tf_op jit(solution)/shard_map/ppermute | solution.py:304
  691.5 11.1 %collective-permute-start.30 = (f32[2304]{0:T(1024)S(1)}, f32[2304]{0:T(1024)S(1)}, u32[]{:S(2)}, u32[]{:S(2)}) collective-permute-start(f32[2304]{0:T(1024)S(1)} %pad_maximum_fusion.13), channel_id=1, source_target_pairs={{0,1},{1,0},{2,3},{3,2},{4,5},{5,4},{6,7},{7,6},{8,9},{9,8},{10,11... | collective-permute-start | bytes 27656 | tf_op jit(solution)/shard_map/ppermute | solution.py:346
  692.3 21.7 %collective-permute-start.26 = (bf16[128,512]{1,0:T(8,128)(2,1)}, bf16[128,512]{1,0:T(8,128)(2,1)}, u32[]{:S(2)}, u32[]{:S(2)}) collective-permute-start(bf16[128,512]{1,0:T(8,128)(2,1)} %dynamic-slice_convert_fusion.13), channel_id=1, source_target_pairs={{0,16},{4,20},{8,24},{12,28},{16,0},{20,4},{24,8},{28,12},{1,17},{... | collective-permute-start | bytes 393224 | tf_op jit(solution)/shard_map/ppermute | solution.py:304
  (121 other events, 2046.3 us)
Sparse Core Ops, SparseCore 0:
  46.6 106.2 all-gather.1
  458.6 140.0 reduce-scatter.3

commit v9 on v7

--- a/solution.py
+++ b/solution.py
@@ -479,35 +479,39 @@
     w_gate, w_up, w_down_t, w_out = split_columns(
         mlp_full, (gate_weight.shape[1], up_weight.shape[1], down_weight.shape[0], o_weight.shape[0])
     )
-
-    def out_term(start, count):
-        return contract_last(out_rows, w_out)
-
-    after_attn = x_float + token_sum(out_term, rows)
+    out_partial = contract_last(out_rows, w_out)
+    late_grad_all, out_partial = lax.optimization_barrier((mlp_grad_all, out_partial))
+    grad_act = jnp.dot(late_grad_all, w_down_t, preferred_element_type=jnp.float32)
+    after_attn = x_float + token_sum(lambda start, count: out_partial, rows)
+    grad_act, after_attn = lax.optimization_barrier((grad_act, after_attn))
     gain_second = gain_post.astype(jnp.float32)
     second_all = token_gather(rms_scale(after_attn, gain_second).astype(jnp.bfloat16))
     gate_out = jnp.dot(second_all, w_gate, preferred_element_type=jnp.float32)
     up_out = jnp.dot(second_all, w_up, preferred_element_type=jnp.float32)
     activated = (jax.nn.silu(gate_out) * up_out).astype(jnp.bfloat16)
 
-    grad_act = jnp.dot(mlp_grad_all, w_down_t, preferred_element_type=jnp.float32)
     unused, pull_gate = jax.vjp(
         lambda gate_in, up_in: jax.nn.silu(gate_in) * up_in, gate_out, up_out
     )
     grad_gate, grad_up = pull_gate(grad_act)
     grad_gate = grad_gate.astype(jnp.bfloat16)
     grad_up = grad_up.astype(jnp.bfloat16)
-    down_grad_t = contract_rows(mlp_grad_all, activated)
-    gate_grad = contract_rows(second_all, grad_gate)
-    up_grad = contract_rows(second_all, grad_up)
-
-    def second_term(start, count):
-        return contract_last(grad_gate, w_gate) + contract_last(grad_up, w_up)
-
-    second_back = token_sum(second_term, rows)
+    second_partial = contract_last(grad_gate, w_gate) + contract_last(grad_up, w_up)
+    grad_inputs, second_partial = lax.optimization_barrier(
+        ((mlp_grad_all, activated, second_all, grad_gate, grad_up), second_partial)
+    )
+    late_c, late_act, late_second, late_gate, late_up = grad_inputs
+    down_grad_t = contract_rows(late_c, late_act)
+    gate_grad = contract_rows(late_second, late_gate)
+    up_grad = contract_rows(late_second, late_up)
+    second_back = token_sum(lambda start, count: second_partial, rows)
     unused, pull_second = jax.vjp(rms_scale, after_attn, gain_second)
     norm_second_grad, post_gain_part = pull_second(second_back)
     residual_grad = cotangent + norm_second_grad
+    weight_grads, residual_grad = lax.optimization_barrier(
+        ((gate_grad, up_grad, down_grad_t), residual_grad)
+    )
+    gate_grad, up_grad, down_grad_t = weight_grads
     attn_grad_all = token_gather(residual_grad.astype(jnp.bfloat16))
     activated_late, attn_grad_all = lax.optimization_barrier((activated, attn_grad_all))
     down_rows = token_sum(lambda start, count: contract_last(activated_late, w_down_t), rows)

time: 725 us -> 692 us (0.954)
  local copies, waits for them, and re-layouts: 119 us -> 103 us
    unnamed x232 -> x207, local copies, waits for them, and re-layouts: 49.5 us -> 33.6 us
    concatenate x1, other arithmetic: 15.9 us -> 2.94 us  [shards(): jnp.concatenate([g.astype(jnp.bfloat16) for g in (gate_grad, up_grad, dow...]
    ppermute x16, waiting for transfers between devices: 139 us -> 127 us  [exchange(): lax.ppermute(values, 'tensor', [(i, i ^ distance) for i in range(count)])]
    dot_general x1, matrix products: 12.7 us -> 3.47 us  [shards(): jnp.dot(late_grad_all, w_down_t, preferred_element_type=jnp.float32)]
    dot_general x7, matrix products: 34.6 us -> 42.6 us  [contract_last(): lax.dot_general(left, right, (((1,), (1,)), ((), ())), preferred_element_...]
  transfers between devices with their start and end apart: 35 -> 35, of which waited for: 20 -> 20; matrix products, arithmetic and copies ran while one was open for 30% -> 32% of each run, Pallas kernels for 19% -> 20%
where the time goes in v9:
time: 692 us; the launch traced here: 683 us
  waiting for transfers between devices  187 us (27%)
  Pallas kernels  135 us (20%)
  other arithmetic  108 us (16%)
  local copies, waits for them, and re-layouts  103 us (15%)
  matrix products  103 us (15%)
  starting transfers between devices  31.8 us (5%)
  between operations  15.6 us (2%)
    ppermute x16, waiting for transfers between devices, exchange(): lax.ppermute(values, 'tensor', [(i, i ^ distance) for i in range(count)])  127 us
    pallas_call x2, Pallas kernels, attention_backward(): pl.pallas_call(functools.partial(_bwd_kernel, scale=scale, block=block),...  83.2 us
    pallas_call x2, Pallas kernels, attention_forward(): pl.pallas_call(functools.partial(_fwd_kernel, scale=scale, block=block),...  51.8 us
    dot_general x7, matrix products, contract_last(): lax.dot_general(left, right, (((1,), (1,)), ((), ())), preferred_element_...  42.6 us
    ppermute x2, waiting for transfers between devices, swapped(): lax.ppermute(shard, axis, [(i, i ^ 1 << distance) for i in range(lax.axis...  33.9 us
    unnamed x207, local copies, waits for them, and re-layouts  33.6 us
    dot_general x7, matrix products, contract_rows(): lax.dot_general(left, right, (((0,), (0,)), ((), ())), preferred_element_...  28.5 us
    ppermute x6, waiting for transfers between devices, halving_scatter(): lax.ppermute(send.astype(jnp.bfloat16), 'fsdp', [(i, i ^ 1 << bit) for i...  20.2 us
  transfers between devices with their start and end apart: 35, of which 20 were waited for; matrix products, arithmetic and copies ran while one was open for 32% of the time, Pallas kernels for 20%

profile of v9, /device:TPU:0, one launch (start us, length us, event | category | flops | bytes accessed | tf_op | source)
XLA Modules:
  0.0 683.5 jit_solution(5839872411758121904)
XLA Ops:
  43.3 5.3 collective-permute-done.5
  51.3 18.4 %collective-permute-done.3 = bf16[512,1024]{1,0:T(8,128)(2,1)S(1)} collective-permute-done((bf16[512,1024]{1,0:T(8,128)(2,1)}, bf16[512,1024]{1,0:T(8,128)(2,1)S(1)}, u32[]{:S(2)}, u32[]{:S(2)}) %collective-permute-start.3) | collective-permute-done | bytes 1048608 | tf_op jit(solution)/shard_map/ppermute | solution.py:338
  96.3 5.3 convolution_convert_fusion.1
  132.7 28.9 %attn_fwd.2 = (f32[2,2,2048,128]{3,2,1,0:T(8,128)}, f32[2,2,2048,128]{3,2,1,0:T(8,128)}) custom-call(s32[7,10]{1,0:T(8,128)S(1)} %broadcast_select_fusion.3.tab_ref, bf16[2,2,2048,128]{3,2,1,0:T(8,128)(2,1)S(1)} %maximum_bitcast_fusion.q_ref, s32[2048,128]{1,0:T(8,128)S(1)} %broadcast_in_dim.45.qs_ref, ...), custom_call_target="tpu_custom_call", output_to_operand_aliasing={{0}: (5, {}), {1}: (6, {})} | custom-call | flops 5368709120 | bytes 20971520 | tf_op jit(solution)/shard_map/attn_fwd/pallas_call | solution.py:124
  161.5 21.2 %collective-permute-done.7 = bf16[2,2,2048,128]{3,2,1,0:T(8,128)(2,1)} collective-permute-done((bf16[2,2,2048,128]{3,2,1,0:T(8,128)(2,1)}, bf16[2,2,2048,128]{3,2,1,0:T(8,128)(2,1)}, u32[]{:S(2)}, u32[]{:S(2)}) %collective-permute-start.7) | collective-permute-done | bytes 2097184 | tf_op jit(solution)/shard_map/ppermute | solution.py:236
  184.5 23.0 %attn_fwd.3 = (f32[2,2,2048,128]{3,2,1,0:T(8,128)}, f32[2,2,2048,128]{3,2,1,0:T(8,128)}) custom-call(s32[7,8]{1,0:T(8,128)S(1)} %broadcast_select_fusion.5.tab_ref, bf16[2,2,2048,128]{3,2,1,0:T(8,128)(2,1)S(1)} %maximum_bitcast_fusion.q_ref, s32[2048,128]{1,0:T(8,128)S(1)} %broadcast_in_dim.45.qs_ref, ...), custom_call_target="tpu_custom_call", output_to_operand_aliasing={{0}: (5, {}), {1}: (6, {})} | custom-call | flops 4294967296 | bytes 16777216 | tf_op jit(solution)/shard_map/attn_fwd/pallas_call | solution.py:124
  230.8 19.9 %collective-permute-done.9 = bf16[512,1024]{1,0:T(8,128)(2,1)S(1)} collective-permute-done((bf16[512,1024]{1,0:T(8,128)(2,1)S(1)}, bf16[512,1024]{1,0:T(8,128)(2,1)S(1)}, u32[]{:S(2)}, u32[]{:S(2)}) %collective-permute-start.9) | collective-permute-done | bytes 1048608 | tf_op jit(solution)/shard_map/ppermute | solution.py:338
  254.2 22.9 %collective-permute-done.10 = bf16[512,1024]{1,0:T(8,128)(2,1)S(1)} collective-permute-done((bf16[512,1024]{1,0:T(8,128)(2,1)S(1)}, bf16[512,1024]{1,0:T(8,128)(2,1)S(1)}, u32[]{:S(2)}, u32[]{:S(2)}) %collective-permute-start.10) | collective-permute-done | bytes 1048608 | tf_op jit(solution)/shard_map/ppermute | solution.py:338
  285.2 5.0 fusion.42
  290.2 5.3 multiply_convert_fusion
  295.5 10.3 %fusion.40 = f32[2048,1024]{1,0:T(8,128)} fusion(bf16[2048,768]{1,0:T(8,128)(2,1)} %get-tuple-element.62, bf16[1024,2816]{0,1:T(8,128)(2,1)} %all-gather.5.cloned.1.call-done), kind=kOutput, calls=%fused_computation.132 | convolution fusion | flops 3221225472 | bytes 13107200 | tf_op jit(solution)/shard_map/dot_general | solution.py:276
  305.9 6.4 convolution_add_fusion
  331.5 14.3 %collective-permute-done.13 = bf16[512,1024]{1,0:T(8,128)(2,1)S(1)} collective-permute-done((bf16[512,1024]{1,0:T(8,128)(2,1)S(1)}, bf16[512,1024]{1,0:T(8,128)(2,1)S(1)}, u32[]{:S(2)}, u32[]{:S(2)}) %collective-permute-start.13) | collective-permute-done | bytes 1048608 | tf_op jit(solution)/shard_map/ppermute | solution.py:338
  350.4 22.9 %collective-permute-done.14 = bf16[512,1024]{1,0:T(8,128)(2,1)S(1)} collective-permute-done((bf16[512,1024]{1,0:T(8,128)(2,1)S(1)}, bf16[512,1024]{1,0:T(8,128)(2,1)S(1)}, u32[]{:S(2)}, u32[]{:S(2)}) %collective-permute-start.14) | collective-permute-done | bytes 1048608 | tf_op jit(solution)/shard_map/ppermute | solution.py:338
  389.4 7.6 %fusion.6 = (f32[2048,2,2]{0,2,1:T(2,128)S(1)}, bf16[2,2,2048,128]{3,2,1,0:T(8,128)(2,1)}) fusion(f32[2048,2,2,128]{3,0,2,1:T(8,128)} %copy.105, f32[2,2,2048,128]{3,2,1,0:T(8,128)} %get-tuple-element.55, f32[2,2,2048]{2,1,0:T(2,128)S(1)} %slice_reduce_fusion, f32[2048,2,2]{0,2,1:T(2,128)S(1)} %bitcast.248), kind=kLoop, calls=%fused_computation.30 | loop fusion | flops 5234688 | bytes 10584064 | tf_op jit(solution)/shard_map/reduce_sum | solution.py:528
  428.9 37.4 %attn_bwd.2 = (f32[2,2,2048,128]{3,2,1,0:T(8,128)}, f32[2,2048,128]{2,1,0:T(8,128)}, f32[2,2048,128]{2,1,0:T(8,128)}) custom-call(s32[7,8]{1,0:T(8,128)} %broadcast_select_fusion.4.tab_ref, bf16[2,2,2048,128]{3,2,1,0:T(8,128)(2,1)} %copy-done.1, bf16[2,2,2048,128]{3,2,1,0:T(8,128)(2,1)} %get-tuple-element.73.h_ref, ...), custom_call_target="tpu_custom_call", output_to_operand_aliasing={{0}: (7, {})} | custom-call | flops 10737418240 | bytes 20971520 | tf_op jit(solution)/shard_map/attn_bwd/pallas_call | solution.py:207
  476.7 45.8 %attn_bwd.3 = (f32[2,2,2048,128]{3,2,1,0:T(8,128)}, f32[2,2048,128]{2,1,0:T(8,128)}, f32[2,2048,128]{2,1,0:T(8,128)}) custom-call(s32[7,10]{1,0:T(8,128)} %broadcast_select_fusion.2.tab_ref, bf16[2,2,2048,128]{3,2,1,0:T(8,128)(2,1)} %copy-done.1, bf16[2,2,2048,128]{3,2,1,0:T(8,128)(2,1)} %get-tuple-element.73.h_ref, ...), custom_call_target="tpu_custom_call", output_to_operand_aliasing={{0}: (7, {})} | custom-call | flops 13421772800 | bytes 26214400 | tf_op jit(solution)/shard_map/attn_bwd/pallas_call | solution.py:207
  522.5 12.7 %collective-permute-done.18 = bf16[2,2,2048,128]{3,2,1,0:T(8,128)(2,1)} collective-permute-done((bf16[2,2,2048,128]{3,2,1,0:T(8,128)(2,1)}, bf16[2,2,2048,128]{3,2,1,0:T(8,128)(2,1)}, u32[]{:S(2)}, u32[]{:S(2)}) %collective-permute-start.18) | collective-permute-done | bytes 2097184 | tf_op jit(solution)/shard_map/ppermute | solution.py:236
  559.7 5.9 fusion.74
  565.5 7.4 %collective-permute-done.24 = bf16[512,512]{0,1:T(8,128)(2,1)} collective-permute-done((bf16[512,512]{0,1:T(8,128)(2,1)}, bf16[512,512]{0,1:T(8,128)(2,1)}, u32[]{:S(2)}, u32[]{:S(2)}) %collective-permute-start.24) | collective-permute-done | bytes 524320 | tf_op jit(solution)/shard_map/ppermute | solution.py:304
  606.6 5.8 fusion.68
  612.4 5.1 add_add_fusion
  624.9 7.9 %collective-permute-done.21 = bf16[512,512]{1,0:T(8,128)(2,1)S(1)} collective-permute-done((bf16[512,512]{1,0:T(8,128)(2,1)S(1)}, bf16[512,512]{1,0:T(8,128)(2,1)S(1)}, u32[]{:S(2)}, u32[]{:S(2)}) %collective-permute-start.21) | collective-permute-done | bytes 524320 | tf_op jit(solution)/shard_map/ppermute | solution.py:304
  641.0 7.6 %collective-permute-done.20 = bf16[512,1024]{1,0:T(8,128)(2,1)S(1)} collective-permute-done((bf16[512,1024]{1,0:T(8,128)(2,1)S(1)}, bf16[512,1024]{1,0:T(8,128)(2,1)S(1)}, u32[]{:S(2)}, u32[]{:S(2)}) %collective-permute-start.20) | collective-permute-done | bytes 1048608 | tf_op jit(solution)/shard_map/ppermute | solution.py:338
  (448 shorter events, 315.7 us)
Async XLA Ops:
  7.2 82.0 %all-gather.3.cloned.1.call-start = ((), (), s32[]{:S(2)}) async-start(), calls=%async_computation.1 | async-start | bytes 2359296 | tf_op jit(solution)/shard_map/all_gather | solution.py:410
  10.8 204.7 %all-gather.5.cloned.1.call-start = ((), (), s32[]{:S(2)}) async-start(), calls=%async_computation.2 | async-start | bytes 6488064 | tf_op jit(solution)/shard_map/all_gather | solution.py:465
  13.5 10.6 %collective-permute-start = (bf16[288]{0:T(512)(128)(2,1)S(1)}, bf16[288]{0:T(512)(128)(2,1)S(1)}, u32[]{:S(2)}, u32[]{:S(2)}) collective-permute-start(bf16[288]{0:T(512)(128)(2,1)S(1)} %pad_maximum_fusion.18), channel_id=1, source_target_pairs={{0,4},{4,0},{8,12},{12,8},{16,20},{20,16},{24,28},{28,24},{1,5},{5... | collective-permute-start | bytes 1736 | tf_op jit(solution)/shard_map/ppermute | solution.py:316
  22.6 26.0 %collective-permute-start.5 = (bf16[512,1024]{1,0:T(8,128)(2,1)S(1)}, bf16[512,1024]{1,0:T(8,128)(2,1)S(1)}, u32[]{:S(2)}, u32[]{:S(2)}) collective-permute-start(bf16[512,1024]{1,0:T(8,128)(2,1)S(1)} %get-tuple-element.156), channel_id=1, source_target_pairs={{0,2},{1,3},{2,0},{3,1},{4,6},{5,7},{6,4},{7,5},{8,10},{9,11},{10,... | collective-permute-start | bytes 3145736 | tf_op jit(solution)/shard_map/ppermute | solution.py:338
  42.7 27.0 %collective-permute-start.3 = (bf16[512,1024]{1,0:T(8,128)(2,1)}, bf16[512,1024]{1,0:T(8,128)(2,1)S(1)}, u32[]{:S(2)}, u32[]{:S(2)}) collective-permute-start(bf16[512,1024]{1,0:T(8,128)(2,1)} %get-tuple-element.158), channel_id=1, source_target_pairs={{0,2},{1,3},{2,0},{3,1},{4,6},{5,7},{6,4},{7,5},{8,10},{9,11},{10,... | collective-permute-start | bytes 3145736 | tf_op jit(solution)/shard_map/ppermute | solution.py:338
  50.2 29.9 %collective-permute-start.6 = (bf16[2,512,1024]{2,1,0:T(8,128)(2,1)}, bf16[2,512,1024]{2,1,0:T(8,128)(2,1)}, u32[]{:S(2)}, u32[]{:S(2)}) collective-permute-start(bf16[2,512,1024]{2,1,0:T(8,128)(2,1)} %pad_maximum_fusion.2), channel_id=1, source_target_pairs={{0,1},{1,0},{2,3},{3,2},{4,5},{5,4},{6,7},{7,6},{8,9},{9,8},{10,11... | collective-permute-start | bytes 6291464 | tf_op jit(solution)/shard_map/ppermute | solution.py:338
  51.1 525.3 %reduce-scatter.2.cloned.1.call-start = ((), (), s32[]{:S(2)}) async-start(), calls=%async_computation.3 | async-start | bytes 6488064 | tf_op jit(solution)/shard_map/reduce_scatter | solution.py:536
  72.9 11.7 %collective-permute-start.4 = (bf16[2,512,1024]{2,1,0:T(8,128)(2,1)}, bf16[2,512,1024]{2,1,0:T(8,128)(2,1)}, u32[]{:S(2)}, u32[]{:S(2)}) collective-permute-start(bf16[2,512,1024]{2,1,0:T(8,128)(2,1)} %pad_maximum_fusion.1), channel_id=1, source_target_pairs={{0,1},{1,0},{2,3},{3,2},{4,5},{5,4},{6,7},{7,6},{8,9},{9,8},{10,11... | collective-permute-start | bytes 6291464 | tf_op jit(solution)/shard_map/ppermute | solution.py:338
  109.4 73.3 %collective-permute-start.7 = (bf16[2,2,2048,128]{3,2,1,0:T(8,128)(2,1)}, bf16[2,2,2048,128]{3,2,1,0:T(8,128)(2,1)}, u32[]{:S(2)}, u32[]{:S(2)}) collective-permute-start(bf16[2,2,2048,128]{3,2,1,0:T(8,128)(2,1)} %pad_maximum_fusion.3), channel_id=1, source_target_pairs={{0,4},{4,0},{8,12},{12,8},{16,20},{20,16},{24,28},{28,24},{1,5},{5... | collective-permute-start | bytes 6291464 | tf_op jit(solution)/shard_map/ppermute | solution.py:236
  225.5 25.3 %collective-permute-start.9 = (bf16[512,1024]{1,0:T(8,128)(2,1)S(1)}, bf16[512,1024]{1,0:T(8,128)(2,1)S(1)}, u32[]{:S(2)}, u32[]{:S(2)}) collective-permute-start(bf16[512,1024]{1,0:T(8,128)(2,1)S(1)} %fusion.30), channel_id=1, source_target_pairs={{0,2},{1,3},{2,0},{3,1},{4,6},{5,7},{6,4},{7,5},{8,10},{9,11},{10,... | collective-permute-start | bytes 3145736 | tf_op jit(solution)/shard_map/ppermute | solution.py:338
  252.6 24.4 %collective-permute-start.10 = (bf16[512,1024]{1,0:T(8,128)(2,1)S(1)}, bf16[512,1024]{1,0:T(8,128)(2,1)S(1)}, u32[]{:S(2)}, u32[]{:S(2)}) collective-permute-start(bf16[512,1024]{1,0:T(8,128)(2,1)S(1)} %get-tuple-element.154), channel_id=1, source_target_pairs={{0,2},{1,3},{2,0},{3,1},{4,6},{5,7},{6,4},{7,5},{8,10},{9,11},{10,... | collective-permute-start | bytes 3145736 | tf_op jit(solution)/shard_map/ppermute | solution.py:338
  312.8 6.9 %collective-permute-start.12 = (bf16[2,512,1024]{2,1,0:T(8,128)(2,1)S(1)}, bf16[2,512,1024]{2,1,0:T(8,128)(2,1)S(1)}, u32[]{:S(2)}, u32[]{:S(2)}) collective-permute-start(bf16[2,512,1024]{2,1,0:T(8,128)(2,1)S(1)} %pad_maximum_fusion.6), channel_id=1, source_target_pairs={{0,1},{1,0},{2,3},{3,2},{4,5},{5,4},{6,7},{7,6},{8,9},{9,8},{10,11... | collective-permute-start | bytes 6291464 | tf_op jit(solution)/shard_map/ppermute | solution.py:338
  320.5 25.3 %collective-permute-start.13 = (bf16[512,1024]{1,0:T(8,128)(2,1)S(1)}, bf16[512,1024]{1,0:T(8,128)(2,1)S(1)}, u32[]{:S(2)}, u32[]{:S(2)}) collective-permute-start(bf16[512,1024]{1,0:T(8,128)(2,1)S(1)} %fusion.26), channel_id=1, source_target_pairs={{0,2},{1,3},{2,0},{3,1},{4,6},{5,7},{6,4},{7,5},{8,10},{9,11},{10,... | collective-permute-start | bytes 3145736 | tf_op jit(solution)/shard_map/ppermute | solution.py:338
  348.9 24.4 %collective-permute-start.14 = (bf16[512,1024]{1,0:T(8,128)(2,1)S(1)}, bf16[512,1024]{1,0:T(8,128)(2,1)S(1)}, u32[]{:S(2)}, u32[]{:S(2)}) collective-permute-start(bf16[512,1024]{1,0:T(8,128)(2,1)S(1)} %get-tuple-element.151), channel_id=1, source_target_pairs={{0,2},{1,3},{2,0},{3,1},{4,6},{5,7},{6,4},{7,5},{8,10},{9,11},{10,... | collective-permute-start | bytes 3145736 | tf_op jit(solution)/shard_map/ppermute | solution.py:338
  425.5 46.6 %collective-permute-start.17 = (bf16[512,1024]{1,0:T(8,128)(2,1)S(1)}, bf16[512,1024]{1,0:T(8,128)(2,1)}, u32[]{:S(2)}, u32[]{:S(2)}) collective-permute-start(bf16[512,1024]{1,0:T(8,128)(2,1)S(1)} %fusion.22), channel_id=1, source_target_pairs={{0,2},{1,3},{2,0},{3,1},{4,6},{5,7},{6,4},{7,5},{8,10},{9,11},{10,... | collective-permute-start | bytes 3145736 | tf_op jit(solution)/shard_map/ppermute | solution.py:338
  469.9 65.3 %collective-permute-start.18 = (bf16[2,2,2048,128]{3,2,1,0:T(8,128)(2,1)}, bf16[2,2,2048,128]{3,2,1,0:T(8,128)(2,1)}, u32[]{:S(2)}, u32[]{:S(2)}) collective-permute-start(bf16[2,2,2048,128]{3,2,1,0:T(8,128)(2,1)} %fusion.5), channel_id=1, source_target_pairs={{0,4},{4,0},{8,12},{12,8},{16,20},{20,16},{24,28},{28,24},{1,5},{5... | collective-permute-start | bytes 6291464 | tf_op jit(solution)/shard_map/ppermute | solution.py:236
  559.1 13.8 %collective-permute-start.24 = (bf16[512,512]{0,1:T(8,128)(2,1)}, bf16[512,512]{0,1:T(8,128)(2,1)}, u32[]{:S(2)}, u32[]{:S(2)}) collective-permute-start(bf16[512,512]{0,1:T(8,128)(2,1)} %dynamic-slice_convert_fusion.8), channel_id=1, source_target_pairs={{0,4},{4,0},{8,12},{12,8},{16,20},{20,16},{24,28},{28,24},{1,5},{5... | collective-permute-start | bytes 1572872 | tf_op jit(solution)/shard_map/ppermute | solution.py:304
  575.8 42.9 %collective-permute-start.25 = (bf16[256,512]{0,1:T(8,128)(2,1)}, bf16[256,512]{0,1:T(8,128)(2,1)}, u32[]{:S(2)}, u32[]{:S(2)}) collective-permute-start(bf16[256,512]{0,1:T(8,128)(2,1)} %dynamic-slice_convert_fusion.10), channel_id=1, source_target_pairs={{0,8},{4,12},{8,0},{12,4},{16,24},{20,28},{24,16},{28,20},{1,9},{5... | collective-permute-start | bytes 786440 | tf_op jit(solution)/shard_map/ppermute | solution.py:304
  618.4 14.4 %collective-permute-start.21 = (bf16[512,512]{1,0:T(8,128)(2,1)S(1)}, bf16[512,512]{1,0:T(8,128)(2,1)S(1)}, u32[]{:S(2)}, u32[]{:S(2)}) collective-permute-start(bf16[512,512]{1,0:T(8,128)(2,1)S(1)} %dynamic-slice_convert_fusion.9), channel_id=1, source_target_pairs={{0,4},{4,0},{8,12},{12,8},{16,20},{20,16},{24,28},{28,24},{1,5},{5... | collective-permute-start | bytes 1572872 | tf_op jit(solution)/shard_map/ppermute | solution.py:304
  620.4 15.6 %collective-permute-start.26 = (bf16[128,512]{0,1:T(8,128)(2,1)S(1)}, bf16[128,512]{0,1:T(8,128)(2,1)S(1)}, u32[]{:S(2)}, u32[]{:S(2)}) collective-permute-start(bf16[128,512]{0,1:T(8,128)(2,1)S(1)} %dynamic-slice_convert_fusion.12), channel_id=1, source_target_pairs={{0,16},{4,20},{8,24},{12,28},{16,0},{20,4},{24,8},{28,12},{1,17},{... | collective-permute-start | bytes 393224 | tf_op jit(solution)/shard_map/ppermute | solution.py:304
  623.3 25.3 %collective-permute-start.20 = (bf16[512,1024]{1,0:T(8,128)(2,1)S(1)}, bf16[512,1024]{1,0:T(8,128)(2,1)S(1)}, u32[]{:S(2)}, u32[]{:S(2)}) collective-permute-start(bf16[512,1024]{1,0:T(8,128)(2,1)S(1)} %fusion.18), channel_id=1, source_target_pairs={{0,2},{1,3},{2,0},{3,1},{4,6},{5,7},{6,4},{7,5},{8,10},{9,11},{10,... | collective-permute-start | bytes 3145736 | tf_op jit(solution)/shard_map/ppermute | solution.py:338
  633.0 7.9 %collective-permute-start.22 = (bf16[256,512]{1,0:T(8,128)(2,1)S(1)}, bf16[256,512]{1,0:T(8,128)(2,1)S(1)}, u32[]{:S(2)}, u32[]{:S(2)}) collective-permute-start(bf16[256,512]{1,0:T(8,128)(2,1)S(1)} %dynamic-slice_convert_fusion.11), channel_id=1, source_target_pairs={{0,8},{4,12},{8,0},{12,4},{16,24},{20,28},{24,16},{28,20},{1,9},{5... | collective-permute-start | bytes 786440 | tf_op jit(solution)/shard_map/ppermute | solution.py:304
  652.2 11.8 %collective-permute-start.23 = (bf16[128,512]{1,0:T(8,128)(2,1)}, bf16[128,512]{1,0:T(8,128)(2,1)}, u32[]{:S(2)}, u32[]{:S(2)}) collective-permute-start(bf16[128,512]{1,0:T(8,128)(2,1)} %dynamic-slice_convert_fusion.13), channel_id=1, source_target_pairs={{0,16},{4,20},{8,24},{12,28},{16,0},{20,4},{24,8},{28,12},{1,17},{... | collective-permute-start | bytes 393224 | tf_op jit(solution)/shard_map/ppermute | solution.py:304
  654.6 8.2 %collective-permute-start.28 = (f32[2304]{0:T(1024)S(1)}, f32[2304]{0:T(1024)}, u32[]{:S(2)}, u32[]{:S(2)}) collective-permute-start(f32[2304]{0:T(1024)S(1)} %fusion.116), channel_id=1, source_target_pairs={{0,2},{1,3},{2,0},{3,1},{4,6},{5,7},{6,4},{7,5},{8,10},{9,11},{10,... | collective-permute-start | bytes 27656 | tf_op jit(solution)/shard_map/ppermute | solution.py:329
  (107 other events, 1186.0 us)
Sparse Core Ops, SparseCore 0:
  10.9 52.1 all-gather.2
  65.1 115.8 all-gather.4
  412.3 126.1 reduce-scatter.1

commit v10 on v9

--- a/solution.py
+++ b/solution.py
@@ -407,21 +407,25 @@
     gain_in, gain_query, gain_keys, gain_post = [
         part.reshape(-1) for part in split_columns(gains_all, gain_sizes)
     ]
-    attn_full = lax.all_gather(
+    kv_full = lax.all_gather(
         jnp.concatenate(
-            [
-                q_weight.astype(jnp.bfloat16),
-                key_matrix.astype(jnp.bfloat16),
-                value_matrix.astype(jnp.bfloat16),
-            ],
-            axis=1,
+            [key_matrix.astype(jnp.bfloat16), value_matrix.astype(jnp.bfloat16)], axis=1
         ),
         "fsdp",
         axis=0,
         tiled=True,
     )
-    widths = (q_weight.shape[1], key_matrix.shape[1], value_matrix.shape[1])
-    w_query, w_key, w_value = split_columns(attn_full, widths)
+    w_key, w_value = split_columns(kv_full, (key_matrix.shape[1], value_matrix.shape[1]))
+    qo_full = lax.all_gather(
+        jnp.concatenate(
+            [q_weight.astype(jnp.bfloat16), jnp.transpose(o_weight).astype(jnp.bfloat16)],
+            axis=1,
+        ),
+        "fsdp",
+        axis=0,
+        tiled=True,
+    )
+    w_query, w_out = split_columns(qo_full, (q_weight.shape[1], o_weight.shape[0]))
     x_float = hidden.astype(jnp.float32)
     gain_first = gain_in.astype(jnp.float32)
     first_all = token_gather(rms_scale(x_float, gain_first).astype(jnp.bfloat16))
@@ -468,7 +472,6 @@
                 gate_weight.astype(jnp.bfloat16),
                 up_weight.astype(jnp.bfloat16),
                 jnp.transpose(down_weight).astype(jnp.bfloat16),
-                jnp.transpose(o_weight).astype(jnp.bfloat16),
             ],
             axis=1,
         ),
@@ -476,8 +479,8 @@
         axis=0,
         tiled=True,
     )
-    w_gate, w_up, w_down_t, w_out = split_columns(
-        mlp_full, (gate_weight.shape[1], up_weight.shape[1], down_weight.shape[0], o_weight.shape[0])
+    w_gate, w_up, w_down_t = split_columns(
+        mlp_full, (gate_weight.shape[1], up_weight.shape[1], down_weight.shape[0])
     )
     out_partial = contract_last(out_rows, w_out)
     late_grad_all, out_partial = lax.optimization_barrier((mlp_grad_all, out_partial))

time: 692 us -> 691 us (level)
    unnamed x207 -> x210, local copies, waits for them, and re-layouts: 33.6 us -> 33.2 us
  transfers between devices with their start and end apart: 35 -> 36, of which waited for: 20 -> 21; matrix products, arithmetic and copies ran while one was open for 32% -> 33% of each run, Pallas kernels for 20% -> 20%
where the time goes in v10:
time: 691 us; the launch traced here: 683 us
  waiting for transfers between devices  184 us (27%)
  Pallas kernels  135 us (20%)
  other arithmetic  109 us (16%)
  local copies, waits for them, and re-layouts  104 us (15%)
  matrix products  103 us (15%)
  starting transfers between devices  32 us (5%)
  between operations  16 us (2%)
    ppermute x16, waiting for transfers between devices, exchange(): lax.ppermute(values, 'tensor', [(i, i ^ distance) for i in range(count)])  126 us
    pallas_call x2, Pallas kernels, attention_backward(): pl.pallas_call(functools.partial(_bwd_kernel, scale=scale, block=block),...  83.1 us
    pallas_call x2, Pallas kernels, attention_forward(): pl.pallas_call(functools.partial(_fwd_kernel, scale=scale, block=block),...  52.1 us
    dot_general x7, matrix products, contract_last(): lax.dot_general(left, right, (((1,), (1,)), ((), ())), preferred_element_...  42.3 us
    unnamed x210, local copies, waits for them, and re-layouts  33.2 us
    ppermute x2, waiting for transfers between devices, swapped(): lax.ppermute(shard, axis, [(i, i ^ 1 << distance) for i in range(lax.axis...  30.3 us
    dot_general x7, matrix products, contract_rows(): lax.dot_general(left, right, (((0,), (0,)), ((), ())), preferred_element_...  28.9 us
    ppermute x6, waiting for transfers between devices, halving_scatter(): lax.ppermute(send.astype(jnp.bfloat16), 'fsdp', [(i, i ^ 1 << bit) for i...  20.3 us
  transfers between devices with their start and end apart: 36, of which 21 were waited for; matrix products, arithmetic and copies ran while one was open for 33% of the time, Pallas kernels for 20%

profile of v10, /device:TPU:0, one launch (start us, length us, event | category | flops | bytes accessed | tf_op | source)
XLA Modules:
  0.0 682.9 jit_solution(6829146447537966660)
XLA Ops:
  40.3 7.7 %collective-permute-done.5 = bf16[512,1024]{1,0:T(8,128)(2,1)S(1)} collective-permute-done((bf16[512,1024]{1,0:T(8,128)(2,1)S(1)}, bf16[512,1024]{1,0:T(8,128)(2,1)S(1)}, u32[]{:S(2)}, u32[]{:S(2)}) %collective-permute-start.5) | collective-permute-done | bytes 1048608 | tf_op jit(solution)/shard_map/ppermute | solution.py:338
  51.5 17.7 %collective-permute-done.3 = bf16[512,1024]{1,0:T(8,128)(2,1)} collective-permute-done((bf16[512,1024]{1,0:T(8,128)(2,1)}, bf16[512,1024]{1,0:T(8,128)(2,1)}, u32[]{:S(2)}, u32[]{:S(2)}) %collective-permute-start.3) | collective-permute-done | bytes 1048608 | tf_op jit(solution)/shard_map/ppermute | solution.py:338
  112.1 5.2 multiply_reduce_fusion.2
  136.5 28.8 %attn_fwd.2 = (f32[2,2,2048,128]{3,2,1,0:T(8,128)}, f32[2,2,2048,128]{3,2,1,0:T(8,128)}) custom-call(s32[7,10]{1,0:T(8,128)S(1)} %broadcast_select_fusion.3.tab_ref, bf16[2,2,2048,128]{3,2,1,0:T(8,128)(2,1)S(1)} %maximum_bitcast_fusion.q_ref, s32[2048,128]{1,0:T(8,128)S(1)} %broadcast_in_dim.45.qs_ref, ...), custom_call_target="tpu_custom_call", output_to_operand_aliasing={{0}: (5, {}), {1}: (6, {})} | custom-call | flops 5368709120 | bytes 20971520 | tf_op jit(solution)/shard_map/attn_fwd/pallas_call | solution.py:124
  165.3 16.6 %collective-permute-done.7 = bf16[2,2,2048,128]{3,2,1,0:T(8,128)(2,1)} collective-permute-done((bf16[2,2,2048,128]{3,2,1,0:T(8,128)(2,1)}, bf16[2,2,2048,128]{3,2,1,0:T(8,128)(2,1)}, u32[]{:S(2)}, u32[]{:S(2)}) %collective-permute-start.7) | collective-permute-done | bytes 2097184 | tf_op jit(solution)/shard_map/ppermute | solution.py:236
  183.6 23.3 %attn_fwd.3 = (f32[2,2,2048,128]{3,2,1,0:T(8,128)}, f32[2,2,2048,128]{3,2,1,0:T(8,128)}) custom-call(s32[7,8]{1,0:T(8,128)S(1)} %broadcast_select_fusion.5.tab_ref, bf16[2,2,2048,128]{3,2,1,0:T(8,128)(2,1)S(1)} %maximum_bitcast_fusion.q_ref, s32[2048,128]{1,0:T(8,128)S(1)} %broadcast_in_dim.45.qs_ref, ...), custom_call_target="tpu_custom_call", output_to_operand_aliasing={{0}: (5, {}), {1}: (6, {})} | custom-call | flops 4294967296 | bytes 16777216 | tf_op jit(solution)/shard_map/attn_fwd/pallas_call | solution.py:124
  227.5 6.0 fusion.46
  233.5 17.8 %collective-permute-done.9 = bf16[512,1024]{1,0:T(8,128)(2,1)} collective-permute-done((bf16[512,1024]{1,0:T(8,128)(2,1)S(1)}, bf16[512,1024]{1,0:T(8,128)(2,1)}, u32[]{:S(2)}, u32[]{:S(2)}) %collective-permute-start.9) | collective-permute-done | bytes 1048608 | tf_op jit(solution)/shard_map/ppermute | solution.py:338
  256.5 22.9 %collective-permute-done.10 = bf16[512,1024]{1,0:T(8,128)(2,1)S(1)} collective-permute-done((bf16[512,1024]{1,0:T(8,128)(2,1)S(1)}, bf16[512,1024]{1,0:T(8,128)(2,1)S(1)}, u32[]{:S(2)}, u32[]{:S(2)}) %collective-permute-start.10) | collective-permute-done | bytes 1048608 | tf_op jit(solution)/shard_map/ppermute | solution.py:338
  291.0 5.5 multiply_convert_fusion
  296.5 10.3 %fusion.40 = f32[2048,1024]{1,0:T(8,128)} fusion(bf16[2048,768]{1,0:T(8,128)(2,1)} %get-tuple-element.62, bf16[1024,2304]{0,1:T(8,128)(2,1)} %all-gather.8.cloned.1.call-done), kind=kOutput, calls=%fused_computation.132 | convolution fusion | flops 3221225472 | bytes 13107200 | tf_op jit(solution)/shard_map/dot_general | solution.py:276
  306.9 6.4 convolution_add_fusion
  327.6 5.1 fusion.127
  332.7 13.9 %collective-permute-done.13 = bf16[512,1024]{1,0:T(8,128)(2,1)S(1)} collective-permute-done((bf16[512,1024]{1,0:T(8,128)(2,1)S(1)}, bf16[512,1024]{1,0:T(8,128)(2,1)S(1)}, u32[]{:S(2)}, u32[]{:S(2)}) %collective-permute-start.13) | collective-permute-done | bytes 1048608 | tf_op jit(solution)/shard_map/ppermute | solution.py:338
  351.3 22.9 %collective-permute-done.14 = bf16[512,1024]{1,0:T(8,128)(2,1)S(1)} collective-permute-done((bf16[512,1024]{1,0:T(8,128)(2,1)S(1)}, bf16[512,1024]{1,0:T(8,128)(2,1)S(1)}, u32[]{:S(2)}, u32[]{:S(2)}) %collective-permute-start.14) | collective-permute-done | bytes 1048608 | tf_op jit(solution)/shard_map/ppermute | solution.py:338
  389.1 7.2 %fusion.6 = (f32[2048,2,2]{0,2,1:T(2,128)S(1)}, bf16[2,2,2048,128]{3,2,1,0:T(8,128)(2,1)}) fusion(f32[2048,2,2,128]{3,0,2,1:T(8,128)} %copy.109, f32[2,2,2048,128]{3,2,1,0:T(8,128)} %get-tuple-element.55, f32[2,2,2048]{2,1,0:T(2,128)S(1)} %slice_reduce_fusion, f32[2048,2,2]{0,2,1:T(2,128)S(1)} %bitcast.247), kind=kLoop, calls=%fused_computation.30 | loop fusion | flops 5234688 | bytes 10584064 | tf_op jit(solution)/shard_map/reduce_sum | solution.py:531
  427.9 37.5 %attn_bwd.2 = (f32[2,2,2048,128]{3,2,1,0:T(8,128)}, f32[2,2048,128]{2,1,0:T(8,128)}, f32[2,2048,128]{2,1,0:T(8,128)}) custom-call(s32[7,8]{1,0:T(8,128)} %broadcast_select_fusion.4.tab_ref, bf16[2,2,2048,128]{3,2,1,0:T(8,128)(2,1)} %copy-done.1, bf16[2,2,2048,128]{3,2,1,0:T(8,128)(2,1)} %get-tuple-element.73.h_ref, ...), custom_call_target="tpu_custom_call", output_to_operand_aliasing={{0}: (7, {})} | custom-call | flops 10737418240 | bytes 20971520 | tf_op jit(solution)/shard_map/attn_bwd/pallas_call | solution.py:207
  475.5 45.6 %attn_bwd.3 = (f32[2,2,2048,128]{3,2,1,0:T(8,128)}, f32[2,2048,128]{2,1,0:T(8,128)}, f32[2,2048,128]{2,1,0:T(8,128)}) custom-call(s32[7,10]{1,0:T(8,128)} %broadcast_select_fusion.2.tab_ref, bf16[2,2,2048,128]{3,2,1,0:T(8,128)(2,1)} %copy-done.1, bf16[2,2,2048,128]{3,2,1,0:T(8,128)(2,1)} %get-tuple-element.73.h_ref, ...), custom_call_target="tpu_custom_call", output_to_operand_aliasing={{0}: (7, {})} | custom-call | flops 13421772800 | bytes 26214400 | tf_op jit(solution)/shard_map/attn_bwd/pallas_call | solution.py:207
  521.1 13.8 %collective-permute-done.18 = bf16[2,2,2048,128]{3,2,1,0:T(8,128)(2,1)} collective-permute-done((bf16[2,2,2048,128]{3,2,1,0:T(8,128)(2,1)}, bf16[2,2,2048,128]{3,2,1,0:T(8,128)(2,1)}, u32[]{:S(2)}, u32[]{:S(2)}) %collective-permute-start.18) | collective-permute-done | bytes 2097184 | tf_op jit(solution)/shard_map/ppermute | solution.py:236
  559.9 5.9 fusion.74
  565.7 7.4 %collective-permute-done.24 = bf16[512,512]{0,1:T(8,128)(2,1)} collective-permute-done((bf16[512,512]{0,1:T(8,128)(2,1)}, bf16[512,512]{0,1:T(8,128)(2,1)}, u32[]{:S(2)}, u32[]{:S(2)}) %collective-permute-start.24) | collective-permute-done | bytes 524320 | tf_op jit(solution)/shard_map/ppermute | solution.py:304
  606.1 5.7 fusion.68
  624.1 8.0 %collective-permute-done.21 = bf16[512,512]{1,0:T(8,128)(2,1)S(1)} collective-permute-done((bf16[512,512]{1,0:T(8,128)(2,1)S(1)}, bf16[512,512]{1,0:T(8,128)(2,1)S(1)}, u32[]{:S(2)}, u32[]{:S(2)}) %collective-permute-start.21) | collective-permute-done | bytes 524320 | tf_op jit(solution)/shard_map/ppermute | solution.py:304
  640.3 7.6 %collective-permute-done.20 = bf16[512,1024]{1,0:T(8,128)(2,1)S(1)} collective-permute-done((bf16[512,1024]{1,0:T(8,128)(2,1)S(1)}, bf16[512,1024]{1,0:T(8,128)(2,1)S(1)}, u32[]{:S(2)}, u32[]{:S(2)}) %collective-permute-start.20) | collective-permute-done | bytes 1048608 | tf_op jit(solution)/shard_map/ppermute | solution.py:338
  (454 shorter events, 318.2 us)
Async XLA Ops:
  7.2 83.9 %all-gather.6.cloned.1.call-start = ((), (), s32[]{:S(2)}) async-start(), calls=%async_computation.2 | async-start | bytes 1179648 | tf_op jit(solution)/shard_map/all_gather | solution.py:410
  9.8 102.3 %all-gather.4.cloned.1.call-start = ((), (), s32[]{:S(2)}) async-start(), calls=%async_computation.1 | async-start | bytes 2359296 | tf_op jit(solution)/shard_map/all_gather | solution.py:419
  12.6 214.8 %all-gather.8.cloned.1.call-start = ((), (), s32[]{:S(2)}) async-start(), calls=%async_computation.3 | async-start | bytes 5308416 | tf_op jit(solution)/shard_map/all_gather | solution.py:469
  12.8 10.7 %collective-permute-start = (bf16[288]{0:T(512)(128)(2,1)S(1)}, bf16[288]{0:T(512)(128)(2,1)S(1)}, u32[]{:S(2)}, u32[]{:S(2)}) collective-permute-start(bf16[288]{0:T(512)(128)(2,1)S(1)} %pad_maximum_fusion.19), channel_id=1, source_target_pairs={{0,4},{4,0},{8,12},{12,8},{16,20},{20,16},{24,28},{28,24},{1,5},{5... | collective-permute-start | bytes 1736 | tf_op jit(solution)/shard_map/ppermute | solution.py:316
  22.0 26.0 %collective-permute-start.5 = (bf16[512,1024]{1,0:T(8,128)(2,1)S(1)}, bf16[512,1024]{1,0:T(8,128)(2,1)S(1)}, u32[]{:S(2)}, u32[]{:S(2)}) collective-permute-start(bf16[512,1024]{1,0:T(8,128)(2,1)S(1)} %get-tuple-element.156), channel_id=1, source_target_pairs={{0,2},{1,3},{2,0},{3,1},{4,6},{5,7},{6,4},{7,5},{8,10},{9,11},{10,... | collective-permute-start | bytes 3145736 | tf_op jit(solution)/shard_map/ppermute | solution.py:338
  36.5 32.8 %collective-permute-start.3 = (bf16[512,1024]{1,0:T(8,128)(2,1)}, bf16[512,1024]{1,0:T(8,128)(2,1)}, u32[]{:S(2)}, u32[]{:S(2)}) collective-permute-start(bf16[512,1024]{1,0:T(8,128)(2,1)} %get-tuple-element.158), channel_id=1, source_target_pairs={{0,2},{1,3},{2,0},{3,1},{4,6},{5,7},{6,4},{7,5},{8,10},{9,11},{10,... | collective-permute-start | bytes 3145736 | tf_op jit(solution)/shard_map/ppermute | solution.py:338
  49.8 32.1 %collective-permute-start.6 = (bf16[2,512,1024]{2,1,0:T(8,128)(2,1)}, bf16[2,512,1024]{2,1,0:T(8,128)(2,1)}, u32[]{:S(2)}, u32[]{:S(2)}) collective-permute-start(bf16[2,512,1024]{2,1,0:T(8,128)(2,1)} %pad_maximum_fusion.2), channel_id=1, source_target_pairs={{0,1},{1,0},{2,3},{3,2},{4,5},{5,4},{6,7},{7,6},{8,9},{9,8},{10,11... | collective-permute-start | bytes 6291464 | tf_op jit(solution)/shard_map/ppermute | solution.py:338
  50.7 525.2 %reduce-scatter.2.cloned.1.call-start = ((), (), s32[]{:S(2)}) async-start(), calls=%async_computation.4 | async-start | bytes 6488064 | tf_op jit(solution)/shard_map/reduce_scatter | solution.py:539
  72.3 14.2 %collective-permute-start.4 = (bf16[2,512,1024]{2,1,0:T(8,128)(2,1)}, bf16[2,512,1024]{2,1,0:T(8,128)(2,1)}, u32[]{:S(2)}, u32[]{:S(2)}) collective-permute-start(bf16[2,512,1024]{2,1,0:T(8,128)(2,1)} %pad_maximum_fusion.1), channel_id=1, source_target_pairs={{0,1},{1,0},{2,3},{3,2},{4,5},{5,4},{6,7},{7,6},{8,9},{9,8},{10,11... | collective-permute-start | bytes 6291464 | tf_op jit(solution)/shard_map/ppermute | solution.py:338
  111.8 70.1 %collective-permute-start.7 = (bf16[2,2,2048,128]{3,2,1,0:T(8,128)(2,1)}, bf16[2,2,2048,128]{3,2,1,0:T(8,128)(2,1)}, u32[]{:S(2)}, u32[]{:S(2)}) collective-permute-start(bf16[2,2,2048,128]{3,2,1,0:T(8,128)(2,1)} %pad_maximum_fusion.3), channel_id=1, source_target_pairs={{0,4},{4,0},{8,12},{12,8},{16,20},{20,16},{24,28},{28,24},{1,5},{5... | collective-permute-start | bytes 6291464 | tf_op jit(solution)/shard_map/ppermute | solution.py:236
  226.0 25.3 %collective-permute-start.9 = (bf16[512,1024]{1,0:T(8,128)(2,1)S(1)}, bf16[512,1024]{1,0:T(8,128)(2,1)}, u32[]{:S(2)}, u32[]{:S(2)}) collective-permute-start(bf16[512,1024]{1,0:T(8,128)(2,1)S(1)} %fusion.30), channel_id=1, source_target_pairs={{0,2},{1,3},{2,0},{3,1},{4,6},{5,7},{6,4},{7,5},{8,10},{9,11},{10,... | collective-permute-start | bytes 3145736 | tf_op jit(solution)/shard_map/ppermute | solution.py:338
  254.9 24.4 %collective-permute-start.10 = (bf16[512,1024]{1,0:T(8,128)(2,1)S(1)}, bf16[512,1024]{1,0:T(8,128)(2,1)S(1)}, u32[]{:S(2)}, u32[]{:S(2)}) collective-permute-start(bf16[512,1024]{1,0:T(8,128)(2,1)S(1)} %get-tuple-element.154), channel_id=1, source_target_pairs={{0,2},{1,3},{2,0},{3,1},{4,6},{5,7},{6,4},{7,5},{8,10},{9,11},{10,... | collective-permute-start | bytes 3145736 | tf_op jit(solution)/shard_map/ppermute | solution.py:338
  321.3 25.3 %collective-permute-start.13 = (bf16[512,1024]{1,0:T(8,128)(2,1)S(1)}, bf16[512,1024]{1,0:T(8,128)(2,1)S(1)}, u32[]{:S(2)}, u32[]{:S(2)}) collective-permute-start(bf16[512,1024]{1,0:T(8,128)(2,1)S(1)} %fusion.26), channel_id=1, source_target_pairs={{0,2},{1,3},{2,0},{3,1},{4,6},{5,7},{6,4},{7,5},{8,10},{9,11},{10,... | collective-permute-start | bytes 3145736 | tf_op jit(solution)/shard_map/ppermute | solution.py:338
  349.7 24.4 %collective-permute-start.14 = (bf16[512,1024]{1,0:T(8,128)(2,1)S(1)}, bf16[512,1024]{1,0:T(8,128)(2,1)S(1)}, u32[]{:S(2)}, u32[]{:S(2)}) collective-permute-start(bf16[512,1024]{1,0:T(8,128)(2,1)S(1)} %get-tuple-element.151), channel_id=1, source_target_pairs={{0,2},{1,3},{2,0},{3,1},{4,6},{5,7},{6,4},{7,5},{8,10},{9,11},{10,... | collective-permute-start | bytes 3145736 | tf_op jit(solution)/shard_map/ppermute | solution.py:338
  424.2 46.7 %collective-permute-start.17 = (bf16[512,1024]{1,0:T(8,128)(2,1)S(1)}, bf16[512,1024]{1,0:T(8,128)(2,1)}, u32[]{:S(2)}, u32[]{:S(2)}) collective-permute-start(bf16[512,1024]{1,0:T(8,128)(2,1)S(1)} %fusion.22), channel_id=1, source_target_pairs={{0,2},{1,3},{2,0},{3,1},{4,6},{5,7},{6,4},{7,5},{8,10},{9,11},{10,... | collective-permute-start | bytes 3145736 | tf_op jit(solution)/shard_map/ppermute | solution.py:338
  468.9 66.0 %collective-permute-start.18 = (bf16[2,2,2048,128]{3,2,1,0:T(8,128)(2,1)}, bf16[2,2,2048,128]{3,2,1,0:T(8,128)(2,1)}, u32[]{:S(2)}, u32[]{:S(2)}) collective-permute-start(bf16[2,2,2048,128]{3,2,1,0:T(8,128)(2,1)} %fusion.5), channel_id=1, source_target_pairs={{0,4},{4,0},{8,12},{12,8},{16,20},{20,16},{24,28},{28,24},{1,5},{5... | collective-permute-start | bytes 6291464 | tf_op jit(solution)/shard_map/ppermute | solution.py:236
  559.3 13.8 %collective-permute-start.24 = (bf16[512,512]{0,1:T(8,128)(2,1)}, bf16[512,512]{0,1:T(8,128)(2,1)}, u32[]{:S(2)}, u32[]{:S(2)}) collective-permute-start(bf16[512,512]{0,1:T(8,128)(2,1)} %dynamic-slice_convert_fusion.8), channel_id=1, source_target_pairs={{0,4},{4,0},{8,12},{12,8},{16,20},{20,16},{24,28},{28,24},{1,5},{5... | collective-permute-start | bytes 1572872 | tf_op jit(solution)/shard_map/ppermute | solution.py:304
  575.2 43.0 %collective-permute-start.25 = (bf16[256,512]{0,1:T(8,128)(2,1)}, bf16[256,512]{0,1:T(8,128)(2,1)}, u32[]{:S(2)}, u32[]{:S(2)}) collective-permute-start(bf16[256,512]{0,1:T(8,128)(2,1)} %dynamic-slice_convert_fusion.10), channel_id=1, source_target_pairs={{0,8},{4,12},{8,0},{12,4},{16,24},{20,28},{24,16},{28,20},{1,9},{5... | collective-permute-start | bytes 786440 | tf_op jit(solution)/shard_map/ppermute | solution.py:304
  617.7 14.4 %collective-permute-start.21 = (bf16[512,512]{1,0:T(8,128)(2,1)S(1)}, bf16[512,512]{1,0:T(8,128)(2,1)S(1)}, u32[]{:S(2)}, u32[]{:S(2)}) collective-permute-start(bf16[512,512]{1,0:T(8,128)(2,1)S(1)} %dynamic-slice_convert_fusion.9), channel_id=1, source_target_pairs={{0,4},{4,0},{8,12},{12,8},{16,20},{20,16},{24,28},{28,24},{1,5},{5... | collective-permute-start | bytes 1572872 | tf_op jit(solution)/shard_map/ppermute | solution.py:304
  619.7 15.6 %collective-permute-start.26 = (bf16[128,512]{0,1:T(8,128)(2,1)S(1)}, bf16[128,512]{0,1:T(8,128)(2,1)S(1)}, u32[]{:S(2)}, u32[]{:S(2)}) collective-permute-start(bf16[128,512]{0,1:T(8,128)(2,1)S(1)} %dynamic-slice_convert_fusion.12), channel_id=1, source_target_pairs={{0,16},{4,20},{8,24},{12,28},{16,0},{20,4},{24,8},{28,12},{1,17},{... | collective-permute-start | bytes 393224 | tf_op jit(solution)/shard_map/ppermute | solution.py:304
  622.5 25.3 %collective-permute-start.20 = (bf16[512,1024]{1,0:T(8,128)(2,1)S(1)}, bf16[512,1024]{1,0:T(8,128)(2,1)S(1)}, u32[]{:S(2)}, u32[]{:S(2)}) collective-permute-start(bf16[512,1024]{1,0:T(8,128)(2,1)S(1)} %fusion.18), channel_id=1, source_target_pairs={{0,2},{1,3},{2,0},{3,1},{4,6},{5,7},{6,4},{7,5},{8,10},{9,11},{10,... | collective-permute-start | bytes 3145736 | tf_op jit(solution)/shard_map/ppermute | solution.py:338
  632.3 7.9 %collective-permute-start.22 = (bf16[256,512]{1,0:T(8,128)(2,1)S(1)}, bf16[256,512]{1,0:T(8,128)(2,1)S(1)}, u32[]{:S(2)}, u32[]{:S(2)}) collective-permute-start(bf16[256,512]{1,0:T(8,128)(2,1)S(1)} %dynamic-slice_convert_fusion.11), channel_id=1, source_target_pairs={{0,8},{4,12},{8,0},{12,4},{16,24},{20,28},{24,16},{28,20},{1,9},{5... | collective-permute-start | bytes 786440 | tf_op jit(solution)/shard_map/ppermute | solution.py:304
  651.5 11.8 %collective-permute-start.23 = (bf16[128,512]{1,0:T(8,128)(2,1)}, bf16[128,512]{1,0:T(8,128)(2,1)}, u32[]{:S(2)}, u32[]{:S(2)}) collective-permute-start(bf16[128,512]{1,0:T(8,128)(2,1)} %dynamic-slice_convert_fusion.13), channel_id=1, source_target_pairs={{0,16},{4,20},{8,24},{12,28},{16,0},{20,4},{24,8},{28,12},{1,17},{... | collective-permute-start | bytes 393224 | tf_op jit(solution)/shard_map/ppermute | solution.py:304
  653.8 8.2 %collective-permute-start.28 = (f32[2304]{0:T(1024)S(1)}, f32[2304]{0:T(1024)}, u32[]{:S(2)}, u32[]{:S(2)}) collective-permute-start(f32[2304]{0:T(1024)S(1)} %fusion.116), channel_id=1, source_target_pairs={{0,2},{1,3},{2,0},{3,1},{4,6},{5,7},{6,4},{7,5},{8,10},{9,11},{10,... | collective-permute-start | bytes 27656 | tf_op jit(solution)/shard_map/ppermute | solution.py:329
  (109 other events, 1263.9 us)
Sparse Core Ops, SparseCore 0:
  10.7 43.1 all-gather.5
  56.5 49.0 all-gather.3
  107.7 100.6 all-gather.7
  411.5 127.2 reduce-scatter.1

commit v11 on v10

--- a/solution.py
+++ b/solution.py
@@ -430,8 +430,8 @@
     gain_first = gain_in.astype(jnp.float32)
     first_all = token_gather(rms_scale(x_float, gain_first).astype(jnp.bfloat16))
     cotangent = out_grad.astype(jnp.float32) * local_valid[:, None].astype(jnp.float32)
-    mlp_grad_all = token_gather(cotangent.astype(jnp.bfloat16))
-    first_all, mlp_grad_all = lax.optimization_barrier((first_all, mlp_grad_all))
+    cotangent_low, first_all = lax.optimization_barrier((cotangent.astype(jnp.bfloat16), first_all))
+    mlp_grad_all = token_gather(cotangent_low)
     query_projected = jnp.dot(first_all, w_query, preferred_element_type=jnp.float32)
     key_projected = jnp.dot(first_all, w_key, preferred_element_type=jnp.float32)
     value_rows = (
@@ -461,6 +461,7 @@
     sums, totals_t = attention_forward(
         query_t, query_start, moved[0], moved[1], sums, totals, piece, quarter, 1
     )
+    mlp_grad_all, sums, totals_t = lax.optimization_barrier((mlp_grad_all, sums, totals_t))
     heads_t = sums / totals_t[..., :1]
     heads_out = jnp.transpose(heads_t, (2, 0, 1, 3))
     row_totals = jnp.transpose(totals_t[..., 0], (2, 0, 1))

time: 691 us -> 667 us (0.965)
  waiting for transfers between devices: 184 us -> 174 us
  matrix products: 103 us -> 95.7 us
    all_gather x1, waiting for transfers between devices: 0.01 us -> 21 us  [shards(): lax.all_gather(jnp.concatenate([q_weight.astype(jnp.bfloat16), jnp.transp...]
    ppermute x2, waiting for transfers between devices: 30.3 us -> 11.7 us  [swapped(): lax.ppermute(shard, axis, [(i, i ^ 1 << distance) for i in range(lax.axis...]
    ppermute x16, waiting for transfers between devices: 126 us -> 114 us  [exchange(): lax.ppermute(values, 'tensor', [(i, i ^ distance) for i in range(count)])]
    unnamed x210 -> x212, local copies, waits for them, and re-layouts: 33.2 us -> 35 us
    dynamic_update_slice x12 -> x13, local copies, waits for them, and re-layouts: 14.4 us -> 13.2 us  [token_gather(): full = lax.dynamic_update_slice_in_dim(full, part, place * rows, 0)]
  transfers between devices with their start and end apart: 36 -> 36, of which waited for: 21 -> 21; matrix products, arithmetic and copies ran while one was open for 33% -> 32% of each run, Pallas kernels for 20% -> 21%
where the time goes in v11:
time: 667 us; the launch traced here: 660 us
  waiting for transfers between devices  174 us (26%)
  Pallas kernels  135 us (20%)
  other arithmetic  104 us (16%)
  local copies, waits for them, and re-layouts  100 us (15%)
  matrix products  95.7 us (14%)
  starting transfers between devices  35.3 us (5%)
  between operations  16 us (2%)
    ppermute x16, waiting for transfers between devices, exchange(): lax.ppermute(values, 'tensor', [(i, i ^ distance) for i in range(count)])  114 us
    pallas_call x2, Pallas kernels, attention_backward(): pl.pallas_call(functools.partial(_bwd_kernel, scale=scale, block=block),...  83.2 us
    pallas_call x2, Pallas kernels, attention_forward(): pl.pallas_call(functools.partial(_fwd_kernel, scale=scale, block=block),...  52.1 us
    dot_general x7, matrix products, contract_last(): lax.dot_general(left, right, (((1,), (1,)), ((), ())), preferred_element_...  37.6 us
    unnamed x212, local copies, waits for them, and re-layouts  35 us
    dot_general x7, matrix products, contract_rows(): lax.dot_general(left, right, (((0,), (0,)), ((), ())), preferred_element_...  26.4 us
    all_gather x1, waiting for transfers between devices, shards(): lax.all_gather(jnp.concatenate([q_weight.astype(jnp.bfloat16), jnp.transp...  21 us
    ppermute x6, waiting for transfers between devices, halving_scatter(): lax.ppermute(send.astype(jnp.bfloat16), 'fsdp', [(i, i ^ 1 << bit) for i...  18.8 us
  transfers between devices with their start and end apart: 36, of which 21 were waited for; matrix products, arithmetic and copies ran while one was open for 32% of the time, Pallas kernels for 21%

profile of v11, /device:TPU:0, one launch (start us, length us, event | category | flops | bytes accessed | tf_op | source)
XLA Modules:
  0.0 659.8 jit_solution(18268298403927601721)
XLA Ops:
  35.8 15.1 %collective-permute-done.3 = bf16[512,1024]{1,0:T(8,128)(2,1)S(1)} collective-permute-done((bf16[512,1024]{1,0:T(8,128)(2,1)S(1)}, bf16[512,1024]{1,0:T(8,128)(2,1)S(1)}, u32[]{:S(2)}, u32[]{:S(2)}) %collective-permute-start.3) | collective-permute-done | bytes 1048608 | tf_op jit(solution)/shard_map/ppermute | solution.py:338
  72.4 5.2 convolution_convert_fusion.1
  91.7 21.0 %all-gather.4.cloned.1.call-done = bf16[1024,1024]{0,1:T(8,128)(2,1)} async-done(((bf16[128,1024]{0,1:T(8,128)(2,1)}), bf16[1024,1024]{0,1:T(8,128)(2,1)}) %all-gather.4.cloned.1.call-update) | async-done | bytes 2097168 | tf_op jit(solution)/shard_map/all_gather | solution.py:419
  136.4 28.8 %attn_fwd.2 = (f32[2,2,2048,128]{3,2,1,0:T(8,128)}, f32[2,2,2048,128]{3,2,1,0:T(8,128)}) custom-call(s32[7,10]{1,0:T(8,128)S(1)} %broadcast_select_fusion.3.tab_ref, bf16[2,2,2048,128]{3,2,1,0:T(8,128)(2,1)S(1)} %maximum_bitcast_fusion.q_ref, s32[2048,128]{1,0:T(8,128)S(1)} %broadcast_in_dim.45.qs_ref, ...), custom_call_target="tpu_custom_call", output_to_operand_aliasing={{0}: (5, {}), {1}: (6, {})} | custom-call | flops 5368709120 | bytes 20971520 | tf_op jit(solution)/shard_map/attn_fwd/pallas_call | solution.py:124
  168.0 23.3 %attn_fwd.3 = (f32[2,2,2048,128]{3,2,1,0:T(8,128)}, f32[2,2,2048,128]{3,2,1,0:T(8,128)}) custom-call(s32[7,8]{1,0:T(8,128)S(1)} %broadcast_select_fusion.5.tab_ref, bf16[2,2,2048,128]{3,2,1,0:T(8,128)(2,1)S(1)} %maximum_bitcast_fusion.q_ref, s32[2048,128]{1,0:T(8,128)S(1)} %broadcast_in_dim.45.qs_ref, ...), custom_call_target="tpu_custom_call", output_to_operand_aliasing={{0}: (5, {}), {1}: (6, {})} | custom-call | flops 4294967296 | bytes 16777216 | tf_op jit(solution)/shard_map/attn_fwd/pallas_call | solution.py:124
  215.3 6.0 fusion.46
  221.3 17.8 %collective-permute-done.9 = bf16[512,1024]{1,0:T(8,128)(2,1)} collective-permute-done((bf16[512,1024]{1,0:T(8,128)(2,1)S(1)}, bf16[512,1024]{1,0:T(8,128)(2,1)}, u32[]{:S(2)}, u32[]{:S(2)}) %collective-permute-start.9) | collective-permute-done | bytes 1048608 | tf_op jit(solution)/shard_map/ppermute | solution.py:338
  244.3 22.9 %collective-permute-done.10 = bf16[512,1024]{1,0:T(8,128)(2,1)S(1)} collective-permute-done((bf16[512,1024]{1,0:T(8,128)(2,1)S(1)}, bf16[512,1024]{1,0:T(8,128)(2,1)S(1)}, u32[]{:S(2)}, u32[]{:S(2)}) %collective-permute-start.10) | collective-permute-done | bytes 1048608 | tf_op jit(solution)/shard_map/ppermute | solution.py:338
  278.9 5.5 multiply_convert_fusion
  284.4 7.0 %fusion.40 = f32[2048,1024]{1,0:T(8,128)S(1)} fusion(bf16[2048,768]{1,0:T(8,128)(2,1)} %get-tuple-element.68, bf16[1024,2304]{0,1:T(8,128)(2,1)} %all-gather.8.cloned.1.call-done), kind=kOutput, calls=%fused_computation.132 | convolution fusion | flops 3221225472 | bytes 13107200 | tf_op jit(solution)/shard_map/dot_general | solution.py:276
  305.9 5.1 fusion.124
  311.1 6.9 %fusion.126 = bf16[1024,768]{1,0:T(8,128)(2,1)} fusion(bf16[2048,1024]{1,0:T(8,128)(2,1)} %fusion.61, bf16[2048,768]{1,0:T(8,128)(2,1)S(1)} %get-tuple-element.74), kind=kOutput, calls=%fused_computation.307 | convolution fusion | flops 3221225472 | bytes 8912896 | tf_op jit(solution)/shard_map/dot_general | solution.py:270
  318.0 11.6 %collective-permute-done.13 = bf16[512,1024]{1,0:T(8,128)(2,1)S(1)} collective-permute-done((bf16[512,1024]{1,0:T(8,128)(2,1)S(1)}, bf16[512,1024]{1,0:T(8,128)(2,1)S(1)}, u32[]{:S(2)}, u32[]{:S(2)}) %collective-permute-start.13) | collective-permute-done | bytes 1048608 | tf_op jit(solution)/shard_map/ppermute | solution.py:338
  334.1 22.9 %collective-permute-done.14 = bf16[512,1024]{1,0:T(8,128)(2,1)S(1)} collective-permute-done((bf16[512,1024]{1,0:T(8,128)(2,1)S(1)}, bf16[512,1024]{1,0:T(8,128)(2,1)S(1)}, u32[]{:S(2)}, u32[]{:S(2)}) %collective-permute-start.14) | collective-permute-done | bytes 1048608 | tf_op jit(solution)/shard_map/ppermute | solution.py:338
  372.0 7.1 %fusion.6 = (f32[2048,2,2]{0,2,1:T(2,128)S(1)}, bf16[2,2,2048,128]{3,2,1,0:T(8,128)(2,1)}) fusion(f32[2048,2,2,128]{3,0,2,1:T(8,128)} %copy.109, f32[2,2,2048,128]{3,2,1,0:T(8,128)} %get-tuple-element.61, f32[2,2,2048]{2,1,0:T(2,128)S(1)} %slice_reduce_fusion, f32[2048,2,2]{0,2,1:T(2,128)S(1)} %bitcast.249), kind=kLoop, calls=%fused_computation.30 | loop fusion | flops 5234688 | bytes 10584064 | tf_op jit(solution)/shard_map/reduce_sum | solution.py:532
  410.9 37.5 %attn_bwd.2 = (f32[2,2,2048,128]{3,2,1,0:T(8,128)}, f32[2,2048,128]{2,1,0:T(8,128)}, f32[2,2048,128]{2,1,0:T(8,128)}) custom-call(s32[7,8]{1,0:T(8,128)} %broadcast_select_fusion.4.tab_ref, bf16[2,2,2048,128]{3,2,1,0:T(8,128)(2,1)} %copy-done.1, bf16[2,2,2048,128]{3,2,1,0:T(8,128)(2,1)} %get-tuple-element.79.h_ref, ...), custom_call_target="tpu_custom_call", output_to_operand_aliasing={{0}: (7, {})} | custom-call | flops 10737418240 | bytes 20971520 | tf_op jit(solution)/shard_map/attn_bwd/pallas_call | solution.py:207
  457.7 45.8 %attn_bwd.3 = (f32[2,2,2048,128]{3,2,1,0:T(8,128)}, f32[2,2048,128]{2,1,0:T(8,128)}, f32[2,2048,128]{2,1,0:T(8,128)}) custom-call(s32[7,10]{1,0:T(8,128)} %broadcast_select_fusion.2.tab_ref, bf16[2,2,2048,128]{3,2,1,0:T(8,128)(2,1)} %copy-done.1, bf16[2,2,2048,128]{3,2,1,0:T(8,128)(2,1)} %get-tuple-element.79.h_ref, ...), custom_call_target="tpu_custom_call", output_to_operand_aliasing={{0}: (7, {})} | custom-call | flops 13421772800 | bytes 26214400 | tf_op jit(solution)/shard_map/attn_bwd/pallas_call | solution.py:207
  503.4 11.7 %collective-permute-done.18 = bf16[2,2,2048,128]{3,2,1,0:T(8,128)(2,1)} collective-permute-done((bf16[2,2,2048,128]{3,2,1,0:T(8,128)(2,1)}, bf16[2,2,2048,128]{3,2,1,0:T(8,128)(2,1)}, u32[]{:S(2)}, u32[]{:S(2)}) %collective-permute-start.18) | collective-permute-done | bytes 2097184 | tf_op jit(solution)/shard_map/ppermute | solution.py:236
  537.7 5.9 fusion.74
  543.5 6.9 %collective-permute-done.24 = bf16[512,512]{0,1:T(8,128)(2,1)} collective-permute-done((bf16[512,512]{0,1:T(8,128)(2,1)}, bf16[512,512]{0,1:T(8,128)(2,1)}, u32[]{:S(2)}, u32[]{:S(2)}) %collective-permute-start.24) | collective-permute-done | bytes 524320 | tf_op jit(solution)/shard_map/ppermute | solution.py:304
  582.3 5.7 fusion.68
  588.0 5.0 add_add_fusion
  600.9 7.4 %collective-permute-done.21 = bf16[512,512]{1,0:T(8,128)(2,1)S(1)} collective-permute-done((bf16[512,512]{1,0:T(8,128)(2,1)S(1)}, bf16[512,512]{1,0:T(8,128)(2,1)S(1)}, u32[]{:S(2)}, u32[]{:S(2)}) %collective-permute-start.21) | collective-permute-done | bytes 524320 | tf_op jit(solution)/shard_map/ppermute | solution.py:304
  616.7 7.7 %collective-permute-done.20 = bf16[512,1024]{1,0:T(8,128)(2,1)S(1)} collective-permute-done((bf16[512,1024]{1,0:T(8,128)(2,1)S(1)}, bf16[512,1024]{1,0:T(8,128)(2,1)S(1)}, u32[]{:S(2)}, u32[]{:S(2)}) %collective-permute-start.20) | collective-permute-done | bytes 1048608 | tf_op jit(solution)/shard_map/ppermute | solution.py:338
  (457 shorter events, 303.9 us)
Async XLA Ops:
  7.2 57.9 %all-gather.6.cloned.1.call-start = ((), (), s32[]{:S(2)}) async-start(), calls=%async_computation.2 | async-start | bytes 1179648 | tf_op jit(solution)/shard_map/all_gather | solution.py:410
  9.9 102.7 %all-gather.4.cloned.1.call-start = ((), (), s32[]{:S(2)}) async-start(), calls=%async_computation.1 | async-start | bytes 2359296 | tf_op jit(solution)/shard_map/all_gather | solution.py:419
  12.7 202.6 %all-gather.8.cloned.1.call-start = ((), (), s32[]{:S(2)}) async-start(), calls=%async_computation.3 | async-start | bytes 5308416 | tf_op jit(solution)/shard_map/all_gather | solution.py:470
  29.2 21.7 %collective-permute-start.3 = (bf16[512,1024]{1,0:T(8,128)(2,1)S(1)}, bf16[512,1024]{1,0:T(8,128)(2,1)S(1)}, u32[]{:S(2)}, u32[]{:S(2)}) collective-permute-start(bf16[512,1024]{1,0:T(8,128)(2,1)S(1)} %get-tuple-element.162), channel_id=1, source_target_pairs={{0,2},{1,3},{2,0},{3,1},{4,6},{5,7},{6,4},{7,5},{8,10},{9,11},{10,... | collective-permute-start | bytes 3145736 | tf_op jit(solution)/shard_map/ppermute | solution.py:338
  34.3 519.2 %reduce-scatter.2.cloned.1.call-start = ((), (), s32[]{:S(2)}) async-start(), calls=%async_computation.4 | async-start | bytes 6488064 | tf_op jit(solution)/shard_map/reduce_scatter | solution.py:540
  52.5 8.1 %collective-permute-start.4 = (bf16[2,512,1024]{2,1,0:T(8,128)(2,1)}, bf16[2,512,1024]{2,1,0:T(8,128)(2,1)}, u32[]{:S(2)}, u32[]{:S(2)}) collective-permute-start(bf16[2,512,1024]{2,1,0:T(8,128)(2,1)} %pad_maximum_fusion.1), channel_id=1, source_target_pairs={{0,1},{1,0},{2,3},{3,2},{4,5},{5,4},{6,7},{7,6},{8,9},{9,8},{10,11... | collective-permute-start | bytes 6291464 | tf_op jit(solution)/shard_map/ppermute | solution.py:338
  85.0 81.3 %collective-permute-start.7 = (bf16[2,2,2048,128]{3,2,1,0:T(8,128)(2,1)}, bf16[2,2,2048,128]{3,2,1,0:T(8,128)(2,1)}, u32[]{:S(2)}, u32[]{:S(2)}) collective-permute-start(bf16[2,2,2048,128]{3,2,1,0:T(8,128)(2,1)} %pad_maximum_fusion.3), channel_id=1, source_target_pairs={{0,4},{4,0},{8,12},{12,8},{16,20},{20,16},{24,28},{28,24},{1,5},{5... | collective-permute-start | bytes 6291464 | tf_op jit(solution)/shard_map/ppermute | solution.py:236
  86.5 33.0 %collective-permute-start.5 = (bf16[512,1024]{1,0:T(8,128)(2,1)S(1)}, bf16[512,1024]{1,0:T(8,128)(2,1)S(1)}, u32[]{:S(2)}, u32[]{:S(2)}) collective-permute-start(bf16[512,1024]{1,0:T(8,128)(2,1)S(1)} %copy-done.20), channel_id=1, source_target_pairs={{0,2},{1,3},{2,0},{3,1},{4,6},{5,7},{6,4},{7,5},{8,10},{9,11},{10,... | collective-permute-start | bytes 3145736 | tf_op jit(solution)/shard_map/ppermute | solution.py:338
  121.2 70.2 %collective-permute-start.6 = (bf16[2,512,1024]{2,1,0:T(8,128)(2,1)}, bf16[2,512,1024]{2,1,0:T(8,128)(2,1)}, u32[]{:S(2)}, u32[]{:S(2)}) collective-permute-start(bf16[2,512,1024]{2,1,0:T(8,128)(2,1)} %pad_maximum_fusion.2), channel_id=1, source_target_pairs={{0,1},{1,0},{2,3},{3,2},{4,5},{5,4},{6,7},{7,6},{8,9},{9,8},{10,11... | collective-permute-start | bytes 6291464 | tf_op jit(solution)/shard_map/ppermute | solution.py:338
  213.9 25.3 %collective-permute-start.9 = (bf16[512,1024]{1,0:T(8,128)(2,1)S(1)}, bf16[512,1024]{1,0:T(8,128)(2,1)}, u32[]{:S(2)}, u32[]{:S(2)}) collective-permute-start(bf16[512,1024]{1,0:T(8,128)(2,1)S(1)} %fusion.30), channel_id=1, source_target_pairs={{0,2},{1,3},{2,0},{3,1},{4,6},{5,7},{6,4},{7,5},{8,10},{9,11},{10,... | collective-permute-start | bytes 3145736 | tf_op jit(solution)/shard_map/ppermute | solution.py:338
  242.8 24.4 %collective-permute-start.10 = (bf16[512,1024]{1,0:T(8,128)(2,1)S(1)}, bf16[512,1024]{1,0:T(8,128)(2,1)S(1)}, u32[]{:S(2)}, u32[]{:S(2)}) collective-permute-start(bf16[512,1024]{1,0:T(8,128)(2,1)S(1)} %get-tuple-element.160), channel_id=1, source_target_pairs={{0,2},{1,3},{2,0},{3,1},{4,6},{5,7},{6,4},{7,5},{8,10},{9,11},{10,... | collective-permute-start | bytes 3145736 | tf_op jit(solution)/shard_map/ppermute | solution.py:338
  296.8 6.7 %collective-permute-start.12 = (bf16[2,512,1024]{2,1,0:T(8,128)(2,1)S(1)}, bf16[2,512,1024]{2,1,0:T(8,128)(2,1)S(1)}, u32[]{:S(2)}, u32[]{:S(2)}) collective-permute-start(bf16[2,512,1024]{2,1,0:T(8,128)(2,1)S(1)} %pad_maximum_fusion.6), channel_id=1, source_target_pairs={{0,1},{1,0},{2,3},{3,2},{4,5},{5,4},{6,7},{7,6},{8,9},{9,8},{10,11... | collective-permute-start | bytes 6291464 | tf_op jit(solution)/shard_map/ppermute | solution.py:338
  304.3 25.3 %collective-permute-start.13 = (bf16[512,1024]{1,0:T(8,128)(2,1)S(1)}, bf16[512,1024]{1,0:T(8,128)(2,1)S(1)}, u32[]{:S(2)}, u32[]{:S(2)}) collective-permute-start(bf16[512,1024]{1,0:T(8,128)(2,1)S(1)} %fusion.26), channel_id=1, source_target_pairs={{0,2},{1,3},{2,0},{3,1},{4,6},{5,7},{6,4},{7,5},{8,10},{9,11},{10,... | collective-permute-start | bytes 3145736 | tf_op jit(solution)/shard_map/ppermute | solution.py:338
  332.7 24.4 %collective-permute-start.14 = (bf16[512,1024]{1,0:T(8,128)(2,1)S(1)}, bf16[512,1024]{1,0:T(8,128)(2,1)S(1)}, u32[]{:S(2)}, u32[]{:S(2)}) collective-permute-start(bf16[512,1024]{1,0:T(8,128)(2,1)S(1)} %get-tuple-element.157), channel_id=1, source_target_pairs={{0,2},{1,3},{2,0},{3,1},{4,6},{5,7},{6,4},{7,5},{8,10},{9,11},{10,... | collective-permute-start | bytes 3145736 | tf_op jit(solution)/shard_map/ppermute | solution.py:338
  407.1 46.0 %collective-permute-start.17 = (bf16[512,1024]{1,0:T(8,128)(2,1)S(1)}, bf16[512,1024]{1,0:T(8,128)(2,1)}, u32[]{:S(2)}, u32[]{:S(2)}) collective-permute-start(bf16[512,1024]{1,0:T(8,128)(2,1)S(1)} %fusion.22), channel_id=1, source_target_pairs={{0,2},{1,3},{2,0},{3,1},{4,6},{5,7},{6,4},{7,5},{8,10},{9,11},{10,... | collective-permute-start | bytes 3145736 | tf_op jit(solution)/shard_map/ppermute | solution.py:338
  451.9 63.2 %collective-permute-start.18 = (bf16[2,2,2048,128]{3,2,1,0:T(8,128)(2,1)}, bf16[2,2,2048,128]{3,2,1,0:T(8,128)(2,1)}, u32[]{:S(2)}, u32[]{:S(2)}) collective-permute-start(bf16[2,2,2048,128]{3,2,1,0:T(8,128)(2,1)} %fusion.5), channel_id=1, source_target_pairs={{0,4},{4,0},{8,12},{12,8},{16,20},{20,16},{24,28},{28,24},{1,5},{5... | collective-permute-start | bytes 6291464 | tf_op jit(solution)/shard_map/ppermute | solution.py:236
  537.3 13.2 %collective-permute-start.24 = (bf16[512,512]{0,1:T(8,128)(2,1)}, bf16[512,512]{0,1:T(8,128)(2,1)}, u32[]{:S(2)}, u32[]{:S(2)}) collective-permute-start(bf16[512,512]{0,1:T(8,128)(2,1)} %dynamic-slice_convert_fusion.8), channel_id=1, source_target_pairs={{0,4},{4,0},{8,12},{12,8},{16,20},{20,16},{24,28},{28,24},{1,5},{5... | collective-permute-start | bytes 1572872 | tf_op jit(solution)/shard_map/ppermute | solution.py:304
  553.4 41.3 %collective-permute-start.25 = (bf16[256,512]{0,1:T(8,128)(2,1)}, bf16[256,512]{0,1:T(8,128)(2,1)}, u32[]{:S(2)}, u32[]{:S(2)}) collective-permute-start(bf16[256,512]{0,1:T(8,128)(2,1)} %dynamic-slice_convert_fusion.10), channel_id=1, source_target_pairs={{0,8},{4,12},{8,0},{12,4},{16,24},{20,28},{24,16},{28,20},{1,9},{5... | collective-permute-start | bytes 786440 | tf_op jit(solution)/shard_map/ppermute | solution.py:304
  594.0 14.4 %collective-permute-start.21 = (bf16[512,512]{1,0:T(8,128)(2,1)S(1)}, bf16[512,512]{1,0:T(8,128)(2,1)S(1)}, u32[]{:S(2)}, u32[]{:S(2)}) collective-permute-start(bf16[512,512]{1,0:T(8,128)(2,1)S(1)} %dynamic-slice_convert_fusion.9), channel_id=1, source_target_pairs={{0,4},{4,0},{8,12},{12,8},{16,20},{20,16},{24,28},{28,24},{1,5},{5... | collective-permute-start | bytes 1572872 | tf_op jit(solution)/shard_map/ppermute | solution.py:304
  596.0 16.1 %collective-permute-start.26 = (bf16[128,512]{0,1:T(8,128)(2,1)S(1)}, bf16[128,512]{0,1:T(8,128)(2,1)S(1)}, u32[]{:S(2)}, u32[]{:S(2)}) collective-permute-start(bf16[128,512]{0,1:T(8,128)(2,1)S(1)} %dynamic-slice_convert_fusion.12), channel_id=1, source_target_pairs={{0,16},{4,20},{8,24},{12,28},{16,0},{20,4},{24,8},{28,12},{1,17},{... | collective-permute-start | bytes 393224 | tf_op jit(solution)/shard_map/ppermute | solution.py:304
  599.1 25.3 %collective-permute-start.20 = (bf16[512,1024]{1,0:T(8,128)(2,1)S(1)}, bf16[512,1024]{1,0:T(8,128)(2,1)S(1)}, u32[]{:S(2)}, u32[]{:S(2)}) collective-permute-start(bf16[512,1024]{1,0:T(8,128)(2,1)S(1)} %fusion.18), channel_id=1, source_target_pairs={{0,2},{1,3},{2,0},{3,1},{4,6},{5,7},{6,4},{7,5},{8,10},{9,11},{10,... | collective-permute-start | bytes 3145736 | tf_op jit(solution)/shard_map/ppermute | solution.py:338
  608.6 8.1 %collective-permute-start.22 = (bf16[256,512]{1,0:T(8,128)(2,1)S(1)}, bf16[256,512]{1,0:T(8,128)(2,1)S(1)}, u32[]{:S(2)}, u32[]{:S(2)}) collective-permute-start(bf16[256,512]{1,0:T(8,128)(2,1)S(1)} %dynamic-slice_convert_fusion.11), channel_id=1, source_target_pairs={{0,8},{4,12},{8,0},{12,4},{16,24},{20,28},{24,16},{28,20},{1,9},{5... | collective-permute-start | bytes 786440 | tf_op jit(solution)/shard_map/ppermute | solution.py:304
  628.1 12.1 %collective-permute-start.23 = (bf16[128,512]{1,0:T(8,128)(2,1)}, bf16[128,512]{1,0:T(8,128)(2,1)}, u32[]{:S(2)}, u32[]{:S(2)}) collective-permute-start(bf16[128,512]{1,0:T(8,128)(2,1)} %dynamic-slice_convert_fusion.13), channel_id=1, source_target_pairs={{0,16},{4,20},{8,24},{12,28},{16,0},{20,4},{24,8},{28,12},{1,17},{... | collective-permute-start | bytes 393224 | tf_op jit(solution)/shard_map/ppermute | solution.py:304
  630.4 8.5 %collective-permute-start.28 = (f32[2304]{0:T(1024)S(1)}, f32[2304]{0:T(1024)}, u32[]{:S(2)}, u32[]{:S(2)}) collective-permute-start(f32[2304]{0:T(1024)S(1)} %fusion.116), channel_id=1, source_target_pairs={{0,2},{1,3},{2,0},{3,1},{4,6},{5,7},{6,4},{7,5},{8,10},{9,11},{10,... | collective-permute-start | bytes 27656 | tf_op jit(solution)/shard_map/ppermute | solution.py:329
  (110 other events, 1241.7 us)
Sparse Core Ops, SparseCore 0:
  10.7 43.0 all-gather.5
  56.4 56.1 all-gather.3
  114.7 85.1 all-gather.7
  394.4 122.0 reduce-scatter.1

commit v12 on v11

--- a/solution.py
+++ b/solution.py
@@ -416,16 +416,7 @@
         tiled=True,
     )
     w_key, w_value = split_columns(kv_full, (key_matrix.shape[1], value_matrix.shape[1]))
-    qo_full = lax.all_gather(
-        jnp.concatenate(
-            [q_weight.astype(jnp.bfloat16), jnp.transpose(o_weight).astype(jnp.bfloat16)],
-            axis=1,
-        ),
-        "fsdp",
-        axis=0,
-        tiled=True,
-    )
-    w_query, w_out = split_columns(qo_full, (q_weight.shape[1], o_weight.shape[0]))
+    w_query = lax.all_gather(q_weight.astype(jnp.bfloat16), "fsdp", axis=0, tiled=True)
     x_float = hidden.astype(jnp.float32)
     gain_first = gain_in.astype(jnp.float32)
     first_all = token_gather(rms_scale(x_float, gain_first).astype(jnp.bfloat16))
@@ -473,6 +464,7 @@
                 gate_weight.astype(jnp.bfloat16),
                 up_weight.astype(jnp.bfloat16),
                 jnp.transpose(down_weight).astype(jnp.bfloat16),
+                jnp.transpose(o_weight).astype(jnp.bfloat16),
             ],
             axis=1,
         ),
@@ -480,8 +472,8 @@
         axis=0,
         tiled=True,
     )
-    w_gate, w_up, w_down_t = split_columns(
-        mlp_full, (gate_weight.shape[1], up_weight.shape[1], down_weight.shape[0])
+    w_gate, w_up, w_down_t, w_out = split_columns(
+        mlp_full, (gate_weight.shape[1], up_weight.shape[1], down_weight.shape[0], o_weight.shape[0])
     )
     out_partial = contract_last(out_rows, w_out)
     late_grad_all, out_partial = lax.optimization_barrier((mlp_grad_all, out_partial))

time: 667 us -> 664 us (level)
    ppermute x16, waiting for transfers between devices: 114 us -> 133 us  [exchange(): lax.ppermute(values, 'tensor', [(i, i ^ distance) for i in range(count)])]
    all_gather x1, waiting for transfers between devices: 21 us -> 5.1 us  [shards(): lax.all_gather(q_weight.astype(jnp.bfloat16), 'fsdp', axis=0, tiled=True)]
    unnamed x212 -> x213, local copies, waits for them, and re-layouts: 35 us -> 36.2 us
  transfers between devices with their start and end apart: 36 -> 36, of which waited for: 21 -> 22; matrix products, arithmetic and copies ran while one was open for 32% -> 30% of each run, Pallas kernels for 21% -> 21%
where the time goes in v12:
time: 664 us; the launch traced here: 657 us
  waiting for transfers between devices  177 us (27%)
  Pallas kernels  135 us (20%)
  other arithmetic  104 us (16%)
  local copies, waits for them, and re-layouts  95.2 us (14%)
  matrix products  94.2 us (14%)
  starting transfers between devices  34.9 us (5%)
  between operations  15.9 us (2%)
    ppermute x16, waiting for transfers between devices, exchange(): lax.ppermute(values, 'tensor', [(i, i ^ distance) for i in range(count)])  133 us
    pallas_call x2, Pallas kernels, attention_backward(): pl.pallas_call(functools.partial(_bwd_kernel, scale=scale, block=block),...  83.2 us
    pallas_call x2, Pallas kernels, attention_forward(): pl.pallas_call(functools.partial(_fwd_kernel, scale=scale, block=block),...  52.2 us
    dot_general x7, matrix products, contract_last(): lax.dot_general(left, right, (((1,), (1,)), ((), ())), preferred_element_...  37.8 us
    unnamed x213, local copies, waits for them, and re-layouts  36.2 us
    dot_general x7, matrix products, contract_rows(): lax.dot_general(left, right, (((0,), (0,)), ((), ())), preferred_element_...  24.2 us
    ppermute x6, waiting for transfers between devices, halving_scatter(): lax.ppermute(send.astype(jnp.bfloat16), 'fsdp', [(i, i ^ 1 << bit) for i...  20.2 us
    another operation x9, local copies, waits for them, and re-layouts  13.7 us
  transfers between devices with their start and end apart: 36, of which 22 were waited for; matrix products, arithmetic and copies ran while one was open for 30% of the time, Pallas kernels for 21%

profile of v12, /device:TPU:0, one launch (start us, length us, event | category | flops | bytes accessed | tf_op | source)
XLA Modules:
  0.0 656.6 jit_solution(3982323820939192702)
XLA Ops:
  35.0 17.6 %collective-permute-done.3 = bf16[512,1024]{1,0:T(8,128)(2,1)S(1)} collective-permute-done((bf16[512,1024]{1,0:T(8,128)(2,1)S(1)}, bf16[512,1024]{1,0:T(8,128)(2,1)S(1)}, u32[]{:S(2)}, u32[]{:S(2)}) %collective-permute-start.3) | collective-permute-done | bytes 1048608 | tf_op jit(solution)/shard_map/ppermute | solution.py:338
  67.4 5.0 multiply_reduce_fusion.8
  74.7 5.2 convolution_convert_fusion.1
  90.4 5.1 all-gather.4.cloned.1.call-done
  102.4 11.7 %collective-permute-done.5 = bf16[512,1024]{1,0:T(8,128)(2,1)S(1)} collective-permute-done((bf16[512,1024]{1,0:T(8,128)(2,1)S(1)}, bf16[512,1024]{1,0:T(8,128)(2,1)S(1)}, u32[]{:S(2)}, u32[]{:S(2)}) %collective-permute-start.5) | collective-permute-done | bytes 1048608 | tf_op jit(solution)/shard_map/ppermute | solution.py:338
  130.9 29.3 %attn_fwd.2 = (f32[2,2,2048,128]{3,2,1,0:T(8,128)}, f32[2,2,2048,128]{3,2,1,0:T(8,128)}) custom-call(s32[7,10]{1,0:T(8,128)S(1)} %broadcast_select_fusion.3.tab_ref, bf16[2,2,2048,128]{3,2,1,0:T(8,128)(2,1)S(1)} %maximum_bitcast_fusion.q_ref, s32[2048,128]{1,0:T(8,128)S(1)} %broadcast_in_dim.45.qs_ref, ...), custom_call_target="tpu_custom_call", output_to_operand_aliasing={{0}: (5, {}), {1}: (6, {})} | custom-call | flops 5368709120 | bytes 20971520 | tf_op jit(solution)/shard_map/attn_fwd/pallas_call | solution.py:124
  162.1 22.9 %attn_fwd.3 = (f32[2,2,2048,128]{3,2,1,0:T(8,128)}, f32[2,2,2048,128]{3,2,1,0:T(8,128)}) custom-call(s32[7,8]{1,0:T(8,128)S(1)} %broadcast_select_fusion.5.tab_ref, bf16[2,2,2048,128]{3,2,1,0:T(8,128)(2,1)S(1)} %maximum_bitcast_fusion.q_ref, s32[2048,128]{1,0:T(8,128)S(1)} %broadcast_in_dim.45.qs_ref, ...), custom_call_target="tpu_custom_call", output_to_operand_aliasing={{0}: (5, {}), {1}: (6, {})} | custom-call | flops 4294967296 | bytes 16777216 | tf_op jit(solution)/shard_map/attn_fwd/pallas_call | solution.py:124
  212.7 19.9 %collective-permute-done.9 = bf16[512,1024]{1,0:T(8,128)(2,1)S(1)} collective-permute-done((bf16[512,1024]{1,0:T(8,128)(2,1)S(1)}, bf16[512,1024]{1,0:T(8,128)(2,1)S(1)}, u32[]{:S(2)}, u32[]{:S(2)}) %collective-permute-start.9) | collective-permute-done | bytes 1048608 | tf_op jit(solution)/shard_map/ppermute | solution.py:338
  236.1 22.8 %collective-permute-done.10 = bf16[512,1024]{1,0:T(8,128)(2,1)S(1)} collective-permute-done((bf16[512,1024]{1,0:T(8,128)(2,1)S(1)}, bf16[512,1024]{1,0:T(8,128)(2,1)S(1)}, u32[]{:S(2)}, u32[]{:S(2)}) %collective-permute-start.10) | collective-permute-done | bytes 1048608 | tf_op jit(solution)/shard_map/ppermute | solution.py:338
  267.1 5.0 fusion.42
  272.1 5.3 multiply_convert_fusion
  277.5 7.1 %fusion.40 = f32[2048,1024]{1,0:T(8,128)S(1)} fusion(bf16[2048,768]{1,0:T(8,128)(2,1)} %get-tuple-element.68, bf16[1024,2816]{0,1:T(8,128)(2,1)} %all-gather.8.cloned.1.call-done), kind=kOutput, calls=%fused_computation.132 | convolution fusion | flops 3221225472 | bytes 13107200 | tf_op jit(solution)/shard_map/dot_general | solution.py:276
  291.9 5.2 fusion.121
  308.9 14.2 %collective-permute-done.13 = bf16[512,1024]{1,0:T(8,128)(2,1)S(1)} collective-permute-done((bf16[512,1024]{1,0:T(8,128)(2,1)S(1)}, bf16[512,1024]{1,0:T(8,128)(2,1)S(1)}, u32[]{:S(2)}, u32[]{:S(2)}) %collective-permute-start.13) | collective-permute-done | bytes 1048608 | tf_op jit(solution)/shard_map/ppermute | solution.py:338
  327.8 22.8 %collective-permute-done.14 = bf16[512,1024]{1,0:T(8,128)(2,1)S(1)} collective-permute-done((bf16[512,1024]{1,0:T(8,128)(2,1)S(1)}, bf16[512,1024]{1,0:T(8,128)(2,1)S(1)}, u32[]{:S(2)}, u32[]{:S(2)}) %collective-permute-start.14) | collective-permute-done | bytes 1048608 | tf_op jit(solution)/shard_map/ppermute | solution.py:338
  366.8 7.2 %fusion.6 = (f32[2048,2,2]{0,2,1:T(2,128)S(1)}, bf16[2,2,2048,128]{3,2,1,0:T(8,128)(2,1)}) fusion(f32[2048,2,2,128]{3,0,2,1:T(8,128)} %copy.105, f32[2,2,2048,128]{3,2,1,0:T(8,128)} %get-tuple-element.61, f32[2,2,2048]{2,1,0:T(2,128)S(1)} %slice_reduce_fusion, f32[2048,2,2]{0,2,1:T(2,128)S(1)} %bitcast.251), kind=kLoop, calls=%fused_computation.30 | loop fusion | flops 5234688 | bytes 10584064 | tf_op jit(solution)/shard_map/reduce_sum | solution.py:524
  405.9 37.6 %attn_bwd.2 = (f32[2,2,2048,128]{3,2,1,0:T(8,128)}, f32[2,2048,128]{2,1,0:T(8,128)}, f32[2,2048,128]{2,1,0:T(8,128)}) custom-call(s32[7,8]{1,0:T(8,128)} %broadcast_select_fusion.4.tab_ref, bf16[2,2,2048,128]{3,2,1,0:T(8,128)(2,1)} %copy-done.1, bf16[2,2,2048,128]{3,2,1,0:T(8,128)(2,1)} %get-tuple-element.79.h_ref, ...), custom_call_target="tpu_custom_call", output_to_operand_aliasing={{0}: (7, {})} | custom-call | flops 10737418240 | bytes 20971520 | tf_op jit(solution)/shard_map/attn_bwd/pallas_call | solution.py:207
  453.5 45.6 %attn_bwd.3 = (f32[2,2,2048,128]{3,2,1,0:T(8,128)}, f32[2,2048,128]{2,1,0:T(8,128)}, f32[2,2048,128]{2,1,0:T(8,128)}) custom-call(s32[7,10]{1,0:T(8,128)} %broadcast_select_fusion.2.tab_ref, bf16[2,2,2048,128]{3,2,1,0:T(8,128)(2,1)} %copy-done.1, bf16[2,2,2048,128]{3,2,1,0:T(8,128)(2,1)} %get-tuple-element.79.h_ref, ...), custom_call_target="tpu_custom_call", output_to_operand_aliasing={{0}: (7, {})} | custom-call | flops 13421772800 | bytes 26214400 | tf_op jit(solution)/shard_map/attn_bwd/pallas_call | solution.py:207
  499.1 12.0 %collective-permute-done.18 = bf16[2,2,2048,128]{3,2,1,0:T(8,128)(2,1)} collective-permute-done((bf16[2,2,2048,128]{3,2,1,0:T(8,128)(2,1)}, bf16[2,2,2048,128]{3,2,1,0:T(8,128)(2,1)}, u32[]{:S(2)}, u32[]{:S(2)}) %collective-permute-start.18) | collective-permute-done | bytes 2097184 | tf_op jit(solution)/shard_map/ppermute | solution.py:236
  533.9 5.8 fusion.70
  539.7 7.3 %collective-permute-done.24 = bf16[512,512]{0,1:T(8,128)(2,1)} collective-permute-done((bf16[512,512]{0,1:T(8,128)(2,1)}, bf16[512,512]{0,1:T(8,128)(2,1)}, u32[]{:S(2)}, u32[]{:S(2)}) %collective-permute-start.24) | collective-permute-done | bytes 524320 | tf_op jit(solution)/shard_map/ppermute | solution.py:304
  579.5 5.8 fusion.123
  597.7 7.9 %collective-permute-done.21 = bf16[512,512]{1,0:T(8,128)(2,1)S(1)} collective-permute-done((bf16[512,512]{1,0:T(8,128)(2,1)S(1)}, bf16[512,512]{1,0:T(8,128)(2,1)S(1)}, u32[]{:S(2)}, u32[]{:S(2)}) %collective-permute-start.21) | collective-permute-done | bytes 524320 | tf_op jit(solution)/shard_map/ppermute | solution.py:304
  613.9 7.7 %collective-permute-done.20 = bf16[512,1024]{1,0:T(8,128)(2,1)S(1)} collective-permute-done((bf16[512,1024]{1,0:T(8,128)(2,1)S(1)}, bf16[512,1024]{1,0:T(8,128)(2,1)S(1)}, u32[]{:S(2)}, u32[]{:S(2)}) %collective-permute-start.20) | collective-permute-done | bytes 1048608 | tf_op jit(solution)/shard_map/ppermute | solution.py:338
  (458 shorter events, 304.5 us)
Async XLA Ops:
  7.2 60.2 %all-gather.6.cloned.1.call-start = ((), (), s32[]{:S(2)}) async-start(), calls=%async_computation.2 | async-start | bytes 1179648 | tf_op jit(solution)/shard_map/all_gather | solution.py:410
  9.7 85.7 %all-gather.4.cloned.1.call-start = ((), (), s32[]{:S(2)}) async-start(), calls=%async_computation.1 | async-start | bytes 1179648 | tf_op jit(solution)/shard_map/all_gather | solution.py:419
  17.1 180.3 %all-gather.8.cloned.1.call-start = ((), (), s32[]{:S(2)}) async-start(), calls=%async_computation.3 | async-start | bytes 6488064 | tf_op jit(solution)/shard_map/all_gather | solution.py:461
  29.9 22.6 %collective-permute-start.3 = (bf16[512,1024]{1,0:T(8,128)(2,1)S(1)}, bf16[512,1024]{1,0:T(8,128)(2,1)S(1)}, u32[]{:S(2)}, u32[]{:S(2)}) collective-permute-start(bf16[512,1024]{1,0:T(8,128)(2,1)S(1)} %get-tuple-element.162), channel_id=1, source_target_pairs={{0,2},{1,3},{2,0},{3,1},{4,6},{5,7},{6,4},{7,5},{8,10},{9,11},{10,... | collective-permute-start | bytes 3145736 | tf_op jit(solution)/shard_map/ppermute | solution.py:338
  34.0 516.6 %reduce-scatter.2.cloned.1.call-start = ((), (), s32[]{:S(2)}) async-start(), calls=%async_computation.4 | async-start | bytes 6488064 | tf_op jit(solution)/shard_map/reduce_scatter | solution.py:532
  54.1 8.8 %collective-permute-start.4 = (bf16[2,512,1024]{2,1,0:T(8,128)(2,1)}, bf16[2,512,1024]{2,1,0:T(8,128)(2,1)}, u32[]{:S(2)}, u32[]{:S(2)}) collective-permute-start(bf16[2,512,1024]{2,1,0:T(8,128)(2,1)} %pad_maximum_fusion.1), channel_id=1, source_target_pairs={{0,1},{1,0},{2,3},{3,2},{4,5},{5,4},{6,7},{7,6},{8,9},{9,8},{10,11... | collective-permute-start | bytes 6291464 | tf_op jit(solution)/shard_map/ppermute | solution.py:338
  87.8 72.6 %collective-permute-start.7 = (bf16[2,2,2048,128]{3,2,1,0:T(8,128)(2,1)}, bf16[2,2,2048,128]{3,2,1,0:T(8,128)(2,1)}, u32[]{:S(2)}, u32[]{:S(2)}) collective-permute-start(bf16[2,2,2048,128]{3,2,1,0:T(8,128)(2,1)} %pad_maximum_fusion.3), channel_id=1, source_target_pairs={{0,4},{4,0},{8,12},{12,8},{16,20},{20,16},{24,28},{28,24},{1,5},{5... | collective-permute-start | bytes 6291464 | tf_op jit(solution)/shard_map/ppermute | solution.py:236
  88.8 25.3 %collective-permute-start.5 = (bf16[512,1024]{1,0:T(8,128)(2,1)S(1)}, bf16[512,1024]{1,0:T(8,128)(2,1)S(1)}, u32[]{:S(2)}, u32[]{:S(2)}) collective-permute-start(bf16[512,1024]{1,0:T(8,128)(2,1)S(1)} %copy-done.18), channel_id=1, source_target_pairs={{0,2},{1,3},{2,0},{3,1},{4,6},{5,7},{6,4},{7,5},{8,10},{9,11},{10,... | collective-permute-start | bytes 3145736 | tf_op jit(solution)/shard_map/ppermute | solution.py:338
  115.8 69.2 %collective-permute-start.6 = (bf16[2,512,1024]{2,1,0:T(8,128)(2,1)}, bf16[2,512,1024]{2,1,0:T(8,128)(2,1)}, u32[]{:S(2)}, u32[]{:S(2)}) collective-permute-start(bf16[2,512,1024]{2,1,0:T(8,128)(2,1)} %pad_maximum_fusion.2), channel_id=1, source_target_pairs={{0,1},{1,0},{2,3},{3,2},{4,5},{5,4},{6,7},{7,6},{8,9},{9,8},{10,11... | collective-permute-start | bytes 6291464 | tf_op jit(solution)/shard_map/ppermute | solution.py:338
  207.4 25.3 %collective-permute-start.9 = (bf16[512,1024]{1,0:T(8,128)(2,1)S(1)}, bf16[512,1024]{1,0:T(8,128)(2,1)S(1)}, u32[]{:S(2)}, u32[]{:S(2)}) collective-permute-start(bf16[512,1024]{1,0:T(8,128)(2,1)S(1)} %fusion.30), channel_id=1, source_target_pairs={{0,2},{1,3},{2,0},{3,1},{4,6},{5,7},{6,4},{7,5},{8,10},{9,11},{10,... | collective-permute-start | bytes 3145736 | tf_op jit(solution)/shard_map/ppermute | solution.py:338
  234.5 24.4 %collective-permute-start.10 = (bf16[512,1024]{1,0:T(8,128)(2,1)S(1)}, bf16[512,1024]{1,0:T(8,128)(2,1)S(1)}, u32[]{:S(2)}, u32[]{:S(2)}) collective-permute-start(bf16[512,1024]{1,0:T(8,128)(2,1)S(1)} %get-tuple-element.160), channel_id=1, source_target_pairs={{0,2},{1,3},{2,0},{3,1},{4,6},{5,7},{6,4},{7,5},{8,10},{9,11},{10,... | collective-permute-start | bytes 3145736 | tf_op jit(solution)/shard_map/ppermute | solution.py:338
  290.0 7.1 %collective-permute-start.12 = (bf16[2,512,1024]{2,1,0:T(8,128)(2,1)S(1)}, bf16[2,512,1024]{2,1,0:T(8,128)(2,1)S(1)}, u32[]{:S(2)}, u32[]{:S(2)}) collective-permute-start(bf16[2,512,1024]{2,1,0:T(8,128)(2,1)S(1)} %pad_maximum_fusion.6), channel_id=1, source_target_pairs={{0,1},{1,0},{2,3},{3,2},{4,5},{5,4},{6,7},{7,6},{8,9},{9,8},{10,11... | collective-permute-start | bytes 6291464 | tf_op jit(solution)/shard_map/ppermute | solution.py:338
  297.9 25.3 %collective-permute-start.13 = (bf16[512,1024]{1,0:T(8,128)(2,1)S(1)}, bf16[512,1024]{1,0:T(8,128)(2,1)S(1)}, u32[]{:S(2)}, u32[]{:S(2)}) collective-permute-start(bf16[512,1024]{1,0:T(8,128)(2,1)S(1)} %fusion.26), channel_id=1, source_target_pairs={{0,2},{1,3},{2,0},{3,1},{4,6},{5,7},{6,4},{7,5},{8,10},{9,11},{10,... | collective-permute-start | bytes 3145736 | tf_op jit(solution)/shard_map/ppermute | solution.py:338
  326.2 24.4 %collective-permute-start.14 = (bf16[512,1024]{1,0:T(8,128)(2,1)S(1)}, bf16[512,1024]{1,0:T(8,128)(2,1)S(1)}, u32[]{:S(2)}, u32[]{:S(2)}) collective-permute-start(bf16[512,1024]{1,0:T(8,128)(2,1)S(1)} %get-tuple-element.157), channel_id=1, source_target_pairs={{0,2},{1,3},{2,0},{3,1},{4,6},{5,7},{6,4},{7,5},{8,10},{9,11},{10,... | collective-permute-start | bytes 3145736 | tf_op jit(solution)/shard_map/ppermute | solution.py:338
  402.0 46.9 %collective-permute-start.17 = (bf16[512,1024]{1,0:T(8,128)(2,1)S(1)}, bf16[512,1024]{1,0:T(8,128)(2,1)}, u32[]{:S(2)}, u32[]{:S(2)}) collective-permute-start(bf16[512,1024]{1,0:T(8,128)(2,1)S(1)} %fusion.22), channel_id=1, source_target_pairs={{0,2},{1,3},{2,0},{3,1},{4,6},{5,7},{6,4},{7,5},{8,10},{9,11},{10,... | collective-permute-start | bytes 3145736 | tf_op jit(solution)/shard_map/ppermute | solution.py:338
  447.0 64.1 %collective-permute-start.18 = (bf16[2,2,2048,128]{3,2,1,0:T(8,128)(2,1)}, bf16[2,2,2048,128]{3,2,1,0:T(8,128)(2,1)}, u32[]{:S(2)}, u32[]{:S(2)}) collective-permute-start(bf16[2,2,2048,128]{3,2,1,0:T(8,128)(2,1)} %fusion.5), channel_id=1, source_target_pairs={{0,4},{4,0},{8,12},{12,8},{16,20},{20,16},{24,28},{28,24},{1,5},{5... | collective-permute-start | bytes 6291464 | tf_op jit(solution)/shard_map/ppermute | solution.py:236
  533.3 13.7 %collective-permute-start.24 = (bf16[512,512]{0,1:T(8,128)(2,1)}, bf16[512,512]{0,1:T(8,128)(2,1)}, u32[]{:S(2)}, u32[]{:S(2)}) collective-permute-start(bf16[512,512]{0,1:T(8,128)(2,1)} %dynamic-slice_convert_fusion.8), channel_id=1, source_target_pairs={{0,4},{4,0},{8,12},{12,8},{16,20},{20,16},{24,28},{28,24},{1,5},{5... | collective-permute-start | bytes 1572872 | tf_op jit(solution)/shard_map/ppermute | solution.py:304
  549.9 41.8 %collective-permute-start.25 = (bf16[256,512]{0,1:T(8,128)(2,1)}, bf16[256,512]{0,1:T(8,128)(2,1)}, u32[]{:S(2)}, u32[]{:S(2)}) collective-permute-start(bf16[256,512]{0,1:T(8,128)(2,1)} %dynamic-slice_convert_fusion.10), channel_id=1, source_target_pairs={{0,8},{4,12},{8,0},{12,4},{16,24},{20,28},{24,16},{28,20},{1,9},{5... | collective-permute-start | bytes 786440 | tf_op jit(solution)/shard_map/ppermute | solution.py:304
  591.2 14.4 %collective-permute-start.21 = (bf16[512,512]{1,0:T(8,128)(2,1)S(1)}, bf16[512,512]{1,0:T(8,128)(2,1)S(1)}, u32[]{:S(2)}, u32[]{:S(2)}) collective-permute-start(bf16[512,512]{1,0:T(8,128)(2,1)S(1)} %dynamic-slice_convert_fusion.9), channel_id=1, source_target_pairs={{0,4},{4,0},{8,12},{12,8},{16,20},{20,16},{24,28},{28,24},{1,5},{5... | collective-permute-start | bytes 1572872 | tf_op jit(solution)/shard_map/ppermute | solution.py:304
  593.3 15.5 %collective-permute-start.26 = (bf16[128,512]{0,1:T(8,128)(2,1)S(1)}, bf16[128,512]{0,1:T(8,128)(2,1)S(1)}, u32[]{:S(2)}, u32[]{:S(2)}) collective-permute-start(bf16[128,512]{0,1:T(8,128)(2,1)S(1)} %dynamic-slice_convert_fusion.12), channel_id=1, source_target_pairs={{0,16},{4,20},{8,24},{12,28},{16,0},{20,4},{24,8},{28,12},{1,17},{... | collective-permute-start | bytes 393224 | tf_op jit(solution)/shard_map/ppermute | solution.py:304
  596.2 25.3 %collective-permute-start.20 = (bf16[512,1024]{1,0:T(8,128)(2,1)S(1)}, bf16[512,1024]{1,0:T(8,128)(2,1)S(1)}, u32[]{:S(2)}, u32[]{:S(2)}) collective-permute-start(bf16[512,1024]{1,0:T(8,128)(2,1)S(1)} %fusion.18), channel_id=1, source_target_pairs={{0,2},{1,3},{2,0},{3,1},{4,6},{5,7},{6,4},{7,5},{8,10},{9,11},{10,... | collective-permute-start | bytes 3145736 | tf_op jit(solution)/shard_map/ppermute | solution.py:338
  605.9 7.9 %collective-permute-start.22 = (bf16[256,512]{1,0:T(8,128)(2,1)S(1)}, bf16[256,512]{1,0:T(8,128)(2,1)S(1)}, u32[]{:S(2)}, u32[]{:S(2)}) collective-permute-start(bf16[256,512]{1,0:T(8,128)(2,1)S(1)} %dynamic-slice_convert_fusion.11), channel_id=1, source_target_pairs={{0,8},{4,12},{8,0},{12,4},{16,24},{20,28},{24,16},{28,20},{1,9},{5... | collective-permute-start | bytes 786440 | tf_op jit(solution)/shard_map/ppermute | solution.py:304
  625.2 11.6 %collective-permute-start.23 = (bf16[128,512]{1,0:T(8,128)(2,1)}, bf16[128,512]{1,0:T(8,128)(2,1)}, u32[]{:S(2)}, u32[]{:S(2)}) collective-permute-start(bf16[128,512]{1,0:T(8,128)(2,1)} %dynamic-slice_convert_fusion.13), channel_id=1, source_target_pairs={{0,16},{4,20},{8,24},{12,28},{16,0},{20,4},{24,8},{28,12},{1,17},{... | collective-permute-start | bytes 393224 | tf_op jit(solution)/shard_map/ppermute | solution.py:304
  627.5 8.2 %collective-permute-start.28 = (f32[2304]{0:T(1024)S(1)}, f32[2304]{0:T(1024)}, u32[]{:S(2)}, u32[]{:S(2)}) collective-permute-start(f32[2304]{0:T(1024)S(1)} %fusion.112), channel_id=1, source_target_pairs={{0,2},{1,3},{2,0},{3,1},{4,6},{5,7},{6,4},{7,5},{8,10},{9,11},{10,... | collective-permute-start | bytes 27656 | tf_op jit(solution)/shard_map/ppermute | solution.py:329
  (111 other events, 1157.8 us)
Sparse Core Ops, SparseCore 0:
  10.7 43.0 all-gather.5
  56.5 38.9 all-gather.3
  97.5 99.8 all-gather.7
  389.3 125.2 reduce-scatter.1

commit v13 on v12

--- a/solution.py
+++ b/solution.py
@@ -339,9 +339,12 @@
 
 
 def token_gather(values):
+    return finish_gather(values, exchange(values, 2))
+
+
+def finish_gather(values, across):
     rows = values.shape[0]
     me = lax.axis_index("tensor")
-    across = exchange(values, 2)
     pair = jnp.stack([values, across])
     beside = exchange(pair, 1)
     full = jnp.zeros((4 * rows,) + values.shape[1:], values.dtype)
@@ -422,7 +425,7 @@
     first_all = token_gather(rms_scale(x_float, gain_first).astype(jnp.bfloat16))
     cotangent = out_grad.astype(jnp.float32) * local_valid[:, None].astype(jnp.float32)
     cotangent_low, first_all = lax.optimization_barrier((cotangent.astype(jnp.bfloat16), first_all))
-    mlp_grad_all = token_gather(cotangent_low)
+    cotangent_across = exchange(cotangent_low, 2)
     query_projected = jnp.dot(first_all, w_query, preferred_element_type=jnp.float32)
     key_projected = jnp.dot(first_all, w_key, preferred_element_type=jnp.float32)
     value_rows = (
@@ -449,6 +452,8 @@
     sums, totals = attention_forward(
         query_t, query_start, own_keys, own_values, sums, totals, piece, quarter, 0
     )
+    cotangent_across, sums, totals = lax.optimization_barrier((cotangent_across, sums, totals))
+    mlp_grad_all = finish_gather(cotangent_low, cotangent_across)
     sums, totals_t = attention_forward(
         query_t, query_start, moved[0], moved[1], sums, totals, piece, quarter, 1
     )

time: 664 us -> 662 us (level)
    all_gather x1, waiting for transfers between devices: 1.74 us -> 12 us  [shards(): lax.all_gather(jnp.concatenate([gate_weight.astype(jnp.bfloat16), up_weig...]
    ppermute x16, waiting for transfers between devices: 133 us -> 123 us  [exchange(): lax.ppermute(values, 'tensor', [(i, i ^ distance) for i in range(count)])]
    unnamed x213 -> x201, local copies, waits for them, and re-layouts: 36.2 us -> 35.7 us
  transfers between devices with their start and end apart: 36 -> 36, of which waited for: 22 -> 21; matrix products, arithmetic and copies ran while one was open for 30% -> 30% of each run, Pallas kernels for 21% -> 21%
where the time goes in v13:
time: 662 us; the launch traced here: 655 us
  waiting for transfers between devices  174 us (26%)
  Pallas kernels  135 us (20%)
  other arithmetic  106 us (16%)
  matrix products  94.3 us (14%)
  local copies, waits for them, and re-layouts  93.8 us (14%)
  starting transfers between devices  36.8 us (6%)
  between operations  15.9 us (2%)
    ppermute x16, waiting for transfers between devices, exchange(): lax.ppermute(values, 'tensor', [(i, i ^ distance) for i in range(count)])  123 us
    pallas_call x2, Pallas kernels, attention_backward(): pl.pallas_call(functools.partial(_bwd_kernel, scale=scale, block=block),...  83.1 us
    pallas_call x2, Pallas kernels, attention_forward(): pl.pallas_call(functools.partial(_fwd_kernel, scale=scale, block=block),...  51.7 us
    dot_general x7, matrix products, contract_last(): lax.dot_general(left, right, (((1,), (1,)), ((), ())), preferred_element_...  37.8 us
    unnamed x201, local copies, waits for them, and re-layouts  35.7 us
    dot_general x7, matrix products, contract_rows(): lax.dot_general(left, right, (((0,), (0,)), ((), ())), preferred_element_...  24.2 us
    ppermute x6, waiting for transfers between devices, halving_scatter(): lax.ppermute(send.astype(jnp.bfloat16), 'fsdp', [(i, i ^ 1 << bit) for i...  18.3 us
    ppermute x16, starting transfers between devices, exchange(): lax.ppermute(values, 'tensor', [(i, i ^ distance) for i in range(count)])  14.3 us
  transfers between devices with their start and end apart: 36, of which 21 were waited for; matrix products, arithmetic and copies ran while one was open for 30% of the time, Pallas kernels for 21%

profile of v13, /device:TPU:0, one launch (start us, length us, event | category | flops | bytes accessed | tf_op | source)
XLA Modules:
  0.0 654.8 jit_solution(12451331992332951403)
XLA Ops:
  32.6 19.5 %collective-permute-done.3 = bf16[512,1024]{1,0:T(8,128)(2,1)S(1)} collective-permute-done((bf16[512,1024]{1,0:T(8,128)(2,1)S(1)}, bf16[512,1024]{1,0:T(8,128)(2,1)S(1)}, u32[]{:S(2)}, u32[]{:S(2)}) %collective-permute-start.3) | collective-permute-done | bytes 1048608 | tf_op jit(solution)/shard_map/ppermute | solution.py:338
  68.7 5.0 multiply_reduce_fusion.8
  76.0 5.2 convolution_convert_fusion.1
  95.6 5.1 multiply_reduce_fusion.2
  118.0 28.8 %attn_fwd.2 = (f32[2,2,2048,128]{3,2,1,0:T(8,128)}, f32[2,2,2048,128]{3,2,1,0:T(8,128)}) custom-call(s32[7,10]{1,0:T(8,128)S(1)} %broadcast_select_fusion.5.tab_ref, bf16[2,2,2048,128]{3,2,1,0:T(8,128)(2,1)S(1)} %maximum_bitcast_fusion.q_ref, s32[2048,128]{1,0:T(8,128)S(1)} %broadcast_in_dim.45.qs_ref, ...), custom_call_target="tpu_custom_call", output_to_operand_aliasing={{0}: (5, {}), {1}: (6, {})} | custom-call | flops 5368709120 | bytes 20971520 | tf_op jit(solution)/shard_map/attn_fwd/pallas_call | solution.py:124
  152.2 22.9 %attn_fwd.3 = (f32[2,2,2048,128]{3,2,1,0:T(8,128)}, f32[2,2,2048,128]{3,2,1,0:T(8,128)}) custom-call(s32[7,8]{1,0:T(8,128)S(1)} %broadcast_select_fusion.3.tab_ref, bf16[2,2,2048,128]{3,2,1,0:T(8,128)(2,1)S(1)} %maximum_bitcast_fusion.q_ref, s32[2048,128]{1,0:T(8,128)S(1)} %broadcast_in_dim.45.qs_ref, ...), custom_call_target="tpu_custom_call", output_to_operand_aliasing={{0}: (5, {}), {1}: (6, {})} | custom-call | flops 4294967296 | bytes 16777216 | tf_op jit(solution)/shard_map/attn_fwd/pallas_call | solution.py:124
  185.5 12.0 %all-gather.8.cloned.1.call-done = bf16[1024,2816]{0,1:T(8,128)(2,1)} async-done(((bf16[128,2816]{0,1:T(8,128)(2,1)}), bf16[1024,2816]{0,1:T(8,128)(2,1)}) %all-gather.8.cloned.1.call-update) | async-done | bytes 5767184 | tf_op jit(solution)/shard_map/all_gather | solution.py:466
  212.9 19.9 %collective-permute-done.9 = bf16[512,1024]{1,0:T(8,128)(2,1)S(1)} collective-permute-done((bf16[512,1024]{1,0:T(8,128)(2,1)S(1)}, bf16[512,1024]{1,0:T(8,128)(2,1)S(1)}, u32[]{:S(2)}, u32[]{:S(2)}) %collective-permute-start.9) | collective-permute-done | bytes 1048608 | tf_op jit(solution)/shard_map/ppermute | solution.py:338
  236.3 22.8 %collective-permute-done.10 = bf16[512,1024]{1,0:T(8,128)(2,1)S(1)} collective-permute-done((bf16[512,1024]{1,0:T(8,128)(2,1)S(1)}, bf16[512,1024]{1,0:T(8,128)(2,1)S(1)}, u32[]{:S(2)}, u32[]{:S(2)}) %collective-permute-start.10) | collective-permute-done | bytes 1048608 | tf_op jit(solution)/shard_map/ppermute | solution.py:338
  267.2 5.0 fusion.42
  272.3 5.3 multiply_convert_fusion
  277.6 7.1 %fusion.40 = f32[2048,1024]{1,0:T(8,128)S(1)} fusion(bf16[2048,768]{1,0:T(8,128)(2,1)} %get-tuple-element.74, bf16[1024,2816]{0,1:T(8,128)(2,1)} %all-gather.8.cloned.1.call-done), kind=kOutput, calls=%fused_computation.132 | convolution fusion | flops 3221225472 | bytes 13107200 | tf_op jit(solution)/shard_map/dot_general | solution.py:276
  292.0 5.2 fusion.121
  309.1 14.2 %collective-permute-done.13 = bf16[512,1024]{1,0:T(8,128)(2,1)S(1)} collective-permute-done((bf16[512,1024]{1,0:T(8,128)(2,1)S(1)}, bf16[512,1024]{1,0:T(8,128)(2,1)S(1)}, u32[]{:S(2)}, u32[]{:S(2)}) %collective-permute-start.13) | collective-permute-done | bytes 1048608 | tf_op jit(solution)/shard_map/ppermute | solution.py:338
  328.0 22.8 %collective-permute-done.14 = bf16[512,1024]{1,0:T(8,128)(2,1)S(1)} collective-permute-done((bf16[512,1024]{1,0:T(8,128)(2,1)S(1)}, bf16[512,1024]{1,0:T(8,128)(2,1)S(1)}, u32[]{:S(2)}, u32[]{:S(2)}) %collective-permute-start.14) | collective-permute-done | bytes 1048608 | tf_op jit(solution)/shard_map/ppermute | solution.py:338
  366.9 7.2 %fusion.6 = (f32[2048,2,2]{0,2,1:T(2,128)S(1)}, bf16[2,2,2048,128]{3,2,1,0:T(8,128)(2,1)}) fusion(f32[2048,2,2,128]{3,0,2,1:T(8,128)} %copy.105, f32[2,2,2048,128]{3,2,1,0:T(8,128)} %get-tuple-element.67, f32[2,2,2048]{2,1,0:T(2,128)S(1)} %slice_reduce_fusion, f32[2048,2,2]{0,2,1:T(2,128)S(1)} %bitcast.250), kind=kLoop, calls=%fused_computation.30 | loop fusion | flops 5234688 | bytes 10584064 | tf_op jit(solution)/shard_map/reduce_sum | solution.py:529
  405.9 37.5 %attn_bwd.2 = (f32[2,2,2048,128]{3,2,1,0:T(8,128)}, f32[2,2048,128]{2,1,0:T(8,128)}, f32[2,2048,128]{2,1,0:T(8,128)}) custom-call(s32[7,8]{1,0:T(8,128)} %broadcast_select_fusion.2.tab_ref, bf16[2,2,2048,128]{3,2,1,0:T(8,128)(2,1)} %copy-done.1, bf16[2,2,2048,128]{3,2,1,0:T(8,128)(2,1)} %get-tuple-element.85.h_ref, ...), custom_call_target="tpu_custom_call", output_to_operand_aliasing={{0}: (7, {})} | custom-call | flops 10737418240 | bytes 20971520 | tf_op jit(solution)/shard_map/attn_bwd/pallas_call | solution.py:207
  453.3 45.6 %attn_bwd.3 = (f32[2,2,2048,128]{3,2,1,0:T(8,128)}, f32[2,2048,128]{2,1,0:T(8,128)}, f32[2,2048,128]{2,1,0:T(8,128)}) custom-call(s32[7,10]{1,0:T(8,128)} %broadcast_select_fusion.4.tab_ref, bf16[2,2,2048,128]{3,2,1,0:T(8,128)(2,1)} %copy-done.1, bf16[2,2,2048,128]{3,2,1,0:T(8,128)(2,1)} %get-tuple-element.85.h_ref, ...), custom_call_target="tpu_custom_call", output_to_operand_aliasing={{0}: (7, {})} | custom-call | flops 13421772800 | bytes 26214400 | tf_op jit(solution)/shard_map/attn_bwd/pallas_call | solution.py:207
  498.9 11.2 %collective-permute-done.18 = bf16[2,2,2048,128]{3,2,1,0:T(8,128)(2,1)} collective-permute-done((bf16[2,2,2048,128]{3,2,1,0:T(8,128)(2,1)}, bf16[2,2,2048,128]{3,2,1,0:T(8,128)(2,1)}, u32[]{:S(2)}, u32[]{:S(2)}) %collective-permute-start.18) | collective-permute-done | bytes 2097184 | tf_op jit(solution)/shard_map/ppermute | solution.py:236
  533.4 5.9 fusion.70
  539.3 6.2 collective-permute-done.24
  577.5 5.8 fusion.123
  596.0 7.6 %collective-permute-done.21 = bf16[512,512]{1,0:T(8,128)(2,1)S(1)} collective-permute-done((bf16[512,512]{1,0:T(8,128)(2,1)S(1)}, bf16[512,512]{1,0:T(8,128)(2,1)S(1)}, u32[]{:S(2)}, u32[]{:S(2)}) %collective-permute-start.21) | collective-permute-done | bytes 524320 | tf_op jit(solution)/shard_map/ppermute | solution.py:304
  611.9 7.7 %collective-permute-done.20 = bf16[512,1024]{1,0:T(8,128)(2,1)S(1)} collective-permute-done((bf16[512,1024]{1,0:T(8,128)(2,1)S(1)}, bf16[512,1024]{1,0:T(8,128)(2,1)S(1)}, u32[]{:S(2)}, u32[]{:S(2)}) %collective-permute-start.20) | collective-permute-done | bytes 1048608 | tf_op jit(solution)/shard_map/ppermute | solution.py:338
  (446 shorter events, 303.7 us)
Async XLA Ops:
  7.2 61.5 %all-gather.6.cloned.1.call-start = ((), (), s32[]{:S(2)}) async-start(), calls=%async_computation.2 | async-start | bytes 1179648 | tf_op jit(solution)/shard_map/all_gather | solution.py:413
  9.7 85.8 %all-gather.4.cloned.1.call-start = ((), (), s32[]{:S(2)}) async-start(), calls=%async_computation.1 | async-start | bytes 1179648 | tf_op jit(solution)/shard_map/all_gather | solution.py:422
  17.1 180.4 %all-gather.8.cloned.1.call-start = ((), (), s32[]{:S(2)}) async-start(), calls=%async_computation.3 | async-start | bytes 6488064 | tf_op jit(solution)/shard_map/all_gather | solution.py:466
  29.5 22.6 %collective-permute-start.3 = (bf16[512,1024]{1,0:T(8,128)(2,1)S(1)}, bf16[512,1024]{1,0:T(8,128)(2,1)S(1)}, u32[]{:S(2)}, u32[]{:S(2)}) collective-permute-start(bf16[512,1024]{1,0:T(8,128)(2,1)S(1)} %get-tuple-element.168), channel_id=1, source_target_pairs={{0,2},{1,3},{2,0},{3,1},{4,6},{5,7},{6,4},{7,5},{8,10},{9,11},{10,... | collective-permute-start | bytes 3145736 | tf_op jit(solution)/shard_map/ppermute | solution.py:338
  53.6 10.5 %collective-permute-start.4 = (bf16[2,512,1024]{2,1,0:T(8,128)(2,1)}, bf16[2,512,1024]{2,1,0:T(8,128)(2,1)}, u32[]{:S(2)}, u32[]{:S(2)}) collective-permute-start(bf16[2,512,1024]{2,1,0:T(8,128)(2,1)} %pad_maximum_fusion.1), channel_id=1, source_target_pairs={{0,1},{1,0},{2,3},{3,2},{4,5},{5,4},{6,7},{7,6},{8,9},{9,8},{10,11... | collective-permute-start | bytes 6291464 | tf_op jit(solution)/shard_map/ppermute | solution.py:338
  54.5 494.1 %reduce-scatter.2.cloned.1.call-start = ((), (), s32[]{:S(2)}) async-start(), calls=%async_computation.4 | async-start | bytes 6488064 | tf_op jit(solution)/shard_map/reduce_scatter | solution.py:537
  89.0 61.4 %collective-permute-start.7 = (bf16[2,2,2048,128]{3,2,1,0:T(8,128)(2,1)}, bf16[2,2,2048,128]{3,2,1,0:T(8,128)(2,1)}, u32[]{:S(2)}, u32[]{:S(2)}) collective-permute-start(bf16[2,2,2048,128]{3,2,1,0:T(8,128)(2,1)} %pad_maximum_fusion.3), channel_id=1, source_target_pairs={{0,4},{4,0},{8,12},{12,8},{16,20},{20,16},{24,28},{28,24},{1,5},{5... | collective-permute-start | bytes 6291464 | tf_op jit(solution)/shard_map/ppermute | solution.py:236
  90.1 56.7 %collective-permute-start.5 = (bf16[512,1024]{1,0:T(8,128)(2,1)S(1)}, bf16[512,1024]{1,0:T(8,128)(2,1)}, u32[]{:S(2)}, u32[]{:S(2)}) collective-permute-start(bf16[512,1024]{1,0:T(8,128)(2,1)S(1)} %copy-done.18), channel_id=1, source_target_pairs={{0,2},{1,3},{2,0},{3,1},{4,6},{5,7},{6,4},{7,5},{8,10},{9,11},{10,... | collective-permute-start | bytes 3145736 | tf_op jit(solution)/shard_map/ppermute | solution.py:338
  148.3 26.8 %collective-permute-start.6 = (bf16[2,512,1024]{2,1,0:T(8,128)(2,1)S(1)}, bf16[2,512,1024]{2,1,0:T(8,128)(2,1)S(1)}, u32[]{:S(2)}, u32[]{:S(2)}) collective-permute-start(bf16[2,512,1024]{2,1,0:T(8,128)(2,1)S(1)} %pad_maximum_fusion.2), channel_id=1, source_target_pairs={{0,1},{1,0},{2,3},{3,2},{4,5},{5,4},{6,7},{7,6},{8,9},{9,8},{10,11... | collective-permute-start | bytes 6291464 | tf_op jit(solution)/shard_map/ppermute | solution.py:338
  207.5 25.3 %collective-permute-start.9 = (bf16[512,1024]{1,0:T(8,128)(2,1)S(1)}, bf16[512,1024]{1,0:T(8,128)(2,1)S(1)}, u32[]{:S(2)}, u32[]{:S(2)}) collective-permute-start(bf16[512,1024]{1,0:T(8,128)(2,1)S(1)} %fusion.30), channel_id=1, source_target_pairs={{0,2},{1,3},{2,0},{3,1},{4,6},{5,7},{6,4},{7,5},{8,10},{9,11},{10,... | collective-permute-start | bytes 3145736 | tf_op jit(solution)/shard_map/ppermute | solution.py:338
  234.7 24.4 %collective-permute-start.10 = (bf16[512,1024]{1,0:T(8,128)(2,1)S(1)}, bf16[512,1024]{1,0:T(8,128)(2,1)S(1)}, u32[]{:S(2)}, u32[]{:S(2)}) collective-permute-start(bf16[512,1024]{1,0:T(8,128)(2,1)S(1)} %get-tuple-element.166), channel_id=1, source_target_pairs={{0,2},{1,3},{2,0},{3,1},{4,6},{5,7},{6,4},{7,5},{8,10},{9,11},{10,... | collective-permute-start | bytes 3145736 | tf_op jit(solution)/shard_map/ppermute | solution.py:338
  290.1 7.2 %collective-permute-start.12 = (bf16[2,512,1024]{2,1,0:T(8,128)(2,1)S(1)}, bf16[2,512,1024]{2,1,0:T(8,128)(2,1)S(1)}, u32[]{:S(2)}, u32[]{:S(2)}) collective-permute-start(bf16[2,512,1024]{2,1,0:T(8,128)(2,1)S(1)} %pad_maximum_fusion.6), channel_id=1, source_target_pairs={{0,1},{1,0},{2,3},{3,2},{4,5},{5,4},{6,7},{7,6},{8,9},{9,8},{10,11... | collective-permute-start | bytes 6291464 | tf_op jit(solution)/shard_map/ppermute | solution.py:338
  298.0 25.3 %collective-permute-start.13 = (bf16[512,1024]{1,0:T(8,128)(2,1)S(1)}, bf16[512,1024]{1,0:T(8,128)(2,1)S(1)}, u32[]{:S(2)}, u32[]{:S(2)}) collective-permute-start(bf16[512,1024]{1,0:T(8,128)(2,1)S(1)} %fusion.26), channel_id=1, source_target_pairs={{0,2},{1,3},{2,0},{3,1},{4,6},{5,7},{6,4},{7,5},{8,10},{9,11},{10,... | collective-permute-start | bytes 3145736 | tf_op jit(solution)/shard_map/ppermute | solution.py:338
  326.3 24.4 %collective-permute-start.14 = (bf16[512,1024]{1,0:T(8,128)(2,1)S(1)}, bf16[512,1024]{1,0:T(8,128)(2,1)S(1)}, u32[]{:S(2)}, u32[]{:S(2)}) collective-permute-start(bf16[512,1024]{1,0:T(8,128)(2,1)S(1)} %get-tuple-element.163), channel_id=1, source_target_pairs={{0,2},{1,3},{2,0},{3,1},{4,6},{5,7},{6,4},{7,5},{8,10},{9,11},{10,... | collective-permute-start | bytes 3145736 | tf_op jit(solution)/shard_map/ppermute | solution.py:338
  402.1 46.7 %collective-permute-start.17 = (bf16[512,1024]{1,0:T(8,128)(2,1)S(1)}, bf16[512,1024]{1,0:T(8,128)(2,1)}, u32[]{:S(2)}, u32[]{:S(2)}) collective-permute-start(bf16[512,1024]{1,0:T(8,128)(2,1)S(1)} %fusion.22), channel_id=1, source_target_pairs={{0,2},{1,3},{2,0},{3,1},{4,6},{5,7},{6,4},{7,5},{8,10},{9,11},{10,... | collective-permute-start | bytes 3145736 | tf_op jit(solution)/shard_map/ppermute | solution.py:338
  447.0 63.2 %collective-permute-start.18 = (bf16[2,2,2048,128]{3,2,1,0:T(8,128)(2,1)}, bf16[2,2,2048,128]{3,2,1,0:T(8,128)(2,1)}, u32[]{:S(2)}, u32[]{:S(2)}) collective-permute-start(bf16[2,2,2048,128]{3,2,1,0:T(8,128)(2,1)} %fusion.5), channel_id=1, source_target_pairs={{0,4},{4,0},{8,12},{12,8},{16,20},{20,16},{24,28},{28,24},{1,5},{5... | collective-permute-start | bytes 6291464 | tf_op jit(solution)/shard_map/ppermute | solution.py:236
  532.3 13.2 %collective-permute-start.24 = (bf16[512,512]{0,1:T(8,128)(2,1)}, bf16[512,512]{0,1:T(8,128)(2,1)}, u32[]{:S(2)}, u32[]{:S(2)}) collective-permute-start(bf16[512,512]{0,1:T(8,128)(2,1)} %dynamic-slice_convert_fusion.8), channel_id=1, source_target_pairs={{0,4},{4,0},{8,12},{12,8},{16,20},{20,16},{24,28},{28,24},{1,5},{5... | collective-permute-start | bytes 1572872 | tf_op jit(solution)/shard_map/ppermute | solution.py:304
  548.4 41.7 %collective-permute-start.25 = (bf16[256,512]{0,1:T(8,128)(2,1)}, bf16[256,512]{0,1:T(8,128)(2,1)}, u32[]{:S(2)}, u32[]{:S(2)}) collective-permute-start(bf16[256,512]{0,1:T(8,128)(2,1)} %dynamic-slice_convert_fusion.10), channel_id=1, source_target_pairs={{0,8},{4,12},{8,0},{12,4},{16,24},{20,28},{24,16},{28,20},{1,9},{5... | collective-permute-start | bytes 786440 | tf_op jit(solution)/shard_map/ppermute | solution.py:304
  589.2 14.4 %collective-permute-start.21 = (bf16[512,512]{1,0:T(8,128)(2,1)S(1)}, bf16[512,512]{1,0:T(8,128)(2,1)S(1)}, u32[]{:S(2)}, u32[]{:S(2)}) collective-permute-start(bf16[512,512]{1,0:T(8,128)(2,1)S(1)} %dynamic-slice_convert_fusion.9), channel_id=1, source_target_pairs={{0,4},{4,0},{8,12},{12,8},{16,20},{20,16},{24,28},{28,24},{1,5},{5... | collective-permute-start | bytes 1572872 | tf_op jit(solution)/shard_map/ppermute | solution.py:304
  591.2 16.0 %collective-permute-start.26 = (bf16[128,512]{0,1:T(8,128)(2,1)S(1)}, bf16[128,512]{0,1:T(8,128)(2,1)S(1)}, u32[]{:S(2)}, u32[]{:S(2)}) collective-permute-start(bf16[128,512]{0,1:T(8,128)(2,1)S(1)} %dynamic-slice_convert_fusion.12), channel_id=1, source_target_pairs={{0,16},{4,20},{8,24},{12,28},{16,0},{20,4},{24,8},{28,12},{1,17},{... | collective-permute-start | bytes 393224 | tf_op jit(solution)/shard_map/ppermute | solution.py:304
  593.9 25.6 %collective-permute-start.20 = (bf16[512,1024]{1,0:T(8,128)(2,1)S(1)}, bf16[512,1024]{1,0:T(8,128)(2,1)S(1)}, u32[]{:S(2)}, u32[]{:S(2)}) collective-permute-start(bf16[512,1024]{1,0:T(8,128)(2,1)S(1)} %fusion.18), channel_id=1, source_target_pairs={{0,2},{1,3},{2,0},{3,1},{4,6},{5,7},{6,4},{7,5},{8,10},{9,11},{10,... | collective-permute-start | bytes 3145736 | tf_op jit(solution)/shard_map/ppermute | solution.py:338
  603.8 8.0 %collective-permute-start.22 = (bf16[256,512]{1,0:T(8,128)(2,1)S(1)}, bf16[256,512]{1,0:T(8,128)(2,1)S(1)}, u32[]{:S(2)}, u32[]{:S(2)}) collective-permute-start(bf16[256,512]{1,0:T(8,128)(2,1)S(1)} %dynamic-slice_convert_fusion.11), channel_id=1, source_target_pairs={{0,8},{4,12},{8,0},{12,4},{16,24},{20,28},{24,16},{28,20},{1,9},{5... | collective-permute-start | bytes 786440 | tf_op jit(solution)/shard_map/ppermute | solution.py:304
  623.1 12.2 %collective-permute-start.23 = (bf16[128,512]{1,0:T(8,128)(2,1)}, bf16[128,512]{1,0:T(8,128)(2,1)}, u32[]{:S(2)}, u32[]{:S(2)}) collective-permute-start(bf16[128,512]{1,0:T(8,128)(2,1)} %dynamic-slice_convert_fusion.13), channel_id=1, source_target_pairs={{0,16},{4,20},{8,24},{12,28},{16,0},{20,4},{24,8},{28,12},{1,17},{... | collective-permute-start | bytes 393224 | tf_op jit(solution)/shard_map/ppermute | solution.py:304
  625.4 8.5 %collective-permute-start.28 = (f32[2304]{0:T(1024)S(1)}, f32[2304]{0:T(1024)}, u32[]{:S(2)}, u32[]{:S(2)}) collective-permute-start(f32[2304]{0:T(1024)S(1)} %fusion.112), channel_id=1, source_target_pairs={{0,2},{1,3},{2,0},{3,1},{4,6},{5,7},{6,4},{7,5},{8,10},{9,11},{10,... | collective-permute-start | bytes 27656 | tf_op jit(solution)/shard_map/ppermute | solution.py:329
  (105 other events, 1107.0 us)
Sparse Core Ops, SparseCore 0:
  10.7 43.0 all-gather.5
  56.5 39.0 all-gather.3
  97.6 99.9 all-gather.7
  389.5 122.0 reduce-scatter.1

commit v14 on v13

--- a/solution.py
+++ b/solution.py
@@ -420,6 +420,9 @@
     )
     w_key, w_value = split_columns(kv_full, (key_matrix.shape[1], value_matrix.shape[1]))
     w_query = lax.all_gather(q_weight.astype(jnp.bfloat16), "fsdp", axis=0, tiled=True)
+    w_out = lax.all_gather(
+        jnp.transpose(o_weight).astype(jnp.bfloat16), "fsdp", axis=0, tiled=True
+    )
     x_float = hidden.astype(jnp.float32)
     gain_first = gain_in.astype(jnp.float32)
     first_all = token_gather(rms_scale(x_float, gain_first).astype(jnp.bfloat16))
@@ -469,7 +472,6 @@
                 gate_weight.astype(jnp.bfloat16),
                 up_weight.astype(jnp.bfloat16),
                 jnp.transpose(down_weight).astype(jnp.bfloat16),
-                jnp.transpose(o_weight).astype(jnp.bfloat16),
             ],
             axis=1,
         ),
@@ -477,8 +479,8 @@
         axis=0,
         tiled=True,
     )
-    w_gate, w_up, w_down_t, w_out = split_columns(
-        mlp_full, (gate_weight.shape[1], up_weight.shape[1], down_weight.shape[0], o_weight.shape[0])
+    w_gate, w_up, w_down_t = split_columns(
+        mlp_full, (gate_weight.shape[1], up_weight.shape[1], down_weight.shape[0])
     )
     out_partial = contract_last(out_rows, w_out)
     late_grad_all, out_partial = lax.optimization_barrier((mlp_grad_all, out_partial))

time: 662 us -> 658 us (level)
  waiting for transfers between devices: 174 us -> 166 us
    ppermute x16, waiting for transfers between devices: 123 us -> 100 us  [exchange(): lax.ppermute(values, 'tensor', [(i, i ^ distance) for i in range(count)])]
    all_gather x1, waiting for transfers between devices: 12 us -> 25.1 us  [shards(): lax.all_gather(jnp.concatenate([gate_weight.astype(jnp.bfloat16), up_weig...]
    unnamed x201 -> x203, local copies, waits for them, and re-layouts: 35.7 us -> 35.9 us
  transfers between devices with their start and end apart: 36 -> 37, of which waited for: 21 -> 20; matrix products, arithmetic and copies ran while one was open for 30% -> 32% of each run, Pallas kernels for 21% -> 21%
where the time goes in v14:
time: 658 us; the launch traced here: 651 us
  waiting for transfers between devices  166 us (25%)
  Pallas kernels  135 us (21%)
  other arithmetic  108 us (16%)
  matrix products  93.7 us (14%)
  local copies, waits for them, and re-layouts  93.4 us (14%)
  starting transfers between devices  38.5 us (6%)
  between operations  16.1 us (2%)
    ppermute x16, waiting for transfers between devices, exchange(): lax.ppermute(values, 'tensor', [(i, i ^ distance) for i in range(count)])  100 us
    pallas_call x2, Pallas kernels, attention_backward(): pl.pallas_call(functools.partial(_bwd_kernel, scale=scale, block=block),...  83.1 us
    pallas_call x2, Pallas kernels, attention_forward(): pl.pallas_call(functools.partial(_fwd_kernel, scale=scale, block=block),...  52.1 us
    dot_general x7, matrix products, contract_last(): lax.dot_general(left, right, (((1,), (1,)), ((), ())), preferred_element_...  37.6 us
    unnamed x203, local copies, waits for them, and re-layouts  35.9 us
    all_gather x1, waiting for transfers between devices, shards(): lax.all_gather(jnp.concatenate([gate_weight.astype(jnp.bfloat16), up_weig...  25.1 us
    dot_general x7, matrix products, contract_rows(): lax.dot_general(left, right, (((0,), (0,)), ((), ())), preferred_element_...  24.2 us
    ppermute x6, waiting for transfers between devices, halving_scatter(): lax.ppermute(send.astype(jnp.bfloat16), 'fsdp', [(i, i ^ 1 << bit) for i...  18.4 us
  transfers between devices with their start and end apart: 37, of which 20 were waited for; matrix products, arithmetic and copies ran while one was open for 32% of the time, Pallas kernels for 21%

profile of v14, /device:TPU:0, one launch (start us, length us, event | category | flops | bytes accessed | tf_op | source)
XLA Modules:
  0.0 651.1 jit_solution(2058932766544110034)
XLA Ops:
  34.7 18.2 %collective-permute-done.3 = bf16[512,1024]{1,0:T(8,128)(2,1)S(1)} collective-permute-done((bf16[512,1024]{1,0:T(8,128)(2,1)S(1)}, bf16[512,1024]{1,0:T(8,128)(2,1)S(1)}, u32[]{:S(2)}, u32[]{:S(2)}) %collective-permute-start.3) | collective-permute-done | bytes 1048608 | tf_op jit(solution)/shard_map/ppermute | solution.py:338
  76.6 5.2 convolution_convert_fusion.1
  90.3 5.2 all-gather.5.cloned.1.call-done
  95.5 5.1 multiply_reduce_fusion.2
  118.2 29.1 %attn_fwd.2 = (f32[2,2,2048,128]{3,2,1,0:T(8,128)}, f32[2,2,2048,128]{3,2,1,0:T(8,128)}) custom-call(s32[7,10]{1,0:T(8,128)S(1)} %broadcast_select_fusion.5.tab_ref, bf16[2,2,2048,128]{3,2,1,0:T(8,128)(2,1)S(1)} %maximum_bitcast_fusion.q_ref, s32[2048,128]{1,0:T(8,128)S(1)} %broadcast_in_dim.45.qs_ref, ...), custom_call_target="tpu_custom_call", output_to_operand_aliasing={{0}: (5, {}), {1}: (6, {})} | custom-call | flops 5368709120 | bytes 20971520 | tf_op jit(solution)/shard_map/attn_fwd/pallas_call | solution.py:124
  152.8 22.9 %attn_fwd.3 = (f32[2,2,2048,128]{3,2,1,0:T(8,128)}, f32[2,2,2048,128]{3,2,1,0:T(8,128)}) custom-call(s32[7,8]{1,0:T(8,128)S(1)} %broadcast_select_fusion.3.tab_ref, bf16[2,2,2048,128]{3,2,1,0:T(8,128)(2,1)S(1)} %maximum_bitcast_fusion.q_ref, s32[2048,128]{1,0:T(8,128)S(1)} %broadcast_in_dim.45.qs_ref, ...), custom_call_target="tpu_custom_call", output_to_operand_aliasing={{0}: (5, {}), {1}: (6, {})} | custom-call | flops 4294967296 | bytes 16777216 | tf_op jit(solution)/shard_map/attn_fwd/pallas_call | solution.py:124
  198.8 25.1 %all-gather.11.cloned.1.call-done = bf16[1024,2304]{0,1:T(8,128)(2,1)} async-done(((bf16[128,2304]{0,1:T(8,128)(2,1)}), bf16[1024,2304]{0,1:T(8,128)(2,1)}) %all-gather.11.cloned.1.call-update) | async-done | bytes 4718608 | tf_op jit(solution)/shard_map/all_gather | solution.py:469
  223.8 6.0 fusion.46
  235.2 22.6 %collective-permute-done.10 = bf16[512,1024]{1,0:T(8,128)(2,1)S(1)} collective-permute-done((bf16[512,1024]{1,0:T(8,128)(2,1)S(1)}, bf16[512,1024]{1,0:T(8,128)(2,1)S(1)}, u32[]{:S(2)}, u32[]{:S(2)}) %collective-permute-start.10) | collective-permute-done | bytes 1048608 | tf_op jit(solution)/shard_map/ppermute | solution.py:338
  269.4 5.5 multiply_convert_fusion
  274.9 7.0 %fusion.40 = f32[2048,1024]{1,0:T(8,128)S(1)} fusion(bf16[2048,768]{1,0:T(8,128)(2,1)} %get-tuple-element.74, bf16[1024,2304]{0,1:T(8,128)(2,1)} %all-gather.11.cloned.1.call-done), kind=kOutput, calls=%fused_computation.132 | convolution fusion | flops 3221225472 | bytes 13107200 | tf_op jit(solution)/shard_map/dot_general | solution.py:276
  301.4 5.1 fusion.120
  306.4 13.7 %collective-permute-done.13 = bf16[512,1024]{1,0:T(8,128)(2,1)S(1)} collective-permute-done((bf16[512,1024]{1,0:T(8,128)(2,1)S(1)}, bf16[512,1024]{1,0:T(8,128)(2,1)S(1)}, u32[]{:S(2)}, u32[]{:S(2)}) %collective-permute-start.13) | collective-permute-done | bytes 1048608 | tf_op jit(solution)/shard_map/ppermute | solution.py:338
  324.9 22.7 %collective-permute-done.14 = bf16[512,1024]{1,0:T(8,128)(2,1)S(1)} collective-permute-done((bf16[512,1024]{1,0:T(8,128)(2,1)S(1)}, bf16[512,1024]{1,0:T(8,128)(2,1)S(1)}, u32[]{:S(2)}, u32[]{:S(2)}) %collective-permute-start.14) | collective-permute-done | bytes 1048608 | tf_op jit(solution)/shard_map/ppermute | solution.py:338
  362.6 7.2 %fusion.6 = (f32[2048,2,2]{0,2,1:T(2,128)S(1)}, bf16[2,2,2048,128]{3,2,1,0:T(8,128)(2,1)}) fusion(f32[2048,2,2,128]{3,0,2,1:T(8,128)} %copy.105, f32[2,2,2048,128]{3,2,1,0:T(8,128)} %get-tuple-element.67, f32[2,2,2048]{2,1,0:T(2,128)S(1)} %slice_reduce_fusion, f32[2048,2,2]{0,2,1:T(2,128)S(1)} %bitcast.252), kind=kLoop, calls=%fused_computation.30 | loop fusion | flops 5234688 | bytes 10584064 | tf_op jit(solution)/shard_map/reduce_sum | solution.py:531
  401.7 37.5 %attn_bwd.2 = (f32[2,2,2048,128]{3,2,1,0:T(8,128)}, f32[2,2048,128]{2,1,0:T(8,128)}, f32[2,2048,128]{2,1,0:T(8,128)}) custom-call(s32[7,8]{1,0:T(8,128)} %broadcast_select_fusion.2.tab_ref, bf16[2,2,2048,128]{3,2,1,0:T(8,128)(2,1)} %copy-done.1, bf16[2,2,2048,128]{3,2,1,0:T(8,128)(2,1)} %get-tuple-element.85.h_ref, ...), custom_call_target="tpu_custom_call", output_to_operand_aliasing={{0}: (7, {})} | custom-call | flops 10737418240 | bytes 20971520 | tf_op jit(solution)/shard_map/attn_bwd/pallas_call | solution.py:207
  450.1 45.7 %attn_bwd.3 = (f32[2,2,2048,128]{3,2,1,0:T(8,128)}, f32[2,2048,128]{2,1,0:T(8,128)}, f32[2,2048,128]{2,1,0:T(8,128)}) custom-call(s32[7,10]{1,0:T(8,128)} %broadcast_select_fusion.4.tab_ref, bf16[2,2,2048,128]{3,2,1,0:T(8,128)(2,1)} %copy-done.1, bf16[2,2,2048,128]{3,2,1,0:T(8,128)(2,1)} %get-tuple-element.85.h_ref, ...), custom_call_target="tpu_custom_call", output_to_operand_aliasing={{0}: (7, {})} | custom-call | flops 13421772800 | bytes 26214400 | tf_op jit(solution)/shard_map/attn_bwd/pallas_call | solution.py:207
  495.8 10.4 %collective-permute-done.18 = bf16[2,2,2048,128]{3,2,1,0:T(8,128)(2,1)} collective-permute-done((bf16[2,2,2048,128]{3,2,1,0:T(8,128)(2,1)}, bf16[2,2,2048,128]{3,2,1,0:T(8,128)(2,1)}, u32[]{:S(2)}, u32[]{:S(2)}) %collective-permute-start.18) | collective-permute-done | bytes 2097184 | tf_op jit(solution)/shard_map/ppermute | solution.py:236
  530.1 5.8 fusion.67
  536.0 5.9 collective-permute-done.24
  574.0 5.7 fusion.121
  579.8 5.0 add_add_fusion
  592.2 7.8 %collective-permute-done.21 = bf16[512,512]{1,0:T(8,128)(2,1)S(1)} collective-permute-done((bf16[512,512]{1,0:T(8,128)(2,1)S(1)}, bf16[512,512]{1,0:T(8,128)(2,1)S(1)}, u32[]{:S(2)}, u32[]{:S(2)}) %collective-permute-start.21) | collective-permute-done | bytes 524320 | tf_op jit(solution)/shard_map/ppermute | solution.py:304
  608.3 7.5 %collective-permute-done.20 = bf16[512,1024]{1,0:T(8,128)(2,1)S(1)} collective-permute-done((bf16[512,1024]{1,0:T(8,128)(2,1)S(1)}, bf16[512,1024]{1,0:T(8,128)(2,1)S(1)}, u32[]{:S(2)}, u32[]{:S(2)}) %collective-permute-start.20) | collective-permute-done | bytes 1048608 | tf_op jit(solution)/shard_map/ppermute | solution.py:338
  (451 shorter events, 303.0 us)
Async XLA Ops:
  7.2 62.2 %all-gather.7.cloned.1.call-start = ((), (), s32[]{:S(2)}) async-start(), calls=%async_computation.2 | async-start | bytes 1179648 | tf_op jit(solution)/shard_map/all_gather | solution.py:413
  9.8 85.7 %all-gather.5.cloned.1.call-start = ((), (), s32[]{:S(2)}) async-start(), calls=%async_computation.1 | async-start | bytes 1179648 | tf_op jit(solution)/shard_map/all_gather | solution.py:422
  11.5 174.3 %all-gather.9.cloned.1.call-start = ((), (), s32[]{:S(2)}) async-start(), calls=%async_computation.3 | async-start | bytes 1179648 | tf_op jit(solution)/shard_map/all_gather | solution.py:423
  18.9 204.9 %all-gather.11.cloned.1.call-start = ((), (), s32[]{:S(2)}) async-start(), calls=%async_computation.4 | async-start | bytes 5308416 | tf_op jit(solution)/shard_map/all_gather | solution.py:469
  30.5 22.4 %collective-permute-start.3 = (bf16[512,1024]{1,0:T(8,128)(2,1)S(1)}, bf16[512,1024]{1,0:T(8,128)(2,1)S(1)}, u32[]{:S(2)}, u32[]{:S(2)}) collective-permute-start(bf16[512,1024]{1,0:T(8,128)(2,1)S(1)} %get-tuple-element.168), channel_id=1, source_target_pairs={{0,2},{1,3},{2,0},{3,1},{4,6},{5,7},{6,4},{7,5},{8,10},{9,11},{10,... | collective-permute-start | bytes 3145736 | tf_op jit(solution)/shard_map/ppermute | solution.py:338
  54.4 10.4 %collective-permute-start.4 = (bf16[2,512,1024]{2,1,0:T(8,128)(2,1)}, bf16[2,512,1024]{2,1,0:T(8,128)(2,1)}, u32[]{:S(2)}, u32[]{:S(2)}) collective-permute-start(bf16[2,512,1024]{2,1,0:T(8,128)(2,1)} %pad_maximum_fusion.1), channel_id=1, source_target_pairs={{0,1},{1,0},{2,3},{3,2},{4,5},{5,4},{6,7},{7,6},{8,9},{9,8},{10,11... | collective-permute-start | bytes 6291464 | tf_op jit(solution)/shard_map/ppermute | solution.py:338
  55.3 489.9 %reduce-scatter.2.cloned.1.call-start = ((), (), s32[]{:S(2)}) async-start(), calls=%async_computation.5 | async-start | bytes 6488064 | tf_op jit(solution)/shard_map/reduce_scatter | solution.py:539
  89.3 61.7 %collective-permute-start.7 = (bf16[2,2,2048,128]{3,2,1,0:T(8,128)(2,1)}, bf16[2,2,2048,128]{3,2,1,0:T(8,128)(2,1)}, u32[]{:S(2)}, u32[]{:S(2)}) collective-permute-start(bf16[2,2,2048,128]{3,2,1,0:T(8,128)(2,1)} %pad_maximum_fusion.3), channel_id=1, source_target_pairs={{0,4},{4,0},{8,12},{12,8},{16,20},{20,16},{24,28},{28,24},{1,5},{5... | collective-permute-start | bytes 6291464 | tf_op jit(solution)/shard_map/ppermute | solution.py:236
  100.6 46.7 %collective-permute-start.5 = (bf16[512,1024]{1,0:T(8,128)(2,1)S(1)}, bf16[512,1024]{1,0:T(8,128)(2,1)}, u32[]{:S(2)}, u32[]{:S(2)}) collective-permute-start(bf16[512,1024]{1,0:T(8,128)(2,1)S(1)} %copy-done.20), channel_id=1, source_target_pairs={{0,2},{1,3},{2,0},{3,1},{4,6},{5,7},{6,4},{7,5},{8,10},{9,11},{10,... | collective-permute-start | bytes 3145736 | tf_op jit(solution)/shard_map/ppermute | solution.py:338
  148.8 27.0 %collective-permute-start.6 = (bf16[2,512,1024]{2,1,0:T(8,128)(2,1)S(1)}, bf16[2,512,1024]{2,1,0:T(8,128)(2,1)S(1)}, u32[]{:S(2)}, u32[]{:S(2)}) collective-permute-start(bf16[2,512,1024]{2,1,0:T(8,128)(2,1)S(1)} %pad_maximum_fusion.2), channel_id=1, source_target_pairs={{0,1},{1,0},{2,3},{3,2},{4,5},{5,4},{6,7},{7,6},{8,9},{9,8},{10,11... | collective-permute-start | bytes 6291464 | tf_op jit(solution)/shard_map/ppermute | solution.py:338
  197.4 32.5 %collective-permute-start.9 = (bf16[512,1024]{1,0:T(8,128)(2,1)S(1)}, bf16[512,1024]{1,0:T(8,128)(2,1)}, u32[]{:S(2)}, u32[]{:S(2)}) collective-permute-start(bf16[512,1024]{1,0:T(8,128)(2,1)S(1)} %fusion.30), channel_id=1, source_target_pairs={{0,2},{1,3},{2,0},{3,1},{4,6},{5,7},{6,4},{7,5},{8,10},{9,11},{10,... | collective-permute-start | bytes 3145736 | tf_op jit(solution)/shard_map/ppermute | solution.py:338
  233.6 24.2 %collective-permute-start.10 = (bf16[512,1024]{1,0:T(8,128)(2,1)S(1)}, bf16[512,1024]{1,0:T(8,128)(2,1)S(1)}, u32[]{:S(2)}, u32[]{:S(2)}) collective-permute-start(bf16[512,1024]{1,0:T(8,128)(2,1)S(1)} %get-tuple-element.166), channel_id=1, source_target_pairs={{0,2},{1,3},{2,0},{3,1},{4,6},{5,7},{6,4},{7,5},{8,10},{9,11},{10,... | collective-permute-start | bytes 3145736 | tf_op jit(solution)/shard_map/ppermute | solution.py:338
  294.9 25.3 %collective-permute-start.13 = (bf16[512,1024]{1,0:T(8,128)(2,1)S(1)}, bf16[512,1024]{1,0:T(8,128)(2,1)S(1)}, u32[]{:S(2)}, u32[]{:S(2)}) collective-permute-start(bf16[512,1024]{1,0:T(8,128)(2,1)S(1)} %fusion.26), channel_id=1, source_target_pairs={{0,2},{1,3},{2,0},{3,1},{4,6},{5,7},{6,4},{7,5},{8,10},{9,11},{10,... | collective-permute-start | bytes 3145736 | tf_op jit(solution)/shard_map/ppermute | solution.py:338
  323.2 24.4 %collective-permute-start.14 = (bf16[512,1024]{1,0:T(8,128)(2,1)S(1)}, bf16[512,1024]{1,0:T(8,128)(2,1)S(1)}, u32[]{:S(2)}, u32[]{:S(2)}) collective-permute-start(bf16[512,1024]{1,0:T(8,128)(2,1)S(1)} %get-tuple-element.163), channel_id=1, source_target_pairs={{0,2},{1,3},{2,0},{3,1},{4,6},{5,7},{6,4},{7,5},{8,10},{9,11},{10,... | collective-permute-start | bytes 3145736 | tf_op jit(solution)/shard_map/ppermute | solution.py:338
  397.7 47.7 %collective-permute-start.17 = (bf16[512,1024]{1,0:T(8,128)(2,1)S(1)}, bf16[512,1024]{1,0:T(8,128)(2,1)}, u32[]{:S(2)}, u32[]{:S(2)}) collective-permute-start(bf16[512,1024]{1,0:T(8,128)(2,1)S(1)} %fusion.22), channel_id=1, source_target_pairs={{0,2},{1,3},{2,0},{3,1},{4,6},{5,7},{6,4},{7,5},{8,10},{9,11},{10,... | collective-permute-start | bytes 3145736 | tf_op jit(solution)/shard_map/ppermute | solution.py:338
  442.7 63.5 %collective-permute-start.18 = (bf16[2,2,2048,128]{3,2,1,0:T(8,128)(2,1)}, bf16[2,2,2048,128]{3,2,1,0:T(8,128)(2,1)}, u32[]{:S(2)}, u32[]{:S(2)}) collective-permute-start(bf16[2,2,2048,128]{3,2,1,0:T(8,128)(2,1)} %fusion.5), channel_id=1, source_target_pairs={{0,4},{4,0},{8,12},{12,8},{16,20},{20,16},{24,28},{28,24},{1,5},{5... | collective-permute-start | bytes 6291464 | tf_op jit(solution)/shard_map/ppermute | solution.py:236
  528.4 13.4 %collective-permute-start.24 = (bf16[512,512]{0,1:T(8,128)(2,1)}, bf16[512,512]{0,1:T(8,128)(2,1)}, u32[]{:S(2)}, u32[]{:S(2)}) collective-permute-start(bf16[512,512]{0,1:T(8,128)(2,1)} %dynamic-slice_convert_fusion.8), channel_id=1, source_target_pairs={{0,4},{4,0},{8,12},{12,8},{16,20},{20,16},{24,28},{28,24},{1,5},{5... | collective-permute-start | bytes 1572872 | tf_op jit(solution)/shard_map/ppermute | solution.py:304
  544.8 42.0 %collective-permute-start.25 = (bf16[256,512]{0,1:T(8,128)(2,1)}, bf16[256,512]{0,1:T(8,128)(2,1)}, u32[]{:S(2)}, u32[]{:S(2)}) collective-permute-start(bf16[256,512]{0,1:T(8,128)(2,1)} %dynamic-slice_convert_fusion.10), channel_id=1, source_target_pairs={{0,8},{4,12},{8,0},{12,4},{16,24},{20,28},{24,16},{28,20},{1,9},{5... | collective-permute-start | bytes 786440 | tf_op jit(solution)/shard_map/ppermute | solution.py:304
  585.7 14.4 %collective-permute-start.21 = (bf16[512,512]{1,0:T(8,128)(2,1)S(1)}, bf16[512,512]{1,0:T(8,128)(2,1)S(1)}, u32[]{:S(2)}, u32[]{:S(2)}) collective-permute-start(bf16[512,512]{1,0:T(8,128)(2,1)S(1)} %dynamic-slice_convert_fusion.9), channel_id=1, source_target_pairs={{0,4},{4,0},{8,12},{12,8},{16,20},{20,16},{24,28},{28,24},{1,5},{5... | collective-permute-start | bytes 1572872 | tf_op jit(solution)/shard_map/ppermute | solution.py:304
  587.8 15.7 %collective-permute-start.26 = (bf16[128,512]{0,1:T(8,128)(2,1)S(1)}, bf16[128,512]{0,1:T(8,128)(2,1)S(1)}, u32[]{:S(2)}, u32[]{:S(2)}) collective-permute-start(bf16[128,512]{0,1:T(8,128)(2,1)S(1)} %dynamic-slice_convert_fusion.12), channel_id=1, source_target_pairs={{0,16},{4,20},{8,24},{12,28},{16,0},{20,4},{24,8},{28,12},{1,17},{... | collective-permute-start | bytes 393224 | tf_op jit(solution)/shard_map/ppermute | solution.py:304
  590.5 25.3 %collective-permute-start.20 = (bf16[512,1024]{1,0:T(8,128)(2,1)S(1)}, bf16[512,1024]{1,0:T(8,128)(2,1)S(1)}, u32[]{:S(2)}, u32[]{:S(2)}) collective-permute-start(bf16[512,1024]{1,0:T(8,128)(2,1)S(1)} %fusion.18), channel_id=1, source_target_pairs={{0,2},{1,3},{2,0},{3,1},{4,6},{5,7},{6,4},{7,5},{8,10},{9,11},{10,... | collective-permute-start | bytes 3145736 | tf_op jit(solution)/shard_map/ppermute | solution.py:338
  600.3 7.9 %collective-permute-start.22 = (bf16[256,512]{1,0:T(8,128)(2,1)S(1)}, bf16[256,512]{1,0:T(8,128)(2,1)S(1)}, u32[]{:S(2)}, u32[]{:S(2)}) collective-permute-start(bf16[256,512]{1,0:T(8,128)(2,1)S(1)} %dynamic-slice_convert_fusion.11), channel_id=1, source_target_pairs={{0,8},{4,12},{8,0},{12,4},{16,24},{20,28},{24,16},{28,20},{1,9},{5... | collective-permute-start | bytes 786440 | tf_op jit(solution)/shard_map/ppermute | solution.py:304
  619.4 12.1 %collective-permute-start.23 = (bf16[128,512]{1,0:T(8,128)(2,1)}, bf16[128,512]{1,0:T(8,128)(2,1)}, u32[]{:S(2)}, u32[]{:S(2)}) collective-permute-start(bf16[128,512]{1,0:T(8,128)(2,1)} %dynamic-slice_convert_fusion.13), channel_id=1, source_target_pairs={{0,16},{4,20},{8,24},{12,28},{16,0},{20,4},{24,8},{28,12},{1,17},{... | collective-permute-start | bytes 393224 | tf_op jit(solution)/shard_map/ppermute | solution.py:304
  621.7 8.4 %collective-permute-start.28 = (f32[2304]{0:T(1024)S(1)}, f32[2304]{0:T(1024)}, u32[]{:S(2)}, u32[]{:S(2)}) collective-permute-start(f32[2304]{0:T(1024)S(1)} %fusion.109), channel_id=1, source_target_pairs={{0,2},{1,3},{2,0},{3,1},{4,6},{5,7},{6,4},{7,5},{8,10},{9,11},{10,... | collective-permute-start | bytes 27656 | tf_op jit(solution)/shard_map/ppermute | solution.py:329
  (107 other events, 1163.7 us)
Sparse Core Ops, SparseCore 0:
  10.7 43.0 all-gather.6
  56.5 38.9 all-gather.4
  98.1 44.8 all-gather.8
  145.0 78.8 all-gather.10
  385.0 122.9 reduce-scatter.1

commit v15 on v14

--- a/solution.py
+++ b/solution.py
@@ -483,12 +483,13 @@
         mlp_full, (gate_weight.shape[1], up_weight.shape[1], down_weight.shape[0])
     )
     out_partial = contract_last(out_rows, w_out)
-    late_grad_all, out_partial = lax.optimization_barrier((mlp_grad_all, out_partial))
+    after_attn = x_float + token_sum(lambda start, count: out_partial, rows)
+    gain_second = gain_post.astype(jnp.float32)
+    second_rows = rms_scale(after_attn, gain_second).astype(jnp.bfloat16)
+    late_grad_all, second_rows = lax.optimization_barrier((mlp_grad_all, second_rows))
     grad_act = jnp.dot(late_grad_all, w_down_t, preferred_element_type=jnp.float32)
-    after_attn = x_float + token_sum(lambda start, count: out_partial, rows)
-    grad_act, after_attn = lax.optimization_barrier((grad_act, after_attn))
-    gain_second = gain_post.astype(jnp.float32)
-    second_all = token_gather(rms_scale(after_attn, gain_second).astype(jnp.bfloat16))
+    second_all = token_gather(second_rows)
+    grad_act, second_all = lax.optimization_barrier((grad_act, second_all))
     gate_out = jnp.dot(second_all, w_gate, preferred_element_type=jnp.float32)
     up_out = jnp.dot(second_all, w_up, preferred_element_type=jnp.float32)
     activated = (jax.nn.silu(gate_out) * up_out).astype(jnp.bfloat16)

time: 658 us -> 680 us (1.033)
  local copies, waits for them, and re-layouts: 93.4 us -> 109 us
  matrix products: 93.7 us -> 107 us
    all_gather x1, waiting for transfers between devices: 25.1 us -> 0.01 us  [shards(): lax.all_gather(jnp.concatenate([gate_weight.astype(jnp.bfloat16), up_weig...]
    ppermute x16, waiting for transfers between devices: 100 us -> 122 us  [exchange(): lax.ppermute(values, 'tensor', [(i, i ^ distance) for i in range(count)])]
    dynamic_update_slice x13 -> x14, local copies, waits for them, and re-layouts: 8.01 us -> 19.4 us  [finish_gather(): full = lax.dynamic_update_slice_in_dim(full, part, place * rows, 0)]
    unnamed x203 -> x215, local copies, waits for them, and re-layouts: 35.9 us -> 37.3 us
  transfers between devices with their start and end apart: 37 -> 37, of which waited for: 20 -> 18; matrix products, arithmetic and copies ran while one was open for 32% -> 34% of each run, Pallas kernels for 21% -> 20%
where the time goes in v15:
time: 680 us; the launch traced here: 676 us
  waiting for transfers between devices  162 us (24%)
  Pallas kernels  135 us (20%)
  other arithmetic  112 us (16%)
  local copies, waits for them, and re-layouts  109 us (16%)
  matrix products  107 us (16%)
  starting transfers between devices  35.1 us (5%)
  between operations  16 us (2%)
    ppermute x16, waiting for transfers between devices, exchange(): lax.ppermute(values, 'tensor', [(i, i ^ distance) for i in range(count)])  122 us
    pallas_call x2, Pallas kernels, attention_backward(): pl.pallas_call(functools.partial(_bwd_kernel, scale=scale, block=block),...  83.3 us
    pallas_call x2, Pallas kernels, attention_forward(): pl.pallas_call(functools.partial(_fwd_kernel, scale=scale, block=block),...  51.9 us
    dot_general x7, matrix products, contract_last(): lax.dot_general(left, right, (((1,), (1,)), ((), ())), preferred_element_...  42.7 us
    unnamed x215, local copies, waits for them, and re-layouts  37.3 us
    dot_general x7, matrix products, contract_rows(): lax.dot_general(left, right, (((0,), (0,)), ((), ())), preferred_element_...  28.9 us
    dynamic_update_slice x14, local copies, waits for them, and re-layouts, finish_gather(): full = lax.dynamic_update_slice_in_dim(full, part, place * rows, 0)  19.4 us
    another operation x9, local copies, waits for them, and re-layouts  16.4 us
  transfers between devices with their start and end apart: 37, of which 18 were waited for; matrix products, arithmetic and copies ran while one was open for 34% of the time, Pallas kernels for 20%

profile of v15, /device:TPU:0, one launch (start us, length us, event | category | flops | bytes accessed | tf_op | source)
XLA Modules:
  0.0 676.0 jit_solution(13680606926204231557)
XLA Ops:
  29.9 20.8 %collective-permute-done.3 = bf16[512,1024]{0,1:T(8,128)(2,1)S(1)} collective-permute-done((bf16[512,1024]{0,1:T(8,128)(2,1)S(1)}, bf16[512,1024]{0,1:T(8,128)(2,1)S(1)}, u32[]{:S(2)}, u32[]{:S(2)}) %collective-permute-start.3) | collective-permute-done | bytes 1048608 | tf_op jit(solution)/shard_map/ppermute | solution.py:338
  89.0 6.4 all-gather.5.cloned.1.call-done
  118.9 28.7 %attn_fwd.2 = (f32[2,2,2048,128]{3,2,1,0:T(8,128)}, f32[2,2,2048,128]{3,2,1,0:T(8,128)}) custom-call(s32[7,10]{1,0:T(8,128)S(1)} %broadcast_select_fusion.5.tab_ref, bf16[2,2,2048,128]{3,2,1,0:T(8,128)(2,1)S(1)} %maximum_bitcast_fusion.q_ref, s32[2048,128]{1,0:T(8,128)S(1)} %broadcast_in_dim.45.qs_ref, ...), custom_call_target="tpu_custom_call", output_to_operand_aliasing={{0}: (5, {}), {1}: (6, {})} | custom-call | flops 5368709120 | bytes 20971520 | tf_op jit(solution)/shard_map/attn_fwd/pallas_call | solution.py:124
  157.3 23.1 %attn_fwd.3 = (f32[2,2,2048,128]{3,2,1,0:T(8,128)}, f32[2,2,2048,128]{3,2,1,0:T(8,128)}) custom-call(s32[7,8]{1,0:T(8,128)S(1)} %broadcast_select_fusion.3.tab_ref, bf16[2,2,2048,128]{3,2,1,0:T(8,128)(2,1)S(1)} %maximum_bitcast_fusion.q_ref, s32[2048,128]{1,0:T(8,128)S(1)} %copy-done.3, ...), custom_call_target="tpu_custom_call", output_to_operand_aliasing={{0}: (5, {}), {1}: (6, {})} | custom-call | flops 4294967296 | bytes 16777216 | tf_op jit(solution)/shard_map/attn_fwd/pallas_call | solution.py:124
  202.9 24.0 %collective-permute-done.9 = bf16[512,1024]{0,1:T(8,128)(2,1)S(1)} collective-permute-done((bf16[512,1024]{0,1:T(8,128)(2,1)S(1)}, bf16[512,1024]{0,1:T(8,128)(2,1)S(1)}, u32[]{:S(2)}, u32[]{:S(2)}) %collective-permute-start.9) | collective-permute-done | bytes 1048608 | tf_op jit(solution)/shard_map/ppermute | solution.py:338
  229.4 23.2 %collective-permute-done.10 = bf16[512,1024]{0,1:T(8,128)(2,1)S(1)} collective-permute-done((bf16[512,1024]{0,1:T(8,128)(2,1)S(1)}, bf16[512,1024]{0,1:T(8,128)(2,1)S(1)}, u32[]{:S(2)}, u32[]{:S(2)}) %collective-permute-start.10) | collective-permute-done | bytes 1048608 | tf_op jit(solution)/shard_map/ppermute | solution.py:338
  257.8 5.8 fusion.46
  270.0 5.5 fusion.38
  275.5 5.3 fusion.42
  280.8 5.3 multiply_convert_fusion
  286.2 10.4 %fusion.40 = f32[2048,1024]{0,1:T(8,128)} fusion(bf16[2048,768]{1,0:T(8,128)(2,1)} %get-tuple-element.74, bf16[1024,2304]{0,1:T(8,128)(2,1)} %all-gather.11.cloned.1.call-done), kind=kOutput, calls=%fused_computation.132 | convolution fusion | flops 3221225472 | bytes 13107200 | tf_op jit(solution)/shard_map/dot_general | solution.py:276
  296.5 6.6 convolution_add_fusion
  304.3 6.8 fusion.119
  313.6 7.0 %fusion.118 = bf16[1024,768]{1,0:T(8,128)(2,1)} fusion(bf16[2048,1024]{0,1:T(8,128)(2,1)} %fusion.59, bf16[2048,768]{1,0:T(8,128)(2,1)S(1)} %copy-done.49), kind=kOutput, calls=%fused_computation.298 | convolution fusion | flops 3221225472 | bytes 8912896 | tf_op jit(solution)/shard_map/dot_general | solution.py:270
  325.4 11.8 %collective-permute-done.13 = bf16[512,1024]{0,1:T(8,128)(2,1)S(1)} collective-permute-done((bf16[512,1024]{0,1:T(8,128)(2,1)S(1)}, bf16[512,1024]{0,1:T(8,128)(2,1)S(1)}, u32[]{:S(2)}, u32[]{:S(2)}) %collective-permute-start.13) | collective-permute-done | bytes 1048608 | tf_op jit(solution)/shard_map/ppermute | solution.py:338
  341.9 22.7 %collective-permute-done.14 = bf16[512,1024]{0,1:T(8,128)(2,1)S(1)} collective-permute-done((bf16[512,1024]{0,1:T(8,128)(2,1)S(1)}, bf16[512,1024]{0,1:T(8,128)(2,1)S(1)}, u32[]{:S(2)}, u32[]{:S(2)}) %collective-permute-start.14) | collective-permute-done | bytes 1048608 | tf_op jit(solution)/shard_map/ppermute | solution.py:338
  379.6 7.2 %fusion.6 = (f32[2048,2,2]{0,2,1:T(2,128)S(1)}, bf16[2,2,2048,128]{3,2,1,0:T(8,128)(2,1)}) fusion(f32[2048,2,2,128]{3,0,2,1:T(8,128)} %copy.152, f32[2,2,2048,128]{3,2,1,0:T(8,128)} %get-tuple-element.66, f32[2,2,2048]{2,1,0:T(2,128)S(1)} %slice_reduce_fusion, f32[2048,2,2]{0,2,1:T(2,128)S(1)} %bitcast.252), kind=kLoop, calls=%fused_computation.30 | loop fusion | flops 5234688 | bytes 10584064 | tf_op jit(solution)/shard_map/reduce_sum | solution.py:532
  419.1 37.5 %attn_bwd.2 = (f32[2,2,2048,128]{3,2,1,0:T(8,128)}, f32[2,2048,128]{2,1,0:T(8,128)}, f32[2,2048,128]{2,1,0:T(8,128)}) custom-call(s32[7,8]{1,0:T(8,128)} %broadcast_select_fusion.2.tab_ref, bf16[2,2,2048,128]{3,2,1,0:T(8,128)(2,1)} %copy-done.1, bf16[2,2,2048,128]{3,2,1,0:T(8,128)(2,1)} %get-tuple-element.85.h_ref, ...), custom_call_target="tpu_custom_call", output_to_operand_aliasing={{0}: (7, {})} | custom-call | flops 10737418240 | bytes 20971520 | tf_op jit(solution)/shard_map/attn_bwd/pallas_call | solution.py:207
  466.5 45.8 %attn_bwd.3 = (f32[2,2,2048,128]{3,2,1,0:T(8,128)}, f32[2,2048,128]{2,1,0:T(8,128)}, f32[2,2048,128]{2,1,0:T(8,128)}) custom-call(s32[7,10]{1,0:T(8,128)} %broadcast_select_fusion.4.tab_ref, bf16[2,2,2048,128]{3,2,1,0:T(8,128)(2,1)} %copy-done.1, bf16[2,2,2048,128]{3,2,1,0:T(8,128)(2,1)} %get-tuple-element.85.h_ref, ...), custom_call_target="tpu_custom_call", output_to_operand_aliasing={{0}: (7, {})} | custom-call | flops 13421772800 | bytes 26214400 | tf_op jit(solution)/shard_map/attn_bwd/pallas_call | solution.py:207
  512.3 11.4 %collective-permute-done.18 = bf16[2,2,2048,128]{3,2,1,0:T(8,128)(2,1)} collective-permute-done((bf16[2,2,2048,128]{3,2,1,0:T(8,128)(2,1)}, bf16[2,2,2048,128]{3,2,1,0:T(8,128)(2,1)}, u32[]{:S(2)}, u32[]{:S(2)}) %collective-permute-start.18) | collective-permute-done | bytes 2097184 | tf_op jit(solution)/shard_map/ppermute | solution.py:236
  546.1 5.8 fusion.67
  551.9 6.9 %collective-permute-done.24 = bf16[512,512]{0,1:T(8,128)(2,1)} collective-permute-done((bf16[512,512]{0,1:T(8,128)(2,1)}, bf16[512,512]{0,1:T(8,128)(2,1)}, u32[]{:S(2)}, u32[]{:S(2)}) %collective-permute-start.24) | collective-permute-done | bytes 524320 | tf_op jit(solution)/shard_map/ppermute | solution.py:304
  591.2 5.7 fusion.124
  627.8 8.4 %collective-permute-done.20 = bf16[512,1024]{0,1:T(8,128)(2,1)} collective-permute-done((bf16[512,1024]{0,1:T(8,128)(2,1)}, bf16[512,1024]{0,1:T(8,128)(2,1)}, u32[]{:S(2)}, u32[]{:S(2)}) %collective-permute-start.20) | collective-permute-done | bytes 1048608 | tf_op jit(solution)/shard_map/ppermute | solution.py:338
  (462 shorter events, 318.1 us)
Async XLA Ops:
  7.2 61.7 %all-gather.7.cloned.1.call-start = ((), (), s32[]{:S(2)}) async-start(), calls=%async_computation.2 | async-start | bytes 1179648 | tf_op jit(solution)/shard_map/all_gather | solution.py:413
  9.7 85.7 %all-gather.5.cloned.1.call-start = ((), (), s32[]{:S(2)}) async-start(), calls=%async_computation.1 | async-start | bytes 1179648 | tf_op jit(solution)/shard_map/all_gather | solution.py:422
  17.1 174.1 %all-gather.9.cloned.1.call-start = ((), (), s32[]{:S(2)}) async-start(), calls=%async_computation.3 | async-start | bytes 1179648 | tf_op jit(solution)/shard_map/all_gather | solution.py:423
  28.4 22.3 %collective-permute-start.3 = (bf16[512,1024]{0,1:T(8,128)(2,1)S(1)}, bf16[512,1024]{0,1:T(8,128)(2,1)S(1)}, u32[]{:S(2)}, u32[]{:S(2)}) collective-permute-start(bf16[512,1024]{0,1:T(8,128)(2,1)S(1)} %get-tuple-element.168), channel_id=1, source_target_pairs={{0,2},{1,3},{2,0},{3,1},{4,6},{5,7},{6,4},{7,5},{8,10},{9,11},{10,... | collective-permute-start | bytes 3145736 | tf_op jit(solution)/shard_map/ppermute | solution.py:338
  52.2 12.0 %collective-permute-start.4 = (bf16[2,512,1024]{1,2,0:T(8,128)(2,1)}, bf16[2,512,1024]{1,2,0:T(8,128)(2,1)}, u32[]{:S(2)}, u32[]{:S(2)}) collective-permute-start(bf16[2,512,1024]{1,2,0:T(8,128)(2,1)} %pad_maximum_fusion.1), channel_id=1, source_target_pairs={{0,1},{1,0},{2,3},{3,2},{4,5},{5,4},{6,7},{7,6},{8,9},{9,8},{10,11... | collective-permute-start | bytes 6291464 | tf_op jit(solution)/shard_map/ppermute | solution.py:338
  52.9 204.9 %all-gather.11.cloned.1.call-start = ((), (), s32[]{:S(2)}) async-start(), calls=%async_computation.4 | async-start | bytes 5308416 | tf_op jit(solution)/shard_map/all_gather | solution.py:469
  88.5 66.9 %collective-permute-start.7 = (bf16[2,2,2048,128]{3,2,1,0:T(8,128)(2,1)}, bf16[2,2,2048,128]{3,2,1,0:T(8,128)(2,1)}, u32[]{:S(2)}, u32[]{:S(2)}) collective-permute-start(bf16[2,2,2048,128]{3,2,1,0:T(8,128)(2,1)} %pad_maximum_fusion.3), channel_id=1, source_target_pairs={{0,4},{4,0},{8,12},{12,8},{16,20},{20,16},{24,28},{28,24},{1,5},{5... | collective-permute-start | bytes 6291464 | tf_op jit(solution)/shard_map/ppermute | solution.py:236
  100.4 47.2 %collective-permute-start.5 = (bf16[512,1024]{0,1:T(8,128)(2,1)}, bf16[512,1024]{0,1:T(8,128)(2,1)}, u32[]{:S(2)}, u32[]{:S(2)}) collective-permute-start(bf16[512,1024]{0,1:T(8,128)(2,1)} %fusion.35), channel_id=1, source_target_pairs={{0,2},{1,3},{2,0},{3,1},{4,6},{5,7},{6,4},{7,5},{8,10},{9,11},{10,... | collective-permute-start | bytes 3145736 | tf_op jit(solution)/shard_map/ppermute | solution.py:338
  150.8 29.7 %collective-permute-start.6 = (bf16[2,512,1024]{1,2,0:T(8,128)(2,1)}, bf16[2,512,1024]{1,2,0:T(8,128)(2,1)}, u32[]{:S(2)}, u32[]{:S(2)}) collective-permute-start(bf16[2,512,1024]{1,2,0:T(8,128)(2,1)} %pad_maximum_fusion.2), channel_id=1, source_target_pairs={{0,1},{1,0},{2,3},{3,2},{4,5},{5,4},{6,7},{7,6},{8,9},{9,8},{10,11... | collective-permute-start | bytes 6291464 | tf_op jit(solution)/shard_map/ppermute | solution.py:338
  152.1 410.3 %reduce-scatter.2.cloned.1.call-start = ((), (), s32[]{:S(2)}) async-start(), calls=%async_computation.5 | async-start | bytes 6488064 | tf_op jit(solution)/shard_map/reduce_scatter | solution.py:540
  201.4 25.5 %collective-permute-start.9 = (bf16[512,1024]{0,1:T(8,128)(2,1)S(1)}, bf16[512,1024]{0,1:T(8,128)(2,1)S(1)}, u32[]{:S(2)}, u32[]{:S(2)}) collective-permute-start(bf16[512,1024]{0,1:T(8,128)(2,1)S(1)} %fusion.30), channel_id=1, source_target_pairs={{0,2},{1,3},{2,0},{3,1},{4,6},{5,7},{6,4},{7,5},{8,10},{9,11},{10,... | collective-permute-start | bytes 3145736 | tf_op jit(solution)/shard_map/ppermute | solution.py:338
  227.8 24.8 %collective-permute-start.10 = (bf16[512,1024]{0,1:T(8,128)(2,1)S(1)}, bf16[512,1024]{0,1:T(8,128)(2,1)S(1)}, u32[]{:S(2)}, u32[]{:S(2)}) collective-permute-start(bf16[512,1024]{0,1:T(8,128)(2,1)S(1)} %multiply_convert_fusion.2), channel_id=1, source_target_pairs={{0,2},{1,3},{2,0},{3,1},{4,6},{5,7},{6,4},{7,5},{8,10},{9,11},{10,... | collective-permute-start | bytes 3145736 | tf_op jit(solution)/shard_map/ppermute | solution.py:338
  254.1 10.6 %collective-permute-start.11 = (bf16[2,512,1024]{1,2,0:T(8,128)(2,1)}, bf16[2,512,1024]{1,2,0:T(8,128)(2,1)}, u32[]{:S(2)}, u32[]{:S(2)}) collective-permute-start(bf16[2,512,1024]{1,2,0:T(8,128)(2,1)} %pad_maximum_fusion.5), channel_id=1, source_target_pairs={{0,1},{1,0},{2,3},{3,2},{4,5},{5,4},{6,7},{7,6},{8,9},{9,8},{10,11... | collective-permute-start | bytes 6291464 | tf_op jit(solution)/shard_map/ppermute | solution.py:338
  312.0 25.1 %collective-permute-start.13 = (bf16[512,1024]{0,1:T(8,128)(2,1)S(1)}, bf16[512,1024]{0,1:T(8,128)(2,1)S(1)}, u32[]{:S(2)}, u32[]{:S(2)}) collective-permute-start(bf16[512,1024]{0,1:T(8,128)(2,1)S(1)} %fusion.26), channel_id=1, source_target_pairs={{0,2},{1,3},{2,0},{3,1},{4,6},{5,7},{6,4},{7,5},{8,10},{9,11},{10,... | collective-permute-start | bytes 3145736 | tf_op jit(solution)/shard_map/ppermute | solution.py:338
  340.4 24.3 %collective-permute-start.14 = (bf16[512,1024]{0,1:T(8,128)(2,1)S(1)}, bf16[512,1024]{0,1:T(8,128)(2,1)S(1)}, u32[]{:S(2)}, u32[]{:S(2)}) collective-permute-start(bf16[512,1024]{0,1:T(8,128)(2,1)S(1)} %get-tuple-element.163), channel_id=1, source_target_pairs={{0,2},{1,3},{2,0},{3,1},{4,6},{5,7},{6,4},{7,5},{8,10},{9,11},{10,... | collective-permute-start | bytes 3145736 | tf_op jit(solution)/shard_map/ppermute | solution.py:338
  415.2 46.9 %collective-permute-start.17 = (bf16[512,1024]{0,1:T(8,128)(2,1)S(1)}, bf16[512,1024]{0,1:T(8,128)(2,1)}, u32[]{:S(2)}, u32[]{:S(2)}) collective-permute-start(bf16[512,1024]{0,1:T(8,128)(2,1)S(1)} %fusion.22), channel_id=1, source_target_pairs={{0,2},{1,3},{2,0},{3,1},{4,6},{5,7},{6,4},{7,5},{8,10},{9,11},{10,... | collective-permute-start | bytes 3145736 | tf_op jit(solution)/shard_map/ppermute | solution.py:338
  460.1 63.6 %collective-permute-start.18 = (bf16[2,2,2048,128]{3,2,1,0:T(8,128)(2,1)}, bf16[2,2,2048,128]{3,2,1,0:T(8,128)(2,1)}, u32[]{:S(2)}, u32[]{:S(2)}) collective-permute-start(bf16[2,2,2048,128]{3,2,1,0:T(8,128)(2,1)} %fusion.5), channel_id=1, source_target_pairs={{0,4},{4,0},{8,12},{12,8},{16,20},{20,16},{24,28},{28,24},{1,5},{5... | collective-permute-start | bytes 6291464 | tf_op jit(solution)/shard_map/ppermute | solution.py:236
  545.2 13.6 %collective-permute-start.24 = (bf16[512,512]{0,1:T(8,128)(2,1)}, bf16[512,512]{0,1:T(8,128)(2,1)}, u32[]{:S(2)}, u32[]{:S(2)}) collective-permute-start(bf16[512,512]{0,1:T(8,128)(2,1)} %dynamic-slice_convert_fusion.8), channel_id=1, source_target_pairs={{0,4},{4,0},{8,12},{12,8},{16,20},{20,16},{24,28},{28,24},{1,5},{5... | collective-permute-start | bytes 1572872 | tf_op jit(solution)/shard_map/ppermute | solution.py:304
  561.7 41.5 %collective-permute-start.25 = (bf16[256,512]{0,1:T(8,128)(2,1)}, bf16[256,512]{0,1:T(8,128)(2,1)}, u32[]{:S(2)}, u32[]{:S(2)}) collective-permute-start(bf16[256,512]{0,1:T(8,128)(2,1)} %dynamic-slice_convert_fusion.10), channel_id=1, source_target_pairs={{0,8},{4,12},{8,0},{12,4},{16,24},{20,28},{24,16},{28,20},{1,9},{5... | collective-permute-start | bytes 786440 | tf_op jit(solution)/shard_map/ppermute | solution.py:304
  602.8 14.4 %collective-permute-start.21 = (bf16[512,512]{1,0:T(8,128)(2,1)S(1)}, bf16[512,512]{1,0:T(8,128)(2,1)S(1)}, u32[]{:S(2)}, u32[]{:S(2)}) collective-permute-start(bf16[512,512]{1,0:T(8,128)(2,1)S(1)} %dynamic-slice_convert_fusion.9), channel_id=1, source_target_pairs={{0,4},{4,0},{8,12},{12,8},{16,20},{20,16},{24,28},{28,24},{1,5},{5... | collective-permute-start | bytes 1572872 | tf_op jit(solution)/shard_map/ppermute | solution.py:304
  606.5 15.4 %collective-permute-start.26 = (bf16[128,512]{0,1:T(8,128)(2,1)}, bf16[128,512]{0,1:T(8,128)(2,1)}, u32[]{:S(2)}, u32[]{:S(2)}) collective-permute-start(bf16[128,512]{0,1:T(8,128)(2,1)} %dynamic-slice_convert_fusion.12), channel_id=1, source_target_pairs={{0,16},{4,20},{8,24},{12,28},{16,0},{20,4},{24,8},{28,12},{1,17},{... | collective-permute-start | bytes 393224 | tf_op jit(solution)/shard_map/ppermute | solution.py:304
  611.5 24.7 %collective-permute-start.20 = (bf16[512,1024]{0,1:T(8,128)(2,1)}, bf16[512,1024]{0,1:T(8,128)(2,1)}, u32[]{:S(2)}, u32[]{:S(2)}) collective-permute-start(bf16[512,1024]{0,1:T(8,128)(2,1)} %fusion.18), channel_id=1, source_target_pairs={{0,2},{1,3},{2,0},{3,1},{4,6},{5,7},{6,4},{7,5},{8,10},{9,11},{10,... | collective-permute-start | bytes 3145736 | tf_op jit(solution)/shard_map/ppermute | solution.py:338
  642.2 11.4 %collective-permute-start.23 = (bf16[128,512]{1,0:T(8,128)(2,1)}, bf16[128,512]{1,0:T(8,128)(2,1)}, u32[]{:S(2)}, u32[]{:S(2)}) collective-permute-start(bf16[128,512]{1,0:T(8,128)(2,1)} %dynamic-slice_convert_fusion.13), channel_id=1, source_target_pairs={{0,16},{4,20},{8,24},{12,28},{16,0},{20,4},{24,8},{28,12},{1,17},{... | collective-permute-start | bytes 393224 | tf_op jit(solution)/shard_map/ppermute | solution.py:304
  643.8 8.4 %collective-permute-start.28 = (f32[2304]{0:T(1024)S(1)}, f32[2304]{0:T(1024)}, u32[]{:S(2)}, u32[]{:S(2)}) collective-permute-start(f32[2304]{0:T(1024)S(1)} %fusion.109), channel_id=1, source_target_pairs={{0,2},{1,3},{2,0},{3,1},{4,6},{5,7},{6,4},{7,5},{8,10},{9,11},{10,... | collective-permute-start | bytes 27656 | tf_op jit(solution)/shard_map/ppermute | solution.py:329
  (111 other events, 1118.6 us)
Sparse Core Ops, SparseCore 0:
  10.7 42.9 all-gather.6
  56.4 38.9 all-gather.4
  98.0 44.8 all-gather.8
  152.2 79.4 all-gather.10
  402.3 125.3 reduce-scatter.1

commit v16 on v14

--- a/solution.py
+++ b/solution.py
@@ -420,9 +420,19 @@
     )
     w_key, w_value = split_columns(kv_full, (key_matrix.shape[1], value_matrix.shape[1]))
     w_query = lax.all_gather(q_weight.astype(jnp.bfloat16), "fsdp", axis=0, tiled=True)
-    w_out = lax.all_gather(
-        jnp.transpose(o_weight).astype(jnp.bfloat16), "fsdp", axis=0, tiled=True
-    )
+    od_full = lax.all_gather(
+        jnp.concatenate(
+            [
+                jnp.transpose(o_weight).astype(jnp.bfloat16),
+                jnp.transpose(down_weight).astype(jnp.bfloat16),
+            ],
+            axis=1,
+        ),
+        "fsdp",
+        axis=0,
+        tiled=True,
+    )
+    w_out, w_down_t = split_columns(od_full, (o_weight.shape[0], down_weight.shape[0]))
     x_float = hidden.astype(jnp.float32)
     gain_first = gain_in.astype(jnp.float32)
     first_all = token_gather(rms_scale(x_float, gain_first).astype(jnp.bfloat16))
@@ -471,7 +481,6 @@
             [
                 gate_weight.astype(jnp.bfloat16),
                 up_weight.astype(jnp.bfloat16),
-                jnp.transpose(down_weight).astype(jnp.bfloat16),
             ],
             axis=1,
         ),
@@ -479,9 +488,7 @@
         axis=0,
         tiled=True,
     )
-    w_gate, w_up, w_down_t = split_columns(
-        mlp_full, (gate_weight.shape[1], up_weight.shape[1], down_weight.shape[0])
-    )
+    w_gate, w_up = split_columns(mlp_full, (gate_weight.shape[1], up_weight.shape[1]))
     out_partial = contract_last(out_rows, w_out)
     late_grad_all, out_partial = lax.optimization_barrier((mlp_grad_all, out_partial))
     grad_act = jnp.dot(late_grad_all, w_down_t, preferred_element_type=jnp.float32)

time: 658 us -> 662 us (level)
  matrix products: 93.7 us -> 105 us
    all_gather x1, waiting for transfers between devices: 25.1 us -> 0.01 us  [shards(): lax.all_gather(jnp.concatenate([gate_weight.astype(jnp.bfloat16), up_weig...]
    ppermute x16, waiting for transfers between devices: 100 us -> 116 us  [exchange(): lax.ppermute(values, 'tensor', [(i, i ^ distance) for i in range(count)])]
    unnamed x203 -> x205, local copies, waits for them, and re-layouts: 35.9 us -> 32.2 us
  transfers between devices with their start and end apart: 37 -> 37, of which waited for: 20 -> 20; matrix products, arithmetic and copies ran while one was open for 32% -> 33% of each run, Pallas kernels for 21% -> 21%
where the time goes in v16:
time: 662 us; the launch traced here: 655 us
  waiting for transfers between devices  161 us (24%)
  Pallas kernels  135 us (20%)
  other arithmetic  108 us (16%)
  matrix products  105 us (16%)
  local copies, waits for them, and re-layouts  94.8 us (14%)
  starting transfers between devices  34.5 us (5%)
  between operations  16 us (2%)
    ppermute x16, waiting for transfers between devices, exchange(): lax.ppermute(values, 'tensor', [(i, i ^ distance) for i in range(count)])  116 us
    pallas_call x2, Pallas kernels, attention_backward(): pl.pallas_call(functools.partial(_bwd_kernel, scale=scale, block=block),...  83.3 us
    pallas_call x2, Pallas kernels, attention_forward(): pl.pallas_call(functools.partial(_fwd_kernel, scale=scale, block=block),...  52.1 us
    dot_general x7, matrix products, contract_last(): lax.dot_general(left, right, (((1,), (1,)), ((), ())), preferred_element_...  36.3 us
    unnamed x205, local copies, waits for them, and re-layouts  32.2 us
    dot_general x7, matrix products, contract_rows(): lax.dot_general(left, right, (((0,), (0,)), ((), ())), preferred_element_...  28.8 us
    ppermute x6, waiting for transfers between devices, halving_scatter(): lax.ppermute(send.astype(jnp.bfloat16), 'fsdp', [(i, i ^ 1 << bit) for i...  19.8 us
    another operation x9, local copies, waits for them, and re-layouts  15.9 us
  transfers between devices with their start and end apart: 37, of which 20 were waited for; matrix products, arithmetic and copies ran while one was open for 33% of the time, Pallas kernels for 21%

profile of v16, /device:TPU:0, one launch (start us, length us, event | category | flops | bytes accessed | tf_op | source)
XLA Modules:
  0.0 655.1 jit_solution(8217202236189836389)
XLA Ops:
  29.4 20.8 %collective-permute-done.3 = bf16[512,1024]{1,0:T(8,128)(2,1)S(1)} collective-permute-done((bf16[512,1024]{1,0:T(8,128)(2,1)S(1)}, bf16[512,1024]{1,0:T(8,128)(2,1)S(1)}, u32[]{:S(2)}, u32[]{:S(2)}) %collective-permute-start.3) | collective-permute-done | bytes 1048608 | tf_op jit(solution)/shard_map/ppermute | solution.py:338
  87.5 8.0 %all-gather.5.cloned.1.call-done = bf16[1024,512]{1,0:T(8,128)(2,1)} async-done(((bf16[128,512]{1,0:T(8,128)(2,1)}), bf16[1024,512]{1,0:T(8,128)(2,1)}) %all-gather.5.cloned.1.call-update) | async-done | bytes 1048592 | tf_op jit(solution)/shard_map/all_gather | solution.py:422
  118.2 29.1 %attn_fwd.2 = (f32[2,2,2048,128]{3,2,1,0:T(8,128)}, f32[2,2,2048,128]{3,2,1,0:T(8,128)}) custom-call(s32[7,10]{1,0:T(8,128)S(1)} %broadcast_select_fusion.5.tab_ref, bf16[2,2,2048,128]{3,2,1,0:T(8,128)(2,1)S(1)} %maximum_bitcast_fusion.q_ref, s32[2048,128]{1,0:T(8,128)S(1)} %broadcast_in_dim.45.qs_ref, ...), custom_call_target="tpu_custom_call", output_to_operand_aliasing={{0}: (5, {}), {1}: (6, {})} | custom-call | flops 5368709120 | bytes 20971520 | tf_op jit(solution)/shard_map/attn_fwd/pallas_call | solution.py:124
  152.7 23.0 %attn_fwd.3 = (f32[2,2,2048,128]{3,2,1,0:T(8,128)}, f32[2,2,2048,128]{3,2,1,0:T(8,128)}) custom-call(s32[7,8]{1,0:T(8,128)S(1)} %broadcast_select_fusion.3.tab_ref, bf16[2,2,2048,128]{3,2,1,0:T(8,128)(2,1)S(1)} %maximum_bitcast_fusion.q_ref, s32[2048,128]{1,0:T(8,128)S(1)} %broadcast_in_dim.45.qs_ref, ...), custom_call_target="tpu_custom_call", output_to_operand_aliasing={{0}: (5, {}), {1}: (6, {})} | custom-call | flops 4294967296 | bytes 16777216 | tf_op jit(solution)/shard_map/attn_fwd/pallas_call | solution.py:124
  199.7 8.9 %fusion.46 = f32[2048,768]{1,0:T(8,128)} fusion(bf16[2048,1024]{1,0:T(8,128)(2,1)} %copy-done.41, bf16[1024,1280]{0,1:T(8,128)(2,1)} %all-gather.9.cloned.1.call-done), kind=kOutput, calls=%fused_computation.138 | convolution fusion | flops 3221225472 | bytes 12058624 | tf_op jit(solution)/shard_map/dot_general | solution.py:494
  208.6 14.2 %collective-permute-done.9 = bf16[512,1024]{1,0:T(8,128)(2,1)} collective-permute-done((bf16[512,1024]{1,0:T(8,128)(2,1)S(1)}, bf16[512,1024]{1,0:T(8,128)(2,1)}, u32[]{:S(2)}, u32[]{:S(2)}) %collective-permute-start.9) | collective-permute-done | bytes 1048608 | tf_op jit(solution)/shard_map/ppermute | solution.py:338
  230.8 23.3 %collective-permute-done.10 = bf16[512,1024]{1,0:T(8,128)(2,1)S(1)} collective-permute-done((bf16[512,1024]{1,0:T(8,128)(2,1)S(1)}, bf16[512,1024]{1,0:T(8,128)(2,1)S(1)}, u32[]{:S(2)}, u32[]{:S(2)}) %collective-permute-start.10) | collective-permute-done | bytes 1048608 | tf_op jit(solution)/shard_map/ppermute | solution.py:338
  260.6 5.8 fusion.38
  266.4 5.3 fusion.42
  271.8 5.5 multiply_convert_fusion
  277.3 7.1 %fusion.40 = f32[2048,1024]{1,0:T(8,128)S(1)} fusion(bf16[2048,768]{1,0:T(8,128)(2,1)} %get-tuple-element.74, bf16[1024,1536]{1,0:T(8,128)(2,1)} %all-gather.11.cloned.1.call-done), kind=kOutput, calls=%fused_computation.132 | convolution fusion | flops 3221225472 | bytes 13107200 | tf_op jit(solution)/shard_map/dot_general | solution.py:276
  288.7 6.9 %fusion.121 = bf16[1024,768]{1,0:T(8,128)(2,1)} fusion(bf16[2048,1024]{1,0:T(8,128)(2,1)} %fusion.59, bf16[2048,768]{1,0:T(8,128)(2,1)S(1)} %copy-done.48), kind=kOutput, calls=%fused_computation.302 | convolution fusion | flops 3221225472 | bytes 8912896 | tf_op jit(solution)/shard_map/dot_general | solution.py:270
  297.9 7.6 %fusion.120 = bf16[1024,768]{1,0:T(8,128)(2,1)} fusion(bf16[2048,1024]{1,0:T(8,128)(2,1)} %fusion.59, bf16[2048,768]{1,0:T(8,128)(2,1)S(1)} %copy-done.47), kind=kOutput, calls=%fused_computation.301 | convolution fusion | flops 3221225472 | bytes 8912896 | tf_op jit(solution)/shard_map/dot_general | solution.py:270
  310.2 11.7 %collective-permute-done.13 = bf16[512,1024]{1,0:T(8,128)(2,1)S(1)} collective-permute-done((bf16[512,1024]{1,0:T(8,128)(2,1)S(1)}, bf16[512,1024]{1,0:T(8,128)(2,1)S(1)}, u32[]{:S(2)}, u32[]{:S(2)}) %collective-permute-start.13) | collective-permute-done | bytes 1048608 | tf_op jit(solution)/shard_map/ppermute | solution.py:338
  326.4 23.3 %collective-permute-done.14 = bf16[512,1024]{1,0:T(8,128)(2,1)S(1)} collective-permute-done((bf16[512,1024]{1,0:T(8,128)(2,1)S(1)}, bf16[512,1024]{1,0:T(8,128)(2,1)S(1)}, u32[]{:S(2)}, u32[]{:S(2)}) %collective-permute-start.14) | collective-permute-done | bytes 1048608 | tf_op jit(solution)/shard_map/ppermute | solution.py:338
  365.8 7.2 %fusion.6 = (f32[2048,2,2]{0,2,1:T(2,128)S(1)}, bf16[2,2,2048,128]{3,2,1,0:T(8,128)(2,1)}) fusion(f32[2048,2,2,128]{3,0,2,1:T(8,128)} %copy.97, f32[2,2,2048,128]{3,2,1,0:T(8,128)} %get-tuple-element.67, f32[2,2,2048]{2,1,0:T(2,128)S(1)} %slice_reduce_fusion, f32[2048,2,2]{0,2,1:T(2,128)S(1)} %bitcast.252), kind=kLoop, calls=%fused_computation.30 | loop fusion | flops 5234688 | bytes 10584064 | tf_op jit(solution)/shard_map/reduce_sum | solution.py:538
  404.8 37.6 %attn_bwd.2 = (f32[2,2,2048,128]{3,2,1,0:T(8,128)}, f32[2,2048,128]{2,1,0:T(8,128)}, f32[2,2048,128]{2,1,0:T(8,128)}) custom-call(s32[7,8]{1,0:T(8,128)} %broadcast_select_fusion.2.tab_ref, bf16[2,2,2048,128]{3,2,1,0:T(8,128)(2,1)} %copy-done.1, bf16[2,2,2048,128]{3,2,1,0:T(8,128)(2,1)} %get-tuple-element.85.h_ref, ...), custom_call_target="tpu_custom_call", output_to_operand_aliasing={{0}: (7, {})} | custom-call | flops 10737418240 | bytes 20971520 | tf_op jit(solution)/shard_map/attn_bwd/pallas_call | solution.py:207
  452.5 45.7 %attn_bwd.3 = (f32[2,2,2048,128]{3,2,1,0:T(8,128)}, f32[2,2048,128]{2,1,0:T(8,128)}, f32[2,2048,128]{2,1,0:T(8,128)}) custom-call(s32[7,10]{1,0:T(8,128)} %broadcast_select_fusion.4.tab_ref, bf16[2,2,2048,128]{3,2,1,0:T(8,128)(2,1)} %copy-done.1, bf16[2,2,2048,128]{3,2,1,0:T(8,128)(2,1)} %get-tuple-element.85.h_ref, ...), custom_call_target="tpu_custom_call", output_to_operand_aliasing={{0}: (7, {})} | custom-call | flops 13421772800 | bytes 26214400 | tf_op jit(solution)/shard_map/attn_bwd/pallas_call | solution.py:207
  498.2 11.6 %collective-permute-done.18 = bf16[2,2,2048,128]{3,2,1,0:T(8,128)(2,1)} collective-permute-done((bf16[2,2,2048,128]{3,2,1,0:T(8,128)(2,1)}, bf16[2,2,2048,128]{3,2,1,0:T(8,128)(2,1)}, u32[]{:S(2)}, u32[]{:S(2)}) %collective-permute-start.18) | collective-permute-done | bytes 2097184 | tf_op jit(solution)/shard_map/ppermute | solution.py:236
  532.5 5.8 fusion.70
  538.4 7.2 %collective-permute-done.24 = bf16[512,512]{0,1:T(8,128)(2,1)} collective-permute-done((bf16[512,512]{0,1:T(8,128)(2,1)}, bf16[512,512]{0,1:T(8,128)(2,1)}, u32[]{:S(2)}, u32[]{:S(2)}) %collective-permute-start.24) | collective-permute-done | bytes 524320 | tf_op jit(solution)/shard_map/ppermute | solution.py:304
  578.0 5.8 fusion.123
  596.3 7.8 %collective-permute-done.21 = bf16[512,512]{1,0:T(8,128)(2,1)S(1)} collective-permute-done((bf16[512,512]{1,0:T(8,128)(2,1)S(1)}, bf16[512,512]{1,0:T(8,128)(2,1)S(1)}, u32[]{:S(2)}, u32[]{:S(2)}) %collective-permute-start.21) | collective-permute-done | bytes 524320 | tf_op jit(solution)/shard_map/ppermute | solution.py:304
  612.4 7.7 %collective-permute-done.20 = bf16[512,1024]{1,0:T(8,128)(2,1)S(1)} collective-permute-done((bf16[512,1024]{1,0:T(8,128)(2,1)S(1)}, bf16[512,1024]{1,0:T(8,128)(2,1)S(1)}, u32[]{:S(2)}, u32[]{:S(2)}) %collective-permute-start.20) | collective-permute-done | bytes 1048608 | tf_op jit(solution)/shard_map/ppermute | solution.py:338
  (456 shorter events, 302.3 us)
Async XLA Ops:
  7.2 59.5 %all-gather.7.cloned.1.call-start = ((), (), s32[]{:S(2)}) async-start(), calls=%async_computation.2 | async-start | bytes 1179648 | tf_op jit(solution)/shard_map/all_gather | solution.py:413
  9.7 85.7 %all-gather.5.cloned.1.call-start = ((), (), s32[]{:S(2)}) async-start(), calls=%async_computation.1 | async-start | bytes 1179648 | tf_op jit(solution)/shard_map/all_gather | solution.py:422
  17.1 168.5 %all-gather.9.cloned.1.call-start = ((), (), s32[]{:S(2)}) async-start(), calls=%async_computation.3 | async-start | bytes 2949120 | tf_op jit(solution)/shard_map/all_gather | solution.py:423
  27.5 22.7 %collective-permute-start.3 = (bf16[512,1024]{1,0:T(8,128)(2,1)S(1)}, bf16[512,1024]{1,0:T(8,128)(2,1)S(1)}, u32[]{:S(2)}, u32[]{:S(2)}) collective-permute-start(bf16[512,1024]{1,0:T(8,128)(2,1)S(1)} %get-tuple-element.168), channel_id=1, source_target_pairs={{0,2},{1,3},{2,0},{3,1},{4,6},{5,7},{6,4},{7,5},{8,10},{9,11},{10,... | collective-permute-start | bytes 3145736 | tf_op jit(solution)/shard_map/ppermute | solution.py:338
  51.8 10.3 %collective-permute-start.4 = (bf16[2,512,1024]{2,1,0:T(8,128)(2,1)}, bf16[2,512,1024]{2,1,0:T(8,128)(2,1)}, u32[]{:S(2)}, u32[]{:S(2)}) collective-permute-start(bf16[2,512,1024]{2,1,0:T(8,128)(2,1)} %pad_maximum_fusion.1), channel_id=1, source_target_pairs={{0,1},{1,0},{2,3},{3,2},{4,5},{5,4},{6,7},{7,6},{8,9},{9,8},{10,11... | collective-permute-start | bytes 6291464 | tf_op jit(solution)/shard_map/ppermute | solution.py:338
  52.5 208.1 %all-gather.11.cloned.1.call-start = ((), (), s32[]{:S(2)}) async-start(), calls=%async_computation.4 | async-start | bytes 3538944 | tf_op jit(solution)/shard_map/all_gather | solution.py:479
  86.6 64.3 %collective-permute-start.7 = (bf16[2,2,2048,128]{3,2,1,0:T(8,128)(2,1)}, bf16[2,2,2048,128]{3,2,1,0:T(8,128)(2,1)}, u32[]{:S(2)}, u32[]{:S(2)}) collective-permute-start(bf16[2,2,2048,128]{3,2,1,0:T(8,128)(2,1)} %pad_maximum_fusion.3), channel_id=1, source_target_pairs={{0,4},{4,0},{8,12},{12,8},{16,20},{20,16},{24,28},{28,24},{1,5},{5... | collective-permute-start | bytes 6291464 | tf_op jit(solution)/shard_map/ppermute | solution.py:236
  100.6 46.7 %collective-permute-start.5 = (bf16[512,1024]{1,0:T(8,128)(2,1)S(1)}, bf16[512,1024]{1,0:T(8,128)(2,1)}, u32[]{:S(2)}, u32[]{:S(2)}) collective-permute-start(bf16[512,1024]{1,0:T(8,128)(2,1)S(1)} %copy-done.20), channel_id=1, source_target_pairs={{0,2},{1,3},{2,0},{3,1},{4,6},{5,7},{6,4},{7,5},{8,10},{9,11},{10,... | collective-permute-start | bytes 3145736 | tf_op jit(solution)/shard_map/ppermute | solution.py:338
  148.8 26.8 %collective-permute-start.6 = (bf16[2,512,1024]{2,1,0:T(8,128)(2,1)S(1)}, bf16[2,512,1024]{2,1,0:T(8,128)(2,1)S(1)}, u32[]{:S(2)}, u32[]{:S(2)}) collective-permute-start(bf16[2,512,1024]{2,1,0:T(8,128)(2,1)S(1)} %pad_maximum_fusion.2), channel_id=1, source_target_pairs={{0,1},{1,0},{2,3},{3,2},{4,5},{5,4},{6,7},{7,6},{8,9},{9,8},{10,11... | collective-permute-start | bytes 6291464 | tf_op jit(solution)/shard_map/ppermute | solution.py:338
  197.3 25.5 %collective-permute-start.9 = (bf16[512,1024]{1,0:T(8,128)(2,1)S(1)}, bf16[512,1024]{1,0:T(8,128)(2,1)}, u32[]{:S(2)}, u32[]{:S(2)}) collective-permute-start(bf16[512,1024]{1,0:T(8,128)(2,1)S(1)} %fusion.30), channel_id=1, source_target_pairs={{0,2},{1,3},{2,0},{3,1},{4,6},{5,7},{6,4},{7,5},{8,10},{9,11},{10,... | collective-permute-start | bytes 3145736 | tf_op jit(solution)/shard_map/ppermute | solution.py:338
  199.5 349.7 %reduce-scatter.2.cloned.1.call-start = ((), (), s32[]{:S(2)}) async-start(), calls=%async_computation.5 | async-start | bytes 6488064 | tf_op jit(solution)/shard_map/reduce_scatter | solution.py:546
  229.5 24.6 %collective-permute-start.10 = (bf16[512,1024]{1,0:T(8,128)(2,1)S(1)}, bf16[512,1024]{1,0:T(8,128)(2,1)S(1)}, u32[]{:S(2)}, u32[]{:S(2)}) collective-permute-start(bf16[512,1024]{1,0:T(8,128)(2,1)S(1)} %get-tuple-element.166), channel_id=1, source_target_pairs={{0,2},{1,3},{2,0},{3,1},{4,6},{5,7},{6,4},{7,5},{8,10},{9,11},{10,... | collective-permute-start | bytes 3145736 | tf_op jit(solution)/shard_map/ppermute | solution.py:338
  296.4 25.5 %collective-permute-start.13 = (bf16[512,1024]{1,0:T(8,128)(2,1)S(1)}, bf16[512,1024]{1,0:T(8,128)(2,1)S(1)}, u32[]{:S(2)}, u32[]{:S(2)}) collective-permute-start(bf16[512,1024]{1,0:T(8,128)(2,1)S(1)} %fusion.26), channel_id=1, source_target_pairs={{0,2},{1,3},{2,0},{3,1},{4,6},{5,7},{6,4},{7,5},{8,10},{9,11},{10,... | collective-permute-start | bytes 3145736 | tf_op jit(solution)/shard_map/ppermute | solution.py:338
  325.0 24.7 %collective-permute-start.14 = (bf16[512,1024]{1,0:T(8,128)(2,1)S(1)}, bf16[512,1024]{1,0:T(8,128)(2,1)S(1)}, u32[]{:S(2)}, u32[]{:S(2)}) collective-permute-start(bf16[512,1024]{1,0:T(8,128)(2,1)S(1)} %get-tuple-element.163), channel_id=1, source_target_pairs={{0,2},{1,3},{2,0},{3,1},{4,6},{5,7},{6,4},{7,5},{8,10},{9,11},{10,... | collective-permute-start | bytes 3145736 | tf_op jit(solution)/shard_map/ppermute | solution.py:338
  401.0 46.9 %collective-permute-start.17 = (bf16[512,1024]{1,0:T(8,128)(2,1)S(1)}, bf16[512,1024]{1,0:T(8,128)(2,1)}, u32[]{:S(2)}, u32[]{:S(2)}) collective-permute-start(bf16[512,1024]{1,0:T(8,128)(2,1)S(1)} %fusion.22), channel_id=1, source_target_pairs={{0,2},{1,3},{2,0},{3,1},{4,6},{5,7},{6,4},{7,5},{8,10},{9,11},{10,... | collective-permute-start | bytes 3145736 | tf_op jit(solution)/shard_map/ppermute | solution.py:338
  445.9 63.8 %collective-permute-start.18 = (bf16[2,2,2048,128]{3,2,1,0:T(8,128)(2,1)}, bf16[2,2,2048,128]{3,2,1,0:T(8,128)(2,1)}, u32[]{:S(2)}, u32[]{:S(2)}) collective-permute-start(bf16[2,2,2048,128]{3,2,1,0:T(8,128)(2,1)} %fusion.5), channel_id=1, source_target_pairs={{0,4},{4,0},{8,12},{12,8},{16,20},{20,16},{24,28},{28,24},{1,5},{5... | collective-permute-start | bytes 6291464 | tf_op jit(solution)/shard_map/ppermute | solution.py:236
  531.9 13.7 %collective-permute-start.24 = (bf16[512,512]{0,1:T(8,128)(2,1)}, bf16[512,512]{0,1:T(8,128)(2,1)}, u32[]{:S(2)}, u32[]{:S(2)}) collective-permute-start(bf16[512,512]{0,1:T(8,128)(2,1)} %dynamic-slice_convert_fusion.8), channel_id=1, source_target_pairs={{0,4},{4,0},{8,12},{12,8},{16,20},{20,16},{24,28},{28,24},{1,5},{5... | collective-permute-start | bytes 1572872 | tf_op jit(solution)/shard_map/ppermute | solution.py:304
  548.5 41.6 %collective-permute-start.25 = (bf16[256,512]{0,1:T(8,128)(2,1)}, bf16[256,512]{0,1:T(8,128)(2,1)}, u32[]{:S(2)}, u32[]{:S(2)}) collective-permute-start(bf16[256,512]{0,1:T(8,128)(2,1)} %dynamic-slice_convert_fusion.10), channel_id=1, source_target_pairs={{0,8},{4,12},{8,0},{12,4},{16,24},{20,28},{24,16},{28,20},{1,9},{5... | collective-permute-start | bytes 786440 | tf_op jit(solution)/shard_map/ppermute | solution.py:304
  589.7 14.4 %collective-permute-start.21 = (bf16[512,512]{1,0:T(8,128)(2,1)S(1)}, bf16[512,512]{1,0:T(8,128)(2,1)S(1)}, u32[]{:S(2)}, u32[]{:S(2)}) collective-permute-start(bf16[512,512]{1,0:T(8,128)(2,1)S(1)} %dynamic-slice_convert_fusion.9), channel_id=1, source_target_pairs={{0,4},{4,0},{8,12},{12,8},{16,20},{20,16},{24,28},{28,24},{1,5},{5... | collective-permute-start | bytes 1572872 | tf_op jit(solution)/shard_map/ppermute | solution.py:304
  591.8 15.6 %collective-permute-start.26 = (bf16[128,512]{0,1:T(8,128)(2,1)S(1)}, bf16[128,512]{0,1:T(8,128)(2,1)S(1)}, u32[]{:S(2)}, u32[]{:S(2)}) collective-permute-start(bf16[128,512]{0,1:T(8,128)(2,1)S(1)} %dynamic-slice_convert_fusion.12), channel_id=1, source_target_pairs={{0,16},{4,20},{8,24},{12,28},{16,0},{20,4},{24,8},{28,12},{1,17},{... | collective-permute-start | bytes 393224 | tf_op jit(solution)/shard_map/ppermute | solution.py:304
  594.8 25.3 %collective-permute-start.20 = (bf16[512,1024]{1,0:T(8,128)(2,1)S(1)}, bf16[512,1024]{1,0:T(8,128)(2,1)S(1)}, u32[]{:S(2)}, u32[]{:S(2)}) collective-permute-start(bf16[512,1024]{1,0:T(8,128)(2,1)S(1)} %fusion.18), channel_id=1, source_target_pairs={{0,2},{1,3},{2,0},{3,1},{4,6},{5,7},{6,4},{7,5},{8,10},{9,11},{10,... | collective-permute-start | bytes 3145736 | tf_op jit(solution)/shard_map/ppermute | solution.py:338
  604.4 7.9 %collective-permute-start.22 = (bf16[256,512]{1,0:T(8,128)(2,1)S(1)}, bf16[256,512]{1,0:T(8,128)(2,1)S(1)}, u32[]{:S(2)}, u32[]{:S(2)}) collective-permute-start(bf16[256,512]{1,0:T(8,128)(2,1)S(1)} %dynamic-slice_convert_fusion.11), channel_id=1, source_target_pairs={{0,8},{4,12},{8,0},{12,4},{16,24},{20,28},{24,16},{28,20},{1,9},{5... | collective-permute-start | bytes 786440 | tf_op jit(solution)/shard_map/ppermute | solution.py:304
  623.6 11.6 %collective-permute-start.23 = (bf16[128,512]{1,0:T(8,128)(2,1)}, bf16[128,512]{1,0:T(8,128)(2,1)}, u32[]{:S(2)}, u32[]{:S(2)}) collective-permute-start(bf16[128,512]{1,0:T(8,128)(2,1)} %dynamic-slice_convert_fusion.13), channel_id=1, source_target_pairs={{0,16},{4,20},{8,24},{12,28},{16,0},{20,4},{24,8},{28,12},{1,17},{... | collective-permute-start | bytes 393224 | tf_op jit(solution)/shard_map/ppermute | solution.py:304
  626.0 8.2 %collective-permute-start.28 = (f32[2304]{0:T(1024)S(1)}, f32[2304]{0:T(1024)}, u32[]{:S(2)}, u32[]{:S(2)}) collective-permute-start(f32[2304]{0:T(1024)S(1)} %fusion.112), channel_id=1, source_target_pairs={{0,2},{1,3},{2,0},{3,1},{4,6},{5,7},{6,4},{7,5},{8,10},{9,11},{10,... | collective-permute-start | bytes 27656 | tf_op jit(solution)/shard_map/ppermute | solution.py:329
  (109 other events, 1190.3 us)
Sparse Core Ops, SparseCore 0:
  10.7 43.0 all-gather.6
  56.5 38.9 all-gather.4
  98.1 65.6 all-gather.8
  199.6 58.9 all-gather.10
  388.4 125.3 reduce-scatter.1

commit v17 on v14

--- a/solution.py
+++ b/solution.py
@@ -69,7 +69,16 @@
     return (kp >= start) & (kp <= qp)
 
 
-def _fwd_kernel(tab_ref, q_ref, qs_ref, k_ref, v_ref, a_in_ref, l_in_ref, a_ref, l_ref, acc_ref, sum_ref, *, scale, block):
+def _block_kind(tab_ref, qb_ref, n, block):
+    j = tab_ref[0, n]
+    key_first = tab_ref[2, n] * block
+    key_last = key_first + block - 1
+    full = (key_last < tab_ref[1, n] * block) & (key_first >= qb_ref[1, j])
+    empty = key_last < qb_ref[0, j]
+    return full, jnp.logical_not(full) & jnp.logical_not(empty)
+
+
+def _fwd_kernel(tab_ref, qb_ref, q_ref, qs_ref, k_ref, v_ref, a_in_ref, l_in_ref, a_ref, l_ref, acc_ref, sum_ref, *, scale, block):
     n = pl.program_id(1)
     share = q_ref.shape[1]
 
@@ -78,16 +87,23 @@
         acc_ref[...] = a_in_ref[0].reshape(share * block, HEAD_SIZE)
         sum_ref[...] = l_in_ref[0][:, :, :1]
 
-    q = q_ref[0].reshape(share * block, HEAD_SIZE)
-    k = k_ref[0]
-    v = v_ref[0]
-    s = lax.dot_general(q, k, TRANS_B, preferred_element_type=jnp.float32) * scale
-    allowed = _mask(tab_ref[1, n], tab_ref[2, n], qs_ref[...], block)
-    e = jnp.where(allowed[None], jnp.exp(s.reshape(share, block, block)), 0.0)
-    sum_ref[...] += jnp.sum(e, axis=-1, keepdims=True)
-    acc_ref[...] += jnp.dot(
-        e.reshape(share * block, block).astype(jnp.bfloat16), v, preferred_element_type=jnp.float32
-    )
+    def step(masked):
+        q = q_ref[0].reshape(share * block, HEAD_SIZE)
+        k = k_ref[0]
+        v = v_ref[0]
+        s = lax.dot_general(q, k, TRANS_B, preferred_element_type=jnp.float32) * scale
+        e = jnp.exp(s.reshape(share, block, block))
+        if masked:
+            allowed = _mask(tab_ref[1, n], tab_ref[2, n], qs_ref[...], block)
+            e = jnp.where(allowed[None], e, 0.0)
+        sum_ref[...] += jnp.sum(e, axis=-1, keepdims=True)
+        acc_ref[...] += jnp.dot(
+            e.reshape(share * block, block).astype(jnp.bfloat16), v, preferred_element_type=jnp.float32
+        )
+
+    full, partial = _block_kind(tab_ref, qb_ref, n, block)
+    pl.when(full)(lambda: step(False))
+    pl.when(partial)(lambda: step(True))
 
     @pl.when(tab_ref[6, n] == 1)
     def _():
@@ -95,20 +111,20 @@
         l_ref[0] = jnp.broadcast_to(sum_ref[...], (share, block, 128))
 
 
-def attention_forward(q, qs, keys, values, a_in, l_in, piece, quarter, source, block=512):
+def attention_forward(q, qs, qb, keys, values, a_in, l_in, piece, quarter, source, block=512):
     kvh, share, _, _ = q.shape
     tab = pair_tables(piece, quarter, block, False, source)
     npairs = tab.shape[1]
     scale = HEAD_SIZE ** (-0.5)
-    row_spec = pl.BlockSpec((1, share, block, HEAD_SIZE), lambda h, n, t: (h, 0, t[0, n], 0))
-    lane_spec = pl.BlockSpec((1, share, block, 128), lambda h, n, t: (h, 0, t[0, n], 0))
-    key_spec = pl.BlockSpec((1, block, HEAD_SIZE), lambda h, n, t: (h, t[4, n], 0))
+    row_spec = pl.BlockSpec((1, share, block, HEAD_SIZE), lambda h, n, t, b: (h, 0, t[0, n], 0))
+    lane_spec = pl.BlockSpec((1, share, block, 128), lambda h, n, t, b: (h, 0, t[0, n], 0))
+    key_spec = pl.BlockSpec((1, block, HEAD_SIZE), lambda h, n, t, b: (h, t[4, n], 0))
     grid_spec = pltpu.PrefetchScalarGridSpec(
-        num_scalar_prefetch=1,
+        num_scalar_prefetch=2,
         grid=(kvh, npairs),
         in_specs=[
             row_spec,
-            pl.BlockSpec((block, 128), lambda h, n, t: (t[0, n], 0)),
+            pl.BlockSpec((block, 128), lambda h, n, t, b: (t[0, n], 0)),
             key_spec,
             key_spec,
             row_spec,
@@ -128,7 +144,7 @@
             jax.ShapeDtypeStruct(a_in.shape, jnp.float32),
             jax.ShapeDtypeStruct(l_in.shape, jnp.float32),
         ],
-        input_output_aliases={5: 0, 6: 1},
+        input_output_aliases={6: 0, 7: 1},
         compiler_params=pltpu.CompilerParams(
             dimension_semantics=("arbitrary", "arbitrary"), vmem_limit_bytes=48 * 1024 * 1024
         ),
@@ -138,10 +154,10 @@
             bytes_accessed=kvh * npairs * (8 * block * HEAD_SIZE * 2),
         ),
         name="attn_fwd",
-    )(tab, q, qs, keys, values, a_in, l_in)
-
-
-def _bwd_kernel(tab_ref, q_ref, h_ref, dl_ref, qs_ref, k_ref, v_ref, dq_in_ref, dq_ref, dk_ref, dv_ref, dk_acc, dv_acc, *, scale, block):
+    )(tab, qb, q, qs, keys, values, a_in, l_in)
+
+
+def _bwd_kernel(tab_ref, qb_ref, q_ref, h_ref, dl_ref, qs_ref, k_ref, v_ref, dq_in_ref, dq_ref, dk_ref, dv_ref, dk_acc, dv_acc, *, scale, block):
     n = pl.program_id(1)
     share = q_ref.shape[1]
 
@@ -154,22 +170,29 @@
         dk_acc[...] = jnp.zeros(dk_acc.shape, dk_acc.dtype)
         dv_acc[...] = jnp.zeros(dv_acc.shape, dv_acc.dtype)
 
-    q = q_ref[0].reshape(share * block, HEAD_SIZE)
-    hh = h_ref[0].reshape(share * block, HEAD_SIZE)
-    k = k_ref[0]
-    v = v_ref[0]
-    s = lax.dot_general(q, k, TRANS_B, preferred_element_type=jnp.float32) * scale
-    allowed = _mask(tab_ref[1, n], tab_ref[2, n], qs_ref[...], block)
-    e = jnp.where(allowed[None], jnp.exp(s.reshape(share, block, block)), 0.0)
-    dp = lax.dot_general(hh, v, TRANS_B, preferred_element_type=jnp.float32).reshape(share, block, block)
-    delta = jnp.tile(dl_ref[0], (1, 1, block // 128))
-    ds = (e * (dp - delta)).reshape(share * block, block).astype(jnp.bfloat16)
-    rows = pl.ds(pl.multiple_of(tab_ref[0, n] * block, block), block)
-    dq_ref[0, :, rows, :] += jnp.dot(ds, k, preferred_element_type=jnp.float32).reshape(share, block, HEAD_SIZE)
-    dk_acc[...] += lax.dot_general(ds, q, TRANS_A, preferred_element_type=jnp.float32)
-    dv_acc[...] += lax.dot_general(
-        e.reshape(share * block, block).astype(jnp.bfloat16), hh, TRANS_A, preferred_element_type=jnp.float32
-    )
+    def step(masked):
+        q = q_ref[0].reshape(share * block, HEAD_SIZE)
+        hh = h_ref[0].reshape(share * block, HEAD_SIZE)
+        k = k_ref[0]
+        v = v_ref[0]
+        s = lax.dot_general(q, k, TRANS_B, preferred_element_type=jnp.float32) * scale
+        e = jnp.exp(s.reshape(share, block, block))
+        if masked:
+            allowed = _mask(tab_ref[1, n], tab_ref[2, n], qs_ref[...], block)
+            e = jnp.where(allowed[None], e, 0.0)
+        dp = lax.dot_general(hh, v, TRANS_B, preferred_element_type=jnp.float32).reshape(share, block, block)
+        delta = jnp.tile(dl_ref[0], (1, 1, block // 128))
+        ds = (e * (dp - delta)).reshape(share * block, block).astype(jnp.bfloat16)
+        rows = pl.ds(pl.multiple_of(tab_ref[0, n] * block, block), block)
+        dq_ref[0, :, rows, :] += jnp.dot(ds, k, preferred_element_type=jnp.float32).reshape(share, block, HEAD_SIZE)
+        dk_acc[...] += lax.dot_general(ds, q, TRANS_A, preferred_element_type=jnp.float32)
+        dv_acc[...] += lax.dot_general(
+            e.reshape(share * block, block).astype(jnp.bfloat16), hh, TRANS_A, preferred_element_type=jnp.float32
+        )
+
+    full, partial = _block_kind(tab_ref, qb_ref, n, block)
+    pl.when(full)(lambda: step(False))
+    pl.when(partial)(lambda: step(True))
 
     @pl.when(tab_ref[6, n] == 1)
     def _():
@@ -177,22 +200,22 @@
         dv_ref[0] = dv_acc[...]
 
 
-def attention_backward(q, hgrad, delta, qs, keys, values, dq_in, piece, quarter, source, block=512):
+def attention_backward(q, hgrad, delta, qs, qb, keys, values, dq_in, piece, quarter, source, block=512):
     kvh, share, rows, _ = q.shape
     tab = pair_tables(piece, quarter, block, True, source)
     npairs = tab.shape[1]
     scale = HEAD_SIZE ** (-0.5)
-    row_spec = pl.BlockSpec((1, share, block, HEAD_SIZE), lambda h, n, t: (h, 0, t[0, n], 0))
-    key_spec = pl.BlockSpec((1, block, HEAD_SIZE), lambda h, n, t: (h, t[4, n], 0))
-    full_spec = pl.BlockSpec((1, share, rows, HEAD_SIZE), lambda h, n, t: (h, 0, 0, 0))
+    row_spec = pl.BlockSpec((1, share, block, HEAD_SIZE), lambda h, n, t, b: (h, 0, t[0, n], 0))
+    key_spec = pl.BlockSpec((1, block, HEAD_SIZE), lambda h, n, t, b: (h, t[4, n], 0))
+    full_spec = pl.BlockSpec((1, share, rows, HEAD_SIZE), lambda h, n, t, b: (h, 0, 0, 0))
     grid_spec = pltpu.PrefetchScalarGridSpec(
-        num_scalar_prefetch=1,
+        num_scalar_prefetch=2,
         grid=(kvh, npairs),
         in_specs=[
             row_spec,
             row_spec,
-            pl.BlockSpec((1, share, block, 128), lambda h, n, t: (h, 0, t[0, n], 0)),
-            pl.BlockSpec((block, 128), lambda h, n, t: (t[0, n], 0)),
+            pl.BlockSpec((1, share, block, 128), lambda h, n, t, b: (h, 0, t[0, n], 0)),
+            pl.BlockSpec((block, 128), lambda h, n, t, b: (t[0, n], 0)),
             key_spec,
             key_spec,
             full_spec,
@@ -212,7 +235,7 @@
             jax.ShapeDtypeStruct(keys.shape, jnp.float32),
             jax.ShapeDtypeStruct(values.shape, jnp.float32),
         ],
-        input_output_aliases={7: 0},
+        input_output_aliases={8: 0},
         compiler_params=pltpu.CompilerParams(
             dimension_semantics=("arbitrary", "arbitrary"), vmem_limit_bytes=56 * 1024 * 1024
         ),
@@ -222,7 +245,7 @@
             bytes_accessed=kvh * npairs * (10 * block * HEAD_SIZE * 2),
         ),
         name="attn_bwd",
-    )(tab, q, hgrad, delta, qs, keys, values, dq_in)
+    )(tab, qb, q, hgrad, delta, qs, keys, values, dq_in)
 
 
 PIECES = 2
@@ -446,6 +469,8 @@
     key_rope = prepare_inputs(key_projected, gain_k, group_offset, kv_heads).astype(jnp.bfloat16)
     quarter = group_rows // 2
     query_start = jnp.broadcast_to(group_start[:, None], (group_rows, 128))
+    starts_by_block = group_start.reshape(group_rows // 512, 512)
+    query_bounds = jnp.stack([jnp.min(starts_by_block, axis=1), jnp.max(starts_by_block, axis=1)])
     query_t = jnp.transpose(query_rope, (1, 2, 0, 3))
     own_keys = jnp.transpose(key_rope, (1, 0, 2))
     own_values = jnp.transpose(value_rows, (1, 0, 2))
@@ -453,12 +478,12 @@
     sums = jnp.zeros(query_t.shape, jnp.float32)
     totals = jnp.zeros(query_t.shape[:3] + (128,), jnp.float32)
     sums, totals = attention_forward(
-        query_t, query_start, own_keys, own_values, sums, totals, piece, quarter, 0
+        query_t, query_start, query_bounds, own_keys, own_values, sums, totals, piece, quarter, 0
     )
     cotangent_across, sums, totals = lax.optimization_barrier((cotangent_across, sums, totals))
     mlp_grad_all = finish_gather(cotangent_low, cotangent_across)
     sums, totals_t = attention_forward(
-        query_t, query_start, moved[0], moved[1], sums, totals, piece, quarter, 1
+        query_t, query_start, query_bounds, moved[0], moved[1], sums, totals, piece, quarter, 1
     )
     mlp_grad_all, sums, totals_t = lax.optimization_barrier((mlp_grad_all, sums, totals_t))
     heads_t = sums / totals_t[..., :1]
@@ -541,7 +566,7 @@
     )
     mlp_shards = [part.astype(jnp.float32) for part in mlp_shards]
     dq_raw, dk_far, dv_far = attention_backward(
-        query_t, grad_t, delta_t, query_start, moved[0], moved[1],
+        query_t, grad_t, delta_t, query_start, query_bounds, moved[0], moved[1],
         jnp.zeros(query_t.shape, jnp.float32), piece, quarter, 1,
     )
     unseen = (piece == 1) & (jnp.arange(group_rows) >= quarter)
@@ -550,7 +575,7 @@
     down_rows, dq_raw = lax.optimization_barrier((down_rows, dq_raw))
     output = (after_attn + down_rows).astype(jnp.bfloat16)
     dq_raw, dk_own, dv_own = attention_backward(
-        query_t, grad_t, delta_t, query_start, own_keys, own_values,
+        query_t, grad_t, delta_t, query_start, query_bounds, own_keys, own_values,
         dq_raw, piece, quarter, 0,
     )
     mlp_shards, dq_raw = lax.optimization_barrier((mlp_shards, dq_raw))

time: 658 us -> 658 us (level)
  Pallas kernels: 135 us -> 122 us
  waiting for transfers between devices: 166 us -> 179 us
    pallas_call x2, Pallas kernels: 52.1 us -> 44.4 us  [attention_forward(): pl.pallas_call(functools.partial(_fwd_kernel, scale=scale, block=block),...]
    all_gather x1, waiting for transfers between devices: 25.1 us -> 31.7 us  [shards(): lax.all_gather(jnp.concatenate([gate_weight.astype(jnp.bfloat16), up_weig...]
    unnamed x203 -> x205, local copies, waits for them, and re-layouts: 35.9 us -> 36.4 us
  transfers between devices with their start and end apart: 37 -> 37, of which waited for: 20 -> 20; matrix products, arithmetic and copies ran while one was open for 32% -> 32% of each run, Pallas kernels for 21% -> 19%
where the time goes in v17:
time: 658 us; the launch traced here: 650 us
  waiting for transfers between devices  179 us (27%)
  Pallas kernels  122 us (19%)
  other arithmetic  109 us (17%)
  local copies, waits for them, and re-layouts  94 us (14%)
  matrix products  93.9 us (14%)
  starting transfers between devices  36.1 us (5%)
  between operations  15.7 us (2%)
    ppermute x16, waiting for transfers between devices, exchange(): lax.ppermute(values, 'tensor', [(i, i ^ distance) for i in range(count)])  98.2 us
    pallas_call x2, Pallas kernels, attention_backward(): pl.pallas_call(functools.partial(_bwd_kernel, scale=scale, block=block),...  77.8 us
    pallas_call x2, Pallas kernels, attention_forward(): pl.pallas_call(functools.partial(_fwd_kernel, scale=scale, block=block),...  44.4 us
    dot_general x7, matrix products, contract_last(): lax.dot_general(left, right, (((1,), (1,)), ((), ())), preferred_element_...  37.7 us
    unnamed x205, local copies, waits for them, and re-layouts  36.4 us
    all_gather x1, waiting for transfers between devices, shards(): lax.all_gather(jnp.concatenate([gate_weight.astype(jnp.bfloat16), up_weig...  31.7 us
    dot_general x7, matrix products, contract_rows(): lax.dot_general(left, right, (((0,), (0,)), ((), ())), preferred_element_...  24.2 us
    ppermute x6, waiting for transfers between devices, halving_scatter(): lax.ppermute(send.astype(jnp.bfloat16), 'fsdp', [(i, i ^ 1 << bit) for i...  20.5 us
  transfers between devices with their start and end apart: 37, of which 20 were waited for; matrix products, arithmetic and copies ran while one was open for 32% of the time, Pallas kernels for 19%

profile of v17, /device:TPU:0, one launch (start us, length us, event | category | flops | bytes accessed | tf_op | source)
XLA Modules:
  0.0 650.1 jit_solution(15894547492764572435)
XLA Ops:
  37.2 15.7 %collective-permute-done.3 = bf16[512,1024]{1,0:T(8,128)(2,1)S(1)} collective-permute-done((bf16[512,1024]{1,0:T(8,128)(2,1)S(1)}, bf16[512,1024]{1,0:T(8,128)(2,1)S(1)}, u32[]{:S(2)}, u32[]{:S(2)}) %collective-permute-start.3) | collective-permute-done | bytes 1048608 | tf_op jit(solution)/shard_map/ppermute | solution.py:361
  74.5 5.2 convolution_convert_fusion.1
  88.1 7.5 %all-gather.5.cloned.1.call-done = bf16[1024,512]{1,0:T(8,128)(2,1)} async-done(((bf16[128,512]{1,0:T(8,128)(2,1)}), bf16[1024,512]{1,0:T(8,128)(2,1)}) %all-gather.5.cloned.1.call-update) | async-done | bytes 1048592 | tf_op jit(solution)/shard_map/all_gather | solution.py:445
  95.5 5.1 multiply_reduce_fusion.2
  118.3 25.9 %attn_fwd.2 = (f32[2,2,2048,128]{3,2,1,0:T(8,128)}, f32[2,2,2048,128]{3,2,1,0:T(8,128)}) custom-call(s32[7,10]{1,0:T(8,128)S(1)} %broadcast_select_fusion.5.tab_ref, s32[2,4]{1,0:T(2,128)S(1)} %pad_add_fusion.2.qb_ref, bf16[2,2,2048,128]{3,2,1,0:T(8,128)(2,1)S(1)} %maximum_bitcast_fusion.q_ref, ...), custom_call_target="tpu_custom_call", output_to_operand_aliasing={{0}: (6, {}), {1}: (7, {})} | custom-call | flops 5368709120 | bytes 20971520 | tf_op jit(solution)/shard_map/attn_fwd/pallas_call | solution.py:140
  150.8 18.5 %attn_fwd.3 = (f32[2,2,2048,128]{3,2,1,0:T(8,128)}, f32[2,2,2048,128]{3,2,1,0:T(8,128)}) custom-call(s32[7,8]{1,0:T(8,128)S(1)} %broadcast_select_fusion.3.tab_ref, s32[2,4]{1,0:T(2,128)S(1)} %pad_add_fusion.2.qb_ref, bf16[2,2,2048,128]{3,2,1,0:T(8,128)(2,1)S(1)} %maximum_bitcast_fusion.q_ref, ...), custom_call_target="tpu_custom_call", output_to_operand_aliasing={{0}: (6, {}), {1}: (7, {})} | custom-call | flops 4294967296 | bytes 16777216 | tf_op jit(solution)/shard_map/attn_fwd/pallas_call | solution.py:140
  192.2 31.7 %all-gather.11.cloned.1.call-done = bf16[1024,2304]{0,1:T(8,128)(2,1)} async-done(((bf16[128,2304]{0,1:T(8,128)(2,1)}), bf16[1024,2304]{0,1:T(8,128)(2,1)}) %all-gather.11.cloned.1.call-update) | async-done | bytes 4718608 | tf_op jit(solution)/shard_map/all_gather | solution.py:494
  223.9 6.0 fusion.46
  235.2 22.6 %collective-permute-done.10 = bf16[512,1024]{1,0:T(8,128)(2,1)S(1)} collective-permute-done((bf16[512,1024]{1,0:T(8,128)(2,1)S(1)}, bf16[512,1024]{1,0:T(8,128)(2,1)S(1)}, u32[]{:S(2)}, u32[]{:S(2)}) %collective-permute-start.10) | collective-permute-done | bytes 1048608 | tf_op jit(solution)/shard_map/ppermute | solution.py:361
  269.5 5.5 multiply_convert_fusion
  275.0 7.0 %fusion.40 = f32[2048,1024]{1,0:T(8,128)S(1)} fusion(bf16[2048,768]{1,0:T(8,128)(2,1)} %get-tuple-element.74, bf16[1024,2304]{0,1:T(8,128)(2,1)} %all-gather.11.cloned.1.call-done), kind=kOutput, calls=%fused_computation.132 | convolution fusion | flops 3221225472 | bytes 13107200 | tf_op jit(solution)/shard_map/dot_general | solution.py:299
  301.4 5.1 fusion.121
  306.5 13.7 %collective-permute-done.13 = bf16[512,1024]{1,0:T(8,128)(2,1)S(1)} collective-permute-done((bf16[512,1024]{1,0:T(8,128)(2,1)S(1)}, bf16[512,1024]{1,0:T(8,128)(2,1)S(1)}, u32[]{:S(2)}, u32[]{:S(2)}) %collective-permute-start.13) | collective-permute-done | bytes 1048608 | tf_op jit(solution)/shard_map/ppermute | solution.py:361
  324.9 22.8 %collective-permute-done.14 = bf16[512,1024]{1,0:T(8,128)(2,1)S(1)} collective-permute-done((bf16[512,1024]{1,0:T(8,128)(2,1)S(1)}, bf16[512,1024]{1,0:T(8,128)(2,1)S(1)}, u32[]{:S(2)}, u32[]{:S(2)}) %collective-permute-start.14) | collective-permute-done | bytes 1048608 | tf_op jit(solution)/shard_map/ppermute | solution.py:361
  362.6 7.2 %fusion.6 = (f32[2048,2,2]{0,2,1:T(2,128)S(1)}, bf16[2,2,2048,128]{3,2,1,0:T(8,128)(2,1)}) fusion(f32[2048,2,2,128]{3,0,2,1:T(8,128)} %copy.105, f32[2,2,2048,128]{3,2,1,0:T(8,128)} %get-tuple-element.67, f32[2,2,2048]{2,1,0:T(2,128)S(1)} %slice_reduce_fusion, f32[2048,2,2]{0,2,1:T(2,128)S(1)} %bitcast.254), kind=kLoop, calls=%fused_computation.30 | loop fusion | flops 5234688 | bytes 10584064 | tf_op jit(solution)/shard_map/reduce_sum | solution.py:556
  401.8 34.3 %attn_bwd.2 = (f32[2,2,2048,128]{3,2,1,0:T(8,128)}, f32[2,2048,128]{2,1,0:T(8,128)}, f32[2,2048,128]{2,1,0:T(8,128)}) custom-call(s32[7,8]{1,0:T(8,128)} %broadcast_select_fusion.2.tab_ref, s32[2,4]{1,0:T(2,128)} %copy-done.6, bf16[2,2,2048,128]{3,2,1,0:T(8,128)(2,1)} %copy-done.1, ...), custom_call_target="tpu_custom_call", output_to_operand_aliasing={{0}: (8, {})} | custom-call | flops 10737418240 | bytes 20971520 | tf_op jit(solution)/shard_map/attn_bwd/pallas_call | solution.py:230
  446.9 43.5 %attn_bwd.3 = (f32[2,2,2048,128]{3,2,1,0:T(8,128)}, f32[2,2048,128]{2,1,0:T(8,128)}, f32[2,2048,128]{2,1,0:T(8,128)}) custom-call(s32[7,10]{1,0:T(8,128)} %broadcast_select_fusion.4.tab_ref, s32[2,4]{1,0:T(2,128)} %copy-done.6, bf16[2,2,2048,128]{3,2,1,0:T(8,128)(2,1)} %copy-done.1, ...), custom_call_target="tpu_custom_call", output_to_operand_aliasing={{0}: (8, {})} | custom-call | flops 13421772800 | bytes 26214400 | tf_op jit(solution)/shard_map/attn_bwd/pallas_call | solution.py:230
  490.4 15.5 %collective-permute-done.18 = bf16[2,2,2048,128]{3,2,1,0:T(8,128)(2,1)} collective-permute-done((bf16[2,2,2048,128]{3,2,1,0:T(8,128)(2,1)}, bf16[2,2,2048,128]{3,2,1,0:T(8,128)(2,1)}, u32[]{:S(2)}, u32[]{:S(2)}) %collective-permute-start.18) | collective-permute-done | bytes 2097184 | tf_op jit(solution)/shard_map/ppermute | solution.py:259
  528.5 5.9 fusion.67
  534.4 7.6 %collective-permute-done.24 = bf16[512,512]{0,1:T(8,128)(2,1)} collective-permute-done((bf16[512,512]{0,1:T(8,128)(2,1)}, bf16[512,512]{0,1:T(8,128)(2,1)}, u32[]{:S(2)}, u32[]{:S(2)}) %collective-permute-start.24) | collective-permute-done | bytes 524320 | tf_op jit(solution)/shard_map/ppermute | solution.py:327
  573.8 5.8 fusion.122
  579.6 5.0 add_add_fusion
  591.7 8.2 %collective-permute-done.21 = bf16[512,512]{1,0:T(8,128)(2,1)S(1)} collective-permute-done((bf16[512,512]{1,0:T(8,128)(2,1)S(1)}, bf16[512,512]{1,0:T(8,128)(2,1)S(1)}, u32[]{:S(2)}, u32[]{:S(2)}) %collective-permute-start.21) | collective-permute-done | bytes 524320 | tf_op jit(solution)/shard_map/ppermute | solution.py:327
  608.5 7.8 %collective-permute-done.20 = bf16[512,1024]{1,0:T(8,128)(2,1)S(1)} collective-permute-done((bf16[512,1024]{1,0:T(8,128)(2,1)S(1)}, bf16[512,1024]{1,0:T(8,128)(2,1)S(1)}, u32[]{:S(2)}, u32[]{:S(2)}) %collective-permute-start.20) | collective-permute-done | bytes 1048608 | tf_op jit(solution)/shard_map/ppermute | solution.py:361
  (456 shorter events, 301.4 us)
Async XLA Ops:
  7.2 60.0 %all-gather.7.cloned.1.call-start = ((), (), s32[]{:S(2)}) async-start(), calls=%async_computation.2 | async-start | bytes 1179648 | tf_op jit(solution)/shard_map/all_gather | solution.py:436
  9.8 85.7 %all-gather.5.cloned.1.call-start = ((), (), s32[]{:S(2)}) async-start(), calls=%async_computation.1 | async-start | bytes 1179648 | tf_op jit(solution)/shard_map/all_gather | solution.py:445
  11.5 167.7 %all-gather.9.cloned.1.call-start = ((), (), s32[]{:S(2)}) async-start(), calls=%async_computation.3 | async-start | bytes 1179648 | tf_op jit(solution)/shard_map/all_gather | solution.py:446
  18.9 205.0 %all-gather.11.cloned.1.call-start = ((), (), s32[]{:S(2)}) async-start(), calls=%async_computation.4 | async-start | bytes 5308416 | tf_op jit(solution)/shard_map/all_gather | solution.py:494
  30.5 22.4 %collective-permute-start.3 = (bf16[512,1024]{1,0:T(8,128)(2,1)S(1)}, bf16[512,1024]{1,0:T(8,128)(2,1)S(1)}, u32[]{:S(2)}, u32[]{:S(2)}) collective-permute-start(bf16[512,1024]{1,0:T(8,128)(2,1)S(1)} %get-tuple-element.170), channel_id=1, source_target_pairs={{0,2},{1,3},{2,0},{3,1},{4,6},{5,7},{6,4},{7,5},{8,10},{9,11},{10,... | collective-permute-start | bytes 3145736 | tf_op jit(solution)/shard_map/ppermute | solution.py:361
  35.6 509.3 %reduce-scatter.2.cloned.1.call-start = ((), (), s32[]{:S(2)}) async-start(), calls=%async_computation.5 | async-start | bytes 6488064 | tf_op jit(solution)/shard_map/reduce_scatter | solution.py:564
  54.4 8.2 %collective-permute-start.4 = (bf16[2,512,1024]{2,1,0:T(8,128)(2,1)}, bf16[2,512,1024]{2,1,0:T(8,128)(2,1)}, u32[]{:S(2)}, u32[]{:S(2)}) collective-permute-start(bf16[2,512,1024]{2,1,0:T(8,128)(2,1)} %pad_maximum_fusion.1), channel_id=1, source_target_pairs={{0,1},{1,0},{2,3},{3,2},{4,5},{5,4},{6,7},{7,6},{8,9},{9,8},{10,11... | collective-permute-start | bytes 6291464 | tf_op jit(solution)/shard_map/ppermute | solution.py:361
  87.1 61.9 %collective-permute-start.7 = (bf16[2,2,2048,128]{3,2,1,0:T(8,128)(2,1)}, bf16[2,2,2048,128]{3,2,1,0:T(8,128)(2,1)}, u32[]{:S(2)}, u32[]{:S(2)}) collective-permute-start(bf16[2,2,2048,128]{3,2,1,0:T(8,128)(2,1)} %pad_maximum_fusion.3), channel_id=1, source_target_pairs={{0,4},{4,0},{8,12},{12,8},{16,20},{20,16},{24,28},{28,24},{1,5},{5... | collective-permute-start | bytes 6291464 | tf_op jit(solution)/shard_map/ppermute | solution.py:259
  100.7 43.5 %collective-permute-start.5 = (bf16[512,1024]{1,0:T(8,128)(2,1)S(1)}, bf16[512,1024]{1,0:T(8,128)(2,1)}, u32[]{:S(2)}, u32[]{:S(2)}) collective-permute-start(bf16[512,1024]{1,0:T(8,128)(2,1)S(1)} %copy-done.21), channel_id=1, source_target_pairs={{0,2},{1,3},{2,0},{3,1},{4,6},{5,7},{6,4},{7,5},{8,10},{9,11},{10,... | collective-permute-start | bytes 3145736 | tf_op jit(solution)/shard_map/ppermute | solution.py:361
  146.9 22.3 %collective-permute-start.6 = (bf16[2,512,1024]{2,1,0:T(8,128)(2,1)}, bf16[2,512,1024]{2,1,0:T(8,128)(2,1)S(1)}, u32[]{:S(2)}, u32[]{:S(2)}) collective-permute-start(bf16[2,512,1024]{2,1,0:T(8,128)(2,1)} %pad_maximum_fusion.2), channel_id=1, source_target_pairs={{0,1},{1,0},{2,3},{3,2},{4,5},{5,4},{6,7},{7,6},{8,9},{9,8},{10,11... | collective-permute-start | bytes 6291464 | tf_op jit(solution)/shard_map/ppermute | solution.py:361
  190.9 39.0 %collective-permute-start.9 = (bf16[512,1024]{1,0:T(8,128)(2,1)S(1)}, bf16[512,1024]{1,0:T(8,128)(2,1)}, u32[]{:S(2)}, u32[]{:S(2)}) collective-permute-start(bf16[512,1024]{1,0:T(8,128)(2,1)S(1)} %fusion.30), channel_id=1, source_target_pairs={{0,2},{1,3},{2,0},{3,1},{4,6},{5,7},{6,4},{7,5},{8,10},{9,11},{10,... | collective-permute-start | bytes 3145736 | tf_op jit(solution)/shard_map/ppermute | solution.py:361
  233.6 24.2 %collective-permute-start.10 = (bf16[512,1024]{1,0:T(8,128)(2,1)S(1)}, bf16[512,1024]{1,0:T(8,128)(2,1)S(1)}, u32[]{:S(2)}, u32[]{:S(2)}) collective-permute-start(bf16[512,1024]{1,0:T(8,128)(2,1)S(1)} %get-tuple-element.168), channel_id=1, source_target_pairs={{0,2},{1,3},{2,0},{3,1},{4,6},{5,7},{6,4},{7,5},{8,10},{9,11},{10,... | collective-permute-start | bytes 3145736 | tf_op jit(solution)/shard_map/ppermute | solution.py:361
  295.0 25.3 %collective-permute-start.13 = (bf16[512,1024]{1,0:T(8,128)(2,1)S(1)}, bf16[512,1024]{1,0:T(8,128)(2,1)S(1)}, u32[]{:S(2)}, u32[]{:S(2)}) collective-permute-start(bf16[512,1024]{1,0:T(8,128)(2,1)S(1)} %fusion.26), channel_id=1, source_target_pairs={{0,2},{1,3},{2,0},{3,1},{4,6},{5,7},{6,4},{7,5},{8,10},{9,11},{10,... | collective-permute-start | bytes 3145736 | tf_op jit(solution)/shard_map/ppermute | solution.py:361
  323.3 24.4 %collective-permute-start.14 = (bf16[512,1024]{1,0:T(8,128)(2,1)S(1)}, bf16[512,1024]{1,0:T(8,128)(2,1)S(1)}, u32[]{:S(2)}, u32[]{:S(2)}) collective-permute-start(bf16[512,1024]{1,0:T(8,128)(2,1)S(1)} %get-tuple-element.165), channel_id=1, source_target_pairs={{0,2},{1,3},{2,0},{3,1},{4,6},{5,7},{6,4},{7,5},{8,10},{9,11},{10,... | collective-permute-start | bytes 3145736 | tf_op jit(solution)/shard_map/ppermute | solution.py:361
  397.8 44.4 %collective-permute-start.17 = (bf16[512,1024]{1,0:T(8,128)(2,1)S(1)}, bf16[512,1024]{1,0:T(8,128)(2,1)}, u32[]{:S(2)}, u32[]{:S(2)}) collective-permute-start(bf16[512,1024]{1,0:T(8,128)(2,1)S(1)} %fusion.22), channel_id=1, source_target_pairs={{0,2},{1,3},{2,0},{3,1},{4,6},{5,7},{6,4},{7,5},{8,10},{9,11},{10,... | collective-permute-start | bytes 3145736 | tf_op jit(solution)/shard_map/ppermute | solution.py:361
  439.6 66.3 %collective-permute-start.18 = (bf16[2,2,2048,128]{3,2,1,0:T(8,128)(2,1)}, bf16[2,2,2048,128]{3,2,1,0:T(8,128)(2,1)}, u32[]{:S(2)}, u32[]{:S(2)}) collective-permute-start(bf16[2,2,2048,128]{3,2,1,0:T(8,128)(2,1)} %fusion.5), channel_id=1, source_target_pairs={{0,4},{4,0},{8,12},{12,8},{16,20},{20,16},{24,28},{28,24},{1,5},{5... | collective-permute-start | bytes 6291464 | tf_op jit(solution)/shard_map/ppermute | solution.py:259
  527.9 14.1 %collective-permute-start.24 = (bf16[512,512]{0,1:T(8,128)(2,1)}, bf16[512,512]{0,1:T(8,128)(2,1)}, u32[]{:S(2)}, u32[]{:S(2)}) collective-permute-start(bf16[512,512]{0,1:T(8,128)(2,1)} %dynamic-slice_convert_fusion.8), channel_id=1, source_target_pairs={{0,4},{4,0},{8,12},{12,8},{16,20},{20,16},{24,28},{28,24},{1,5},{5... | collective-permute-start | bytes 1572872 | tf_op jit(solution)/shard_map/ppermute | solution.py:327
  544.9 41.1 %collective-permute-start.25 = (bf16[256,512]{0,1:T(8,128)(2,1)}, bf16[256,512]{0,1:T(8,128)(2,1)}, u32[]{:S(2)}, u32[]{:S(2)}) collective-permute-start(bf16[256,512]{0,1:T(8,128)(2,1)} %dynamic-slice_convert_fusion.10), channel_id=1, source_target_pairs={{0,8},{4,12},{8,0},{12,4},{16,24},{20,28},{24,16},{28,20},{1,9},{5... | collective-permute-start | bytes 786440 | tf_op jit(solution)/shard_map/ppermute | solution.py:327
  585.5 14.4 %collective-permute-start.21 = (bf16[512,512]{1,0:T(8,128)(2,1)S(1)}, bf16[512,512]{1,0:T(8,128)(2,1)S(1)}, u32[]{:S(2)}, u32[]{:S(2)}) collective-permute-start(bf16[512,512]{1,0:T(8,128)(2,1)S(1)} %dynamic-slice_convert_fusion.9), channel_id=1, source_target_pairs={{0,4},{4,0},{8,12},{12,8},{16,20},{20,16},{24,28},{28,24},{1,5},{5... | collective-permute-start | bytes 1572872 | tf_op jit(solution)/shard_map/ppermute | solution.py:327
  587.6 16.1 %collective-permute-start.26 = (bf16[128,512]{0,1:T(8,128)(2,1)S(1)}, bf16[128,512]{0,1:T(8,128)(2,1)S(1)}, u32[]{:S(2)}, u32[]{:S(2)}) collective-permute-start(bf16[128,512]{0,1:T(8,128)(2,1)S(1)} %dynamic-slice_convert_fusion.12), channel_id=1, source_target_pairs={{0,16},{4,20},{8,24},{12,28},{16,0},{20,4},{24,8},{28,12},{1,17},{... | collective-permute-start | bytes 393224 | tf_op jit(solution)/shard_map/ppermute | solution.py:327
  590.9 25.3 %collective-permute-start.20 = (bf16[512,1024]{1,0:T(8,128)(2,1)S(1)}, bf16[512,1024]{1,0:T(8,128)(2,1)S(1)}, u32[]{:S(2)}, u32[]{:S(2)}) collective-permute-start(bf16[512,1024]{1,0:T(8,128)(2,1)S(1)} %fusion.18), channel_id=1, source_target_pairs={{0,2},{1,3},{2,0},{3,1},{4,6},{5,7},{6,4},{7,5},{8,10},{9,11},{10,... | collective-permute-start | bytes 3145736 | tf_op jit(solution)/shard_map/ppermute | solution.py:361
  600.2 8.2 %collective-permute-start.22 = (bf16[256,512]{1,0:T(8,128)(2,1)S(1)}, bf16[256,512]{1,0:T(8,128)(2,1)S(1)}, u32[]{:S(2)}, u32[]{:S(2)}) collective-permute-start(bf16[256,512]{1,0:T(8,128)(2,1)S(1)} %dynamic-slice_convert_fusion.11), channel_id=1, source_target_pairs={{0,8},{4,12},{8,0},{12,4},{16,24},{20,28},{24,16},{28,20},{1,9},{5... | collective-permute-start | bytes 786440 | tf_op jit(solution)/shard_map/ppermute | solution.py:327
  619.8 10.9 %collective-permute-start.23 = (bf16[128,512]{1,0:T(8,128)(2,1)}, bf16[128,512]{1,0:T(8,128)(2,1)}, u32[]{:S(2)}, u32[]{:S(2)}) collective-permute-start(bf16[128,512]{1,0:T(8,128)(2,1)} %dynamic-slice_convert_fusion.13), channel_id=1, source_target_pairs={{0,16},{4,20},{8,24},{12,28},{16,0},{20,4},{24,8},{28,12},{1,17},{... | collective-permute-start | bytes 393224 | tf_op jit(solution)/shard_map/ppermute | solution.py:327
  622.2 7.3 %collective-permute-start.28 = (f32[2304]{0:T(1024)S(1)}, f32[2304]{0:T(1024)}, u32[]{:S(2)}, u32[]{:S(2)}) collective-permute-start(f32[2304]{0:T(1024)S(1)} %fusion.109), channel_id=1, source_target_pairs={{0,2},{1,3},{2,0},{3,1},{4,6},{5,7},{6,4},{7,5},{8,10},{9,11},{10,... | collective-permute-start | bytes 27656 | tf_op jit(solution)/shard_map/ppermute | solution.py:352
  (108 other events, 1263.0 us)
Sparse Core Ops, SparseCore 0:
  10.7 42.9 all-gather.6
  56.4 39.0 all-gather.4
  98.2 44.8 all-gather.8
  145.0 78.8 all-gather.10
  385.2 130.3 reduce-scatter.1

commit v18 on v17

--- a/solution.py
+++ b/solution.py
@@ -443,9 +443,19 @@
     )
     w_key, w_value = split_columns(kv_full, (key_matrix.shape[1], value_matrix.shape[1]))
     w_query = lax.all_gather(q_weight.astype(jnp.bfloat16), "fsdp", axis=0, tiled=True)
-    w_out = lax.all_gather(
-        jnp.transpose(o_weight).astype(jnp.bfloat16), "fsdp", axis=0, tiled=True
-    )
+    od_full = lax.all_gather(
+        jnp.concatenate(
+            [
+                jnp.transpose(o_weight).astype(jnp.bfloat16),
+                jnp.transpose(down_weight).astype(jnp.bfloat16),
+            ],
+            axis=1,
+        ),
+        "fsdp",
+        axis=0,
+        tiled=True,
+    )
+    w_out, w_down_t = split_columns(od_full, (o_weight.shape[0], down_weight.shape[0]))
     x_float = hidden.astype(jnp.float32)
     gain_first = gain_in.astype(jnp.float32)
     first_all = token_gather(rms_scale(x_float, gain_first).astype(jnp.bfloat16))
@@ -496,7 +506,6 @@
             [
                 gate_weight.astype(jnp.bfloat16),
                 up_weight.astype(jnp.bfloat16),
-                jnp.transpose(down_weight).astype(jnp.bfloat16),
             ],
             axis=1,
         ),
@@ -504,9 +513,7 @@
         axis=0,
         tiled=True,
     )
-    w_gate, w_up, w_down_t = split_columns(
-        mlp_full, (gate_weight.shape[1], up_weight.shape[1], down_weight.shape[0])
-    )
+    w_gate, w_up = split_columns(mlp_full, (gate_weight.shape[1], up_weight.shape[1]))
     out_partial = contract_last(out_rows, w_out)
     late_grad_all, out_partial = lax.optimization_barrier((mlp_grad_all, out_partial))
     grad_act = jnp.dot(late_grad_all, w_down_t, preferred_element_type=jnp.float32)
@@ -560,11 +567,6 @@
         jnp.transpose(delta, (1, 2, 0))[..., None], (kv_heads, share, group_rows, 128)
     )
     mlp_packed, grad_t, delta_t = lax.optimization_barrier((mlp_packed, grad_t, delta_t))
-    mlp_shards = split_columns(
-        lax.psum_scatter(mlp_packed, "fsdp", scatter_dimension=0, tiled=True),
-        [g.shape[1] for g in (gate_grad, up_grad, down_grad_t, out_weight_grad_t)],
-    )
-    mlp_shards = [part.astype(jnp.float32) for part in mlp_shards]
     dq_raw, dk_far, dv_far = attention_backward(
         query_t, grad_t, delta_t, query_start, query_bounds, moved[0], moved[1],
         jnp.zeros(query_t.shape, jnp.float32), piece, quarter, 1,
@@ -578,7 +580,12 @@
         query_t, grad_t, delta_t, query_start, query_bounds, own_keys, own_values,
         dq_raw, piece, quarter, 0,
     )
-    mlp_shards, dq_raw = lax.optimization_barrier((mlp_shards, dq_raw))
+    mlp_packed, dq_raw = lax.optimization_barrier((mlp_packed, dq_raw))
+    mlp_shards = split_columns(
+        lax.psum_scatter(mlp_packed, "fsdp", scatter_dimension=0, tiled=True),
+        [g.shape[1] for g in (gate_grad, up_grad, down_grad_t, out_weight_grad_t)],
+    )
+    mlp_shards = [part.astype(jnp.float32) for part in mlp_shards]
     grad_keys_total = jnp.transpose(dk_own + returned[0].astype(jnp.float32), (1, 0, 2))
     grad_values_total = jnp.transpose(dv_own + returned[1].astype(jnp.float32), (1, 0, 2))
     query_grads = jnp.transpose(dq_raw, (2, 0, 1, 3)) * scale

time: 658 us -> 646 us (0.982)
  waiting for transfers between devices: 179 us -> 167 us
    all_gather x1, waiting for transfers between devices: 31.7 us -> 0.01 us  [shards(): lax.all_gather(jnp.concatenate([gate_weight.astype(jnp.bfloat16), up_weig...]
    reduce_scatter x1, waiting for transfers between devices: 0.01 us -> 16.6 us  [shards(): lax.psum_scatter(mlp_packed, 'fsdp', scatter_dimension=0, tiled=True)]
    ppermute x2, waiting for transfers between devices: 15.5 us -> 0.01 us  [swapped(): lax.ppermute(shard, axis, [(i, i ^ 1 << distance) for i in range(lax.axis...]
    ppermute x6, waiting for transfers between devices: 20.5 us -> 32 us  [halving_scatter(): lax.ppermute(send.astype(jnp.bfloat16), 'fsdp', [(i, i ^ 1 << bit) for i...]
    dynamic_update_slice x13, local copies, waits for them, and re-layouts: 7.95 us -> 16.1 us  [finish_gather(): full = lax.dynamic_update_slice_in_dim(full, part, place * rows, 0)]
    dot_general x7, matrix products: 37.7 us -> 30.7 us  [contract_last(): lax.dot_general(left, right, (((1,), (1,)), ((), ())), preferred_element_...]
    unnamed x205 -> x207, local copies, waits for them, and re-layouts: 36.4 us -> 35.1 us
  transfers between devices with their start and end apart: 37 -> 37, of which waited for: 20 -> 19; matrix products, arithmetic and copies ran while one was open for 32% -> 28% of each run, Pallas kernels for 19% -> 19%
where the time goes in v18:
time: 646 us; the launch traced here: 639 us
  waiting for transfers between devices  167 us (26%)
  Pallas kernels  122 us (19%)
  other arithmetic  104 us (16%)
  local copies, waits for them, and re-layouts  99.5 us (15%)
  matrix products  98.3 us (15%)
  starting transfers between devices  32.4 us (5%)
  between operations  16 us (2%)
    ppermute x16, waiting for transfers between devices, exchange(): lax.ppermute(values, 'tensor', [(i, i ^ distance) for i in range(count)])  100 us
    pallas_call x2, Pallas kernels, attention_backward(): pl.pallas_call(functools.partial(_bwd_kernel, scale=scale, block=block),...  77.6 us
    pallas_call x2, Pallas kernels, attention_forward(): pl.pallas_call(functools.partial(_fwd_kernel, scale=scale, block=block),...  44 us
    unnamed x207, local copies, waits for them, and re-layouts  35.1 us
    ppermute x6, waiting for transfers between devices, halving_scatter(): lax.ppermute(send.astype(jnp.bfloat16), 'fsdp', [(i, i ^ 1 << bit) for i...  32 us
    dot_general x7, matrix products, contract_last(): lax.dot_general(left, right, (((1,), (1,)), ((), ())), preferred_element_...  30.7 us
    dot_general x7, matrix products, contract_rows(): lax.dot_general(left, right, (((0,), (0,)), ((), ())), preferred_element_...  26.2 us
    reduce_scatter x1, waiting for transfers between devices, shards(): lax.psum_scatter(mlp_packed, 'fsdp', scatter_dimension=0, tiled=True)  16.6 us
  transfers between devices with their start and end apart: 37, of which 19 were waited for; matrix products, arithmetic and copies ran while one was open for 28% of the time, Pallas kernels for 19%

profile of v18, /device:TPU:0, one launch (start us, length us, event | category | flops | bytes accessed | tf_op | source)
XLA Modules:
  0.0 638.9 jit_solution(2138176588903343963)
XLA Ops:
  33.6 18.4 %collective-permute-done.3 = bf16[512,1024]{1,0:T(8,128)(2,1)S(1)} collective-permute-done((bf16[512,1024]{1,0:T(8,128)(2,1)S(1)}, bf16[512,1024]{1,0:T(8,128)(2,1)S(1)}, u32[]{:S(2)}, u32[]{:S(2)}) %collective-permute-start.3) | collective-permute-done | bytes 1048608 | tf_op jit(solution)/shard_map/ppermute | solution.py:361
  73.6 5.2 convolution_convert_fusion.1
  87.2 8.3 %all-gather.5.cloned.1.call-done = bf16[1024,512]{1,0:T(8,128)(2,1)} async-done(((bf16[128,512]{1,0:T(8,128)(2,1)}), bf16[1024,512]{1,0:T(8,128)(2,1)}) %all-gather.5.cloned.1.call-update) | async-done | bytes 1048592 | tf_op jit(solution)/shard_map/all_gather | solution.py:445
  118.2 25.6 %attn_fwd.2 = (f32[2,2,2048,128]{3,2,1,0:T(8,128)}, f32[2,2,2048,128]{3,2,1,0:T(8,128)}) custom-call(s32[7,10]{1,0:T(8,128)S(1)} %broadcast_select_fusion.5.tab_ref, s32[2,4]{1,0:T(2,128)S(1)} %pad_add_fusion.2.qb_ref, bf16[2,2,2048,128]{3,2,1,0:T(8,128)(2,1)S(1)} %maximum_bitcast_fusion.q_ref, ...), custom_call_target="tpu_custom_call", output_to_operand_aliasing={{0}: (6, {}), {1}: (7, {})} | custom-call | flops 5368709120 | bytes 20971520 | tf_op jit(solution)/shard_map/attn_fwd/pallas_call | solution.py:140
  150.4 18.3 %attn_fwd.3 = (f32[2,2,2048,128]{3,2,1,0:T(8,128)}, f32[2,2,2048,128]{3,2,1,0:T(8,128)}) custom-call(s32[7,8]{1,0:T(8,128)S(1)} %broadcast_select_fusion.3.tab_ref, s32[2,4]{1,0:T(2,128)S(1)} %pad_add_fusion.2.qb_ref, bf16[2,2,2048,128]{3,2,1,0:T(8,128)(2,1)S(1)} %maximum_bitcast_fusion.q_ref, ...), custom_call_target="tpu_custom_call", output_to_operand_aliasing={{0}: (6, {}), {1}: (7, {})} | custom-call | flops 4294967296 | bytes 16777216 | tf_op jit(solution)/shard_map/attn_fwd/pallas_call | solution.py:140
  193.0 8.9 %fusion.46 = f32[2048,768]{1,0:T(8,128)} fusion(bf16[2048,1024]{1,0:T(8,128)(2,1)} %copy-done.47, bf16[1024,1280]{0,1:T(8,128)(2,1)} %all-gather.9.cloned.1.call-done), kind=kOutput, calls=%fused_computation.138 | convolution fusion | flops 3221225472 | bytes 12058624 | tf_op jit(solution)/shard_map/dot_general | solution.py:519
  201.9 14.0 %collective-permute-done.9 = bf16[512,1024]{1,0:T(8,128)(2,1)} collective-permute-done((bf16[512,1024]{1,0:T(8,128)(2,1)S(1)}, bf16[512,1024]{1,0:T(8,128)(2,1)}, u32[]{:S(2)}, u32[]{:S(2)}) %collective-permute-start.9) | collective-permute-done | bytes 1048608 | tf_op jit(solution)/shard_map/ppermute | solution.py:361
  223.8 23.3 %collective-permute-done.10 = bf16[512,1024]{1,0:T(8,128)(2,1)S(1)} collective-permute-done((bf16[512,1024]{1,0:T(8,128)(2,1)S(1)}, bf16[512,1024]{1,0:T(8,128)(2,1)S(1)}, u32[]{:S(2)}, u32[]{:S(2)}) %collective-permute-start.10) | collective-permute-done | bytes 1048608 | tf_op jit(solution)/shard_map/ppermute | solution.py:361
  253.6 5.8 fusion.38
  259.5 5.4 fusion.42
  264.8 5.4 multiply_convert_fusion
  270.3 7.1 %fusion.40 = f32[2048,1024]{1,0:T(8,128)S(1)} fusion(bf16[2048,768]{1,0:T(8,128)(2,1)} %get-tuple-element.71, bf16[1024,1536]{1,0:T(8,128)(2,1)} %all-gather.11.cloned.1.call-done), kind=kOutput, calls=%fused_computation.132 | convolution fusion | flops 3221225472 | bytes 13107200 | tf_op jit(solution)/shard_map/dot_general | solution.py:299
  281.6 6.9 %fusion.122 = bf16[1024,768]{1,0:T(8,128)(2,1)} fusion(bf16[2048,1024]{1,0:T(8,128)(2,1)} %fusion.59, bf16[2048,768]{1,0:T(8,128)(2,1)S(1)} %copy-done.51), kind=kOutput, calls=%fused_computation.304 | convolution fusion | flops 3221225472 | bytes 8912896 | tf_op jit(solution)/shard_map/dot_general | solution.py:293
  290.9 7.4 %fusion.121 = bf16[1024,768]{1,0:T(8,128)(2,1)} fusion(bf16[2048,1024]{1,0:T(8,128)(2,1)} %fusion.59, bf16[2048,768]{1,0:T(8,128)(2,1)S(1)} %copy-done.50), kind=kOutput, calls=%fused_computation.303 | convolution fusion | flops 3221225472 | bytes 8912896 | tf_op jit(solution)/shard_map/dot_general | solution.py:293
  302.9 11.9 %collective-permute-done.13 = bf16[512,1024]{1,0:T(8,128)(2,1)S(1)} collective-permute-done((bf16[512,1024]{1,0:T(8,128)(2,1)S(1)}, bf16[512,1024]{1,0:T(8,128)(2,1)S(1)}, u32[]{:S(2)}, u32[]{:S(2)}) %collective-permute-start.13) | collective-permute-done | bytes 1048608 | tf_op jit(solution)/shard_map/ppermute | solution.py:361
  319.4 23.2 %collective-permute-done.14 = bf16[512,1024]{1,0:T(8,128)(2,1)S(1)} collective-permute-done((bf16[512,1024]{1,0:T(8,128)(2,1)S(1)}, bf16[512,1024]{1,0:T(8,128)(2,1)S(1)}, u32[]{:S(2)}, u32[]{:S(2)}) %collective-permute-start.14) | collective-permute-done | bytes 1048608 | tf_op jit(solution)/shard_map/ppermute | solution.py:361
  353.2 6.2 convolution_convert_fusion
  363.9 5.9 fusion.44
  399.0 34.4 %attn_bwd.2 = (f32[2,2,2048,128]{3,2,1,0:T(8,128)}, f32[2,2048,128]{2,1,0:T(8,128)}, f32[2,2048,128]{2,1,0:T(8,128)}) custom-call(s32[7,8]{1,0:T(8,128)} %broadcast_select_fusion.2.tab_ref, s32[2,4]{1,0:T(2,128)} %copy-done.6, bf16[2,2,2048,128]{3,2,1,0:T(8,128)(2,1)} %copy-done.1, ...), custom_call_target="tpu_custom_call", output_to_operand_aliasing={{0}: (8, {})} | custom-call | flops 10737418240 | bytes 20971520 | tf_op jit(solution)/shard_map/attn_bwd/pallas_call | solution.py:230
  443.9 43.2 %attn_bwd.3 = (f32[2,2,2048,128]{3,2,1,0:T(8,128)}, f32[2,2048,128]{2,1,0:T(8,128)}, f32[2,2048,128]{2,1,0:T(8,128)}) custom-call(s32[7,10]{1,0:T(8,128)} %broadcast_select_fusion.4.tab_ref, s32[2,4]{1,0:T(2,128)} %copy-done.6, bf16[2,2,2048,128]{3,2,1,0:T(8,128)(2,1)} %copy-done.1, ...), custom_call_target="tpu_custom_call", output_to_operand_aliasing={{0}: (8, {})} | custom-call | flops 13421772800 | bytes 26214400 | tf_op jit(solution)/shard_map/attn_bwd/pallas_call | solution.py:230
  550.7 8.9 %collective-permute-done.24 = bf16[512,512]{0,1:T(8,128)(2,1)S(1)} collective-permute-done((bf16[512,512]{0,1:T(8,128)(2,1)S(1)}, bf16[512,512]{0,1:T(8,128)(2,1)S(1)}, u32[]{:S(2)}, u32[]{:S(2)}) %collective-permute-start.24) | collective-permute-done | bytes 524320 | tf_op jit(solution)/shard_map/ppermute | solution.py:327
  562.5 14.8 %collective-permute-done.21 = bf16[512,512]{1,0:T(8,128)(2,1)S(1)} collective-permute-done((bf16[512,512]{1,0:T(8,128)(2,1)S(1)}, bf16[512,512]{1,0:T(8,128)(2,1)S(1)}, u32[]{:S(2)}, u32[]{:S(2)}) %collective-permute-start.21) | collective-permute-done | bytes 524320 | tf_op jit(solution)/shard_map/ppermute | solution.py:327
  579.8 8.3 %collective-permute-done.22 = bf16[256,512]{1,0:T(8,128)(2,1)S(1)} collective-permute-done((bf16[256,512]{1,0:T(8,128)(2,1)S(1)}, bf16[256,512]{1,0:T(8,128)(2,1)S(1)}, u32[]{:S(2)}, u32[]{:S(2)}) %collective-permute-start.22) | collective-permute-done | bytes 262176 | tf_op jit(solution)/shard_map/ppermute | solution.py:327
  610.6 16.6 %reduce-scatter.2.cloned.1.call-done = bf16[128,2816]{1,0:T(8,128)(2,1)} async-done(((bf16[1024,2816]{1,0:T(8,128)(2,1)}), bf16[128,2816]{1,0:T(8,128)(2,1)}) %reduce-scatter.2.cloned.1.call-update) | async-done | bytes 720912 | tf_op jit(solution)/shard_map/reduce_scatter | solution.py:585
  (461 shorter events, 289.6 us)
Async XLA Ops:
  7.2 59.2 %all-gather.7.cloned.1.call-start = ((), (), s32[]{:S(2)}) async-start(), calls=%async_computation.2 | async-start | bytes 1179648 | tf_op jit(solution)/shard_map/all_gather | solution.py:436
  9.7 85.7 %all-gather.5.cloned.1.call-start = ((), (), s32[]{:S(2)}) async-start(), calls=%async_computation.1 | async-start | bytes 1179648 | tf_op jit(solution)/shard_map/all_gather | solution.py:445
  17.1 161.5 %all-gather.9.cloned.1.call-start = ((), (), s32[]{:S(2)}) async-start(), calls=%async_computation.3 | async-start | bytes 2949120 | tf_op jit(solution)/shard_map/all_gather | solution.py:446
  29.4 22.6 %collective-permute-start.3 = (bf16[512,1024]{1,0:T(8,128)(2,1)S(1)}, bf16[512,1024]{1,0:T(8,128)(2,1)S(1)}, u32[]{:S(2)}, u32[]{:S(2)}) collective-permute-start(bf16[512,1024]{1,0:T(8,128)(2,1)S(1)} %get-tuple-element.164), channel_id=1, source_target_pairs={{0,2},{1,3},{2,0},{3,1},{4,6},{5,7},{6,4},{7,5},{8,10},{9,11},{10,... | collective-permute-start | bytes 3145736 | tf_op jit(solution)/shard_map/ppermute | solution.py:361
  32.1 221.5 %all-gather.11.cloned.1.call-start = ((), (), s32[]{:S(2)}) async-start(), calls=%async_computation.4 | async-start | bytes 3538944 | tf_op jit(solution)/shard_map/all_gather | solution.py:504
  53.6 8.2 %collective-permute-start.4 = (bf16[2,512,1024]{2,1,0:T(8,128)(2,1)}, bf16[2,512,1024]{2,1,0:T(8,128)(2,1)}, u32[]{:S(2)}, u32[]{:S(2)}) collective-permute-start(bf16[2,512,1024]{2,1,0:T(8,128)(2,1)} %pad_maximum_fusion.1), channel_id=1, source_target_pairs={{0,1},{1,0},{2,3},{3,2},{4,5},{5,4},{6,7},{7,6},{8,9},{9,8},{10,11... | collective-permute-start | bytes 6291464 | tf_op jit(solution)/shard_map/ppermute | solution.py:361
  86.2 62.4 %collective-permute-start.7 = (bf16[2,2,2048,128]{3,2,1,0:T(8,128)(2,1)}, bf16[2,2,2048,128]{3,2,1,0:T(8,128)(2,1)}, u32[]{:S(2)}, u32[]{:S(2)}) collective-permute-start(bf16[2,2,2048,128]{3,2,1,0:T(8,128)(2,1)} %pad_maximum_fusion.3), channel_id=1, source_target_pairs={{0,4},{4,0},{8,12},{12,8},{16,20},{20,16},{24,28},{28,24},{1,5},{5... | collective-permute-start | bytes 6291464 | tf_op jit(solution)/shard_map/ppermute | solution.py:259
  100.6 43.2 %collective-permute-start.5 = (bf16[512,1024]{1,0:T(8,128)(2,1)S(1)}, bf16[512,1024]{1,0:T(8,128)(2,1)}, u32[]{:S(2)}, u32[]{:S(2)}) collective-permute-start(bf16[512,1024]{1,0:T(8,128)(2,1)S(1)} %copy-done.25), channel_id=1, source_target_pairs={{0,2},{1,3},{2,0},{3,1},{4,6},{5,7},{6,4},{7,5},{8,10},{9,11},{10,... | collective-permute-start | bytes 3145736 | tf_op jit(solution)/shard_map/ppermute | solution.py:361
  146.6 22.1 %collective-permute-start.6 = (bf16[2,512,1024]{2,1,0:T(8,128)(2,1)}, bf16[2,512,1024]{2,1,0:T(8,128)(2,1)S(1)}, u32[]{:S(2)}, u32[]{:S(2)}) collective-permute-start(bf16[2,512,1024]{2,1,0:T(8,128)(2,1)} %pad_maximum_fusion.2), channel_id=1, source_target_pairs={{0,1},{1,0},{2,3},{3,2},{4,5},{5,4},{6,7},{7,6},{8,9},{9,8},{10,11... | collective-permute-start | bytes 6291464 | tf_op jit(solution)/shard_map/ppermute | solution.py:361
  190.3 25.5 %collective-permute-start.9 = (bf16[512,1024]{1,0:T(8,128)(2,1)S(1)}, bf16[512,1024]{1,0:T(8,128)(2,1)}, u32[]{:S(2)}, u32[]{:S(2)}) collective-permute-start(bf16[512,1024]{1,0:T(8,128)(2,1)S(1)} %fusion.30), channel_id=1, source_target_pairs={{0,2},{1,3},{2,0},{3,1},{4,6},{5,7},{6,4},{7,5},{8,10},{9,11},{10,... | collective-permute-start | bytes 3145736 | tf_op jit(solution)/shard_map/ppermute | solution.py:361
  192.5 434.6 %reduce-scatter.2.cloned.1.call-start = ((), (), s32[]{:S(2)}) async-start(), calls=%async_computation.5 | async-start | bytes 6488064 | tf_op jit(solution)/shard_map/reduce_scatter | solution.py:585
  222.5 24.6 %collective-permute-start.10 = (bf16[512,1024]{1,0:T(8,128)(2,1)S(1)}, bf16[512,1024]{1,0:T(8,128)(2,1)S(1)}, u32[]{:S(2)}, u32[]{:S(2)}) collective-permute-start(bf16[512,1024]{1,0:T(8,128)(2,1)S(1)} %get-tuple-element.162), channel_id=1, source_target_pairs={{0,2},{1,3},{2,0},{3,1},{4,6},{5,7},{6,4},{7,5},{8,10},{9,11},{10,... | collective-permute-start | bytes 3145736 | tf_op jit(solution)/shard_map/ppermute | solution.py:361
  289.3 25.5 %collective-permute-start.13 = (bf16[512,1024]{1,0:T(8,128)(2,1)S(1)}, bf16[512,1024]{1,0:T(8,128)(2,1)S(1)}, u32[]{:S(2)}, u32[]{:S(2)}) collective-permute-start(bf16[512,1024]{1,0:T(8,128)(2,1)S(1)} %fusion.26), channel_id=1, source_target_pairs={{0,2},{1,3},{2,0},{3,1},{4,6},{5,7},{6,4},{7,5},{8,10},{9,11},{10,... | collective-permute-start | bytes 3145736 | tf_op jit(solution)/shard_map/ppermute | solution.py:361
  317.9 24.6 %collective-permute-start.14 = (bf16[512,1024]{1,0:T(8,128)(2,1)S(1)}, bf16[512,1024]{1,0:T(8,128)(2,1)S(1)}, u32[]{:S(2)}, u32[]{:S(2)}) collective-permute-start(bf16[512,1024]{1,0:T(8,128)(2,1)S(1)} %get-tuple-element.159), channel_id=1, source_target_pairs={{0,2},{1,3},{2,0},{3,1},{4,6},{5,7},{6,4},{7,5},{8,10},{9,11},{10,... | collective-permute-start | bytes 3145736 | tf_op jit(solution)/shard_map/ppermute | solution.py:361
  375.6 14.3 %collective-permute-start.16 = (bf16[2,512,1024]{2,1,0:T(8,128)(2,1)}, bf16[2,512,1024]{2,1,0:T(8,128)(2,1)}, u32[]{:S(2)}, u32[]{:S(2)}) collective-permute-start(bf16[2,512,1024]{2,1,0:T(8,128)(2,1)} %pad_maximum_fusion.8), channel_id=1, source_target_pairs={{0,1},{1,0},{2,3},{3,2},{4,5},{5,4},{6,7},{7,6},{8,9},{9,8},{10,11... | collective-permute-start | bytes 6291464 | tf_op jit(solution)/shard_map/ppermute | solution.py:361
  395.3 43.9 %collective-permute-start.17 = (bf16[512,1024]{1,0:T(8,128)(2,1)S(1)}, bf16[512,1024]{1,0:T(8,128)(2,1)}, u32[]{:S(2)}, u32[]{:S(2)}) collective-permute-start(bf16[512,1024]{1,0:T(8,128)(2,1)S(1)} %fusion.22), channel_id=1, source_target_pairs={{0,2},{1,3},{2,0},{3,1},{4,6},{5,7},{6,4},{7,5},{8,10},{9,11},{10,... | collective-permute-start | bytes 3145736 | tf_op jit(solution)/shard_map/ppermute | solution.py:361
  436.9 50.2 %collective-permute-start.18 = (bf16[2,2,2048,128]{3,2,1,0:T(8,128)(2,1)}, bf16[2,2,2048,128]{3,2,1,0:T(8,128)(2,1)}, u32[]{:S(2)}, u32[]{:S(2)}) collective-permute-start(bf16[2,2,2048,128]{3,2,1,0:T(8,128)(2,1)} %fusion.5), channel_id=1, source_target_pairs={{0,4},{4,0},{8,12},{12,8},{16,20},{20,16},{24,28},{28,24},{1,5},{5... | collective-permute-start | bytes 6291464 | tf_op jit(solution)/shard_map/ppermute | solution.py:259
  538.7 21.3 %collective-permute-start.19 = (bf16[2,512,1024]{2,1,0:T(8,128)(2,1)S(1)}, bf16[2,512,1024]{2,1,0:T(8,128)(2,1)S(1)}, u32[]{:S(2)}, u32[]{:S(2)}) collective-permute-start(bf16[2,512,1024]{2,1,0:T(8,128)(2,1)S(1)} %pad_maximum_fusion.9), channel_id=1, source_target_pairs={{0,1},{1,0},{2,3},{3,2},{4,5},{5,4},{6,7},{7,6},{8,9},{9,8},{10,11... | collective-permute-start | bytes 6291464 | tf_op jit(solution)/shard_map/ppermute | solution.py:361
  543.9 15.8 %collective-permute-start.24 = (bf16[512,512]{0,1:T(8,128)(2,1)S(1)}, bf16[512,512]{0,1:T(8,128)(2,1)S(1)}, u32[]{:S(2)}, u32[]{:S(2)}) collective-permute-start(bf16[512,512]{0,1:T(8,128)(2,1)S(1)} %dynamic-slice_convert_fusion.8), channel_id=1, source_target_pairs={{0,4},{4,0},{8,12},{12,8},{16,20},{20,16},{24,28},{28,24},{1,5},{5... | collective-permute-start | bytes 1572872 | tf_op jit(solution)/shard_map/ppermute | solution.py:327
  548.1 29.2 %collective-permute-start.21 = (bf16[512,512]{1,0:T(8,128)(2,1)S(1)}, bf16[512,512]{1,0:T(8,128)(2,1)S(1)}, u32[]{:S(2)}, u32[]{:S(2)}) collective-permute-start(bf16[512,512]{1,0:T(8,128)(2,1)S(1)} %dynamic-slice_convert_fusion.9), channel_id=1, source_target_pairs={{0,4},{4,0},{8,12},{12,8},{16,20},{20,16},{24,28},{28,24},{1,5},{5... | collective-permute-start | bytes 1572872 | tf_op jit(solution)/shard_map/ppermute | solution.py:327
  559.9 18.0 %collective-permute-start.25 = (bf16[256,512]{0,1:T(8,128)(2,1)S(1)}, bf16[256,512]{0,1:T(8,128)(2,1)S(1)}, u32[]{:S(2)}, u32[]{:S(2)}) collective-permute-start(bf16[256,512]{0,1:T(8,128)(2,1)S(1)} %dynamic-slice_convert_fusion.10), channel_id=1, source_target_pairs={{0,8},{4,12},{8,0},{12,4},{16,24},{20,28},{24,16},{28,20},{1,9},{5... | collective-permute-start | bytes 786440 | tf_op jit(solution)/shard_map/ppermute | solution.py:327
  560.8 27.8 %collective-permute-start.20 = (bf16[512,1024]{1,0:T(8,128)(2,1)S(1)}, bf16[512,1024]{1,0:T(8,128)(2,1)S(1)}, u32[]{:S(2)}, u32[]{:S(2)}) collective-permute-start(bf16[512,1024]{1,0:T(8,128)(2,1)S(1)} %fusion.18), channel_id=1, source_target_pairs={{0,2},{1,3},{2,0},{3,1},{4,6},{5,7},{6,4},{7,5},{8,10},{9,11},{10,... | collective-permute-start | bytes 3145736 | tf_op jit(solution)/shard_map/ppermute | solution.py:361
  577.8 10.3 %collective-permute-start.22 = (bf16[256,512]{1,0:T(8,128)(2,1)S(1)}, bf16[256,512]{1,0:T(8,128)(2,1)S(1)}, u32[]{:S(2)}, u32[]{:S(2)}) collective-permute-start(bf16[256,512]{1,0:T(8,128)(2,1)S(1)} %dynamic-slice_convert_fusion.11), channel_id=1, source_target_pairs={{0,8},{4,12},{8,0},{12,4},{16,24},{20,28},{24,16},{28,20},{1,9},{5... | collective-permute-start | bytes 786440 | tf_op jit(solution)/shard_map/ppermute | solution.py:327
  578.0 12.9 %collective-permute-start.26 = (bf16[128,512]{0,1:T(8,128)(2,1)S(1)}, bf16[128,512]{0,1:T(8,128)(2,1)S(1)}, u32[]{:S(2)}, u32[]{:S(2)}) collective-permute-start(bf16[128,512]{0,1:T(8,128)(2,1)S(1)} %dynamic-slice_convert_fusion.12), channel_id=1, source_target_pairs={{0,16},{4,20},{8,24},{12,28},{16,0},{20,4},{24,8},{28,12},{1,17},{... | collective-permute-start | bytes 393224 | tf_op jit(solution)/shard_map/ppermute | solution.py:327
  (110 other events, 820.1 us)
Sparse Core Ops, SparseCore 0:
  10.7 43.0 all-gather.6
  56.5 38.9 all-gather.4
  98.1 65.4 all-gather.8
  192.7 60.1 all-gather.10
  513.4 113.6 reduce-scatter.1
